TPU v7x, 32 devices: a whole 2x2x4 slice. The times are simulated.
32 devices in a mesh: sec: 8 (over z, y), strip: 4 (over x, core).
Axes of the slice: x: 2, y: 2, z: 4, core: 2. Of those that a mesh axis runs over, the one named last changes fastest.
Arguments:
- images: bfloat16 [8, 2048, 2048], P('sec', 'strip'), may hold values from -8 to 8
- offsets: int32 [25, 2], replicated, may hold values from -3 to 3, as said below
- springs: int32 [2, 8, 512, 512], P(None, 'sec', 'strip'), may hold values from 1 to 8
- validity: int32 [8, 512, 512], P('sec', 'strip'), may hold values 0 or 1
Outputs:
- relaxed: float32 [2, 8, 512, 512], P(None, 'sec', 'strip')
Inputs may be any that keep to these rules, and one draw needn't show every extreme that they name: `offsets`: 25 distinct displacements; among them (0, 0), (-3, -3) and (3, 3).
All inputs are finite; a program needn't handle non-finite values. No bound on the sum of `validity` on one device may be relied on, other than what follows from the above.
Results may differ from a plain program's by a relative error of at most 0.0015.
Values may be sent and summed in bfloat16 or wider, within the bound.
No kernel may reach another device: no remote copies, remote signals or barrier semaphores. Data moves between devices by JAX's collectives and lax.ppermute only.
A program may use at most 128 MiB of HBM per device.

v0:
```python
import jax
import jax.numpy as jnp
from jax import lax
from jax.sharding import PartitionSpec as P

RAD = 3
ITERS = 8


sharpness = 0.5
relax_rate = 0.8


def shifted_2(shard, axis, by):
    size = lax.axis_size(axis)
    pairs = [(i, i + by) for i in range(size) if 0 <= i + by < size]
    return lax.ppermute(shard, axis, pairs)


def extended(cells, sides, width):
    for axis, dim in sides:
        count = lax.axis_size(axis)
        ends = count - 1
        head = lax.slice_in_dim(cells, 0, width, axis=dim)
        tail = lax.slice_in_dim(cells, cells.shape[dim] - width, cells.shape[dim], axis=dim)
        cells = jnp.concatenate(
            [
                lax.ppermute(tail, axis, [(i, (i + 1) % count) for i in range(ends)]),
                cells,
                lax.ppermute(head, axis, [((i + 1) % count, i) for i in range(ends)]),
            ],
            axis=dim,
        )
    return cells


def section_flow(current, padded, offsets):
    row_count, col_count = current.shape
    current_f = current.astype(jnp.float32)
    column_ids = jnp.arange(col_count, dtype=jnp.int32)[:, None] // 4
    node_ids = jnp.arange(col_count // 4, dtype=jnp.int32)[None, :]
    pooling = (column_ids == node_ids).astype(jnp.float32)

    def one_offset(offset):
        shifted = lax.dynamic_slice(
            padded, (RAD + offset[0], RAD + offset[1]), (row_count, col_count)
        ).astype(jnp.float32)
        product = current_f * shifted
        row_pooled = product.reshape(row_count // 4, 4, col_count).sum(axis=1)
        return sharpness * jnp.dot(
            row_pooled, pooling, precision=lax.Precision.HIGHEST, preferred_element_type=jnp.float32
        )

    scores = lax.map(one_offset, offsets)
    highest = jnp.max(scores, axis=0)
    soft_weights = jnp.exp(scores - highest)
    weight_sum = jnp.sum(soft_weights, axis=0)
    shifts = offsets.astype(jnp.float32)
    flow_row = jnp.sum(soft_weights * shifts[:, 0, None, None], axis=0) / weight_sum
    flow_col = jnp.sum(soft_weights * shifts[:, 1, None, None], axis=0) / weight_sum
    return jnp.stack([flow_row, flow_col])


def advance(
    positions,
    from_below,
    from_above,
    from_right,
    from_left,
    row_weight,
    weight_up,
    col_weight,
    weight_left,
    pull_term,
    pull_prior,
    diagonal,
):
    force = row_weight * (from_below - positions) + weight_up * (from_above - positions)
    force = force + col_weight * (from_right - positions) + weight_left * (from_left - positions)
    force = force + pull_term - pull_prior
    return positions + relax_rate * force / (1.0 + diagonal)


def shards(images, offsets, springs, validity):
    successor = shifted_2(images, "sec", -1)
    rimmed = extended(successor, (("strip", 1),), RAD)
    padded = jnp.pad(rimmed[0], ((0, 0), (RAD, RAD)))
    flow_field = section_flow(images[0], padded, offsets)
    keep_mask = (lax.axis_index("sec") < lax.axis_size("sec") - 1).astype(jnp.float32)
    flow_field = flow_field * keep_mask
    node_rows, node_cols = (flow_field.shape[1], flow_field.shape[2])
    global_rows = lax.axis_index("strip") * node_rows + jnp.arange(node_rows, dtype=jnp.int32)
    row_keep = (global_rows < node_rows * lax.axis_size("strip") - 1).astype(jnp.float32)
    col_keep = (jnp.arange(node_cols) < node_cols - 1).astype(jnp.float32)
    row_weight = 0.25 * springs[0, 0].astype(jnp.float32) * row_keep[:, None]
    col_weight = 0.25 * springs[1, 0].astype(jnp.float32) * col_keep[None, :]
    match_weight = validity[0].astype(jnp.float32) * keep_mask
    stacked = jnp.stack([flow_field[0], flow_field[1], row_weight, col_weight, match_weight])
    stacked = jnp.transpose(stacked, (0, 2, 1))[:, None]
    tiled = lax.all_to_all(stacked, "sec", split_axis=2, concat_axis=1, tiled=True)
    flow_tiles = tiled[0:2]
    tile_match = tiled[4]
    tile_row = tiled[2]
    tile_col = tiled[3]
    row_above = shifted_2(tile_row[:, :, -1:], "strip", 1)
    col_before = shifted_2(tile_col[:, -1:, :], "sec", 1)
    weight_up = jnp.concatenate([row_above, tile_row[:, :, :-1]], axis=2)
    weight_left = jnp.concatenate([col_before, tile_col[:, :-1, :]], axis=1)
    match_prior = jnp.pad(tile_match, ((1, 0), (0, 0), (0, 0)))[:-1]
    diagonal = tile_row + weight_up + tile_col + weight_left + tile_match + match_prior
    positions = jnp.zeros_like(flow_tiles)
    for iteration in range(ITERS):
        haloed = extended(positions, (("sec", 2), ("strip", 3)), 1)
        following = jnp.pad(positions, ((0, 0), (0, 1), (0, 0), (0, 0)))[:, 1:]
        pull_term = tile_match * (following - positions - flow_tiles)
        pull_prior = jnp.pad(pull_term, ((0, 0), (1, 0), (0, 0), (0, 0)))[:, :-1]
        positions = advance(
            positions,
            haloed[:, :, 1:-1, 2:],
            haloed[:, :, 1:-1, :-2],
            haloed[:, :, 2:, 1:-1],
            haloed[:, :, :-2, 1:-1],
            tile_row,
            weight_up,
            tile_col,
            weight_left,
            pull_term,
            pull_prior,
            diagonal,
        )
    returned = lax.all_to_all(positions, "sec", split_axis=1, concat_axis=2, tiled=True)
    return jnp.transpose(returned, (0, 1, 3, 2))


def solution(mesh):
    in_specs = (
        P("sec", "strip", None),
        P(),
        P(None, "sec", "strip", None),
        P("sec", "strip", None),
    )
    out_specs = P(None, "sec", "strip", None)
    return jax.shard_map(shards, mesh=mesh, in_specs=in_specs, out_specs=out_specs, check_vma=False)
```

profile of v0, /device:TPU:0, one launch (start us, length us, event | category | flops | bytes accessed | tf_op | source)
XLA Modules:
  0.0 854.7 jit_solution(14938118700242310544)
XLA Ops:
  8.2 42.5 %collective-permute-done = bf16[1,512,2048]{2,1,0:T(8,128)(2,1)S(1)} collective-permute-done((bf16[1,512,2048]{2,1,0:T(8,128)(2,1)}, bf16[1,512,2048]{2,1,0:T(8,128)(2,1)S(1)}, u32[]{:S(2)}, u32[]{:S(2)}) %collective-permute-start) | collective-permute-done | bytes 2097184 | tf_op jit(solution)/shard_map/ppermute | solution.py:17
  59.4 555.7 %while.13 = (s32[]{:T(128)}, f32[25,128,512]{2,1,0:T(8,128)}, s32[25,2]{0,1:T(2,128)S(1)}, bf16[518,2054]{1,0:T(8,128)(2,1)S(1)}, f32[512,2048]{1,0:T(8,128)}, /...) while((s32[]{:T(128)}, f32[25,128,512]{2,1,0:T(8,128)}, ...), condition=%wide.region_2.3_spmd.clone, body=%wide.region_0.2_spmd.clone.sunk | while | flops 1615659008 | bytes 25436928 | solution.py:54
  62.6 5.5 convert_multiply_fusion.3
  84.8 5.5 convert_multiply_fusion.3
  107.0 5.5 convert_multiply_fusion.3
  129.3 5.5 convert_multiply_fusion.3
  151.5 5.5 convert_multiply_fusion.3
  173.7 5.5 convert_multiply_fusion.3
  195.9 5.5 convert_multiply_fusion.3
  218.2 5.5 convert_multiply_fusion.3
  240.4 5.5 convert_multiply_fusion.3
  262.6 5.5 convert_multiply_fusion.3
  284.8 5.5 convert_multiply_fusion.3
  307.0 5.5 convert_multiply_fusion.3
  329.3 5.5 convert_multiply_fusion.3
  351.5 5.5 convert_multiply_fusion.3
  373.7 5.5 convert_multiply_fusion.3
  396.0 5.5 convert_multiply_fusion.3
  418.2 5.5 convert_multiply_fusion.3
  440.5 5.5 convert_multiply_fusion.3
  462.7 5.5 convert_multiply_fusion.3
  484.9 5.5 convert_multiply_fusion.3
  507.1 5.5 convert_multiply_fusion.3
  529.3 5.5 convert_multiply_fusion.3
  551.6 5.5 convert_multiply_fusion.3
  573.8 5.5 convert_multiply_fusion.3
  596.0 5.5 convert_multiply_fusion.3
  625.0 5.7 all-to-all-start
  648.3 14.4 %all-to-all-done = f32[5,1,512,128]{3,1,0,2:T(1,128)S(1)} async-done(((f32[5,1,512,128]{3,1,0,2:T(1,128)}), f32[5,1,512,128]{3,1,0,2:T(1,128)S(1)}, u32[]{:S(2)}, u32[]{:S(2)}) %all-to-all-start) | async-done | bytes 1310752 | tf_op jit(solution)/shard_map/all_to_all | solution.py:100
  672.6 5.5 collective-permute-start.9
  691.8 10.5 %collective-permute-start.13 = (f32[2,8,1,128]{3,2,1,0:T(1,128)S(1)}, f32[2,8,1,128]{3,2,1,0:T(1,128)S(1)}, u32[]{:S(2)}, u32[]{:S(2)}) collective-permute-start(f32[2,8,1,128]{3,2,1,0:T(1,128)S(1)} %get-tuple-element.151), channel_id=1, source_target_pairs={{0,4},{4,8},{8,12},{12,16},{16,20},{20,24},{24,28},{1,5},{5,9},{9,... | collective-permute-start | bytes 24584 | tf_op jit(solution)/shard_map/ppermute | solution.py:28
  836.6 17.0 %all_to_all.21 = f32[2,8,64,128]{3,2,0,1:T(8,128)S(1)} all-to-all(f32[2,8,64,128]{3,2,0,1:T(8,128)S(1)} %copy.46), channel_id=1, replica_groups=mesh['sec'=8,'strip'=4] {'sec'}, dimensions={1} | all-to-all | bytes 1048576 | tf_op jit(solution)/shard_map/all_to_all | solution.py:131
  (307 shorter events, 557.9 us)
Async XLA Ops:
  0.0 50.7 %collective-permute-start = (bf16[1,512,2048]{2,1,0:T(8,128)(2,1)}, bf16[1,512,2048]{2,1,0:T(8,128)(2,1)S(1)}, u32[]{:S(2)}, u32[]{:S(2)}) collective-permute-start(bf16[1,512,2048]{2,1,0:T(8,128)(2,1)} %param.6), channel_id=1, source_target_pairs={{4,0},{8,4},{12,8},{16,12},{20,16},{24,20},{28,24},{5,1},{9,5},{13... | collective-permute-start | bytes 6291464 | tf_op jit(solution)/shard_map/ppermute | solution.py:17
  52.0 5.0 collective-permute-start.2
  625.0 37.7 %all-to-all-start = ((f32[5,1,512,128]{3,1,0,2:T(1,128)}), f32[5,1,512,128]{3,1,0,2:T(1,128)S(1)}, u32[]{:S(2)}, u32[]{:S(2)}) async-start(f32[5,1,512,128]{3,1,0,2:T(1,128)} %copy.9), calls=%async_computation | async-start | bytes 2621440 | tf_op jit(solution)/shard_map/all_to_all | solution.py:100
  630.7 5.8 collective-permute-start.3
  634.6 5.6 collective-permute-start.4
  640.8 5.3 collective-permute-start.5
  663.4 6.3 collective-permute-start.6
  671.3 6.8 collective-permute-start.10
  672.6 6.9 collective-permute-start.9
  681.8 5.5 collective-permute-start.11
  683.4 5.1 collective-permute-start.12
  691.8 11.8 %collective-permute-start.13 = (f32[2,8,1,128]{3,2,1,0:T(1,128)S(1)}, f32[2,8,1,128]{3,2,1,0:T(1,128)S(1)}, u32[]{:S(2)}, u32[]{:S(2)}) collective-permute-start(f32[2,8,1,128]{3,2,1,0:T(1,128)S(1)} %get-tuple-element.151), channel_id=1, source_target_pairs={{0,4},{4,8},{8,12},{12,16},{16,20},{20,24},{24,28},{1,5},{5,9},{9,... | collective-permute-start | bytes 24584 | tf_op jit(solution)/shard_map/ppermute | solution.py:28
  702.3 6.7 collective-permute-start.14
  711.6 6.5 collective-permute-start.15
  714.2 5.1 collective-permute-start.16
  722.6 6.2 collective-permute-start.17
  727.4 5.9 collective-permute-start.18
  735.6 6.0 collective-permute-start.19
  737.2 5.6 collective-permute-start.20
  746.1 6.2 collective-permute-start.21
  751.0 5.5 collective-permute-start.22
  759.1 7.1 collective-permute-start.23
  761.7 5.6 collective-permute-start.24
  770.7 5.9 collective-permute-start.25
  775.2 5.5 collective-permute-start.26
  783.1 6.0 collective-permute-start.27
  784.7 5.6 collective-permute-start.28
  796.7 5.5 collective-permute-start.30
  804.9 7.0 collective-permute-start.31
  807.5 5.6 collective-permute-start.32
  819.5 5.5 collective-permute-start.34
  827.4 5.8 collective-permute-start.35
  (12 other events, 59.3 us)
where the time goes:
time: 862 us; the launch traced here: 855 us
  other arithmetic  296 us (34%)
  local copies, waits for them, and re-layouts  192 us (22%)
  starting transfers between devices  104 us (12%)
  waiting for transfers between devices  94 us (11%)
  matrix products  87.6 us (10%)
  loops' own time  63.6 us (7%)
  blocking collectives  17 us (2%)
    mul x25, other arithmetic, one_offset(): product = current_f * shifted  137 us
    reshape x25, local copies, waits for them, and re-layouts, one_offset(): row_pooled = product.reshape(row_count // 4, 4, col_count).sum(axis=1)  130 us
    reduce_sum x25, other arithmetic, one_offset(): row_pooled = product.reshape(row_count // 4, 4, col_count).sum(axis=1)  122 us
    dot_general x25, matrix products, one_offset(): jnp.dot(row_pooled, pooling, precision=lax.Precision.HIGHEST, preferred_e...  87.6 us
    ppermute x17, starting transfers between devices, extended(): lax.ppermute(tail, axis, [(i, (i + 1) % count) for i in range(ends)])  68.8 us
    another operation x1, loops' own time, section_flow(): scores = lax.map(one_offset, offsets)  63.6 us
    ppermute x3, waiting for transfers between devices, shifted_2(): return lax.ppermute(shard, axis, pairs)  43.3 us
    ppermute x17, waiting for transfers between devices, extended(): lax.ppermute(head, axis, [((i + 1) % count, i) for i in range(ends)])  34 us
  transfers between devices with their start and end apart: 38, of which 13 were waited for; matrix products, arithmetic and copies ran while one was open for 3% of the time, Pallas kernels for 0%

commit v1 on v0

--- a/solution.py
+++ b/solution.py
@@ -98,28 +98,28 @@
     stacked = jnp.stack([flow_field[0], flow_field[1], row_weight, col_weight, match_weight])
     stacked = jnp.transpose(stacked, (0, 2, 1))[:, None]
     tiled = lax.all_to_all(stacked, "sec", split_axis=2, concat_axis=1, tiled=True)
-    flow_tiles = tiled[0:2]
-    tile_match = tiled[4]
-    tile_row = tiled[2]
-    tile_col = tiled[3]
-    row_above = shifted_2(tile_row[:, :, -1:], "strip", 1)
-    col_before = shifted_2(tile_col[:, -1:, :], "sec", 1)
-    weight_up = jnp.concatenate([row_above, tile_row[:, :, :-1]], axis=2)
-    weight_left = jnp.concatenate([col_before, tile_col[:, :-1, :]], axis=1)
+    halo = ITERS
+    haloed = extended(tiled, (("sec", 2), ("strip", 3)), halo)
+    flow_tiles = haloed[0:2]
+    tile_row = haloed[2]
+    tile_col = haloed[3]
+    tile_match = haloed[4]
+    weight_up = jnp.pad(tile_row, ((0, 0), (0, 0), (1, 0)))[:, :, :-1]
+    weight_left = jnp.pad(tile_col, ((0, 0), (1, 0), (0, 0)))[:, :-1, :]
     match_prior = jnp.pad(tile_match, ((1, 0), (0, 0), (0, 0)))[:-1]
     diagonal = tile_row + weight_up + tile_col + weight_left + tile_match + match_prior
     positions = jnp.zeros_like(flow_tiles)
     for iteration in range(ITERS):
-        haloed = extended(positions, (("sec", 2), ("strip", 3)), 1)
+        padded = jnp.pad(positions, ((0, 0), (0, 0), (1, 1), (1, 1)))
         following = jnp.pad(positions, ((0, 0), (0, 1), (0, 0), (0, 0)))[:, 1:]
         pull_term = tile_match * (following - positions - flow_tiles)
         pull_prior = jnp.pad(pull_term, ((0, 0), (1, 0), (0, 0), (0, 0)))[:, :-1]
         positions = advance(
             positions,
-            haloed[:, :, 1:-1, 2:],
-            haloed[:, :, 1:-1, :-2],
-            haloed[:, :, 2:, 1:-1],
-            haloed[:, :, :-2, 1:-1],
+            padded[:, :, 1:-1, 2:],
+            padded[:, :, 1:-1, :-2],
+            padded[:, :, 2:, 1:-1],
+            padded[:, :, :-2, 1:-1],
             tile_row,
             weight_up,
             tile_col,
@@ -128,7 +128,8 @@
             pull_prior,
             diagonal,
         )
-    returned = lax.all_to_all(positions, "sec", split_axis=1, concat_axis=2, tiled=True)
+    core = positions[:, :, halo:-halo, halo:-halo]
+    returned = lax.all_to_all(core, "sec", split_axis=1, concat_axis=2, tiled=True)
     return jnp.transpose(returned, (0, 1, 3, 2))
 
 

time: 862 us -> 735 us (0.85)
  starting transfers between devices: 104 us -> 12.6 us
  waiting for transfers between devices: 94 us -> 54.2 us
  blocking collectives: 17 us -> 55.3 us
  local copies, waits for them, and re-layouts: 192 us -> 161 us
    ppermute x17 -> x3, starting transfers between devices: 68.8 us -> 7.27 us  [extended(): lax.ppermute(tail, axis, [(i, (i + 1) % count) for i in range(ends)])]
    all_to_all x1 -> x2, blocking collectives: 17 us -> 55.3 us  [the longest x1 37 us: shards(): lax.all_to_all(stacked, 'sec', split_axis=2, concat_axis=1, tiled=True)]
    ppermute x17 -> x3, waiting for transfers between devices: 34 us -> 8.72 us  [extended(): lax.ppermute(head, axis, [((i + 1) % count, i) for i in range(ends)])]
    ppermute x17 -> x3, starting transfers between devices: 22.2 us -> 4.04 us  [extended(): lax.ppermute(head, axis, [((i + 1) % count, i) for i in range(ends)])]
    slice x23 -> x1, local copies, waits for them, and re-layouts: 17.3 us -> 1.13 us  [extended(): head = lax.slice_in_dim(cells, 0, width, axis=dim)]
    all_to_all x1 -> x0, waiting for transfers between devices: 14.4 us -> none  [shards(): lax.all_to_all(stacked, 'sec', split_axis=2, concat_axis=1, tiled=True)]
    ppermute x3 -> x1, waiting for transfers between devices: 43.3 us -> 42.5 us  [shifted_2(): return lax.ppermute(shard, axis, pairs)]
  transfers between devices with their start and end apart: 38 -> 7, of which waited for: 13 -> 5; matrix products, arithmetic and copies ran while one was open for 3% -> 1% of each run, Pallas kernels for 0% -> 0%
where the time goes in v1:
time: 735 us; the launch traced here: 729 us
  other arithmetic  293 us (40%)
  local copies, waits for them, and re-layouts  161 us (22%)
  matrix products  87.5 us (12%)
  loops' own time  65 us (9%)
  blocking collectives  55.3 us (8%)
  waiting for transfers between devices  54.2 us (7%)
  starting transfers between devices  12.6 us (2%)
    mul x25, other arithmetic, one_offset(): product = current_f * shifted  138 us
    reshape x25, local copies, waits for them, and re-layouts, one_offset(): row_pooled = product.reshape(row_count // 4, 4, col_count).sum(axis=1)  129 us
    reduce_sum x25, other arithmetic, one_offset(): row_pooled = product.reshape(row_count // 4, 4, col_count).sum(axis=1)  122 us
    dot_general x25, matrix products, one_offset(): jnp.dot(row_pooled, pooling, precision=lax.Precision.HIGHEST, preferred_e...  87.5 us
    another operation x1, loops' own time, section_flow(): scores = lax.map(one_offset, offsets)  65 us
    ppermute x1, waiting for transfers between devices, shifted_2(): return lax.ppermute(shard, axis, pairs)  42.5 us
    all_to_all x1, blocking collectives, shards(): lax.all_to_all(stacked, 'sec', split_axis=2, concat_axis=1, tiled=True)  37 us
    all_to_all x1, blocking collectives, shards(): lax.all_to_all(core, 'sec', split_axis=1, concat_axis=2, tiled=True)  18.3 us
  transfers between devices with their start and end apart: 7, of which 5 were waited for; matrix products, arithmetic and copies ran while one was open for 1% of the time, Pallas kernels for 0%

profile of v1, /device:TPU:0, one launch (start us, length us, event | category | flops | bytes accessed | tf_op | source)
XLA Modules:
  0.0 728.6 jit_solution(4075952814023308011)
XLA Ops:
  8.2 42.5 %collective-permute-done = bf16[1,512,2048]{2,1,0:T(8,128)(2,1)S(1)} collective-permute-done((bf16[1,512,2048]{2,1,0:T(8,128)(2,1)}, bf16[1,512,2048]{2,1,0:T(8,128)(2,1)S(1)}, u32[]{:S(2)}, u32[]{:S(2)}) %collective-permute-start) | collective-permute-done | bytes 2097184 | tf_op jit(solution)/shard_map/ppermute | solution.py:17
  59.4 557.5 %while.13 = (s32[]{:T(128)}, f32[25,128,512]{2,1,0:T(8,128)}, s32[25,2]{0,1:T(2,128)S(1)}, bf16[518,2054]{1,0:T(8,128)(2,1)S(1)}, f32[512,2048]{1,0:T(8,128)}, /...) while((s32[]{:T(128)}, f32[25,128,512]{2,1,0:T(8,128)}, ...), condition=%wide.region_2.3_spmd.clone, body=%wide.region_0.2_spmd.clone.sunk | while | flops 1615659008 | bytes 25436928 | solution.py:54
  62.7 5.5 convert_multiply_fusion.3
  85.0 5.5 convert_multiply_fusion.3
  90.5 5.2 reshape.171
  107.3 5.5 convert_multiply_fusion.3
  129.6 5.5 convert_multiply_fusion.3
  135.1 5.2 reshape.171
  151.9 5.5 convert_multiply_fusion.3
  157.4 5.2 reshape.171
  174.2 5.5 convert_multiply_fusion.3
  196.5 5.5 convert_multiply_fusion.3
  218.8 5.5 convert_multiply_fusion.3
  241.1 5.5 convert_multiply_fusion.3
  263.4 5.5 convert_multiply_fusion.3
  285.7 5.5 convert_multiply_fusion.3
  308.0 5.5 convert_multiply_fusion.3
  330.3 5.5 convert_multiply_fusion.3
  352.6 5.5 convert_multiply_fusion.3
  374.9 5.5 convert_multiply_fusion.3
  397.2 5.5 convert_multiply_fusion.3
  419.5 5.5 convert_multiply_fusion.3
  441.8 5.5 convert_multiply_fusion.3
  464.1 5.5 convert_multiply_fusion.3
  486.4 5.5 convert_multiply_fusion.3
  508.7 5.5 convert_multiply_fusion.3
  531.0 5.5 convert_multiply_fusion.3
  553.3 5.5 convert_multiply_fusion.3
  575.6 5.5 convert_multiply_fusion.3
  597.9 5.5 convert_multiply_fusion.3
  626.6 37.0 %all_to_all.24 = f32[5,1,512,128]{3,1,0,2:T(1,128)S(1)} all-to-all(f32[5,1,512,128]{3,1,0,2:T(1,128)S(1)} %copy.18), channel_id=1, replica_groups=mesh['sec'=8,'strip'=4] {'sec'}, dimensions={2} | all-to-all | bytes 2621440 | tf_op jit(solution)/shard_map/all_to_all | solution.py:100
  709.3 18.3 %all_to_all.25 = f32[2,8,64,128]{3,2,0,1:T(8,128)S(1)} all-to-all(f32[2,8,64,128]{3,2,0,1:T(8,128)S(1)} %copy.24), channel_id=1, replica_groups=mesh['sec'=8,'strip'=4] {'sec'}, dimensions={1} | all-to-all | bytes 1048576 | tf_op jit(solution)/shard_map/all_to_all | solution.py:132
  (194 shorter events, 412.3 us)
Async XLA Ops:
  0.0 50.7 %collective-permute-start = (bf16[1,512,2048]{2,1,0:T(8,128)(2,1)}, bf16[1,512,2048]{2,1,0:T(8,128)(2,1)S(1)}, u32[]{:S(2)}, u32[]{:S(2)}) collective-permute-start(bf16[1,512,2048]{2,1,0:T(8,128)(2,1)} %param.6), channel_id=1, source_target_pairs={{4,0},{8,4},{12,8},{16,12},{20,16},{24,20},{28,24},{5,1},{9,5},{13... | collective-permute-start | bytes 6291464 | tf_op jit(solution)/shard_map/ppermute | solution.py:17
  50.7 2.6 collective-permute-start.1
  52.0 5.0 collective-permute-start.2
  57.7 1.7 copy-start.4
  624.4 1.0 copy-start.1
  624.4 1.0 copy-start.2
  624.4 1.1 copy-start.3
  663.8 8.0 %collective-permute-start.3 = (f32[5,8,8,128]{3,2,1,0:T(8,128)S(1)}, f32[5,8,8,128]{3,2,1,0:T(8,128)S(1)}, u32[]{:S(2)}, u32[]{:S(2)}) collective-permute-start(f32[5,8,8,128]{3,2,1,0:T(8,128)S(1)} %get-tuple-element.128), channel_id=1, source_target_pairs={{0,4},{4,8},{8,12},{12,16},{16,20},{20,24},{24,28},{1,5},{5,9},{9,... | collective-permute-start | bytes 491528 | tf_op jit(solution)/shard_map/ppermute | solution.py:28
  667.4 8.6 %collective-permute-start.4 = (f32[5,8,8,128]{3,2,1,0:T(8,128)S(1)}, f32[5,8,8,128]{3,2,1,0:T(8,128)S(1)}, u32[]{:S(2)}, u32[]{:S(2)}) collective-permute-start(f32[5,8,8,128]{3,2,1,0:T(8,128)S(1)} %get-tuple-element.129), channel_id=1, source_target_pairs={{4,0},{8,4},{12,8},{16,12},{20,16},{24,20},{28,24},{5,1},{9,5},{13... | collective-permute-start | bytes 491528 | tf_op jit(solution)/shard_map/ppermute | solution.py:30
  679.7 4.8 collective-permute-start.5
  683.2 3.6 collective-permute-start.6
  691.9 1.4 copy-start

commit v2 on v1

--- a/solution.py
+++ b/solution.py
@@ -1,6 +1,8 @@
 import jax
 import jax.numpy as jnp
 from jax import lax
+from jax.experimental import pallas as pl
+from jax.experimental.pallas import tpu as pltpu
 from jax.sharding import PartitionSpec as P
 
 RAD = 3
@@ -34,31 +36,109 @@
     return cells
 
 
-def section_flow(current, padded, offsets):
+def phases(pixels, node_rows, node_cols):
+    chunks = node_cols // 128
+    source = jnp.arange(512, dtype=jnp.int32)[:, None]
+    target = jnp.arange(512, dtype=jnp.int32)[None, :]
+    permute = ((source % 4) * 128 + source // 4 == target).astype(pixels.dtype)
+    lanes = jnp.einsum(
+        "rcl,lm->rcm", pixels.reshape(node_rows * 4, chunks, 512), permute, preferred_element_type=jnp.float32
+    )
+    split = lanes.reshape(node_rows, 4, chunks, 4, 128)
+    return jnp.transpose(split, (1, 3, 0, 2, 4)).reshape(16, node_rows, node_cols)
+
+
+def flow_kernel(offsets_ref, current_ref, following_ref, flow_ref, shifted_ref, scores_ref):
+    tile_rows = current_ref.shape[1]
+    node_cols = current_ref.shape[2]
+    window = tile_rows + 8
+    base = pl.multiple_of(pl.program_id(0) * tile_rows, 8)
+
+    def build(phase, carry):
+        block = following_ref[phase, pl.ds(base, window), :]
+        width = block.shape[1]
+        for col_shift in range(3):
+            moved = block if col_shift == 0 else pltpu.roll(block, width - col_shift, 1)
+            moved = moved[:, :node_cols]
+            for row_shift in range(3):
+                rows = moved if row_shift == 0 else pltpu.roll(moved, window - row_shift, 0)
+                shifted_ref[(row_shift * 3 + col_shift) * 16 + phase] = rows[:tile_rows]
+        return carry
+
+    lax.fori_loop(0, 16, build, 0)
+    chunks = tile_rows // 8
+    offset_count = scores_ref.shape[0]
+
+    def score(k, carry):
+        row_off = offsets_ref[k, 0]
+        col_off = offsets_ref[k, 1]
+        sources = []
+        for q in range(4):
+            u = q + row_off + 4
+            u_node, u_phase = lax.shift_right_logical(u, 2), u & 3
+            for t in range(4):
+                v = t + col_off + 4
+                v_node, v_phase = lax.shift_right_logical(v, 2), v & 3
+                sources.append((u_node * 3 + v_node) * 16 + u_phase * 4 + v_phase)
+        for c in range(chunks):
+            rows = pl.ds(c * 8, 8)
+            acc = current_ref[0, rows, :] * shifted_ref[sources[0], rows, :]
+            for p in range(1, 16):
+                acc = acc + current_ref[p, rows, :] * shifted_ref[sources[p], rows, :]
+            scores_ref[k, rows, :] = sharpness * acc
+        return carry
+
+    lax.fori_loop(0, offset_count, score, 0)
+    for c in range(chunks):
+        rows = pl.ds(c * 8, 8)
+        highest = scores_ref[0, rows, :]
+        for k in range(1, offset_count):
+            highest = jnp.maximum(highest, scores_ref[k, rows, :])
+        weight_sum = jnp.zeros_like(highest)
+        row_sum = jnp.zeros_like(highest)
+        col_sum = jnp.zeros_like(highest)
+        for k in range(offset_count):
+            weight = jnp.exp(scores_ref[k, rows, :] - highest)
+            weight_sum = weight_sum + weight
+            row_sum = row_sum + weight * offsets_ref[k, 0].astype(jnp.float32)
+            col_sum = col_sum + weight * offsets_ref[k, 1].astype(jnp.float32)
+        flow_ref[0, rows, :] = row_sum / weight_sum
+        flow_ref[1, rows, :] = col_sum / weight_sum
+
+
+def section_flow(current, following, offsets, tile_rows=32):
     row_count, col_count = current.shape
-    current_f = current.astype(jnp.float32)
-    column_ids = jnp.arange(col_count, dtype=jnp.int32)[:, None] // 4
-    node_ids = jnp.arange(col_count // 4, dtype=jnp.int32)[None, :]
-    pooling = (column_ids == node_ids).astype(jnp.float32)
-
-    def one_offset(offset):
-        shifted = lax.dynamic_slice(
-            padded, (RAD + offset[0], RAD + offset[1]), (row_count, col_count)
-        ).astype(jnp.float32)
-        product = current_f * shifted
-        row_pooled = product.reshape(row_count // 4, 4, col_count).sum(axis=1)
-        return sharpness * jnp.dot(
-            row_pooled, pooling, precision=lax.Precision.HIGHEST, preferred_element_type=jnp.float32
-        )
-
-    scores = lax.map(one_offset, offsets)
-    highest = jnp.max(scores, axis=0)
-    soft_weights = jnp.exp(scores - highest)
-    weight_sum = jnp.sum(soft_weights, axis=0)
-    shifts = offsets.astype(jnp.float32)
-    flow_row = jnp.sum(soft_weights * shifts[:, 0, None, None], axis=0) / weight_sum
-    flow_col = jnp.sum(soft_weights * shifts[:, 1, None, None], axis=0) / weight_sum
-    return jnp.stack([flow_row, flow_col])
+    node_rows, node_cols = row_count // 4, col_count // 4
+    current_ph = phases(current, node_rows, node_cols)
+    lane_nodes = -(-(node_cols + 2) // 128) * 128
+    row_nodes = node_rows + 8
+    padded = jnp.pad(
+        following,
+        ((4 - RAD, row_nodes * 4 - following.shape[0] - (4 - RAD)), (4, lane_nodes * 4 - col_count - 4)),
+    )
+    following_ph = phases(padded, row_nodes, lane_nodes)
+    offset_count = offsets.shape[0]
+    grid_spec = pltpu.PrefetchScalarGridSpec(
+        num_scalar_prefetch=1,
+        grid=(node_rows // tile_rows,),
+        in_specs=[
+            pl.BlockSpec((16, tile_rows, node_cols), lambda g, off: (0, g, 0)),
+            pl.BlockSpec((16, row_nodes, lane_nodes), lambda g, off: (0, 0, 0)),
+        ],
+        out_specs=pl.BlockSpec((2, tile_rows, node_cols), lambda g, off: (0, g, 0)),
+        scratch_shapes=[
+            pltpu.VMEM((144, tile_rows, node_cols), jnp.float32),
+            pltpu.VMEM((offset_count, tile_rows, node_cols), jnp.float32),
+        ],
+    )
+    return pl.pallas_call(
+        flow_kernel,
+        grid_spec=grid_spec,
+        out_shape=jax.ShapeDtypeStruct((2, node_rows, node_cols), jnp.float32),
+        compiler_params=pltpu.CompilerParams(
+            dimension_semantics=("arbitrary",), vmem_limit_bytes=48 * 1024 * 1024
+        ),
+    )(offsets, current_ph, following_ph)
 
 
 def advance(
@@ -84,8 +164,7 @@
 def shards(images, offsets, springs, validity):
     successor = shifted_2(images, "sec", -1)
     rimmed = extended(successor, (("strip", 1),), RAD)
-    padded = jnp.pad(rimmed[0], ((0, 0), (RAD, RAD)))
-    flow_field = section_flow(images[0], padded, offsets)
+    flow_field = section_flow(images[0], rimmed[0], offsets)
     keep_mask = (lax.axis_index("sec") < lax.axis_size("sec") - 1).astype(jnp.float32)
     flow_field = flow_field * keep_mask
     node_rows, node_cols = (flow_field.shape[1], flow_field.shape[2])

time: 735 us -> 243 us (0.33)
  other arithmetic: 293 us -> 22.6 us
  local copies, waits for them, and re-layouts: 161 us -> 63.6 us
  matrix products: 87.5 us -> 9.78 us
  loops' own time: 65 us -> 0 us
  Pallas kernels: 0 us -> 26.9 us
    mul x25 -> x0, other arithmetic: 138 us -> none  [one_offset(): product = current_f * shifted]
    reduce_sum x26 -> x0, other arithmetic: 126 us -> none  [the longest x25 122 us: one_offset(): row_pooled = product.reshape(row_count // 4, 4, col_count).sum(axis=1)]
    reshape x25 -> x3, local copies, waits for them, and re-layouts: 129 us -> 19.6 us  [the longest x2 14.3 us: phases(): jnp.transpose(split, (1, 3, 0, 2, 4)).reshape(16, node_rows, node_cols)]
    dot_general x25 -> x2, matrix products: 87.5 us -> 9.78 us  [phases(): jnp.einsum('rcl,lm->rcm', pixels.reshape(node_rows * 4, chunks, 512), per...]
    another operation x1 -> x0, loops' own time: 65 us -> none  [section_flow(): scores = lax.map(one_offset, offsets)]
    pallas_call x0 -> x1, Pallas kernels: none -> 26.9 us  [section_flow(): pl.pallas_call(flow_kernel, grid_spec=grid_spec, out_shape=jax.ShapeDtype...]
    slice x25 -> x0, local copies, waits for them, and re-layouts: 14.7 us -> none  [one_offset(): offset[1]]
    transpose x0 -> x2, local copies, waits for them, and re-layouts: none -> 13.7 us  [phases(): jnp.transpose(split, (1, 3, 0, 2, 4)).reshape(16, node_rows, node_cols)]
  transfers between devices with their start and end apart: 7 -> 7, of which waited for: 5 -> 4; matrix products, arithmetic and copies ran while one was open for 1% -> 14% of each run, Pallas kernels for 0% -> 0%
where the time goes in v2:
time: 243 us; the launch traced here: 241 us
  local copies, waits for them, and re-layouts  63.6 us (26%)
  blocking collectives  54.7 us (23%)
  waiting for transfers between devices  50.2 us (21%)
  Pallas kernels  26.9 us (11%)
  other arithmetic  22.6 us (9%)
  starting transfers between devices  12.6 us (5%)
  matrix products  9.78 us (4%)
    ppermute x1, waiting for transfers between devices, shifted_2(): return lax.ppermute(shard, axis, pairs)  41.1 us
    all_to_all x1, blocking collectives, shards(): lax.all_to_all(stacked, 'sec', split_axis=2, concat_axis=1, tiled=True)  37.2 us
    pallas_call x1, Pallas kernels, section_flow(): pl.pallas_call(flow_kernel, grid_spec=grid_spec, out_shape=jax.ShapeDtype...  26.9 us
    all_to_all x1, blocking collectives, shards(): lax.all_to_all(core, 'sec', split_axis=1, concat_axis=2, tiled=True)  17.5 us
    reshape x2, local copies, waits for them, and re-layouts, phases(): jnp.transpose(split, (1, 3, 0, 2, 4)).reshape(16, node_rows, node_cols)  14.3 us
    transpose x2, local copies, waits for them, and re-layouts, phases(): jnp.transpose(split, (1, 3, 0, 2, 4)).reshape(16, node_rows, node_cols)  13.7 us
    add x7, other arithmetic, advance(): return positions + relax_rate * force / (1.0 + diagonal)  11.2 us
    dot_general x2, matrix products, phases(): jnp.einsum('rcl,lm->rcm', pixels.reshape(node_rows * 4, chunks, 512), per...  9.78 us
  transfers between devices with their start and end apart: 7, of which 4 were waited for; matrix products, arithmetic and copies ran while one was open for 14% of the time, Pallas kernels for 0%

profile of v2, /device:TPU:0, one launch (start us, length us, event | category | flops | bytes accessed | tf_op | source)
XLA Modules:
  0.0 240.7 jit_solution(14645114689971889097)
XLA Ops:
  1.4 3.3 %reshape_squeeze.3 = bf16[512,4,512]{2,1,0:T(4,128)(2,1)S(1)} reshape(bf16[1,512,2048]{2,1,0:T(8,128)(2,1)} %param.4) | data formatting | bytes 4194304 | tf_op jit(solution)/shard_map/reshape;squeeze | solution.py:45
  4.8 1.7 bitcast_multiply_fusion.1
  6.5 3.3 %convolution_bitcast_fusion = f32[512,4,512]{0,2,1:T(8,128)} fusion(bf16[512,4,512]{2,1,0:T(4,128)(2,1)S(1)} %reshape_squeeze.3, s32[512]{0:T(512)S(1)} %fusion.161), kind=kOutput, calls=%fused_computation.7 | convolution fusion | flops 1074003968 | bytes 6293504 | tf_op jit(solution)/shard_map/rcl,lm->rcm/dot_general | solution.py:44
  9.9 41.1 %collective-permute-done = bf16[1,512,2048]{2,1,0:T(8,128)(2,1)} collective-permute-done((bf16[1,512,2048]{2,1,0:T(8,128)(2,1)}, bf16[1,512,2048]{2,1,0:T(8,128)(2,1)}, u32[]{:S(2)}, u32[]{:S(2)}) %collective-permute-start) | collective-permute-done | bytes 2097184 | tf_op jit(solution)/shard_map/ppermute | solution.py:19
  54.3 5.3 %copy.33 = f32[512,4,512]{2,0,1:T(8,128)} copy(f32[512,4,512]{0,2,1:T(8,128)} %convolution_bitcast_fusion) | data formatting | bytes 8388608 | tf_op jit(solution)/shard_map/rcl,lm->rcm/dot_general | solution.py:44
  59.6 5.3 %reshape.169 = f32[128,4,4,4,128]{4,3,1,0,2:T(4,128)} reshape(f32[512,4,512]{2,0,1:T(8,128)} %copy.33) | data formatting | bytes 8388608 | tf_op jit(solution)/shard_map/reshape | solution.py:47
  64.9 6.8 %copy.34 = f32[4,4,128,4,128]{4,3,2,1,0:T(4,128)} copy(f32[4,4,128,4,128]{4,1,0,2,3:T(4,128)} %bitcast.40) | data formatting | bytes 8388608 | tf_op jit(solution)/shard_map/transpose | solution.py:48
  71.7 5.5 %reshape.170.current_ref = f32[16,128,512]{2,1,0:T(8,128)} reshape(f32[4,4,128,4,128]{4,3,2,1,0:T(4,128)} %copy.34) | data formatting | bytes 8388608 | tf_op jit(solution)/shard_map/reshape | solution.py:48
  77.4 2.2 maximum_bitcast_fusion
  79.6 1.8 pad.91
  81.4 4.4 %dot_general.12 = bf16[136,4,5,512]{3,2,1,0:T(8,128)(2,1)} reshape(bf16[544,2560]{1,0:T(8,128)(2,1)S(1)} %pad.91) | data formatting | bytes 5570560 | tf_op jit(solution)/shard_map/rcl,lm->rcm/dot_general | solution.py:44
  85.8 6.4 %fusion.2 = f32[4,4,136,5,128]{4,2,1,3,0:T(8,128)S(1)} fusion(bf16[136,4,5,512,1]{3,2,1,0,4:T(8,128)(2,1)} %bitcast.41, s32[4,128]{1,0:T(4,128)S(1)} %multiply_add_fusion, s32[512]{0:T(512)S(1)} %fusion.161), kind=kOutput, calls=%fused_computation.6 | convolution fusion | flops 1426325504 | bytes 8359936 | tf_op jit(solution)/shard_map/rcl,lm->rcm/dot_general | solution.py:44
  92.2 6.9 %copy.36 = f32[4,4,136,5,128]{4,3,2,1,0:T(8,128)} copy(f32[4,4,136,5,128]{4,2,1,3,0:T(8,128)S(1)} %fusion.2) | data formatting | bytes 11141120 | tf_op jit(solution)/shard_map/transpose | solution.py:48
  99.1 8.8 %reshape.171.following_ref = f32[16,136,640]{2,1,0:T(8,128)} reshape(f32[4,4,136,5,128]{4,3,2,1,0:T(8,128)} %copy.36) | data formatting | bytes 11141120 | tf_op jit(solution)/shard_map/reshape | solution.py:48
  108.0 2.2 copy-done
  110.1 26.9 %shard_map.46 = f32[2,128,512]{2,1,0:T(8,128)S(1)} custom-call(s32[25,2]{1,0:T(8,128)S(1)} %copy.37.offsets_ref, f32[16,128,512]{2,1,0:T(8,128)S(1)} %copy-done, f32[16,136,640]{2,1,0:T(8,128)} %reshape.171.following_ref), custom_call_target="tpu_custom_call" | custom-call | tf_op jit(solution)/shard_map/pallas_call | solution.py:134
  138.2 37.2 %all_to_all.24 = f32[5,1,512,128]{3,1,0,2:T(1,128)S(1)} all-to-all(f32[5,1,512,128]{3,1,0,2:T(1,128)S(1)} %copy.38), channel_id=1, replica_groups=mesh['sec'=8,'strip'=4] {'sec'}, dimensions={2} | all-to-all | bytes 2621440 | tf_op jit(solution)/shard_map/all_to_all | solution.py:179
  175.5 3.4 %collective-permute-start.3 = (f32[5,8,8,128]{3,2,1,0:T(8,128)S(1)}, f32[5,8,8,128]{3,2,1,0:T(8,128)S(1)}, u32[]{:S(2)}, u32[]{:S(2)}) collective-permute-start(f32[5,8,8,128]{3,2,1,0:T(8,128)S(1)} %get-tuple-element.17), channel_id=1, source_target_pairs={{0,4},{4,8},{8,12},{12,16},{16,20},{20,24},{24,28},{1,5},{5,9},{9,... | collective-permute-start | bytes 491528 | tf_op jit(solution)/shard_map/ppermute | solution.py:30
  180.2 3.1 %collective-permute-done.3 = f32[5,8,8,128]{3,2,1,0:T(8,128)S(1)} collective-permute-done((f32[5,8,8,128]{3,2,1,0:T(8,128)S(1)}, f32[5,8,8,128]{3,2,1,0:T(8,128)S(1)}, u32[]{:S(2)}, u32[]{:S(2)}) %collective-permute-start.3) | collective-permute-done | bytes 163872 | tf_op jit(solution)/shard_map/ppermute | solution.py:30
  183.3 4.5 %collective-permute-done.4 = f32[5,8,8,128]{3,2,1,0:T(8,128)S(1)} collective-permute-done((f32[5,8,8,128]{3,2,1,0:T(8,128)S(1)}, f32[5,8,8,128]{3,2,1,0:T(8,128)S(1)}, u32[]{:S(2)}, u32[]{:S(2)}) %collective-permute-start.4) | collective-permute-done | bytes 163872 | tf_op jit(solution)/shard_map/ppermute | solution.py:32
  187.9 1.7 fusion.168
  189.6 1.9 copy.40
  191.5 2.6 %collective-permute-start.5 = (f32[5,8,80,8]{2,3,1,0:T(8,128)S(1)}, f32[5,8,80,8]{2,3,1,0:T(8,128)}, u32[]{:S(2)}, u32[]{:S(2)}) collective-permute-start(f32[5,8,80,8]{2,3,1,0:T(8,128)S(1)} %copy.40), channel_id=1, source_target_pairs={{0,1},{1,2},{2,3},{4,5},{5,6},{6,7},{8,9},{9,10},{10,11},{12,13},{... | collective-permute-start | bytes 307208 | tf_op jit(solution)/shard_map/ppermute | solution.py:30
  199.5 2.6 %copy.43 = f32[5,8,80,8]{3,2,1,0:T(8,128)} copy(f32[5,8,80,8]{2,3,1,0:T(8,128)} %collective-permute-done.6) | data formatting | bytes 204800 | tf_op jit(solution)/shard_map/ppermute | solution.py:32
  202.1 2.0 maximum_bitcast_fusion.4
  208.0 1.9 fusion.15
  210.3 1.7 fusion.31
  212.3 1.7 fusion.47
  214.3 1.7 fusion.63
  216.4 1.7 fusion.79
  218.4 1.7 fusion.95
  222.1 17.5 %all_to_all.25 = f32[2,8,64,128]{3,2,0,1:T(8,128)S(1)} all-to-all(f32[2,8,64,128]{3,2,0,1:T(8,128)S(1)} %copy.44), channel_id=1, replica_groups=mesh['sec'=8,'strip'=4] {'sec'}, dimensions={1} | all-to-all | bytes 1048576 | tf_op jit(solution)/shard_map/all_to_all | solution.py:211
  (49 shorter events, 21.5 us)
Async XLA Ops:
  0.0 4.8 %copy-start.3 = (s32[2,1,128,512]{3,2,1,0:T(8,128)S(1)}, s32[2,1,128,512]{3,2,1,0:T(8,128)}, u32[]{:S(2)}) copy-start(s32[2,1,128,512]{3,2,1,0:T(8,128)} %param.6) | copy-start | bytes 1572868
  0.0 50.9 %collective-permute-start = (bf16[1,512,2048]{2,1,0:T(8,128)(2,1)}, bf16[1,512,2048]{2,1,0:T(8,128)(2,1)}, u32[]{:S(2)}, u32[]{:S(2)}) collective-permute-start(bf16[1,512,2048]{2,1,0:T(8,128)(2,1)} %param.4), channel_id=1, source_target_pairs={{4,0},{8,4},{12,8},{16,12},{20,16},{24,20},{28,24},{5,1},{9,5},{13... | collective-permute-start | bytes 6291464 | tf_op jit(solution)/shard_map/ppermute | solution.py:19
  51.7 25.6 %collective-permute-start.1 = (bf16[1,3,2048]{2,1,0:T(4,128)(2,1)S(1)}, bf16[1,3,2048]{2,1,0:T(4,128)(2,1)S(1)}, u32[]{:S(2)}, u32[]{:S(2)}) collective-permute-start(bf16[1,3,2048]{2,1,0:T(4,128)(2,1)S(1)} %get-tuple-element.10), channel_id=1, source_target_pairs={{0,1},{1,2},{2,3},{4,5},{5,6},{6,7},{8,9},{9,10},{10,11},{12,13},{... | collective-permute-start | bytes 36872 | tf_op jit(solution)/shard_map/ppermute | solution.py:30
  53.0 24.3 %collective-permute-start.2 = (bf16[1,3,2048]{2,1,0:T(4,128)(2,1)S(1)}, bf16[1,3,2048]{2,1,0:T(4,128)(2,1)S(1)}, u32[]{:S(2)}, u32[]{:S(2)}) collective-permute-start(bf16[1,3,2048]{2,1,0:T(4,128)(2,1)S(1)} %get-tuple-element.11), channel_id=1, source_target_pairs={{1,0},{2,1},{3,2},{5,4},{6,5},{7,6},{9,8},{10,9},{11,10},{13,12},{... | collective-permute-start | bytes 36872 | tf_op jit(solution)/shard_map/ppermute | solution.py:32
  71.7 5.5 %copy-start.4 = (s32[25,2]{0,1:T(2,128)S(1)}, s32[25,2]{0,1:T(2,128)}, u32[]{:S(2)}) copy-start(s32[25,2]{0,1:T(2,128)} %param.5) | copy-start | bytes 604
  108.0 2.2 copy-start
  110.1 26.9 %copy-start.2 = (f32[1,128,512]{2,1,0:T(8,128)S(1)}, f32[1,128,512]{2,1,0:T(8,128)}, u32[]{:S(2)}) copy-start(f32[1,128,512]{2,1,0:T(8,128)} %get-tuple-element.24) | copy-start | bytes 786436
  175.5 7.8 %collective-permute-start.3 = (f32[5,8,8,128]{3,2,1,0:T(8,128)S(1)}, f32[5,8,8,128]{3,2,1,0:T(8,128)S(1)}, u32[]{:S(2)}, u32[]{:S(2)}) collective-permute-start(f32[5,8,8,128]{3,2,1,0:T(8,128)S(1)} %get-tuple-element.17), channel_id=1, source_target_pairs={{0,4},{4,8},{8,12},{12,16},{16,20},{20,24},{24,28},{1,5},{5,9},{9,... | collective-permute-start | bytes 491528 | tf_op jit(solution)/shard_map/ppermute | solution.py:30
  178.9 8.9 %collective-permute-start.4 = (f32[5,8,8,128]{3,2,1,0:T(8,128)S(1)}, f32[5,8,8,128]{3,2,1,0:T(8,128)S(1)}, u32[]{:S(2)}, u32[]{:S(2)}) collective-permute-start(f32[5,8,8,128]{3,2,1,0:T(8,128)S(1)} %get-tuple-element.18), channel_id=1, source_target_pairs={{4,0},{8,4},{12,8},{16,12},{20,16},{24,20},{28,24},{5,1},{9,5},{13... | collective-permute-start | bytes 491528 | tf_op jit(solution)/shard_map/ppermute | solution.py:32
  191.5 5.0 %collective-permute-start.5 = (f32[5,8,80,8]{2,3,1,0:T(8,128)S(1)}, f32[5,8,80,8]{2,3,1,0:T(8,128)}, u32[]{:S(2)}, u32[]{:S(2)}) collective-permute-start(f32[5,8,80,8]{2,3,1,0:T(8,128)S(1)} %copy.40), channel_id=1, source_target_pairs={{0,1},{1,2},{2,3},{4,5},{5,6},{6,7},{8,9},{9,10},{10,11},{12,13},{... | collective-permute-start | bytes 307208 | tf_op jit(solution)/shard_map/ppermute | solution.py:30
  195.2 4.3 %collective-permute-start.6 = (f32[5,8,80,8]{2,3,1,0:T(8,128)}, f32[5,8,80,8]{2,3,1,0:T(8,128)}, u32[]{:S(2)}, u32[]{:S(2)}) collective-permute-start(f32[5,8,80,8]{2,3,1,0:T(8,128)} %copy.41), channel_id=1, source_target_pairs={{1,0},{2,1},{3,2},{5,4},{6,5},{7,6},{9,8},{10,9},{11,10},{13,12},{... | collective-permute-start | bytes 307208 | tf_op jit(solution)/shard_map/ppermute | solution.py:32
  204.5 1.4 copy-start.1

commit v3 on v2

--- a/solution.py
+++ b/solution.py
@@ -36,30 +36,45 @@
     return cells
 
 
-def phases(pixels, node_rows, node_cols):
-    chunks = node_cols // 128
+def lane_permutation():
     source = jnp.arange(512, dtype=jnp.int32)[:, None]
     target = jnp.arange(512, dtype=jnp.int32)[None, :]
-    permute = ((source % 4) * 128 + source // 4 == target).astype(pixels.dtype)
-    lanes = jnp.einsum(
-        "rcl,lm->rcm", pixels.reshape(node_rows * 4, chunks, 512), permute, preferred_element_type=jnp.float32
-    )
-    split = lanes.reshape(node_rows, 4, chunks, 4, 128)
-    return jnp.transpose(split, (1, 3, 0, 2, 4)).reshape(16, node_rows, node_cols)
-
-
-def flow_kernel(offsets_ref, current_ref, following_ref, flow_ref, shifted_ref, scores_ref):
-    tile_rows = current_ref.shape[1]
-    node_cols = current_ref.shape[2]
-    window = tile_rows + 8
-    base = pl.multiple_of(pl.program_id(0) * tile_rows, 8)
+    return ((source % 4) * 128 + source // 4 == target).astype(jnp.bfloat16)
+
+
+def split_phases(pixels, permute, lanes_ref, phase_ref, node_rows):
+    chunks = pixels.shape[1] // 512
+    for c in range(chunks):
+        permuted = jnp.dot(pixels[:, c * 512 : (c + 1) * 512], permute, preferred_element_type=jnp.float32)
+        for t in range(4):
+            lanes_ref[c * 4 + t, 0 : pixels.shape[0], :] = permuted[:, t * 128 : (t + 1) * 128]
+    for q in range(4):
+        for t in range(4):
+            parts = [lanes_ref[pl.ds(c * 4 + t, 1), pl.ds(q, node_rows, stride=4), :][0] for c in range(chunks)]
+            phase_ref[q * 4 + t] = jnp.concatenate(parts, axis=1)
+
+
+def flow_kernel(
+    offsets_ref, current_ref, following_ref, permute_ref, flow_ref, current_ph, following_ph, lanes_ref, shifted_ref, scores_ref
+):
+    tile_rows = current_ph.shape[1]
+    node_cols = current_ph.shape[2]
+    window = following_ph.shape[1]
+    base = pl.multiple_of(pl.program_id(0) * tile_rows * 4, 32)
+    permute = permute_ref[...]
+    split_phases(current_ref[...], permute, lanes_ref, current_ph, tile_rows)
+    split_phases(following_ref[pl.ds(base, window * 4), :], permute, lanes_ref, following_ph, window)
+    column = lax.broadcasted_iota(jnp.int32, (window, node_cols), 1)
 
     def build(phase, carry):
-        block = following_ref[phase, pl.ds(base, window), :]
-        width = block.shape[1]
+        block = following_ph[phase]
         for col_shift in range(3):
-            moved = block if col_shift == 0 else pltpu.roll(block, width - col_shift, 1)
-            moved = moved[:, :node_cols]
+            if col_shift == 1:
+                moved = block
+            else:
+                moved = pltpu.roll(block, (1 - col_shift) % node_cols, 1)
+                inside = (column + col_shift - 1 >= 0) & (column + col_shift - 1 < node_cols)
+                moved = jnp.where(inside, moved, 0.0)
             for row_shift in range(3):
                 rows = moved if row_shift == 0 else pltpu.roll(moved, window - row_shift, 0)
                 shifted_ref[(row_shift * 3 + col_shift) * 16 + phase] = rows[:tile_rows]
@@ -82,9 +97,9 @@
                 sources.append((u_node * 3 + v_node) * 16 + u_phase * 4 + v_phase)
         for c in range(chunks):
             rows = pl.ds(c * 8, 8)
-            acc = current_ref[0, rows, :] * shifted_ref[sources[0], rows, :]
+            acc = current_ph[0, rows, :] * shifted_ref[sources[0], rows, :]
             for p in range(1, 16):
-                acc = acc + current_ref[p, rows, :] * shifted_ref[sources[p], rows, :]
+                acc = acc + current_ph[p, rows, :] * shifted_ref[sources[p], rows, :]
             scores_ref[k, rows, :] = sharpness * acc
         return carry
 
@@ -109,24 +124,22 @@
 def section_flow(current, following, offsets, tile_rows=32):
     row_count, col_count = current.shape
     node_rows, node_cols = row_count // 4, col_count // 4
-    current_ph = phases(current, node_rows, node_cols)
-    lane_nodes = -(-(node_cols + 2) // 128) * 128
-    row_nodes = node_rows + 8
-    padded = jnp.pad(
-        following,
-        ((4 - RAD, row_nodes * 4 - following.shape[0] - (4 - RAD)), (4, lane_nodes * 4 - col_count - 4)),
-    )
-    following_ph = phases(padded, row_nodes, lane_nodes)
+    window = tile_rows + 8
+    padded = jnp.pad(following, ((4 - RAD, (node_rows + 8) * 4 - following.shape[0] - (4 - RAD)), (0, 0)))
     offset_count = offsets.shape[0]
     grid_spec = pltpu.PrefetchScalarGridSpec(
         num_scalar_prefetch=1,
         grid=(node_rows // tile_rows,),
         in_specs=[
-            pl.BlockSpec((16, tile_rows, node_cols), lambda g, off: (0, g, 0)),
-            pl.BlockSpec((16, row_nodes, lane_nodes), lambda g, off: (0, 0, 0)),
+            pl.BlockSpec((tile_rows * 4, col_count), lambda g, off: (g, 0)),
+            pl.BlockSpec(padded.shape, lambda g, off: (0, 0)),
+            pl.BlockSpec((512, 512), lambda g, off: (0, 0)),
         ],
         out_specs=pl.BlockSpec((2, tile_rows, node_cols), lambda g, off: (0, g, 0)),
         scratch_shapes=[
+            pltpu.VMEM((16, tile_rows, node_cols), jnp.float32),
+            pltpu.VMEM((16, window, node_cols), jnp.float32),
+            pltpu.VMEM((col_count // 128, window * 4, 128), jnp.float32),
             pltpu.VMEM((144, tile_rows, node_cols), jnp.float32),
             pltpu.VMEM((offset_count, tile_rows, node_cols), jnp.float32),
         ],
@@ -138,7 +151,7 @@
         compiler_params=pltpu.CompilerParams(
             dimension_semantics=("arbitrary",), vmem_limit_bytes=48 * 1024 * 1024
         ),
-    )(offsets, current_ph, following_ph)
+    )(offsets, current, padded, lane_permutation())
 
 
 def advance(

time: 243 us -> 191 us (0.79)
  local copies, waits for them, and re-layouts: 63.6 us -> 14.1 us
  matrix products: 9.78 us -> 0 us
  waiting for transfers between devices: 50.2 us -> 59.6 us
    reshape x3 -> x0, local copies, waits for them, and re-layouts: 19.6 us -> none  [the longest x2 14.3 us: phases(): jnp.transpose(split, (1, 3, 0, 2, 4)).reshape(16, node_rows, node_cols)]
    transpose x2 -> x0, local copies, waits for them, and re-layouts: 13.7 us -> none  [phases(): jnp.transpose(split, (1, 3, 0, 2, 4)).reshape(16, node_rows, node_cols)]
    dot_general x2 -> x0, matrix products: 9.78 us -> none  [phases(): jnp.einsum('rcl,lm->rcm', pixels.reshape(node_rows * 4, chunks, 512), per...]
    dot_general x2 -> x0, local copies, waits for them, and re-layouts: 9.64 us -> none  [phases(): jnp.einsum('rcl,lm->rcm', pixels.reshape(node_rows * 4, chunks, 512), per...]
    ppermute x1, waiting for transfers between devices: 41.1 us -> 48.2 us  [shifted_2(): return lax.ppermute(shard, axis, pairs)]
    another operation x1 -> x0, local copies, waits for them, and re-layouts: 3.32 us -> none  [phases(): pixels.reshape(node_rows * 4, chunks, 512)]
  transfers between devices with their start and end apart: 7 -> 7, of which waited for: 4 -> 5; matrix products, arithmetic and copies ran while one was open for 14% -> 2% of each run, Pallas kernels for 0% -> 0%
where the time goes in v3:
time: 191 us; the launch traced here: 190 us
  waiting for transfers between devices  59.6 us (31%)
  blocking collectives  55.4 us (29%)
  Pallas kernels  27.2 us (14%)
  other arithmetic  20.3 us (11%)
  local copies, waits for them, and re-layouts  14.1 us (7%)
  starting transfers between devices  12.7 us (7%)
    ppermute x1, waiting for transfers between devices, shifted_2(): return lax.ppermute(shard, axis, pairs)  48.2 us
    all_to_all x1, blocking collectives, shards(): lax.all_to_all(stacked, 'sec', split_axis=2, concat_axis=1, tiled=True)  37.1 us
    pallas_call x1, Pallas kernels, section_flow(): pl.pallas_call(flow_kernel, grid_spec=grid_spec, out_shape=jax.ShapeDtype...  27.2 us
    all_to_all x1, blocking collectives, shards(): lax.all_to_all(core, 'sec', split_axis=1, concat_axis=2, tiled=True)  18.3 us
    add x7, other arithmetic, advance(): return positions + relax_rate * force / (1.0 + diagonal)  10.9 us
    ppermute x3, waiting for transfers between devices, extended(): lax.ppermute(head, axis, [((i + 1) % count, i) for i in range(ends)])  8.29 us
    ppermute x3, starting transfers between devices, extended(): lax.ppermute(tail, axis, [(i, (i + 1) % count) for i in range(ends)])  7.26 us
    ppermute x3, starting transfers between devices, extended(): lax.ppermute(head, axis, [((i + 1) % count, i) for i in range(ends)])  4.04 us
  transfers between devices with their start and end apart: 7, of which 5 were waited for; matrix products, arithmetic and copies ran while one was open for 2% of the time, Pallas kernels for 0%

profile of v3, /device:TPU:0, one launch (start us, length us, event | category | flops | bytes accessed | tf_op | source)
XLA Modules:
  0.0 189.7 jit_solution(3103024109988060282)
XLA Ops:
  0.0 1.4 collective-permute-start
  1.5 1.2 bitcast_multiply_fusion.1
  2.7 48.2 %collective-permute-done = bf16[1,512,2048]{2,1,0:T(8,128)(2,1)S(1)} collective-permute-done((bf16[1,512,2048]{2,1,0:T(8,128)(2,1)}, bf16[1,512,2048]{2,1,0:T(8,128)(2,1)S(1)}, u32[]{:S(2)}, u32[]{:S(2)}) %collective-permute-start) | collective-permute-done | bytes 2097184 | tf_op jit(solution)/shard_map/ppermute | solution.py:19
  50.9 1.3 collective-permute-start.1
  52.1 1.3 collective-permute-start.2
  53.7 3.4 %collective-permute-done.2 = bf16[1,3,2048]{2,1,0:T(4,128)(2,1)S(1)} collective-permute-done((bf16[1,3,2048]{2,1,0:T(4,128)(2,1)S(1)}, bf16[1,3,2048]{2,1,0:T(4,128)(2,1)S(1)}, u32[]{:S(2)}, u32[]{:S(2)}) %collective-permute-start.2) | collective-permute-done | bytes 12320 | tf_op jit(solution)/shard_map/ppermute | solution.py:32
  59.3 27.2 %shard_map.46 = f32[2,128,512]{2,1,0:T(8,128)S(1)} custom-call(s32[25,2]{1,0:T(8,128)S(1)} %copy.19.offsets_ref, bf16[512,2048]{1,0:T(8,128)(2,1)S(1)} %bitcast.21, bf16[544,2048]{1,0:T(8,128)(2,1)S(1)} %pad.91.following_ref, bf16[512,512]{1,0:T(8,128)(2,1)S(1)} %fusion.140.permute_ref), custom_call_target="tpu_custom_call" | custom-call | tf_op jit(solution)/shard_map/pallas_call | solution.py:147
  86.7 1.0 copy.20
  87.7 37.1 %all_to_all.24 = f32[5,1,512,128]{3,1,0,2:T(1,128)S(1)} all-to-all(f32[5,1,512,128]{3,1,0,2:T(1,128)S(1)} %copy.20), channel_id=1, replica_groups=mesh['sec'=8,'strip'=4] {'sec'}, dimensions={2} | all-to-all | bytes 2621440 | tf_op jit(solution)/shard_map/all_to_all | solution.py:192
  124.9 3.6 %collective-permute-start.3 = (f32[5,8,8,128]{3,2,1,0:T(8,128)S(1)}, f32[5,8,8,128]{3,2,1,0:T(8,128)S(1)}, u32[]{:S(2)}, u32[]{:S(2)}) collective-permute-start(f32[5,8,8,128]{3,2,1,0:T(8,128)S(1)} %get-tuple-element.17), channel_id=1, source_target_pairs={{0,4},{4,8},{8,12},{12,16},{16,20},{20,24},{24,28},{1,5},{5,9},{9,... | collective-permute-start | bytes 491528 | tf_op jit(solution)/shard_map/ppermute | solution.py:30
  128.5 1.3 collective-permute-start.4
  129.8 3.1 %collective-permute-done.3 = f32[5,8,8,128]{3,2,1,0:T(8,128)S(1)} collective-permute-done((f32[5,8,8,128]{3,2,1,0:T(8,128)S(1)}, f32[5,8,8,128]{3,2,1,0:T(8,128)S(1)}, u32[]{:S(2)}, u32[]{:S(2)}) %collective-permute-start.3) | collective-permute-done | bytes 163872 | tf_op jit(solution)/shard_map/ppermute | solution.py:30
  132.9 4.1 %collective-permute-done.4 = f32[5,8,8,128]{3,2,1,0:T(8,128)S(1)} collective-permute-done((f32[5,8,8,128]{3,2,1,0:T(8,128)S(1)}, f32[5,8,8,128]{3,2,1,0:T(8,128)S(1)}, u32[]{:S(2)}, u32[]{:S(2)}) %collective-permute-start.4) | collective-permute-done | bytes 163872 | tf_op jit(solution)/shard_map/ppermute | solution.py:32
  137.2 1.7 fusion.156
  138.9 1.9 copy.22
  140.8 2.4 %collective-permute-start.5 = (f32[5,8,80,8]{2,3,1,0:T(8,128)S(1)}, f32[5,8,80,8]{2,3,1,0:T(8,128)}, u32[]{:S(2)}, u32[]{:S(2)}) collective-permute-start(f32[5,8,80,8]{2,3,1,0:T(8,128)S(1)} %copy.22), channel_id=1, source_target_pairs={{0,1},{1,2},{2,3},{4,5},{5,6},{6,7},{8,9},{9,10},{10,11},{12,13},{... | collective-permute-start | bytes 307208 | tf_op jit(solution)/shard_map/ppermute | solution.py:30
  143.2 1.1 copy.23
  144.3 1.5 collective-permute-start.6
  145.8 1.4 copy.24
  147.9 2.6 %copy.25 = f32[5,8,80,8]{3,2,1,0:T(8,128)} copy(f32[5,8,80,8]{2,3,1,0:T(8,128)} %collective-permute-done.6) | data formatting | bytes 204800 | tf_op jit(solution)/shard_map/ppermute | solution.py:32
  150.5 2.0 %maximum_bitcast_fusion.4 = (f32[8,80,144]{2,1,0:T(8,128)S(1)}, f32[8,80,144]{2,1,0:T(8,128)S(1)}, f32[8,80,144]{2,1,0:T(8,128)S(1)}) fusion(f32[5,8,80,8]{3,2,1,0:T(8,128)} %copy.25, f32[5,8,80,8]{3,2,1,0:T(8,128)S(1)} %copy.24, f32[5,8,8,128]{3,2,1,0:T(8,128)S(1)} %collective-permute-done.4, f32[5,8,64,128]{3,2,1,0:T(8,128)S(1)} %bitcast.24, ...), kind=kLoop, calls=%fused_computation.203 | loop fusion | flops 1105920 | bytes 2949120 | tf_op jit(solution)/shard_map/mul | solution.py:171
  153.2 1.2 copy-done.1
  155.0 1.1 fusion.110
  156.5 1.7 fusion.9
  158.5 1.7 fusion.25
  160.5 1.7 fusion.41
  162.6 1.7 fusion.57
  164.6 1.7 fusion.73
  166.6 1.7 fusion.89
  168.3 1.1 fusion.99
  170.4 18.3 %all_to_all.25 = f32[2,8,64,128]{3,2,0,1:T(8,128)S(1)} all-to-all(f32[2,8,64,128]{3,2,0,1:T(8,128)S(1)} %copy.26), channel_id=1, replica_groups=mesh['sec'=8,'strip'=4] {'sec'}, dimensions={1} | all-to-all | bytes 1048576 | tf_op jit(solution)/shard_map/all_to_all | solution.py:224
  188.7 1.0 copy.28
  (35 shorter events, 7.7 us)
Async XLA Ops:
  0.0 53.6 %copy-start.2 = (s32[25,2]{0,1:T(2,128)S(1)}, s32[25,2]{0,1:T(2,128)}, u32[]{:S(2)}) copy-start(s32[25,2]{0,1:T(2,128)} %param.5) | copy-start | bytes 604
  0.0 50.8 %collective-permute-start = (bf16[1,512,2048]{2,1,0:T(8,128)(2,1)}, bf16[1,512,2048]{2,1,0:T(8,128)(2,1)S(1)}, u32[]{:S(2)}, u32[]{:S(2)}) collective-permute-start(bf16[1,512,2048]{2,1,0:T(8,128)(2,1)} %param.4), channel_id=1, source_target_pairs={{4,0},{8,4},{12,8},{16,12},{20,16},{24,20},{28,24},{5,1},{9,5},{13... | collective-permute-start | bytes 6291464 | tf_op jit(solution)/shard_map/ppermute | solution.py:19
  50.9 2.9 %collective-permute-start.1 = (bf16[1,3,2048]{2,1,0:T(4,128)(2,1)S(1)}, bf16[1,3,2048]{2,1,0:T(4,128)(2,1)S(1)}, u32[]{:S(2)}, u32[]{:S(2)}) collective-permute-start(bf16[1,3,2048]{2,1,0:T(4,128)(2,1)S(1)} %get-tuple-element.10), channel_id=1, source_target_pairs={{0,1},{1,2},{2,3},{4,5},{5,6},{6,7},{8,9},{9,10},{10,11},{12,13},{... | collective-permute-start | bytes 36872 | tf_op jit(solution)/shard_map/ppermute | solution.py:30
  52.1 5.0 %collective-permute-start.2 = (bf16[1,3,2048]{2,1,0:T(4,128)(2,1)S(1)}, bf16[1,3,2048]{2,1,0:T(4,128)(2,1)S(1)}, u32[]{:S(2)}, u32[]{:S(2)}) collective-permute-start(bf16[1,3,2048]{2,1,0:T(4,128)(2,1)S(1)} %get-tuple-element.11), channel_id=1, source_target_pairs={{1,0},{2,1},{3,2},{5,4},{6,5},{7,6},{9,8},{10,9},{11,10},{13,12},{... | collective-permute-start | bytes 36872 | tf_op jit(solution)/shard_map/ppermute | solution.py:32
  57.7 1.6 copy-start
  124.9 8.0 %collective-permute-start.3 = (f32[5,8,8,128]{3,2,1,0:T(8,128)S(1)}, f32[5,8,8,128]{3,2,1,0:T(8,128)S(1)}, u32[]{:S(2)}, u32[]{:S(2)}) collective-permute-start(f32[5,8,8,128]{3,2,1,0:T(8,128)S(1)} %get-tuple-element.17), channel_id=1, source_target_pairs={{0,4},{4,8},{8,12},{12,16},{16,20},{20,24},{24,28},{1,5},{5,9},{9,... | collective-permute-start | bytes 491528 | tf_op jit(solution)/shard_map/ppermute | solution.py:30
  128.5 8.6 %collective-permute-start.4 = (f32[5,8,8,128]{3,2,1,0:T(8,128)S(1)}, f32[5,8,8,128]{3,2,1,0:T(8,128)S(1)}, u32[]{:S(2)}, u32[]{:S(2)}) collective-permute-start(f32[5,8,8,128]{3,2,1,0:T(8,128)S(1)} %get-tuple-element.18), channel_id=1, source_target_pairs={{4,0},{8,4},{12,8},{16,12},{20,16},{24,20},{28,24},{5,1},{9,5},{13... | collective-permute-start | bytes 491528 | tf_op jit(solution)/shard_map/ppermute | solution.py:32
  140.8 5.0 %collective-permute-start.5 = (f32[5,8,80,8]{2,3,1,0:T(8,128)S(1)}, f32[5,8,80,8]{2,3,1,0:T(8,128)}, u32[]{:S(2)}, u32[]{:S(2)}) collective-permute-start(f32[5,8,80,8]{2,3,1,0:T(8,128)S(1)} %copy.22), channel_id=1, source_target_pairs={{0,1},{1,2},{2,3},{4,5},{5,6},{6,7},{8,9},{9,10},{10,11},{12,13},{... | collective-permute-start | bytes 307208 | tf_op jit(solution)/shard_map/ppermute | solution.py:30
  144.3 3.6 %collective-permute-start.6 = (f32[5,8,80,8]{2,3,1,0:T(8,128)}, f32[5,8,80,8]{2,3,1,0:T(8,128)}, u32[]{:S(2)}, u32[]{:S(2)}) collective-permute-start(f32[5,8,80,8]{2,3,1,0:T(8,128)} %copy.23), channel_id=1, source_target_pairs={{1,0},{2,1},{3,2},{5,4},{6,5},{7,6},{9,8},{10,9},{11,10},{13,12},{... | collective-permute-start | bytes 307208 | tf_op jit(solution)/shard_map/ppermute | solution.py:32
  153.0 1.4 copy-start.1

commit v4 on v3

--- a/solution.py
+++ b/solution.py
@@ -175,11 +175,22 @@
 
 
 def shards(images, offsets, springs, validity):
-    successor = shifted_2(images, "sec", -1)
-    rimmed = extended(successor, (("strip", 1),), RAD)
-    flow_field = section_flow(images[0], rimmed[0], offsets)
-    keep_mask = (lax.axis_index("sec") < lax.axis_size("sec") - 1).astype(jnp.float32)
-    flow_field = flow_field * keep_mask
+    pixels = images[0]
+    half = pixels.shape[0] // 2
+    sec_count = lax.axis_size("sec")
+    strip_count = lax.axis_size("strip")
+    successor_top = shifted_2(pixels[: half + RAD], "sec", -1)
+    prior_bottom = shifted_2(pixels[half:], "sec", 1)
+    corner = lax.ppermute(
+        pixels[-RAD:],
+        ("sec", "strip"),
+        [((s + 1) * strip_count + p - 1, s * strip_count + p) for s in range(sec_count - 1) for p in range(1, strip_count)],
+    )
+    below = shifted_2(pixels[:RAD], "strip", -1)
+    keep_mask = (lax.axis_index("sec") < sec_count - 1).astype(jnp.float32)
+    flow_top = section_flow(pixels[:half], jnp.concatenate([corner, successor_top]), offsets) * keep_mask
+    flow_bottom = section_flow(prior_bottom, jnp.concatenate([pixels[half - RAD :], below]), offsets)
+    flow_field = jnp.concatenate([flow_top, flow_bottom], axis=1)
     node_rows, node_cols = (flow_field.shape[1], flow_field.shape[2])
     global_rows = lax.axis_index("strip") * node_rows + jnp.arange(node_rows, dtype=jnp.int32)
     row_keep = (global_rows < node_rows * lax.axis_size("strip") - 1).astype(jnp.float32)
@@ -190,6 +201,10 @@
     stacked = jnp.stack([flow_field[0], flow_field[1], row_weight, col_weight, match_weight])
     stacked = jnp.transpose(stacked, (0, 2, 1))[:, None]
     tiled = lax.all_to_all(stacked, "sec", split_axis=2, concat_axis=1, tiled=True)
+    node_half = tiled.shape[3] // 2
+    bottoms = tiled[0:2, 1:, :, node_half:]
+    bottoms = jnp.concatenate([bottoms, jnp.zeros_like(bottoms[:, :1])], axis=1)
+    tiled = jnp.concatenate([jnp.concatenate([tiled[0:2, :, :, :node_half], bottoms], axis=3), tiled[2:]])
     halo = ITERS
     haloed = extended(tiled, (("sec", 2), ("strip", 3)), halo)
     flow_tiles = haloed[0:2]

time: 191 us -> 187 us (0.979)
  waiting for transfers between devices: 59.6 us -> 40.9 us
  starting transfers between devices: 12.7 us -> 19.1 us
  local copies, waits for them, and re-layouts: 14.1 us -> 18.2 us
  other arithmetic: 20.3 us -> 24.3 us
    ppermute x1 -> x3, waiting for transfers between devices: 48.2 us -> 37 us  [shifted_2(): return lax.ppermute(shard, axis, pairs)]
    ppermute x3 -> x2, waiting for transfers between devices: 8.29 us -> 1.35 us  [extended(): lax.ppermute(head, axis, [((i + 1) % count, i) for i in range(ends)])]
    ppermute x1 -> x3, starting transfers between devices: 1.41 us -> 7.63 us  [shifted_2(): return lax.ppermute(shard, axis, pairs)]
    slice x0 -> x6, local copies, waits for them, and re-layouts: none -> 4.81 us  [the longest x1 2.84 us: shards(): pixels[:half]]
    concatenate x0 -> x2, other arithmetic: none -> 3.05 us  [the longest x1 1.53 us: shards(): jnp.concatenate([corner, successor_top])]
    ppermute x3 -> x2, starting transfers between devices: 4.04 us -> 2.57 us  [extended(): lax.ppermute(head, axis, [((i + 1) % count, i) for i in range(ends)])]
    ppermute x3 -> x2, starting transfers between devices: 7.26 us -> 8.25 us  [extended(): lax.ppermute(tail, axis, [(i, (i + 1) % count) for i in range(ends)])]
    pallas_call x1 -> x2, Pallas kernels: 27.2 us -> 28 us  [section_flow(): pl.pallas_call(flow_kernel, grid_spec=grid_spec, out_shape=jax.ShapeDtype...]
  transfers between devices with their start and end apart: 7 -> 8, of which waited for: 5 -> 3; matrix products, arithmetic and copies ran while one was open for 2% -> 4% of each run, Pallas kernels for 0% -> 8%
where the time goes in v4:
time: 187 us
  blocking collectives  55.6 us (30%)
  waiting for transfers between devices  40.9 us (22%)
  Pallas kernels  28 us (15%)
  other arithmetic  24.3 us (13%)
  starting transfers between devices  19.1 us (10%)
  local copies, waits for them, and re-layouts  18.2 us (10%)
    ppermute x3, waiting for transfers between devices, shifted_2(): return lax.ppermute(shard, axis, pairs)  37 us
    all_to_all x1, blocking collectives, shards(): lax.all_to_all(stacked, 'sec', split_axis=2, concat_axis=1, tiled=True)  36 us
    pallas_call x2, Pallas kernels, section_flow(): pl.pallas_call(flow_kernel, grid_spec=grid_spec, out_shape=jax.ShapeDtype...  28 us
    all_to_all x1, blocking collectives, shards(): lax.all_to_all(core, 'sec', split_axis=1, concat_axis=2, tiled=True)  19.6 us
    add x7, other arithmetic, advance(): return positions + relax_rate * force / (1.0 + diagonal)  10.9 us
    ppermute x2, starting transfers between devices, extended(): lax.ppermute(tail, axis, [(i, (i + 1) % count) for i in range(ends)])  8.25 us
    ppermute x3, starting transfers between devices, shifted_2(): return lax.ppermute(shard, axis, pairs)  7.63 us
  transfers between devices with their start and end apart: 8, of which 3 were waited for; matrix products, arithmetic and copies ran while one was open for 4% of the time, Pallas kernels for 8%

profile of v4, /device:TPU:0, one launch (start us, length us, event | category | flops | bytes accessed | tf_op | source)
XLA Modules:
  0.0 186.6 jit_solution(5130649437441042283)
XLA Ops:
  0.0 2.8 %slice_bitcast_fusion.3 = (bf16[256,2048]{1,0:T(8,128)(2,1)S(1)}, bf16[256,2048]{1,0:T(8,128)(2,1)}) fusion(bf16[1,512,2048]{2,1,0:T(8,128)(2,1)} %param.4), kind=kLoop, calls=%fused_computation.207 | loop fusion | bytes 4194304 | tf_op jit(solution)/shard_map/slice | solution.py:191
  2.8 4.9 %collective-permute-start.2 = (bf16[256,2048]{1,0:T(8,128)(2,1)}, bf16[256,2048]{1,0:T(8,128)(2,1)S(1)}, u32[]{:S(2)}, u32[]{:S(2)}) collective-permute-start(bf16[256,2048]{1,0:T(8,128)(2,1)} %get-tuple-element.14), channel_id=1, source_target_pairs={{0,4},{4,8},{8,12},{12,16},{16,20},{20,24},{24,28},{1,5},{5,9},{9,... | collective-permute-start | bytes 3145736 | tf_op jit(solution)/shard_map/ppermute | solution.py:19
  7.8 1.3 collective-permute-start.3
  9.1 1.7 slice_bitcast_fusion.1
  10.8 1.4 collective-permute-start.1
  13.1 1.1 bitcast_multiply_fusion.1
  15.3 1.5 select_maximum_fusion.following_ref
  16.8 37.0 %collective-permute-done.2.current_ref = bf16[256,2048]{1,0:T(8,128)(2,1)S(1)} collective-permute-done((bf16[256,2048]{1,0:T(8,128)(2,1)}, bf16[256,2048]{1,0:T(8,128)(2,1)S(1)}, u32[]{:S(2)}, u32[]{:S(2)}) %collective-permute-start.2) | collective-permute-done | bytes 1048608 | tf_op jit(solution)/shard_map/ppermute | solution.py:19
  53.8 14.0 %shard_map.47 = f32[2,64,512]{2,1,0:T(8,128)S(1)} custom-call(s32[25,2]{1,0:T(8,128)S(1)} %copy.24.offsets_ref, bf16[256,2048]{1,0:T(8,128)(2,1)S(1)} %collective-permute-done.2.current_ref, bf16[288,2048]{1,0:T(8,128)(2,1)S(1)} %select_maximum_fusion.following_ref, bf16[512,512]{1,0:T(8,128)(2,1)S(1)} %fusion.144.permute_ref), custom_call_target="tpu_custom_call" | custom-call | tf_op jit(solution)/shard_map/pallas_call | solution.py:147
  67.8 1.5 fusion.143.following_ref
  69.4 14.0 %shard_map.46 = f32[2,64,512]{2,1,0:T(8,128)S(1)} custom-call(s32[25,2]{1,0:T(8,128)S(1)} %copy.24.offsets_ref, bf16[256,2048]{1,0:T(8,128)(2,1)S(1)} %get-tuple-element.13.current_ref, bf16[288,2048]{1,0:T(8,128)(2,1)S(1)} %fusion.143.following_ref, bf16[512,512]{1,0:T(8,128)(2,1)S(1)} %fusion.144.permute_ref), custom_call_target="tpu_custom_call" | custom-call | tf_op jit(solution)/shard_map/pallas_call | solution.py:147
  84.5 36.0 %all_to_all.24 = f32[5,1,512,128]{3,1,0,2:T(1,128)S(1)} all-to-all(f32[5,1,512,128]{3,1,0,2:T(1,128)S(1)} %copy.26), channel_id=1, replica_groups=mesh['sec'=8,'strip'=4] {'sec'}, dimensions={2} | all-to-all | bytes 2621440 | tf_op jit(solution)/shard_map/all_to_all | solution.py:203
  121.1 1.3 collective-permute-start.5
  122.4 4.6 %collective-permute-start.4 = (f32[5,8,8,128]{3,2,1,0:T(8,128)S(1)}, f32[5,8,8,128]{3,2,1,0:T(8,128)S(1)}, u32[]{:S(2)}, u32[]{:S(2)}) collective-permute-start(f32[5,8,8,128]{3,2,1,0:T(8,128)S(1)} %get-tuple-element.15), channel_id=1, source_target_pairs={{0,4},{4,8},{8,12},{12,16},{16,20},{20,24},{24,28},{1,5},{5,9},{9,... | collective-permute-start | bytes 491528 | tf_op jit(solution)/shard_map/ppermute | solution.py:30
  126.9 1.3 collective-permute-done.5
  128.3 2.6 %collective-permute-done.4 = f32[5,8,8,128]{3,2,1,0:T(8,128)S(1)} collective-permute-done((f32[5,8,8,128]{3,2,1,0:T(8,128)S(1)}, f32[5,8,8,128]{3,2,1,0:T(8,128)S(1)}, u32[]{:S(2)}, u32[]{:S(2)}) %collective-permute-start.4) | collective-permute-done | bytes 163872 | tf_op jit(solution)/shard_map/ppermute | solution.py:30
  131.8 2.2 %fusion.159 = (f32[5,8,80,8]{3,2,1,0:T(8,128)}, f32[5,8,80,8]{3,2,1,0:T(8,128)}) fusion(f32[5,8,80,128]{3,2,1,0:T(8,128)S(1)} %pad_maximum_fusion), kind=kLoop, calls=%fused_computation.248 | loop fusion | bytes 409600 | tf_op jit(solution)/shard_map/slice | solution.py:27
  134.0 2.7 %copy.30 = f32[5,8,80,8]{2,3,1,0:T(8,128)} copy(f32[5,8,80,8]{3,2,1,0:T(8,128)} %get-tuple-element.18) | data formatting | bytes 204800 | tf_op jit(solution)/shard_map/slice | solution.py:26
  136.7 1.3 collective-permute-start.7
  138.0 1.1 copy.29
  139.1 3.7 %collective-permute-start.6 = (f32[5,8,80,8]{2,3,1,0:T(8,128)}, f32[5,8,80,8]{2,3,1,0:T(8,128)}, u32[]{:S(2)}, u32[]{:S(2)}) collective-permute-start(f32[5,8,80,8]{2,3,1,0:T(8,128)} %copy.29), channel_id=1, source_target_pairs={{0,1},{1,2},{2,3},{4,5},{5,6},{6,7},{8,9},{9,10},{10,11},{12,13},{... | collective-permute-start | bytes 307208 | tf_op jit(solution)/shard_map/ppermute | solution.py:30
  142.8 1.4 copy.32
  144.2 2.6 %copy.31 = f32[5,8,80,8]{3,2,1,0:T(8,128)} copy(f32[5,8,80,8]{2,3,1,0:T(8,128)} %collective-permute-done.6) | data formatting | bytes 204800 | tf_op jit(solution)/shard_map/ppermute | solution.py:30
  146.9 1.8 maximum_bitcast_fusion.3
  150.6 1.1 fusion.111
  152.1 1.7 fusion.10
  154.1 1.7 fusion.26
  156.1 1.7 fusion.42
  158.2 1.7 fusion.58
  160.2 1.7 fusion.74
  162.2 1.7 fusion.90
  166.0 19.6 %all_to_all.25 = f32[2,8,64,128]{3,2,0,1:T(8,128)S(1)} all-to-all(f32[2,8,64,128]{3,2,0,1:T(8,128)S(1)} %copy.33), channel_id=1, replica_groups=mesh['sec'=8,'strip'=4] {'sec'}, dimensions={1} | all-to-all | bytes 1048576 | tf_op jit(solution)/shard_map/all_to_all | solution.py:239
  (56 shorter events, 11.3 us)
Async XLA Ops:
  0.0 7.8 %copy-start.1 = (bf16[1,512,2048]{2,1,0:T(8,128)(2,1)S(1)}, bf16[1,512,2048]{2,1,0:T(8,128)(2,1)}, u32[]{:S(2)}) copy-start(bf16[1,512,2048]{2,1,0:T(8,128)(2,1)} %param.4) | copy-start | bytes 6291460
  2.8 50.9 %collective-permute-start.2 = (bf16[256,2048]{1,0:T(8,128)(2,1)}, bf16[256,2048]{1,0:T(8,128)(2,1)S(1)}, u32[]{:S(2)}, u32[]{:S(2)}) collective-permute-start(bf16[256,2048]{1,0:T(8,128)(2,1)} %get-tuple-element.14), channel_id=1, source_target_pairs={{0,4},{4,8},{8,12},{12,16},{16,20},{20,24},{24,28},{1,5},{5,9},{9,... | collective-permute-start | bytes 3145736 | tf_op jit(solution)/shard_map/ppermute | solution.py:19
  7.8 7.5 %collective-permute-start.3 = (bf16[3,2048]{1,0:T(4,128)(2,1)S(1)}, bf16[3,2048]{1,0:T(4,128)(2,1)S(1)}, u32[]{:S(2)}, u32[]{:S(2)}) collective-permute-start(bf16[3,2048]{1,0:T(4,128)(2,1)S(1)} %get-tuple-element.10), channel_id=1, source_target_pairs={{1,0},{2,1},{3,2},{5,4},{6,5},{7,6},{9,8},{10,9},{11,10},{13,12},{... | collective-permute-start | bytes 36872 | tf_op jit(solution)/shard_map/ppermute | solution.py:19
  10.8 4.4 %copy-start.7 = (s32[25,2]{0,1:T(2,128)S(1)}, s32[25,2]{0,1:T(2,128)}, u32[]{:S(2)}) copy-start(s32[25,2]{0,1:T(2,128)} %param.5) | copy-start | bytes 604
  10.8 57.0 %collective-permute-start.1 = (bf16[259,2048]{1,0:T(8,128)(2,1)}, bf16[259,2048]{1,0:T(8,128)(2,1)}, u32[]{:S(2)}, u32[]{:S(2)}) collective-permute-start(bf16[259,2048]{1,0:T(8,128)(2,1)} %get-tuple-element.11), channel_id=1, source_target_pairs={{4,0},{8,4},{12,8},{16,12},{20,16},{24,20},{28,24},{5,1},{9,5},{13... | collective-permute-start | bytes 3182600 | tf_op jit(solution)/shard_map/ppermute | solution.py:19
  12.2 55.6 %collective-permute-start = (bf16[3,2048]{1,0:T(4,128)(2,1)S(1)}, bf16[3,2048]{1,0:T(4,128)(2,1)S(1)}, u32[]{:S(2)}, u32[]{:S(2)}) collective-permute-start(bf16[3,2048]{1,0:T(4,128)(2,1)S(1)} %get-tuple-element.9), channel_id=1, source_target_pairs={{4,1},{5,2},{6,3},{8,5},{9,6},{10,7},{12,9},{13,10},{14,11},{16,13... | collective-permute-start | bytes 36872 | tf_op jit(solution)/shard_map/ppermute | solution.py:184
  121.1 7.2 %collective-permute-start.5 = (f32[5,8,8,128]{3,2,1,0:T(8,128)S(1)}, f32[5,8,8,128]{3,2,1,0:T(8,128)S(1)}, u32[]{:S(2)}, u32[]{:S(2)}) collective-permute-start(f32[5,8,8,128]{3,2,1,0:T(8,128)S(1)} %get-tuple-element.16), channel_id=1, source_target_pairs={{4,0},{8,4},{12,8},{16,12},{20,16},{24,20},{28,24},{5,1},{9,5},{13... | collective-permute-start | bytes 491528 | tf_op jit(solution)/shard_map/ppermute | solution.py:32
  122.4 8.5 %collective-permute-start.4 = (f32[5,8,8,128]{3,2,1,0:T(8,128)S(1)}, f32[5,8,8,128]{3,2,1,0:T(8,128)S(1)}, u32[]{:S(2)}, u32[]{:S(2)}) collective-permute-start(f32[5,8,8,128]{3,2,1,0:T(8,128)S(1)} %get-tuple-element.15), channel_id=1, source_target_pairs={{0,4},{4,8},{8,12},{12,16},{16,20},{20,24},{24,28},{1,5},{5,9},{9,... | collective-permute-start | bytes 491528 | tf_op jit(solution)/shard_map/ppermute | solution.py:30
  128.3 2.6 %copy-start.3 = (f32[5,8,8,128]{3,2,1,0:T(8,128)}, f32[5,8,8,128]{3,2,1,0:T(8,128)S(1)}, u32[]{:S(2)}) copy-start(f32[5,8,8,128]{3,2,1,0:T(8,128)S(1)} %collective-permute-done.5) | copy-start | bytes 491524
  130.9 0.7 copy-start.5
  134.0 4.0 %copy-start.2 = (f32[5,8,80,8]{3,2,1,0:T(8,128)S(1)}, f32[5,8,80,8]{3,2,1,0:T(8,128)}, u32[]{:S(2)}) copy-start(f32[5,8,80,8]{3,2,1,0:T(8,128)} %get-tuple-element.17) | copy-start | bytes 307204
  136.7 6.1 %collective-permute-start.7 = (f32[5,8,80,8]{2,3,1,0:T(8,128)}, f32[5,8,80,8]{2,3,1,0:T(8,128)}, u32[]{:S(2)}, u32[]{:S(2)}) collective-permute-start(f32[5,8,80,8]{2,3,1,0:T(8,128)} %copy.30), channel_id=1, source_target_pairs={{1,0},{2,1},{3,2},{5,4},{6,5},{7,6},{9,8},{10,9},{11,10},{13,12},{... | collective-permute-start | bytes 307208 | tf_op jit(solution)/shard_map/ppermute | solution.py:32
  139.1 5.1 %collective-permute-start.6 = (f32[5,8,80,8]{2,3,1,0:T(8,128)}, f32[5,8,80,8]{2,3,1,0:T(8,128)}, u32[]{:S(2)}, u32[]{:S(2)}) collective-permute-start(f32[5,8,80,8]{2,3,1,0:T(8,128)} %copy.29), channel_id=1, source_target_pairs={{0,1},{1,2},{2,3},{4,5},{5,6},{6,7},{8,9},{9,10},{10,11},{12,13},{... | collective-permute-start | bytes 307208 | tf_op jit(solution)/shard_map/ppermute | solution.py:30
  146.9 1.8 copy-start
  146.9 1.8 copy-start.4
  146.9 1.8 copy-start.6

commit v5 on v4

--- a/solution.py
+++ b/solution.py
@@ -188,29 +188,31 @@
     )
     below = shifted_2(pixels[:RAD], "strip", -1)
     keep_mask = (lax.axis_index("sec") < sec_count - 1).astype(jnp.float32)
-    flow_top = section_flow(pixels[:half], jnp.concatenate([corner, successor_top]), offsets) * keep_mask
-    flow_bottom = section_flow(prior_bottom, jnp.concatenate([pixels[half - RAD :], below]), offsets)
-    flow_field = jnp.concatenate([flow_top, flow_bottom], axis=1)
-    node_rows, node_cols = (flow_field.shape[1], flow_field.shape[2])
+    match_weight = validity[0].astype(jnp.float32) * keep_mask
+    node_rows, node_cols = (springs.shape[2], springs.shape[3])
     global_rows = lax.axis_index("strip") * node_rows + jnp.arange(node_rows, dtype=jnp.int32)
     row_keep = (global_rows < node_rows * lax.axis_size("strip") - 1).astype(jnp.float32)
     col_keep = (jnp.arange(node_cols) < node_cols - 1).astype(jnp.float32)
     row_weight = 0.25 * springs[0, 0].astype(jnp.float32) * row_keep[:, None]
     col_weight = 0.25 * springs[1, 0].astype(jnp.float32) * col_keep[None, :]
-    match_weight = validity[0].astype(jnp.float32) * keep_mask
-    stacked = jnp.stack([flow_field[0], flow_field[1], row_weight, col_weight, match_weight])
-    stacked = jnp.transpose(stacked, (0, 2, 1))[:, None]
-    tiled = lax.all_to_all(stacked, "sec", split_axis=2, concat_axis=1, tiled=True)
+    halo = ITERS
+    weights = jnp.stack([row_weight, col_weight, match_weight]).astype(jnp.bfloat16)
+    weights = lax.all_to_all(jnp.transpose(weights, (0, 2, 1))[:, None], "sec", split_axis=2, concat_axis=1, tiled=True)
+    weights = extended(weights, (("sec", 2), ("strip", 3)), halo).astype(jnp.float32)
+    weights, successor_top, prior_bottom = lax.optimization_barrier((weights, successor_top, prior_bottom))
+    flow_top = section_flow(pixels[:half], jnp.concatenate([corner, successor_top]), offsets) * keep_mask
+    flow_bottom = section_flow(prior_bottom, jnp.concatenate([pixels[half - RAD :], below]), offsets)
+    flow_field = jnp.concatenate([flow_top, flow_bottom], axis=1)
+    flows = jnp.transpose(flow_field, (0, 2, 1))[:, None]
+    tiled = lax.all_to_all(flows, "sec", split_axis=2, concat_axis=1, tiled=True)
     node_half = tiled.shape[3] // 2
-    bottoms = tiled[0:2, 1:, :, node_half:]
+    bottoms = tiled[:, 1:, :, node_half:]
     bottoms = jnp.concatenate([bottoms, jnp.zeros_like(bottoms[:, :1])], axis=1)
-    tiled = jnp.concatenate([jnp.concatenate([tiled[0:2, :, :, :node_half], bottoms], axis=3), tiled[2:]])
-    halo = ITERS
-    haloed = extended(tiled, (("sec", 2), ("strip", 3)), halo)
-    flow_tiles = haloed[0:2]
-    tile_row = haloed[2]
-    tile_col = haloed[3]
-    tile_match = haloed[4]
+    tiled = jnp.concatenate([tiled[:, :, :, :node_half], bottoms], axis=3)
+    flow_tiles = extended(tiled, (("sec", 2), ("strip", 3)), halo)
+    tile_row = weights[0]
+    tile_col = weights[1]
+    tile_match = weights[2]
     weight_up = jnp.pad(tile_row, ((0, 0), (0, 0), (1, 0)))[:, :, :-1]
     weight_left = jnp.pad(tile_col, ((0, 0), (1, 0), (0, 0)))[:, :-1, :]
     match_prior = jnp.pad(tile_match, ((1, 0), (0, 0), (0, 0)))[:-1]

time: 187 us -> 192 us (1.027)
  blocking collectives: 55.6 us -> 33.3 us
  starting transfers between devices: 19.1 us -> 37.5 us
  waiting for transfers between devices: 40.9 us -> 50.4 us
  local copies, waits for them, and re-layouts: 18.2 us -> 16.1 us
    ppermute x3, waiting for transfers between devices: 37 us -> 0.01 us  [shifted_2(): return lax.ppermute(shard, axis, pairs)]
    ppermute x2 -> x4, waiting for transfers between devices: 2.6 us -> 35.3 us  [extended(): lax.ppermute(tail, axis, [(i, (i + 1) % count) for i in range(ends)])]
    all_to_all x1, blocking collectives: 36 us -> 15.3 us  [shards(): lax.all_to_all(flows, 'sec', split_axis=2, concat_axis=1, tiled=True)]
    all_to_all x0 -> x1, starting transfers between devices: none -> 8.47 us  [shards(): lax.all_to_all(jnp.transpose(weights, (0, 2, 1))[:, None], 'sec', split_a...]
    ppermute x2 -> x4, starting transfers between devices: 8.25 us -> 16.4 us  [extended(): lax.ppermute(tail, axis, [(i, (i + 1) % count) for i in range(ends)])]
    all_to_all x0 -> x1, waiting for transfers between devices: none -> 7.74 us  [shards(): lax.all_to_all(jnp.transpose(weights, (0, 2, 1))[:, None], 'sec', split_a...]
    ppermute x2 -> x4, waiting for transfers between devices: 1.35 us -> 7.38 us  [extended(): lax.ppermute(head, axis, [((i + 1) % count, i) for i in range(ends)])]
    mul x3 -> x0, other arithmetic: 3.11 us -> none  [the longest x1 1.81 us: advance(): row_weight * (from_below - positions) + weight_up * (from_above - positions)]
  transfers between devices with their start and end apart: 8 -> 13, of which waited for: 3 -> 5; matrix products, arithmetic and copies ran while one was open for 4% -> 7% of each run, Pallas kernels for 8% -> 0%
where the time goes in v5:
time: 192 us; the launch traced here: 190 us
  waiting for transfers between devices  50.4 us (26%)
  starting transfers between devices  37.5 us (20%)
  blocking collectives  33.3 us (17%)
  Pallas kernels  28 us (15%)
  other arithmetic  24.5 us (13%)
  local copies, waits for them, and re-layouts  16.1 us (8%)
    ppermute x4, waiting for transfers between devices, extended(): lax.ppermute(tail, axis, [(i, (i + 1) % count) for i in range(ends)])  35.3 us
    pallas_call x2, Pallas kernels, section_flow(): pl.pallas_call(flow_kernel, grid_spec=grid_spec, out_shape=jax.ShapeDtype...  28 us
    all_to_all x1, blocking collectives, shards(): lax.all_to_all(core, 'sec', split_axis=1, concat_axis=2, tiled=True)  18 us
    ppermute x4, starting transfers between devices, extended(): lax.ppermute(tail, axis, [(i, (i + 1) % count) for i in range(ends)])  16.4 us
    all_to_all x1, blocking collectives, shards(): lax.all_to_all(flows, 'sec', split_axis=2, concat_axis=1, tiled=True)  15.3 us
    add x7, other arithmetic, advance(): return positions + relax_rate * force / (1.0 + diagonal)  10.9 us
    all_to_all x1, starting transfers between devices, shards(): lax.all_to_all(jnp.transpose(weights, (0, 2, 1))[:, None], 'sec', split_a...  8.47 us
    all_to_all x1, waiting for transfers between devices, shards(): lax.all_to_all(jnp.transpose(weights, (0, 2, 1))[:, None], 'sec', split_a...  7.74 us
  transfers between devices with their start and end apart: 13, of which 5 were waited for; matrix products, arithmetic and copies ran while one was open for 7% of the time, Pallas kernels for 0%

profile of v5, /device:TPU:0, one launch (start us, length us, event | category | flops | bytes accessed | tf_op | source)
XLA Modules:
  0.0 190.4 jit_solution(12340510897497989638)
XLA Ops:
  3.8 8.5 %all-to-all-start = ((bf16[3,1,512,128]{3,0,1,2:T(4,128)(2,1)}), bf16[3,1,512,128]{3,0,1,2:T(4,128)(2,1)}, u32[]{:S(2)}, u32[]{:S(2)}) async-start(bf16[3,1,512,128]{3,0,1,2:T(4,128)(2,1)} %copy.30), calls=%async_computation | async-start | bytes 1048576 | tf_op jit(solution)/shard_map/all_to_all | solution.py:200
  13.5 4.0 %collective-permute-start.5 = (bf16[256,2048]{1,0:T(8,128)(2,1)}, bf16[256,2048]{1,0:T(8,128)(2,1)S(1)}, u32[]{:S(2)}, u32[]{:S(2)}) collective-permute-start(bf16[256,2048]{1,0:T(8,128)(2,1)} %get-tuple-element.16), channel_id=1, source_target_pairs={{0,4},{4,8},{8,12},{12,16},{16,20},{20,24},{24,28},{1,5},{5,9},{9,... | collective-permute-start | bytes 3145736 | tf_op jit(solution)/shard_map/ppermute | solution.py:19
  17.5 1.6 slice_bitcast_fusion
  19.2 1.4 collective-permute-start.4
  20.6 7.7 %all-to-all-done = bf16[3,1,512,128]{3,0,1,2:T(4,128)(2,1)} async-done(((bf16[3,1,512,128]{3,0,1,2:T(4,128)(2,1)}), bf16[3,1,512,128]{3,0,1,2:T(4,128)(2,1)}, u32[]{:S(2)}, u32[]{:S(2)}) %all-to-all-start) | async-done | bytes 393248 | tf_op jit(solution)/shard_map/all_to_all | solution.py:200
  29.5 3.1 %collective-permute-start = (bf16[3,8,8,128]{3,2,1,0:T(8,128)(2,1)S(1)}, bf16[3,8,8,128]{3,2,1,0:T(8,128)(2,1)S(1)}, u32[]{:S(2)}, u32[]{:S(2)}) collective-permute-start(bf16[3,8,8,128]{3,2,1,0:T(8,128)(2,1)S(1)} %get-tuple-element.36), channel_id=1, source_target_pairs={{0,4},{4,8},{8,12},{12,16},{16,20},{20,24},{24,28},{1,5},{5,9},{9,... | collective-permute-start | bytes 147464 | tf_op jit(solution)/shard_map/ppermute | solution.py:30
  32.6 1.3 collective-permute-start.1
  34.1 34.8 %collective-permute-done = bf16[3,8,8,128]{3,2,1,0:T(8,128)(2,1)S(1)} collective-permute-done((bf16[3,8,8,128]{3,2,1,0:T(8,128)(2,1)S(1)}, bf16[3,8,8,128]{3,2,1,0:T(8,128)(2,1)S(1)}, u32[]{:S(2)}, u32[]{:S(2)}) %collective-permute-start) | collective-permute-done | bytes 49184 | tf_op jit(solution)/shard_map/ppermute | solution.py:30
  69.0 1.4 collective-permute-start.7
  70.6 3.1 %collective-permute-start.2 = (bf16[3,8,80,8]{3,2,1,0:T(8,128)(2,1)S(1)}, bf16[3,8,80,8]{3,2,1,0:T(8,128)(2,1)S(1)}, u32[]{:S(2)}, u32[]{:S(2)}) collective-permute-start(bf16[3,8,80,8]{3,2,1,0:T(8,128)(2,1)S(1)} %get-tuple-element.34), channel_id=1, source_target_pairs={{0,1},{1,2},{2,3},{4,5},{5,6},{6,7},{8,9},{9,10},{10,11},{12,13},{... | collective-permute-start | bytes 92168 | tf_op jit(solution)/shard_map/ppermute | solution.py:30
  73.7 1.3 collective-permute-start.3
  75.3 3.1 %collective-permute-done.3 = bf16[3,8,80,8]{3,2,1,0:T(8,128)(2,1)S(1)} collective-permute-done((bf16[3,8,80,8]{3,2,1,0:T(8,128)(2,1)S(1)}, bf16[3,8,80,8]{3,2,1,0:T(8,128)(2,1)S(1)}, u32[]{:S(2)}, u32[]{:S(2)}) %collective-permute-start.3) | collective-permute-done | bytes 30752 | tf_op jit(solution)/shard_map/ppermute | solution.py:32
  78.4 1.9 maximum_convert_fusion
  80.3 1.5 fusion.143.following_ref
  81.9 14.0 %shard_map.46 = f32[2,64,512]{2,1,0:T(8,128)S(1)} custom-call(s32[25,2]{1,0:T(8,128)S(1)} %copy.32.offsets_ref, bf16[256,2048]{1,0:T(8,128)(2,1)S(1)} %get-tuple-element.15.current_ref, bf16[288,2048]{1,0:T(8,128)(2,1)S(1)} %fusion.143.following_ref, bf16[512,512]{1,0:T(8,128)(2,1)S(1)} %fusion.144.permute_ref), custom_call_target="tpu_custom_call" | custom-call | tf_op jit(solution)/shard_map/pallas_call | solution.py:147
  95.9 14.0 %shard_map.47 = f32[2,64,512]{2,1,0:T(8,128)S(1)} custom-call(s32[25,2]{1,0:T(8,128)S(1)} %copy.32.offsets_ref, bf16[256,2048]{1,0:T(8,128)(2,1)S(1)} %collective-permute-done.5.current_ref, bf16[288,2048]{1,0:T(8,128)(2,1)S(1)} %select_maximum_fusion.following_ref, bf16[512,512]{1,0:T(8,128)(2,1)S(1)} %fusion.144.permute_ref), custom_call_target="tpu_custom_call" | custom-call | tf_op jit(solution)/shard_map/pallas_call | solution.py:147
  110.2 15.3 %all_to_all.36 = f32[2,1,512,128]{3,0,1,2:T(2,128)S(1)} all-to-all(f32[2,1,512,128]{3,0,1,2:T(2,128)S(1)} %copy.34), channel_id=1, replica_groups=mesh['sec'=8,'strip'=4] {'sec'}, dimensions={2} | all-to-all | bytes 1048576 | tf_op jit(solution)/shard_map/all_to_all | solution.py:207
  125.9 3.5 %collective-permute-start.8 = (f32[2,8,8,128]{3,2,1,0:T(8,128)S(1)}, f32[2,8,8,128]{3,2,1,0:T(8,128)S(1)}, u32[]{:S(2)}, u32[]{:S(2)}) collective-permute-start(f32[2,8,8,128]{3,2,1,0:T(8,128)S(1)} %get-tuple-element.25), channel_id=1, source_target_pairs={{0,4},{4,8},{8,12},{12,16},{16,20},{20,24},{24,28},{1,5},{5,9},{9,... | collective-permute-start | bytes 196616 | tf_op jit(solution)/shard_map/ppermute | solution.py:30
  129.4 1.3 collective-permute-start.9
  131.3 4.3 %collective-permute-done.9 = f32[2,8,8,128]{3,2,1,0:T(8,128)S(1)} collective-permute-done((f32[2,8,8,128]{3,2,1,0:T(8,128)S(1)}, f32[2,8,8,128]{3,2,1,0:T(8,128)S(1)}, u32[]{:S(2)}, u32[]{:S(2)}) %collective-permute-start.9) | collective-permute-done | bytes 65568 | tf_op jit(solution)/shard_map/ppermute | solution.py:32
  139.2 6.8 %collective-permute-start.10 = (f32[2,8,80,8]{2,3,1,0:T(8,128)}, f32[2,8,80,8]{2,3,1,0:T(8,128)}, u32[]{:S(2)}, u32[]{:S(2)}) collective-permute-start(f32[2,8,80,8]{2,3,1,0:T(8,128)} %copy.36), channel_id=1, source_target_pairs={{0,1},{1,2},{2,3},{4,5},{5,6},{6,7},{8,9},{9,10},{10,11},{12,13},{... | collective-permute-start | bytes 122888 | tf_op jit(solution)/shard_map/ppermute | solution.py:30
  145.9 1.7 pad_slice_fusion.50
  148.7 1.9 %copy.38 = f32[2,8,80,8]{3,2,1,0:T(8,128)} copy(f32[2,8,80,8]{2,3,1,0:T(8,128)} %collective-permute-done.10) | data formatting | bytes 81920 | tf_op jit(solution)/shard_map/ppermute | solution.py:30
  150.6 1.9 %copy.39 = f32[2,8,80,8]{3,2,1,0:T(8,128)} copy(f32[2,8,80,8]{2,3,1,0:T(8,128)} %collective-permute-done.11) | data formatting | bytes 81920 | tf_op jit(solution)/shard_map/ppermute | solution.py:32
  153.7 2.2 %fusion.108 = (f32[2,8,80,144]{3,2,1,0:T(8,128)S(1)}, f32[2,8,80,144]{3,2,1,0:T(8,128)S(1)}) fusion(f32[2,8,80,144]{3,2,1,0:T(8,128)S(1)} %broadcast_in_dim.7, f32[8,80,144]{2,1,0:T(8,128)S(1)} %get-tuple-element.20, f32[2,8,80,8]{3,2,1,0:T(8,128)} %copy.39, f32[2,8,8,128]{3,2,1,0:T(8,128)S(1)} %copy-done.13, f32[2,8,64,64]{3,2,1,0:T(8,128)S(1)} %copy-done.8, ...), kind=kLoop, calls=%fused_computation.158 | loop fusion | flops 1290240 | bytes 3317760 | tf_op jit(solution)/shard_map/mul | solution.py:224
  157.4 1.7 fusion.10
  159.5 1.7 fusion.26
  161.5 1.7 fusion.42
  163.5 1.7 fusion.58
  165.6 1.7 fusion.74
  167.6 1.7 fusion.90
  171.3 18.0 %all_to_all.37 = f32[2,8,64,128]{3,2,0,1:T(8,128)S(1)} all-to-all(f32[2,8,64,128]{3,2,0,1:T(8,128)S(1)} %copy.40), channel_id=1, replica_groups=mesh['sec'=8,'strip'=4] {'sec'}, dimensions={1} | all-to-all | bytes 1048576 | tf_op jit(solution)/shard_map/all_to_all | solution.py:241
  (83 shorter events, 20.0 us)
Async XLA Ops:
  0.8 79.5 %collective-permute-start.6 = (bf16[3,2048]{1,0:T(4,128)(2,1)S(1)}, bf16[3,2048]{1,0:T(4,128)(2,1)S(1)}, u32[]{:S(2)}, u32[]{:S(2)}) collective-permute-start(bf16[3,2048]{1,0:T(4,128)(2,1)S(1)} %get-tuple-element.13), channel_id=1, source_target_pairs={{4,1},{5,2},{6,3},{8,5},{9,6},{10,7},{12,9},{13,10},{14,11},{16,13... | collective-permute-start | bytes 36872 | tf_op jit(solution)/shard_map/ppermute | solution.py:184
  2.7 9.6 %copy-start.5 = (bf16[1,512,2048]{2,1,0:T(8,128)(2,1)S(1)}, bf16[1,512,2048]{2,1,0:T(8,128)(2,1)}, u32[]{:S(2)}) copy-start(bf16[1,512,2048]{2,1,0:T(8,128)(2,1)} %param.4) | copy-start | bytes 6291460
  3.8 24.5 %all-to-all-start = ((bf16[3,1,512,128]{3,0,1,2:T(4,128)(2,1)}), bf16[3,1,512,128]{3,0,1,2:T(4,128)(2,1)}, u32[]{:S(2)}, u32[]{:S(2)}) async-start(bf16[3,1,512,128]{3,0,1,2:T(4,128)(2,1)} %copy.30), calls=%async_computation | async-start | bytes 1048576 | tf_op jit(solution)/shard_map/all_to_all | solution.py:200
  12.3 5.2 %copy-start.6 = (bf16[1,512,2048]{2,1,0:T(8,128)(2,1)S(1)}, bf16[1,512,2048]{2,1,0:T(8,128)(2,1)}, u32[]{:S(2)}) copy-start(bf16[1,512,2048]{2,1,0:T(8,128)(2,1)} %param.4) | copy-start | bytes 6291460
  13.5 66.8 %collective-permute-start.5 = (bf16[256,2048]{1,0:T(8,128)(2,1)}, bf16[256,2048]{1,0:T(8,128)(2,1)S(1)}, u32[]{:S(2)}, u32[]{:S(2)}) collective-permute-start(bf16[256,2048]{1,0:T(8,128)(2,1)} %get-tuple-element.16), channel_id=1, source_target_pairs={{0,4},{4,8},{8,12},{12,16},{16,20},{20,24},{24,28},{1,5},{5,9},{9,... | collective-permute-start | bytes 3145736 | tf_op jit(solution)/shard_map/ppermute | solution.py:19
  19.2 14.9 %copy-start.14 = (s32[25,2]{0,1:T(2,128)S(1)}, s32[25,2]{0,1:T(2,128)}, u32[]{:S(2)}) copy-start(s32[25,2]{0,1:T(2,128)} %param.5) | copy-start | bytes 604
  19.2 61.2 %collective-permute-start.4 = (bf16[259,2048]{1,0:T(8,128)(2,1)}, bf16[259,2048]{1,0:T(8,128)(2,1)}, u32[]{:S(2)}, u32[]{:S(2)}) collective-permute-start(bf16[259,2048]{1,0:T(8,128)(2,1)} %get-tuple-element.18), channel_id=1, source_target_pairs={{4,0},{8,4},{12,8},{16,12},{20,16},{24,20},{28,24},{5,1},{9,5},{13... | collective-permute-start | bytes 3182600 | tf_op jit(solution)/shard_map/ppermute | solution.py:19
  29.5 39.5 %collective-permute-start = (bf16[3,8,8,128]{3,2,1,0:T(8,128)(2,1)S(1)}, bf16[3,8,8,128]{3,2,1,0:T(8,128)(2,1)S(1)}, u32[]{:S(2)}, u32[]{:S(2)}) collective-permute-start(bf16[3,8,8,128]{3,2,1,0:T(8,128)(2,1)S(1)} %get-tuple-element.36), channel_id=1, source_target_pairs={{0,4},{4,8},{8,12},{12,16},{16,20},{20,24},{24,28},{1,5},{5,9},{9,... | collective-permute-start | bytes 147464 | tf_op jit(solution)/shard_map/ppermute | solution.py:30
  32.6 37.8 %collective-permute-start.1 = (bf16[3,8,8,128]{3,2,1,0:T(8,128)(2,1)S(1)}, bf16[3,8,8,128]{3,2,1,0:T(8,128)(2,1)S(1)}, u32[]{:S(2)}, u32[]{:S(2)}) collective-permute-start(bf16[3,8,8,128]{3,2,1,0:T(8,128)(2,1)S(1)} %get-tuple-element.37), channel_id=1, source_target_pairs={{4,0},{8,4},{12,8},{16,12},{20,16},{24,20},{28,24},{5,1},{9,5},{13... | collective-permute-start | bytes 147464 | tf_op jit(solution)/shard_map/ppermute | solution.py:32
  69.0 6.1 %copy-start.9 = (bf16[259,2048]{1,0:T(8,128)(2,1)S(1)}, bf16[259,2048]{1,0:T(8,128)(2,1)}, u32[]{:S(2)}) copy-start(bf16[259,2048]{1,0:T(8,128)(2,1)} %get-tuple-element.17) | copy-start | bytes 3182596
  69.0 4.8 %collective-permute-start.7 = (bf16[3,2048]{1,0:T(4,128)(2,1)S(1)}, bf16[3,2048]{1,0:T(4,128)(2,1)S(1)}, u32[]{:S(2)}, u32[]{:S(2)}) collective-permute-start(bf16[3,2048]{1,0:T(4,128)(2,1)S(1)} %get-tuple-element.14), channel_id=1, source_target_pairs={{1,0},{2,1},{3,2},{5,4},{6,5},{7,6},{9,8},{10,9},{11,10},{13,12},{... | collective-permute-start | bytes 36872 | tf_op jit(solution)/shard_map/ppermute | solution.py:19
  70.6 4.7 %collective-permute-start.2 = (bf16[3,8,80,8]{3,2,1,0:T(8,128)(2,1)S(1)}, bf16[3,8,80,8]{3,2,1,0:T(8,128)(2,1)S(1)}, u32[]{:S(2)}, u32[]{:S(2)}) collective-permute-start(bf16[3,8,80,8]{3,2,1,0:T(8,128)(2,1)S(1)} %get-tuple-element.34), channel_id=1, source_target_pairs={{0,1},{1,2},{2,3},{4,5},{5,6},{6,7},{8,9},{9,10},{10,11},{12,13},{... | collective-permute-start | bytes 92168 | tf_op jit(solution)/shard_map/ppermute | solution.py:30
  73.7 4.7 %collective-permute-start.3 = (bf16[3,8,80,8]{3,2,1,0:T(8,128)(2,1)S(1)}, bf16[3,8,80,8]{3,2,1,0:T(8,128)(2,1)S(1)}, u32[]{:S(2)}, u32[]{:S(2)}) collective-permute-start(bf16[3,8,80,8]{3,2,1,0:T(8,128)(2,1)S(1)} %get-tuple-element.35), channel_id=1, source_target_pairs={{1,0},{2,1},{3,2},{5,4},{6,5},{7,6},{9,8},{10,9},{11,10},{13,12},{... | collective-permute-start | bytes 92168 | tf_op jit(solution)/shard_map/ppermute | solution.py:32
  125.5 10.1 %copy-start.3 = (f32[2,1,512,128]{3,2,0,1:T(8,128)}, f32[2,1,512,128]{3,2,0,1:T(8,128)S(1)}, u32[]{:S(2)}) copy-start(f32[2,1,512,128]{3,2,0,1:T(8,128)S(1)} %copy.35) | copy-start | bytes 1572868
  125.7 5.0 %copy-start.2 = (f32[3,8,80,144]{3,2,1,0:T(8,128)S(1)}, f32[3,8,80,144]{3,2,1,0:T(8,128)}, u32[]{:S(2)}) copy-start(f32[3,8,80,144]{3,2,1,0:T(8,128)} %maximum_convert_fusion) | copy-start | bytes 3317764
  125.8 9.8 %copy-start.7 = (f32[2,8,64,64]{3,2,1,0:T(8,128)}, f32[2,8,64,64]{3,2,1,0:T(8,128)S(1)}, u32[]{:S(2)}) copy-start(f32[2,8,64,64]{3,2,1,0:T(8,128)S(1)} %concatenate.32) | copy-start | bytes 786436
  125.9 5.4 %collective-permute-start.8 = (f32[2,8,8,128]{3,2,1,0:T(8,128)S(1)}, f32[2,8,8,128]{3,2,1,0:T(8,128)S(1)}, u32[]{:S(2)}, u32[]{:S(2)}) collective-permute-start(f32[2,8,8,128]{3,2,1,0:T(8,128)S(1)} %get-tuple-element.25), channel_id=1, source_target_pairs={{0,4},{4,8},{8,12},{12,16},{16,20},{20,24},{24,28},{1,5},{5,9},{9,... | collective-permute-start | bytes 196616 | tf_op jit(solution)/shard_map/ppermute | solution.py:30
  129.4 6.2 %collective-permute-start.9 = (f32[2,8,8,128]{3,2,1,0:T(8,128)S(1)}, f32[2,8,8,128]{3,2,1,0:T(8,128)S(1)}, u32[]{:S(2)}, u32[]{:S(2)}) collective-permute-start(f32[2,8,8,128]{3,2,1,0:T(8,128)S(1)} %get-tuple-element.26), channel_id=1, source_target_pairs={{4,0},{8,4},{12,8},{16,12},{20,16},{24,20},{28,24},{5,1},{9,5},{13... | collective-permute-start | bytes 196616 | tf_op jit(solution)/shard_map/ppermute | solution.py:32
  131.3 4.7 %copy-start.10 = (f32[2,8,8,128]{3,2,1,0:T(8,128)}, f32[2,8,8,128]{3,2,1,0:T(8,128)S(1)}, u32[]{:S(2)}) copy-start(f32[2,8,8,128]{3,2,1,0:T(8,128)S(1)} %collective-permute-done.8) | copy-start | bytes 196612
  135.6 0.6 copy-start.12
  137.9 12.7 %collective-permute-start.11 = (f32[2,8,80,8]{2,3,1,0:T(8,128)}, f32[2,8,80,8]{2,3,1,0:T(8,128)}, u32[]{:S(2)}, u32[]{:S(2)}) collective-permute-start(f32[2,8,80,8]{2,3,1,0:T(8,128)} %copy.37), channel_id=1, source_target_pairs={{1,0},{2,1},{3,2},{5,4},{6,5},{7,6},{9,8},{10,9},{11,10},{13,12},{... | collective-permute-start | bytes 122888 | tf_op jit(solution)/shard_map/ppermute | solution.py:32
  139.2 9.5 %collective-permute-start.10 = (f32[2,8,80,8]{2,3,1,0:T(8,128)}, f32[2,8,80,8]{2,3,1,0:T(8,128)}, u32[]{:S(2)}, u32[]{:S(2)}) collective-permute-start(f32[2,8,80,8]{2,3,1,0:T(8,128)} %copy.36), channel_id=1, source_target_pairs={{0,1},{1,2},{2,3},{4,5},{5,6},{6,7},{8,9},{9,10},{10,11},{12,13},{... | collective-permute-start | bytes 122888 | tf_op jit(solution)/shard_map/ppermute | solution.py:30
  147.7 0.9 copy-start
  152.5 1.0 copy-start.4
  152.5 1.2 copy-start.8
  152.5 1.2 copy-start.11
  152.5 1.2 copy-start.13
  153.7 2.2 %copy-start.1 = (f32[8,80,144]{2,1,0:T(8,128)S(1)}, f32[8,80,144]{2,1,0:T(8,128)}, u32[]{:S(2)}) copy-start(f32[8,80,144]{2,1,0:T(8,128)} %copy-done) | copy-start | bytes 1105924

commit v6 on v5

--- a/solution.py
+++ b/solution.py
@@ -188,6 +188,7 @@
     )
     below = shifted_2(pixels[:RAD], "strip", -1)
     keep_mask = (lax.axis_index("sec") < sec_count - 1).astype(jnp.float32)
+    springs, validity, prior_bottom = lax.optimization_barrier((springs, validity, prior_bottom))
     match_weight = validity[0].astype(jnp.float32) * keep_mask
     node_rows, node_cols = (springs.shape[2], springs.shape[3])
     global_rows = lax.axis_index("strip") * node_rows + jnp.arange(node_rows, dtype=jnp.int32)
@@ -199,7 +200,6 @@
     weights = jnp.stack([row_weight, col_weight, match_weight]).astype(jnp.bfloat16)
     weights = lax.all_to_all(jnp.transpose(weights, (0, 2, 1))[:, None], "sec", split_axis=2, concat_axis=1, tiled=True)
     weights = extended(weights, (("sec", 2), ("strip", 3)), halo).astype(jnp.float32)
-    weights, successor_top, prior_bottom = lax.optimization_barrier((weights, successor_top, prior_bottom))
     flow_top = section_flow(pixels[:half], jnp.concatenate([corner, successor_top]), offsets) * keep_mask
     flow_bottom = section_flow(prior_bottom, jnp.concatenate([pixels[half - RAD :], below]), offsets)
     flow_field = jnp.concatenate([flow_top, flow_bottom], axis=1)

time: 192 us -> 191 us (level)
  blocking collectives: 33.3 us -> 22.6 us
  starting transfers between devices: 37.5 us -> 42.9 us
  waiting for transfers between devices: 50.4 us -> 54.5 us
    ppermute x3, waiting for transfers between devices: 0.01 us -> 40.7 us  [shifted_2(): return lax.ppermute(shard, axis, pairs)]
    ppermute x4, waiting for transfers between devices: 35.3 us -> 1.15 us  [extended(): lax.ppermute(tail, axis, [(i, (i + 1) % count) for i in range(ends)])]
    all_to_all x1 -> x0, blocking collectives: 15.3 us -> none  [shards(): lax.all_to_all(flows, 'sec', split_axis=2, concat_axis=1, tiled=True)]
    all_to_all x1, waiting for transfers between devices: 7.74 us -> 0.01 us  [shards(): lax.all_to_all(jnp.transpose(weights, (0, 2, 1))[:, None], 'sec', split_a...]
    all_to_all x0 -> x1, starting transfers between devices: none -> 5.97 us  [shards(): lax.all_to_all(flows, 'sec', split_axis=2, concat_axis=1, tiled=True)]
    ppermute x4, waiting for transfers between devices: 7.38 us -> 12.6 us  [extended(): lax.ppermute(head, axis, [((i + 1) % count, i) for i in range(ends)])]
    all_to_all x1, blocking collectives: 18 us -> 22.6 us  [shards(): lax.all_to_all(core, 'sec', split_axis=1, concat_axis=2, tiled=True)]
    all_to_all x1, starting transfers between devices: 8.47 us -> 5.68 us  [shards(): lax.all_to_all(jnp.transpose(weights, (0, 2, 1))[:, None], 'sec', split_a...]
  transfers between devices with their start and end apart: 13 -> 14, of which waited for: 5 -> 7; matrix products, arithmetic and copies ran while one was open for 7% -> 7% of each run, Pallas kernels for 0% -> 15%
where the time goes in v6:
time: 191 us; the launch traced here: 190 us
  waiting for transfers between devices  54.5 us (29%)
  starting transfers between devices  42.9 us (22%)
  Pallas kernels  28 us (15%)
  other arithmetic  24.7 us (13%)
  blocking collectives  22.6 us (12%)
  local copies, waits for them, and re-layouts  16.7 us (9%)
    ppermute x3, waiting for transfers between devices, shifted_2(): return lax.ppermute(shard, axis, pairs)  40.7 us
    pallas_call x2, Pallas kernels, section_flow(): pl.pallas_call(flow_kernel, grid_spec=grid_spec, out_shape=jax.ShapeDtype...  28 us
    all_to_all x1, blocking collectives, shards(): lax.all_to_all(core, 'sec', split_axis=1, concat_axis=2, tiled=True)  22.6 us
    ppermute x4, starting transfers between devices, extended(): lax.ppermute(tail, axis, [(i, (i + 1) % count) for i in range(ends)])  17.6 us
    ppermute x4, waiting for transfers between devices, extended(): lax.ppermute(head, axis, [((i + 1) % count, i) for i in range(ends)])  12.6 us
    add x7, other arithmetic, advance(): return positions + relax_rate * force / (1.0 + diagonal)  10.9 us
    ppermute x3, starting transfers between devices, shifted_2(): return lax.ppermute(shard, axis, pairs)  7.63 us
    all_to_all x1, starting transfers between devices, shards(): lax.all_to_all(flows, 'sec', split_axis=2, concat_axis=1, tiled=True)  5.97 us
  transfers between devices with their start and end apart: 14, of which 7 were waited for; matrix products, arithmetic and copies ran while one was open for 7% of the time, Pallas kernels for 15%

profile of v6, /device:TPU:0, one launch (start us, length us, event | category | flops | bytes accessed | tf_op | source)
XLA Modules:
  0.0 189.9 jit_solution(7531258254338077157)
XLA Ops:
  0.0 2.9 %slice_bitcast_fusion.2 = (bf16[256,2048]{1,0:T(8,128)(2,1)S(1)}, bf16[256,2048]{1,0:T(8,128)(2,1)}) fusion(bf16[1,512,2048]{2,1,0:T(8,128)(2,1)} %param.4), kind=kLoop, calls=%fused_computation.199 | loop fusion | bytes 4194304 | tf_op jit(solution)/shard_map/slice | solution.py:203
  2.9 5.1 %collective-permute-start = (bf16[256,2048]{1,0:T(8,128)(2,1)}, bf16[256,2048]{1,0:T(8,128)(2,1)S(1)}, u32[]{:S(2)}, u32[]{:S(2)}) collective-permute-start(bf16[256,2048]{1,0:T(8,128)(2,1)} %get-tuple-element.18), channel_id=1, source_target_pairs={{0,4},{4,8},{8,12},{12,16},{16,20},{20,24},{24,28},{1,5},{5,9},{9,... | collective-permute-start | bytes 3145736 | tf_op jit(solution)/shard_map/ppermute | solution.py:19
  7.9 1.7 slice_bitcast_fusion.1
  11.6 1.3 collective-permute-start.7
  13.2 40.7 %collective-permute-done.current_ref = bf16[256,2048]{1,0:T(8,128)(2,1)S(1)} collective-permute-done((bf16[256,2048]{1,0:T(8,128)(2,1)}, bf16[256,2048]{1,0:T(8,128)(2,1)S(1)}, u32[]{:S(2)}, u32[]{:S(2)}) %collective-permute-start) | collective-permute-done | bytes 1048608 | tf_op jit(solution)/shard_map/ppermute | solution.py:19
  55.1 5.7 %all-to-all-start = ((bf16[3,1,512,128]{3,0,1,2:T(4,128)(2,1)}), bf16[3,1,512,128]{3,0,1,2:T(4,128)(2,1)S(1)}, u32[]{:S(2)}, u32[]{:S(2)}) async-start(bf16[3,1,512,128]{3,0,1,2:T(4,128)(2,1)} %copy.30), calls=%async_computation | async-start | bytes 1048576 | tf_op jit(solution)/shard_map/all_to_all | solution.py:201
  60.8 1.5 select_maximum_fusion.following_ref
  62.4 14.0 %shard_map.47 = f32[2,64,512]{2,1,0:T(8,128)S(1)} custom-call(s32[25,2]{1,0:T(8,128)S(1)} %copy.32.offsets_ref, bf16[256,2048]{1,0:T(8,128)(2,1)S(1)} %collective-permute-done.current_ref, bf16[288,2048]{1,0:T(8,128)(2,1)S(1)} %select_maximum_fusion.following_ref, bf16[512,512]{1,0:T(8,128)(2,1)S(1)} %fusion.144.permute_ref), custom_call_target="tpu_custom_call" | custom-call | tf_op jit(solution)/shard_map/pallas_call | solution.py:147
  76.4 1.5 fusion.143.following_ref
  77.9 14.0 %shard_map.46 = f32[2,64,512]{2,1,0:T(8,128)S(1)} custom-call(s32[25,2]{1,0:T(8,128)S(1)} %copy.32.offsets_ref, bf16[256,2048]{1,0:T(8,128)(2,1)S(1)} %get-tuple-element.17.current_ref, bf16[288,2048]{1,0:T(8,128)(2,1)S(1)} %fusion.143.following_ref, bf16[512,512]{1,0:T(8,128)(2,1)S(1)} %fusion.144.permute_ref), custom_call_target="tpu_custom_call" | custom-call | tf_op jit(solution)/shard_map/pallas_call | solution.py:147
  93.0 6.0 %all-to-all-start.1 = ((f32[2,1,512,128]{3,0,1,2:T(2,128)}), f32[2,1,512,128]{3,0,1,2:T(2,128)S(1)}, u32[]{:S(2)}, u32[]{:S(2)}) async-start(f32[2,1,512,128]{3,0,1,2:T(2,128)} %copy.34), calls=%async_computation.1 | async-start | bytes 1048576 | tf_op jit(solution)/shard_map/all_to_all | solution.py:207
  99.1 3.9 %collective-permute-start.1 = (bf16[3,8,8,128]{3,2,1,0:T(8,128)(2,1)S(1)}, bf16[3,8,8,128]{3,2,1,0:T(8,128)(2,1)S(1)}, u32[]{:S(2)}, u32[]{:S(2)}) collective-permute-start(bf16[3,8,8,128]{3,2,1,0:T(8,128)(2,1)S(1)} %get-tuple-element.36), channel_id=1, source_target_pairs={{0,4},{4,8},{8,12},{12,16},{16,20},{20,24},{24,28},{1,5},{5,9},{9,... | collective-permute-start | bytes 147464 | tf_op jit(solution)/shard_map/ppermute | solution.py:30
  104.9 4.1 %collective-permute-done.2 = bf16[3,8,8,128]{3,2,1,0:T(8,128)(2,1)S(1)} collective-permute-done((bf16[3,8,8,128]{3,2,1,0:T(8,128)(2,1)S(1)}, bf16[3,8,8,128]{3,2,1,0:T(8,128)(2,1)S(1)}, u32[]{:S(2)}, u32[]{:S(2)}) %collective-permute-start.2) | collective-permute-done | bytes 49184 | tf_op jit(solution)/shard_map/ppermute | solution.py:32
  109.3 1.3 collective-permute-start.3
  112.1 4.2 %collective-permute-done.4 = bf16[3,8,80,8]{3,2,1,0:T(8,128)(2,1)S(1)} collective-permute-done((bf16[3,8,80,8]{3,2,1,0:T(8,128)(2,1)S(1)}, bf16[3,8,80,8]{3,2,1,0:T(8,128)(2,1)S(1)}, u32[]{:S(2)}, u32[]{:S(2)}) %collective-permute-start.4) | collective-permute-done | bytes 30752 | tf_op jit(solution)/shard_map/ppermute | solution.py:32
  116.3 1.9 maximum_convert_fusion
  118.6 4.4 %collective-permute-start.8 = (f32[2,8,8,128]{3,2,1,0:T(8,128)S(1)}, f32[2,8,8,128]{3,2,1,0:T(8,128)S(1)}, u32[]{:S(2)}, u32[]{:S(2)}) collective-permute-start(f32[2,8,8,128]{3,2,1,0:T(8,128)S(1)} %get-tuple-element.25), channel_id=1, source_target_pairs={{0,4},{4,8},{8,12},{12,16},{16,20},{20,24},{24,28},{1,5},{5,9},{9,... | collective-permute-start | bytes 196616 | tf_op jit(solution)/shard_map/ppermute | solution.py:30
  123.0 1.3 collective-permute-start.9
  124.8 4.3 %collective-permute-done.9 = f32[2,8,8,128]{3,2,1,0:T(8,128)S(1)} collective-permute-done((f32[2,8,8,128]{3,2,1,0:T(8,128)S(1)}, f32[2,8,8,128]{3,2,1,0:T(8,128)S(1)}, u32[]{:S(2)}, u32[]{:S(2)}) %collective-permute-start.9) | collective-permute-done | bytes 65568 | tf_op jit(solution)/shard_map/ppermute | solution.py:32
  130.6 8.0 %collective-permute-start.10 = (f32[2,8,80,8]{2,3,1,0:T(8,128)}, f32[2,8,80,8]{2,3,1,0:T(8,128)}, u32[]{:S(2)}, u32[]{:S(2)}) collective-permute-start(f32[2,8,80,8]{2,3,1,0:T(8,128)} %copy.36), channel_id=1, source_target_pairs={{0,1},{1,2},{2,3},{4,5},{5,6},{6,7},{8,9},{9,10},{10,11},{12,13},{... | collective-permute-start | bytes 122888 | tf_op jit(solution)/shard_map/ppermute | solution.py:30
  139.4 1.5 collective-permute-start.11
  140.9 1.7 pad_slice_fusion.50
  143.6 2.0 %copy.38 = f32[2,8,80,8]{3,2,1,0:T(8,128)} copy(f32[2,8,80,8]{2,3,1,0:T(8,128)} %collective-permute-done.10) | data formatting | bytes 81920 | tf_op jit(solution)/shard_map/ppermute | solution.py:30
  145.6 1.9 %copy.39 = f32[2,8,80,8]{3,2,1,0:T(8,128)} copy(f32[2,8,80,8]{2,3,1,0:T(8,128)} %collective-permute-done.11) | data formatting | bytes 81920 | tf_op jit(solution)/shard_map/ppermute | solution.py:32
  148.7 2.2 %fusion.108 = (f32[2,8,80,144]{3,2,1,0:T(8,128)S(1)}, f32[2,8,80,144]{3,2,1,0:T(8,128)S(1)}) fusion(f32[2,8,80,144]{3,2,1,0:T(8,128)S(1)} %broadcast_in_dim.7, f32[8,80,144]{2,1,0:T(8,128)S(1)} %get-tuple-element.20, f32[2,8,80,8]{3,2,1,0:T(8,128)} %copy.39, f32[2,8,8,128]{3,2,1,0:T(8,128)S(1)} %copy-done.12, f32[2,8,64,64]{3,2,1,0:T(8,128)S(1)} %copy-done.7, ...), kind=kLoop, calls=%fused_computation.158 | loop fusion | flops 1290240 | bytes 3317760 | tf_op jit(solution)/shard_map/mul | solution.py:224
  152.4 1.7 fusion.10
  154.4 1.7 fusion.26
  156.5 1.7 fusion.42
  158.5 1.7 fusion.58
  160.5 1.7 fusion.74
  162.6 1.7 fusion.90
  166.3 22.6 %all_to_all.36 = f32[2,8,64,128]{3,2,0,1:T(8,128)S(1)} all-to-all(f32[2,8,64,128]{3,2,0,1:T(8,128)S(1)} %copy.40), channel_id=1, replica_groups=mesh['sec'=8,'strip'=4] {'sec'}, dimensions={1} | all-to-all | bytes 1048576 | tf_op jit(solution)/shard_map/all_to_all | solution.py:241
  (84 shorter events, 19.6 us)
Async XLA Ops:
  0.0 7.9 %copy-start.5 = (bf16[1,512,2048]{2,1,0:T(8,128)(2,1)S(1)}, bf16[1,512,2048]{2,1,0:T(8,128)(2,1)}, u32[]{:S(2)}) copy-start(bf16[1,512,2048]{2,1,0:T(8,128)(2,1)} %param.4) | copy-start | bytes 6291460
  2.9 10.0 %copy-start.14 = (s32[25,2]{0,1:T(2,128)S(1)}, s32[25,2]{0,1:T(2,128)}, u32[]{:S(2)}) copy-start(s32[25,2]{0,1:T(2,128)} %param.5) | copy-start | bytes 604
  2.9 51.1 %copy-start.8 = (s32[2,1,128,512]{3,2,1,0:T(8,128)S(1)}, s32[2,1,128,512]{3,2,1,0:T(8,128)}, u32[]{:S(2)}) copy-start(s32[2,1,128,512]{3,2,1,0:T(8,128)} %param.6) | copy-start | bytes 1572868
  2.9 51.1 %copy-start.13 = (s32[1,128,512]{2,1,0:T(8,128)S(1)}, s32[1,128,512]{2,1,0:T(8,128)}, u32[]{:S(2)}) copy-start(s32[1,128,512]{2,1,0:T(8,128)} %param.7) | copy-start | bytes 786436
  2.9 51.1 %collective-permute-start = (bf16[256,2048]{1,0:T(8,128)(2,1)}, bf16[256,2048]{1,0:T(8,128)(2,1)S(1)}, u32[]{:S(2)}, u32[]{:S(2)}) collective-permute-start(bf16[256,2048]{1,0:T(8,128)(2,1)} %get-tuple-element.18), channel_id=1, source_target_pairs={{0,4},{4,8},{8,12},{12,16},{16,20},{20,24},{24,28},{1,5},{5,9},{9,... | collective-permute-start | bytes 3145736 | tf_op jit(solution)/shard_map/ppermute | solution.py:19
  9.6 66.8 %collective-permute-start.6 = (bf16[259,2048]{1,0:T(8,128)(2,1)}, bf16[259,2048]{1,0:T(8,128)(2,1)}, u32[]{:S(2)}, u32[]{:S(2)}) collective-permute-start(bf16[259,2048]{1,0:T(8,128)(2,1)} %get-tuple-element.15), channel_id=1, source_target_pairs={{4,0},{8,4},{12,8},{16,12},{20,16},{24,20},{28,24},{5,1},{9,5},{13... | collective-permute-start | bytes 3182600 | tf_op jit(solution)/shard_map/ppermute | solution.py:19
  10.9 65.4 %collective-permute-start.5 = (bf16[3,2048]{1,0:T(4,128)(2,1)S(1)}, bf16[3,2048]{1,0:T(4,128)(2,1)S(1)}, u32[]{:S(2)}, u32[]{:S(2)}) collective-permute-start(bf16[3,2048]{1,0:T(4,128)(2,1)S(1)} %get-tuple-element.13), channel_id=1, source_target_pairs={{4,1},{5,2},{6,3},{8,5},{9,6},{10,7},{12,9},{13,10},{14,11},{16,13... | collective-permute-start | bytes 36872 | tf_op jit(solution)/shard_map/ppermute | solution.py:184
  11.6 49.2 %collective-permute-start.7 = (bf16[3,2048]{1,0:T(4,128)(2,1)S(1)}, bf16[3,2048]{1,0:T(4,128)(2,1)S(1)}, u32[]{:S(2)}, u32[]{:S(2)}) collective-permute-start(bf16[3,2048]{1,0:T(4,128)(2,1)S(1)} %get-tuple-element.14), channel_id=1, source_target_pairs={{1,0},{2,1},{3,2},{5,4},{6,5},{7,6},{9,8},{10,9},{11,10},{13,12},{... | collective-permute-start | bytes 36872 | tf_op jit(solution)/shard_map/ppermute | solution.py:19
  55.1 37.9 %all-to-all-start = ((bf16[3,1,512,128]{3,0,1,2:T(4,128)(2,1)}), bf16[3,1,512,128]{3,0,1,2:T(4,128)(2,1)S(1)}, u32[]{:S(2)}, u32[]{:S(2)}) async-start(bf16[3,1,512,128]{3,0,1,2:T(4,128)(2,1)} %copy.30), calls=%async_computation | async-start | bytes 1048576 | tf_op jit(solution)/shard_map/all_to_all | solution.py:201
  93.0 25.1 %all-to-all-start.1 = ((f32[2,1,512,128]{3,0,1,2:T(2,128)}), f32[2,1,512,128]{3,0,1,2:T(2,128)S(1)}, u32[]{:S(2)}, u32[]{:S(2)}) async-start(f32[2,1,512,128]{3,0,1,2:T(2,128)} %copy.34), calls=%async_computation.1 | async-start | bytes 1048576 | tf_op jit(solution)/shard_map/all_to_all | solution.py:207
  99.1 5.8 %collective-permute-start.1 = (bf16[3,8,8,128]{3,2,1,0:T(8,128)(2,1)S(1)}, bf16[3,8,8,128]{3,2,1,0:T(8,128)(2,1)S(1)}, u32[]{:S(2)}, u32[]{:S(2)}) collective-permute-start(bf16[3,8,8,128]{3,2,1,0:T(8,128)(2,1)S(1)} %get-tuple-element.36), channel_id=1, source_target_pairs={{0,4},{4,8},{8,12},{12,16},{16,20},{20,24},{24,28},{1,5},{5,9},{9,... | collective-permute-start | bytes 147464 | tf_op jit(solution)/shard_map/ppermute | solution.py:30
  103.0 6.0 %collective-permute-start.2 = (bf16[3,8,8,128]{3,2,1,0:T(8,128)(2,1)S(1)}, bf16[3,8,8,128]{3,2,1,0:T(8,128)(2,1)S(1)}, u32[]{:S(2)}, u32[]{:S(2)}) collective-permute-start(bf16[3,8,8,128]{3,2,1,0:T(8,128)(2,1)S(1)} %get-tuple-element.37), channel_id=1, source_target_pairs={{4,0},{8,4},{12,8},{16,12},{20,16},{24,20},{28,24},{5,1},{9,5},{13... | collective-permute-start | bytes 147464 | tf_op jit(solution)/shard_map/ppermute | solution.py:32
  109.3 2.8 %collective-permute-start.3 = (bf16[3,8,80,8]{3,2,1,0:T(8,128)(2,1)S(1)}, bf16[3,8,80,8]{3,2,1,0:T(8,128)(2,1)S(1)}, u32[]{:S(2)}, u32[]{:S(2)}) collective-permute-start(bf16[3,8,80,8]{3,2,1,0:T(8,128)(2,1)S(1)} %get-tuple-element.34), channel_id=1, source_target_pairs={{0,1},{1,2},{2,3},{4,5},{5,6},{6,7},{8,9},{9,10},{10,11},{12,13},{... | collective-permute-start | bytes 92168 | tf_op jit(solution)/shard_map/ppermute | solution.py:30
  110.6 5.7 %collective-permute-start.4 = (bf16[3,8,80,8]{3,2,1,0:T(8,128)(2,1)S(1)}, bf16[3,8,80,8]{3,2,1,0:T(8,128)(2,1)S(1)}, u32[]{:S(2)}, u32[]{:S(2)}) collective-permute-start(bf16[3,8,80,8]{3,2,1,0:T(8,128)(2,1)S(1)} %get-tuple-element.35), channel_id=1, source_target_pairs={{1,0},{2,1},{3,2},{5,4},{6,5},{7,6},{9,8},{10,9},{11,10},{13,12},{... | collective-permute-start | bytes 92168 | tf_op jit(solution)/shard_map/ppermute | solution.py:32
  118.2 10.9 %copy-start.3 = (f32[2,1,512,128]{3,2,0,1:T(8,128)}, f32[2,1,512,128]{3,2,0,1:T(8,128)S(1)}, u32[]{:S(2)}) copy-start(f32[2,1,512,128]{3,2,0,1:T(8,128)S(1)} %copy.35) | copy-start | bytes 1572868
  118.4 5.9 %copy-start.2 = (f32[3,8,80,144]{3,2,1,0:T(8,128)S(1)}, f32[3,8,80,144]{3,2,1,0:T(8,128)}, u32[]{:S(2)}) copy-start(f32[3,8,80,144]{3,2,1,0:T(8,128)} %maximum_convert_fusion) | copy-start | bytes 3317764
  118.5 10.7 %copy-start.6 = (f32[2,8,64,64]{3,2,1,0:T(8,128)}, f32[2,8,64,64]{3,2,1,0:T(8,128)S(1)}, u32[]{:S(2)}) copy-start(f32[2,8,64,64]{3,2,1,0:T(8,128)S(1)} %concatenate.32) | copy-start | bytes 786436
  118.6 6.3 %collective-permute-start.8 = (f32[2,8,8,128]{3,2,1,0:T(8,128)S(1)}, f32[2,8,8,128]{3,2,1,0:T(8,128)S(1)}, u32[]{:S(2)}, u32[]{:S(2)}) collective-permute-start(f32[2,8,8,128]{3,2,1,0:T(8,128)S(1)} %get-tuple-element.25), channel_id=1, source_target_pairs={{0,4},{4,8},{8,12},{12,16},{16,20},{20,24},{24,28},{1,5},{5,9},{9,... | collective-permute-start | bytes 196616 | tf_op jit(solution)/shard_map/ppermute | solution.py:30
  123.0 6.2 %collective-permute-start.9 = (f32[2,8,8,128]{3,2,1,0:T(8,128)S(1)}, f32[2,8,8,128]{3,2,1,0:T(8,128)S(1)}, u32[]{:S(2)}, u32[]{:S(2)}) collective-permute-start(f32[2,8,8,128]{3,2,1,0:T(8,128)S(1)} %get-tuple-element.26), channel_id=1, source_target_pairs={{4,0},{8,4},{12,8},{16,12},{20,16},{24,20},{28,24},{5,1},{9,5},{13... | collective-permute-start | bytes 196616 | tf_op jit(solution)/shard_map/ppermute | solution.py:32
  124.8 4.7 %copy-start.9 = (f32[2,8,8,128]{3,2,1,0:T(8,128)}, f32[2,8,8,128]{3,2,1,0:T(8,128)S(1)}, u32[]{:S(2)}) copy-start(f32[2,8,8,128]{3,2,1,0:T(8,128)S(1)} %collective-permute-done.8) | copy-start | bytes 196612
  129.1 0.6 copy-start.11
  130.6 13.0 %collective-permute-start.10 = (f32[2,8,80,8]{2,3,1,0:T(8,128)}, f32[2,8,80,8]{2,3,1,0:T(8,128)}, u32[]{:S(2)}, u32[]{:S(2)}) collective-permute-start(f32[2,8,80,8]{2,3,1,0:T(8,128)} %copy.36), channel_id=1, source_target_pairs={{0,1},{1,2},{2,3},{4,5},{5,6},{6,7},{8,9},{9,10},{10,11},{12,13},{... | collective-permute-start | bytes 122888 | tf_op jit(solution)/shard_map/ppermute | solution.py:30
  139.4 6.2 %collective-permute-start.11 = (f32[2,8,80,8]{2,3,1,0:T(8,128)}, f32[2,8,80,8]{2,3,1,0:T(8,128)}, u32[]{:S(2)}, u32[]{:S(2)}) collective-permute-start(f32[2,8,80,8]{2,3,1,0:T(8,128)} %copy.37), channel_id=1, source_target_pairs={{1,0},{2,1},{3,2},{5,4},{6,5},{7,6},{9,8},{10,9},{11,10},{13,12},{... | collective-permute-start | bytes 122888 | tf_op jit(solution)/shard_map/ppermute | solution.py:32
  142.6 0.8 copy-start
  147.5 1.0 copy-start.4
  147.5 1.2 copy-start.7
  147.5 1.2 copy-start.10
  147.5 1.2 copy-start.12
  148.7 2.2 %copy-start.1 = (f32[8,80,144]{2,1,0:T(8,128)S(1)}, f32[8,80,144]{2,1,0:T(8,128)}, u32[]{:S(2)}) copy-start(f32[8,80,144]{2,1,0:T(8,128)} %copy-done) | copy-start | bytes 1105924

commit v7 on v6

--- a/solution.py
+++ b/solution.py
@@ -174,6 +174,15 @@
     return positions + relax_rate * force / (1.0 + diagonal)
 
 
+def tiles_with_halo(fields, halo):
+    count = lax.axis_size("sec")
+    columns = jnp.transpose(fields, (0, 2, 1))
+    width = columns.shape[1] // count
+    columns = jnp.pad(columns, ((0, 0), (halo, halo), (0, 0)))
+    windows = jnp.stack([columns[:, j * width : (j + 1) * width + 2 * halo] for j in range(count)], axis=1)
+    return lax.all_to_all(windows, "sec", split_axis=1, concat_axis=1, tiled=True)
+
+
 def shards(images, offsets, springs, validity):
     pixels = images[0]
     half = pixels.shape[0] // 2
@@ -198,18 +207,16 @@
     col_weight = 0.25 * springs[1, 0].astype(jnp.float32) * col_keep[None, :]
     halo = ITERS
     weights = jnp.stack([row_weight, col_weight, match_weight]).astype(jnp.bfloat16)
-    weights = lax.all_to_all(jnp.transpose(weights, (0, 2, 1))[:, None], "sec", split_axis=2, concat_axis=1, tiled=True)
-    weights = extended(weights, (("sec", 2), ("strip", 3)), halo).astype(jnp.float32)
+    weights = extended(tiles_with_halo(weights, halo), (("strip", 3),), halo).astype(jnp.float32)
     flow_top = section_flow(pixels[:half], jnp.concatenate([corner, successor_top]), offsets) * keep_mask
     flow_bottom = section_flow(prior_bottom, jnp.concatenate([pixels[half - RAD :], below]), offsets)
     flow_field = jnp.concatenate([flow_top, flow_bottom], axis=1)
-    flows = jnp.transpose(flow_field, (0, 2, 1))[:, None]
-    tiled = lax.all_to_all(flows, "sec", split_axis=2, concat_axis=1, tiled=True)
+    tiled = tiles_with_halo(flow_field, halo)
     node_half = tiled.shape[3] // 2
     bottoms = tiled[:, 1:, :, node_half:]
     bottoms = jnp.concatenate([bottoms, jnp.zeros_like(bottoms[:, :1])], axis=1)
     tiled = jnp.concatenate([tiled[:, :, :, :node_half], bottoms], axis=3)
-    flow_tiles = extended(tiled, (("sec", 2), ("strip", 3)), halo)
+    flow_tiles = extended(tiled, (("strip", 3),), halo)
     tile_row = weights[0]
     tile_col = weights[1]
     tile_match = weights[2]

time: 191 us -> 191 us (level)
  local copies, waits for them, and re-layouts: 16.7 us -> 40.4 us
  starting transfers between devices: 42.9 us -> 27.5 us
  waiting for transfers between devices: 54.5 us -> 46.6 us
  blocking collectives: 22.6 us -> 18.2 us
  other arithmetic: 24.7 us -> 26.8 us
    ppermute x4 -> x2, starting transfers between devices: 17.6 us -> 3.19 us  [extended(): lax.ppermute(tail, axis, [(i, (i + 1) % count) for i in range(ends)])]
    ppermute x4 -> x2, waiting for transfers between devices: 12.6 us -> 3.71 us  [extended(): lax.ppermute(head, axis, [((i + 1) % count, i) for i in range(ends)])]
    all_to_all x2, waiting for transfers between devices: 0.01 us -> 6.83 us  [tiles_with_halo(): lax.all_to_all(windows, 'sec', split_axis=1, concat_axis=1, tiled=True)]
    unnamed x31, local copies, waits for them, and re-layouts: 2.22 us -> 7.12 us
    ppermute x3, waiting for transfers between devices: 40.7 us -> 36.1 us  [shifted_2(): return lax.ppermute(shard, axis, pairs)]
    all_to_all x1, blocking collectives: 22.6 us -> 18.2 us  [shards(): lax.all_to_all(core, 'sec', split_axis=1, concat_axis=2, tiled=True)]
    mul x0 -> x3, local copies, waits for them, and re-layouts: none -> 2.9 us  [the longest x2 1.46 us: advance(): row_weight * (from_below - positions) + weight_up * (from_above - positions)]
    slice x4 -> x3, local copies, waits for them, and re-layouts: 1.29 us -> 4.08 us  [extended(): lax.slice_in_dim(cells, cells.shape[dim] - width, cells.shape[dim], axis=...]
  transfers between devices with their start and end apart: 14 -> 10, of which waited for: 7 -> 4; matrix products, arithmetic and copies ran while one was open for 7% -> 19% of each run, Pallas kernels for 15% -> 15%
where the time goes in v7:
time: 191 us; the launch traced here: 189 us
  waiting for transfers between devices  46.6 us (24%)
  local copies, waits for them, and re-layouts  40.4 us (21%)
  Pallas kernels  29.1 us (15%)
  starting transfers between devices  27.5 us (14%)
  other arithmetic  26.8 us (14%)
  blocking collectives  18.2 us (10%)
    ppermute x3, waiting for transfers between devices, shifted_2(): return lax.ppermute(shard, axis, pairs)  36.1 us
    pallas_call x2, Pallas kernels, section_flow(): pl.pallas_call(flow_kernel, grid_spec=grid_spec, out_shape=jax.ShapeDtype...  29.1 us
    all_to_all x1, blocking collectives, shards(): lax.all_to_all(core, 'sec', split_axis=1, concat_axis=2, tiled=True)  18.2 us
    all_to_all x2, starting transfers between devices, tiles_with_halo(): lax.all_to_all(windows, 'sec', split_axis=1, concat_axis=1, tiled=True)  11.8 us
    add x7, other arithmetic, advance(): return positions + relax_rate * force / (1.0 + diagonal)  11.6 us
    ppermute x3, starting transfers between devices, shifted_2(): return lax.ppermute(shard, axis, pairs)  8.54 us
    unnamed x31, local copies, waits for them, and re-layouts  7.12 us
    all_to_all x2, waiting for transfers between devices, tiles_with_halo(): lax.all_to_all(windows, 'sec', split_axis=1, concat_axis=1, tiled=True)  6.83 us
  transfers between devices with their start and end apart: 10, of which 4 were waited for; matrix products, arithmetic and copies ran while one was open for 19% of the time, Pallas kernels for 15%

profile of v7, /device:TPU:0, one launch (start us, length us, event | category | flops | bytes accessed | tf_op | source)
XLA Modules:
  0.0 189.0 jit_solution(9935350553003471111)
XLA Ops:
  0.0 2.9 %slice_bitcast_fusion.2 = (bf16[256,2048]{1,0:T(8,128)(2,1)S(1)}, bf16[256,2048]{1,0:T(8,128)(2,1)}) fusion(bf16[1,512,2048]{2,1,0:T(8,128)(2,1)} %param.4), kind=kLoop, calls=%fused_computation.199 | loop fusion | bytes 4194304 | tf_op jit(solution)/shard_map/slice | solution.py:211
  2.9 6.0 %collective-permute-start = (bf16[256,2048]{1,0:T(8,128)(2,1)}, bf16[256,2048]{1,0:T(8,128)(2,1)}, u32[]{:S(2)}, u32[]{:S(2)}) collective-permute-start(bf16[256,2048]{1,0:T(8,128)(2,1)} %get-tuple-element.18), channel_id=1, source_target_pairs={{0,4},{4,8},{8,12},{12,16},{16,20},{20,24},{24,28},{1,5},{5,9},{9,... | collective-permute-start | bytes 3145736 | tf_op jit(solution)/shard_map/ppermute | solution.py:19
  8.9 1.7 slice_bitcast_fusion.1
  16.8 1.5 select_maximum_fusion.following_ref
  18.3 35.7 %collective-permute-done.current_ref = bf16[256,2048]{1,0:T(8,128)(2,1)} collective-permute-done((bf16[256,2048]{1,0:T(8,128)(2,1)}, bf16[256,2048]{1,0:T(8,128)(2,1)}, u32[]{:S(2)}, u32[]{:S(2)}) %collective-permute-start) | collective-permute-done | bytes 1048608 | tf_op jit(solution)/shard_map/ppermute | solution.py:19
  62.2 5.8 %all-to-all-start = ((bf16[3,8,80,128]{3,2,0,1:T(8,128)(2,1)}), bf16[3,8,80,128]{3,2,0,1:T(8,128)(2,1)S(1)}, u32[]{:S(2)}, u32[]{:S(2)}) async-start(bf16[3,8,80,128]{3,2,0,1:T(8,128)(2,1)} %fusion.168), calls=%async_computation | async-start | bytes 983040 | tf_op jit(solution)/shard_map/all_to_all | solution.py:183
  68.0 15.1 %shard_map.47 = f32[2,64,512]{2,1,0:T(8,128)S(1)} custom-call(s32[25,2]{1,0:T(8,128)S(1)} %copy.50.offsets_ref, bf16[256,2048]{1,0:T(8,128)(2,1)} %collective-permute-done.current_ref, bf16[288,2048]{1,0:T(8,128)(2,1)S(1)} %select_maximum_fusion.following_ref, bf16[512,512]{1,0:T(8,128)(2,1)S(1)} %fusion.144.permute_ref), custom_call_target="tpu_custom_call" | custom-call | tf_op jit(solution)/shard_map/pallas_call | solution.py:147
  83.1 1.5 fusion.143.following_ref
  84.6 14.0 %shard_map.46 = f32[2,64,512]{2,1,0:T(8,128)S(1)} custom-call(s32[25,2]{1,0:T(8,128)S(1)} %copy.50.offsets_ref, bf16[256,2048]{1,0:T(8,128)(2,1)S(1)} %get-tuple-element.17.current_ref, bf16[288,2048]{1,0:T(8,128)(2,1)S(1)} %fusion.143.following_ref, bf16[512,512]{1,0:T(8,128)(2,1)S(1)} %fusion.144.permute_ref), custom_call_target="tpu_custom_call" | custom-call | tf_op jit(solution)/shard_map/pallas_call | solution.py:147
  101.5 6.0 %all-to-all-start.1 = ((f32[2,8,80,128]{3,2,0,1:T(8,128)}), f32[2,8,80,128]{3,2,0,1:T(8,128)S(1)}, u32[]{:S(2)}, u32[]{:S(2)}) async-start(f32[2,8,80,128]{3,2,0,1:T(8,128)} %copy.52), calls=%async_computation.1 | async-start | bytes 1310720 | tf_op jit(solution)/shard_map/all_to_all | solution.py:183
  107.5 1.4 copy.42
  111.6 3.7 %collective-permute-done.2 = bf16[3,8,80,8]{2,3,1,0:T(8,128)(2,1)S(1)} collective-permute-done((bf16[3,8,80,8]{2,3,1,0:T(8,128)(2,1)S(1)}, bf16[3,8,80,8]{2,3,1,0:T(8,128)(2,1)S(1)}, u32[]{:S(2)}, u32[]{:S(2)}) %collective-permute-start.2) | collective-permute-done | bytes 30752 | tf_op jit(solution)/shard_map/ppermute | solution.py:32
  116.5 6.8 %all-to-all-done.1 = f32[2,8,80,128]{3,2,0,1:T(8,128)S(1)} async-done(((f32[2,8,80,128]{3,2,0,1:T(8,128)}), f32[2,8,80,128]{3,2,0,1:T(8,128)S(1)}, u32[]{:S(2)}, u32[]{:S(2)}) %all-to-all-start.1) | async-done | bytes 655392 | tf_op jit(solution)/shard_map/all_to_all | solution.py:183
  124.4 2.1 %pad_slice_fusion.55 = f32[2,8,80,8]{3,2,0,1:T(8,128)} fusion(f32[2,7,80,64]{3,2,0,1:T(8,128)} %slice.396), kind=kLoop, calls=%fused_computation.275 | loop fusion | bytes 327680 | tf_op jit(solution)/shard_map/slice | solution.py:27
  126.6 1.9 %copy.53 = f32[2,8,80,8]{2,3,1,0:T(8,128)} copy(f32[2,8,80,8]{3,2,0,1:T(8,128)} %pad_slice_fusion.55) | data formatting | bytes 81920 | tf_op jit(solution)/shard_map/slice | solution.py:27
  128.5 1.9 %collective-permute-start.6 = (f32[2,8,80,8]{2,3,1,0:T(8,128)}, f32[2,8,80,8]{2,3,1,0:T(8,128)}, u32[]{:S(2)}, u32[]{:S(2)}) collective-permute-start(f32[2,8,80,8]{2,3,1,0:T(8,128)} %copy.53), channel_id=1, source_target_pairs={{0,1},{1,2},{2,3},{4,5},{5,6},{6,7},{8,9},{9,10},{10,11},{12,13},{... | collective-permute-start | bytes 122888 | tf_op jit(solution)/shard_map/ppermute | solution.py:30
  131.2 1.5 collective-permute-start.7
  132.7 3.2 %pad_slice_fusion.51 = (f32[8,80,144]{1,2,0:T(8,128)}, f32[8,80,144]{1,2,0:T(8,128)}, f32[8,80,144]{1,2,0:T(8,128)}) fusion(f32[8,80,144]{1,2,0:T(8,128)} %get-tuple-element.19, f32[8,80,144]{1,2,0:T(8,128)} %get-tuple-element.20, f32[8,80,144]{1,2,0:T(8,128)S(1)} %get-tuple-element.21, f32[3,8,80,144]{2,3,1,0:T(8,128)S(1)} %maximum_convert_fusion), kind=kLoop, calls=%fused_computation.206 | loop fusion | flops 552960 | bytes 2949120 | tf_op jit(solution)/shard_map/slice | solution.py:223
  135.9 1.4 copy.49
  138.0 1.4 copy.46
  140.8 2.3 %copy.57 = f32[8,80,144]{2,1,0:T(8,128)} copy(f32[8,80,144]{1,2,0:T(8,128)} %get-tuple-element.28) | data formatting | bytes 737280 | tf_op jit(solution)/shard_map/add | solution.py:174
  144.2 2.0 %concatenate.22 = f32[2,8,80,64]{3,2,0,1:T(8,128)} pad(f32[2,7,80,64]{3,2,0,1:T(8,128)} %slice.396, f32[]{:T(128)} %constant.55.clone.1), padding=0_0x0_1x0_0x0_0 | pad | bytes 614404 | tf_op jit(solution)/shard_map/concatenate | solution.py:217
  146.2 1.9 %copy.55 = f32[2,8,80,8]{3,2,0,1:T(8,128)} copy(f32[2,8,80,8]{2,3,1,0:T(8,128)} %collective-permute-done.6) | data formatting | bytes 81920 | tf_op jit(solution)/shard_map/ppermute | solution.py:30
  148.1 1.9 %copy.56 = f32[2,8,80,8]{3,2,0,1:T(8,128)} copy(f32[2,8,80,8]{2,3,1,0:T(8,128)} %collective-permute-done.7) | data formatting | bytes 81920 | tf_op jit(solution)/shard_map/ppermute | solution.py:32
  151.3 2.3 %fusion.108 = (f32[2,8,80,144]{3,2,0,1:T(8,128)S(1)}, f32[2,8,80,144]{3,2,0,1:T(8,128)S(1)}) fusion(f32[2,8,80,144]{3,2,0,1:T(8,128)S(1)} %broadcast_in_dim.2, f32[8,80,144]{2,1,0:T(8,128)S(1)} %copy.49, f32[2,8,80,8]{3,2,0,1:T(8,128)} %copy.56, f32[2,8,80,64]{3,2,0,1:T(8,128)S(1)} %copy-done.5, f32[2,8,80,64]{3,2,0,1:T(8,128)S(1)} %bitcast.108, ...), kind=kLoop, calls=%fused_computation.158 | loop fusion | flops 921600 | bytes 3317760 | tf_op jit(solution)/shard_map/mul | solution.py:231
  155.2 2.0 %fusion.10 = f32[2,8,80,144]{3,2,0,1:T(8,128)S(1)} fusion(f32[2,8,80,144]{3,2,0,1:T(8,128)S(1)} %fusion.111, f32[2,8,80,144]{3,2,0,1:T(8,128)S(1)} %get-tuple-element.12, f32[2,8,80,144]{3,2,0,1:T(8,128)S(1)} %fusion.114, f32[8,80,144]{2,1,0:T(8,128)S(1)} %copy-done, f32[8,80,144]{2,1,0:T(8,128)S(1)} %copy.49, f32[8,80,144]{2,1,0:T(8,128)S(1)} %copy.48, ...), kind=kLoop, calls=%fused_computation.60 | loop fusion | flops 3502080 | bytes 5160960 | tf_op jit(solution)/shard_map/add | solution.py:174
  157.5 1.8 fusion.26
  159.6 1.8 fusion.42
  161.7 1.8 fusion.58
  163.8 1.8 fusion.74
  165.9 1.8 fusion.90
  169.8 18.2 %all_to_all.22 = f32[2,8,64,128]{3,2,0,1:T(8,128)S(1)} all-to-all(f32[2,8,64,128]{3,2,0,1:T(8,128)S(1)} %slice_add_fusion), channel_id=1, replica_groups=mesh['sec'=8,'strip'=4] {'sec'}, dimensions={1} | all-to-all | bytes 1048576 | tf_op jit(solution)/shard_map/all_to_all | solution.py:248
  (79 shorter events, 33.7 us)
Async XLA Ops:
  0.0 8.9 %copy-start.3 = (bf16[1,512,2048]{2,1,0:T(8,128)(2,1)S(1)}, bf16[1,512,2048]{2,1,0:T(8,128)(2,1)}, u32[]{:S(2)}) copy-start(bf16[1,512,2048]{2,1,0:T(8,128)(2,1)} %param.4) | copy-start | bytes 6291460
  2.9 13.4 %copy-start.7 = (s32[25,2]{0,1:T(2,128)S(1)}, s32[25,2]{0,1:T(2,128)}, u32[]{:S(2)}) copy-start(s32[25,2]{0,1:T(2,128)} %param.5) | copy-start | bytes 604
  2.9 51.1 %collective-permute-start = (bf16[256,2048]{1,0:T(8,128)(2,1)}, bf16[256,2048]{1,0:T(8,128)(2,1)}, u32[]{:S(2)}, u32[]{:S(2)}) collective-permute-start(bf16[256,2048]{1,0:T(8,128)(2,1)} %get-tuple-element.18), channel_id=1, source_target_pairs={{0,4},{4,8},{8,12},{12,16},{16,20},{20,24},{24,28},{1,5},{5,9},{9,... | collective-permute-start | bytes 3145736 | tf_op jit(solution)/shard_map/ppermute | solution.py:19
  10.6 72.5 %collective-permute-start.4 = (bf16[259,2048]{1,0:T(8,128)(2,1)}, bf16[259,2048]{1,0:T(8,128)(2,1)}, u32[]{:S(2)}, u32[]{:S(2)}) collective-permute-start(bf16[259,2048]{1,0:T(8,128)(2,1)} %get-tuple-element.15), channel_id=1, source_target_pairs={{4,0},{8,4},{12,8},{16,12},{20,16},{24,20},{28,24},{5,1},{9,5},{13... | collective-permute-start | bytes 3182600 | tf_op jit(solution)/shard_map/ppermute | solution.py:19
  12.5 70.6 %collective-permute-start.3 = (bf16[3,2048]{1,0:T(4,128)(2,1)}, bf16[3,2048]{1,0:T(4,128)(2,1)}, u32[]{:S(2)}, u32[]{:S(2)}) collective-permute-start(bf16[3,2048]{1,0:T(4,128)(2,1)} %get-tuple-element.13), channel_id=1, source_target_pairs={{4,1},{5,2},{6,3},{8,5},{9,6},{10,7},{12,9},{13,10},{14,11},{16,13... | collective-permute-start | bytes 36872 | tf_op jit(solution)/shard_map/ppermute | solution.py:193
  13.7 3.1 %collective-permute-start.5 = (bf16[3,2048]{1,0:T(4,128)(2,1)S(1)}, bf16[3,2048]{1,0:T(4,128)(2,1)S(1)}, u32[]{:S(2)}, u32[]{:S(2)}) collective-permute-start(bf16[3,2048]{1,0:T(4,128)(2,1)S(1)} %get-tuple-element.14), channel_id=1, source_target_pairs={{1,0},{2,1},{3,2},{5,4},{6,5},{7,6},{9,8},{10,9},{11,10},{13,12},{... | collective-permute-start | bytes 36872 | tf_op jit(solution)/shard_map/ppermute | solution.py:19
  62.2 38.5 %all-to-all-start = ((bf16[3,8,80,128]{3,2,0,1:T(8,128)(2,1)}), bf16[3,8,80,128]{3,2,0,1:T(8,128)(2,1)S(1)}, u32[]{:S(2)}, u32[]{:S(2)}) async-start(bf16[3,8,80,128]{3,2,0,1:T(8,128)(2,1)} %fusion.168), calls=%async_computation | async-start | bytes 983040 | tf_op jit(solution)/shard_map/all_to_all | solution.py:183
  100.7 0.8 copy-start.6
  101.5 21.9 %all-to-all-start.1 = ((f32[2,8,80,128]{3,2,0,1:T(8,128)}), f32[2,8,80,128]{3,2,0,1:T(8,128)S(1)}, u32[]{:S(2)}, u32[]{:S(2)}) async-start(f32[2,8,80,128]{3,2,0,1:T(8,128)} %copy.52), calls=%async_computation.1 | async-start | bytes 1310720 | tf_op jit(solution)/shard_map/all_to_all | solution.py:183
  108.9 2.6 %collective-permute-start.1 = (bf16[3,8,80,8]{2,3,1,0:T(8,128)(2,1)S(1)}, bf16[3,8,80,8]{2,3,1,0:T(8,128)(2,1)S(1)}, u32[]{:S(2)}, u32[]{:S(2)}) collective-permute-start(bf16[3,8,80,8]{2,3,1,0:T(8,128)(2,1)S(1)} %get-tuple-element.25), channel_id=1, source_target_pairs={{0,1},{1,2},{2,3},{4,5},{5,6},{6,7},{8,9},{9,10},{10,11},{12,13},{... | collective-permute-start | bytes 92168 | tf_op jit(solution)/shard_map/ppermute | solution.py:30
  110.2 5.0 %collective-permute-start.2 = (bf16[3,8,80,8]{2,3,1,0:T(8,128)(2,1)S(1)}, bf16[3,8,80,8]{2,3,1,0:T(8,128)(2,1)S(1)}, u32[]{:S(2)}, u32[]{:S(2)}) collective-permute-start(bf16[3,8,80,8]{2,3,1,0:T(8,128)(2,1)S(1)} %get-tuple-element.26), channel_id=1, source_target_pairs={{1,0},{2,1},{3,2},{5,4},{6,5},{7,6},{9,8},{10,9},{11,10},{13,12},{... | collective-permute-start | bytes 92168 | tf_op jit(solution)/shard_map/ppermute | solution.py:32
  123.4 7.0 %copy-start.1 = (f32[2,8,80,128]{3,2,0,1:T(8,128)}, f32[2,8,80,128]{3,2,0,1:T(8,128)S(1)}, u32[]{:S(2)}) copy-start(f32[2,8,80,128]{3,2,0,1:T(8,128)S(1)} %all-to-all-done.1) | copy-start | bytes 1966084
  128.5 17.7 %collective-permute-start.6 = (f32[2,8,80,8]{2,3,1,0:T(8,128)}, f32[2,8,80,8]{2,3,1,0:T(8,128)}, u32[]{:S(2)}, u32[]{:S(2)}) collective-permute-start(f32[2,8,80,8]{2,3,1,0:T(8,128)} %copy.53), channel_id=1, source_target_pairs={{0,1},{1,2},{2,3},{4,5},{5,6},{6,7},{8,9},{9,10},{10,11},{12,13},{... | collective-permute-start | bytes 122888 | tf_op jit(solution)/shard_map/ppermute | solution.py:30
  131.2 16.9 %collective-permute-start.7 = (f32[2,8,80,8]{2,3,1,0:T(8,128)}, f32[2,8,80,8]{2,3,1,0:T(8,128)}, u32[]{:S(2)}, u32[]{:S(2)}) collective-permute-start(f32[2,8,80,8]{2,3,1,0:T(8,128)} %copy.54), channel_id=1, source_target_pairs={{1,0},{2,1},{3,2},{5,4},{6,5},{7,6},{9,8},{10,9},{11,10},{13,12},{... | collective-permute-start | bytes 122888 | tf_op jit(solution)/shard_map/ppermute | solution.py:32
  135.9 1.5 copy-start.4
  150.0 1.1 copy-start.2
  150.0 1.3 copy-start.5
  151.3 2.3 %copy-start = (f32[8,80,144]{2,1,0:T(8,128)S(1)}, f32[8,80,144]{2,1,0:T(8,128)}, u32[]{:S(2)}) copy-start(f32[8,80,144]{2,1,0:T(8,128)} %copy.57) | copy-start | bytes 1105924

commit v8 on v7

--- a/solution.py
+++ b/solution.py
@@ -188,8 +188,11 @@
     half = pixels.shape[0] // 2
     sec_count = lax.axis_size("sec")
     strip_count = lax.axis_size("strip")
-    successor_top = shifted_2(pixels[: half + RAD], "sec", -1)
-    prior_bottom = shifted_2(pixels[half:], "sec", 1)
+    quarter = half // 2
+    successor_first = shifted_2(pixels[: quarter + RAD], "sec", -1)
+    successor_second = shifted_2(pixels[quarter + RAD : half + RAD], "sec", -1)
+    prior_first = shifted_2(pixels[half : half + quarter], "sec", 1)
+    prior_second = shifted_2(pixels[half + quarter :], "sec", 1)
     corner = lax.ppermute(
         pixels[-RAD:],
         ("sec", "strip"),
@@ -197,7 +200,7 @@
     )
     below = shifted_2(pixels[:RAD], "strip", -1)
     keep_mask = (lax.axis_index("sec") < sec_count - 1).astype(jnp.float32)
-    springs, validity, prior_bottom = lax.optimization_barrier((springs, validity, prior_bottom))
+    springs, validity, prior_first = lax.optimization_barrier((springs, validity, prior_first))
     match_weight = validity[0].astype(jnp.float32) * keep_mask
     node_rows, node_cols = (springs.shape[2], springs.shape[3])
     global_rows = lax.axis_index("strip") * node_rows + jnp.arange(node_rows, dtype=jnp.int32)
@@ -208,9 +211,15 @@
     halo = ITERS
     weights = jnp.stack([row_weight, col_weight, match_weight]).astype(jnp.bfloat16)
     weights = extended(tiles_with_halo(weights, halo), (("strip", 3),), halo).astype(jnp.float32)
-    flow_top = section_flow(pixels[:half], jnp.concatenate([corner, successor_top]), offsets) * keep_mask
-    flow_bottom = section_flow(prior_bottom, jnp.concatenate([pixels[half - RAD :], below]), offsets)
-    flow_field = jnp.concatenate([flow_top, flow_bottom], axis=1)
+    first_top = section_flow(pixels[:quarter], jnp.concatenate([corner, successor_first]), offsets)
+    first_bottom = section_flow(prior_first, pixels[half - RAD : half + quarter + RAD], offsets)
+    second_top = section_flow(
+        pixels[quarter:half], jnp.concatenate([successor_first[quarter - RAD :], successor_second]), offsets
+    )
+    second_bottom = section_flow(prior_second, jnp.concatenate([pixels[half + quarter - RAD :], below]), offsets)
+    flow_field = jnp.concatenate(
+        [first_top * keep_mask, second_top * keep_mask, first_bottom, second_bottom], axis=1
+    )
     tiled = tiles_with_halo(flow_field, halo)
     node_half = tiled.shape[3] // 2
     bottoms = tiled[:, 1:, :, node_half:]

time: 191 us -> 202 us (1.058)
  starting transfers between devices: 27.5 us -> 36.3 us
    ppermute x3 -> x5, starting transfers between devices: 8.54 us -> 15.8 us  [shifted_2(): return lax.ppermute(shard, axis, pairs)]
    pallas_call x2 -> x4, Pallas kernels: 29.1 us -> 30.6 us  [section_flow(): pl.pallas_call(flow_kernel, grid_spec=grid_spec, out_shape=jax.ShapeDtype...]
    ppermute x3 -> x5, waiting for transfers between devices: 36.1 us -> 35.7 us  [shifted_2(): return lax.ppermute(shard, axis, pairs)]
    slice x2 -> x4, local copies, waits for them, and re-layouts: 4.58 us -> 4.65 us  [the longest x1 2.35 us: shards(): successor_first = shifted_2(pixels[:quarter + RAD], 'sec', -1)]
  transfers between devices with their start and end apart: 10 -> 12, of which waited for: 4 -> 3; matrix products, arithmetic and copies ran while one was open for 19% -> 21% of each run, Pallas kernels for 15% -> 15%
where the time goes in v8:
time: 202 us; the launch traced here: 201 us
  waiting for transfers between devices  47.4 us (23%)
  local copies, waits for them, and re-layouts  40.4 us (20%)
  starting transfers between devices  36.3 us (18%)
  Pallas kernels  30.6 us (15%)
  other arithmetic  26.4 us (13%)
  blocking collectives  19 us (9%)
    ppermute x5, waiting for transfers between devices, shifted_2(): return lax.ppermute(shard, axis, pairs)  35.7 us
    pallas_call x4, Pallas kernels, section_flow(): pl.pallas_call(flow_kernel, grid_spec=grid_spec, out_shape=jax.ShapeDtype...  30.6 us
    all_to_all x1, blocking collectives, shards(): lax.all_to_all(core, 'sec', split_axis=1, concat_axis=2, tiled=True)  19 us
    ppermute x5, starting transfers between devices, shifted_2(): return lax.ppermute(shard, axis, pairs)  15.8 us
    all_to_all x2, starting transfers between devices, tiles_with_halo(): lax.all_to_all(windows, 'sec', split_axis=1, concat_axis=1, tiled=True)  12.3 us
    add x7, other arithmetic, advance(): return positions + relax_rate * force / (1.0 + diagonal)  11.4 us
    all_to_all x2, waiting for transfers between devices, tiles_with_halo(): lax.all_to_all(windows, 'sec', split_axis=1, concat_axis=1, tiled=True)  7.83 us
    unnamed x31, local copies, waits for them, and re-layouts  7.04 us
  transfers between devices with their start and end apart: 12, of which 3 were waited for; matrix products, arithmetic and copies ran while one was open for 21% of the time, Pallas kernels for 15%

profile of v8, /device:TPU:0, one launch (start us, length us, event | category | flops | bytes accessed | tf_op | source)
XLA Modules:
  0.0 200.6 jit_solution(17430014065723934935)
XLA Ops:
  2.9 2.4 %slice_bitcast_fusion.5 = (bf16[131,2048]{1,0:T(8,128)(2,1)}, bf16[131,2048]{1,0:T(8,128)(2,1)}) fusion(bf16[1,512,2048]{2,1,0:T(8,128)(2,1)} %param.4), kind=kLoop, calls=%fused_computation.210 | loop fusion | bytes 2146304 | tf_op jit(solution)/shard_map/slice | solution.py:192
  7.9 6.3 %collective-permute-start.6 = (bf16[128,2048]{1,0:T(8,128)(2,1)}, bf16[128,2048]{1,0:T(8,128)(2,1)S(1)}, u32[]{:S(2)}, u32[]{:S(2)}) collective-permute-start(bf16[128,2048]{1,0:T(8,128)(2,1)} %get-tuple-element.16), channel_id=1, source_target_pairs={{0,4},{4,8},{8,12},{12,16},{16,20},{20,24},{24,28},{1,5},{5,9},{9,... | collective-permute-start | bytes 1572872 | tf_op jit(solution)/shard_map/ppermute | solution.py:19
  14.2 5.7 %collective-permute-start = (bf16[128,2048]{1,0:T(8,128)(2,1)}, bf16[128,2048]{1,0:T(8,128)(2,1)}, u32[]{:S(2)}, u32[]{:S(2)}) collective-permute-start(bf16[128,2048]{1,0:T(8,128)(2,1)} %get-tuple-element.19), channel_id=1, source_target_pairs={{0,4},{4,8},{8,12},{12,16},{16,20},{20,24},{24,28},{1,5},{5,9},{9,... | collective-permute-start | bytes 1572872 | tf_op jit(solution)/shard_map/ppermute | solution.py:19
  23.0 35.7 %collective-permute-done.current_ref = bf16[128,2048]{1,0:T(8,128)(2,1)} collective-permute-done((bf16[128,2048]{1,0:T(8,128)(2,1)}, bf16[128,2048]{1,0:T(8,128)(2,1)}, u32[]{:S(2)}, u32[]{:S(2)}) %collective-permute-start) | collective-permute-done | bytes 524320 | tf_op jit(solution)/shard_map/ppermute | solution.py:19
  58.7 1.8 copy.49
  60.4 2.0 %copy.47 = s32[2,1,128,512]{2,3,1,0:T(8,128)} copy(s32[2,1,128,512]{3,2,1,0:T(8,128)} %param.6) | data formatting | bytes 1048576 | tf_op jit(solution)/shard_map/optimization_barrier | solution.py:203
  68.8 6.3 %all-to-all-start = ((bf16[3,8,80,128]{3,2,0,1:T(8,128)(2,1)}), bf16[3,8,80,128]{3,2,0,1:T(8,128)(2,1)}, u32[]{:S(2)}, u32[]{:S(2)}) async-start(bf16[3,8,80,128]{3,2,0,1:T(8,128)(2,1)} %fusion.165), calls=%async_computation | async-start | bytes 983040 | tf_op jit(solution)/shard_map/all_to_all | solution.py:183
  75.1 8.4 %shard_map.48 = f32[2,32,512]{2,1,0:T(8,128)S(1)} custom-call(s32[25,2]{1,0:T(8,128)S(1)} %copy.58.offsets_ref, bf16[128,2048]{1,0:T(8,128)(2,1)} %collective-permute-done.current_ref, bf16[160,2048]{1,0:T(8,128)(2,1)S(1)} %pad.116.following_ref, bf16[512,512]{1,0:T(8,128)(2,1)S(1)} %fusion.141.permute_ref), custom_call_target="tpu_custom_call" | custom-call | tf_op jit(solution)/shard_map/pallas_call | solution.py:147
  83.5 7.4 %shard_map.49 = f32[2,32,512]{2,1,0:T(8,128)S(1)} custom-call(s32[25,2]{1,0:T(8,128)S(1)} %copy.58.offsets_ref, bf16[128,2048]{1,0:T(8,128)(2,1)S(1)} %collective-permute-done.6.current_ref, bf16[160,2048]{1,0:T(8,128)(2,1)S(1)} %select_maximum_fusion.following_ref, bf16[512,512]{1,0:T(8,128)(2,1)S(1)} %fusion.141.permute_ref), custom_call_target="tpu_custom_call" | custom-call | tf_op jit(solution)/shard_map/pallas_call | solution.py:147
  92.1 7.4 %shard_map.46 = f32[2,32,512]{2,1,0:T(8,128)S(1)} custom-call(s32[25,2]{1,0:T(8,128)S(1)} %copy.58.offsets_ref, bf16[128,2048]{1,0:T(8,128)(2,1)S(1)} %get-tuple-element.15.current_ref, bf16[160,2048]{1,0:T(8,128)(2,1)S(1)} %select_maximum_fusion.2.following_ref, bf16[512,512]{1,0:T(8,128)(2,1)S(1)} %fusion.141.permute_ref), custom_call_target="tpu_custom_call" | custom-call | tf_op jit(solution)/shard_map/pallas_call | solution.py:147
  101.6 7.4 %shard_map.47 = f32[2,32,512]{2,1,0:T(8,128)S(1)} custom-call(s32[25,2]{1,0:T(8,128)S(1)} %copy.58.offsets_ref, bf16[128,2048]{1,0:T(8,128)(2,1)S(1)} %get-tuple-element.18.current_ref, bf16[160,2048]{1,0:T(8,128)(2,1)S(1)} %select_maximum_fusion.1.following_ref, bf16[512,512]{1,0:T(8,128)(2,1)S(1)} %fusion.141.permute_ref), custom_call_target="tpu_custom_call" | custom-call | tf_op jit(solution)/shard_map/pallas_call | solution.py:147
  111.0 6.0 %all-to-all-start.1 = ((f32[2,8,80,128]{3,2,0,1:T(8,128)}), f32[2,8,80,128]{3,2,0,1:T(8,128)S(1)}, u32[]{:S(2)}, u32[]{:S(2)}) async-start(f32[2,8,80,128]{3,2,0,1:T(8,128)} %copy.62), calls=%async_computation.1 | async-start | bytes 1310720 | tf_op jit(solution)/shard_map/all_to_all | solution.py:183
  117.1 1.4 copy.50
  121.1 3.8 %collective-permute-done.2 = bf16[3,8,80,8]{2,3,1,0:T(8,128)(2,1)S(1)} collective-permute-done((bf16[3,8,80,8]{2,3,1,0:T(8,128)(2,1)S(1)}, bf16[3,8,80,8]{2,3,1,0:T(8,128)(2,1)S(1)}, u32[]{:S(2)}, u32[]{:S(2)}) %collective-permute-start.2) | collective-permute-done | bytes 30752 | tf_op jit(solution)/shard_map/ppermute | solution.py:32
  126.2 7.8 %all-to-all-done.1 = f32[2,8,80,128]{3,2,0,1:T(8,128)S(1)} async-done(((f32[2,8,80,128]{3,2,0,1:T(8,128)}), f32[2,8,80,128]{3,2,0,1:T(8,128)S(1)}, u32[]{:S(2)}, u32[]{:S(2)}) %all-to-all-start.1) | async-done | bytes 655392 | tf_op jit(solution)/shard_map/all_to_all | solution.py:183
  137.3 2.1 %pad_slice_fusion.55 = f32[2,8,80,8]{3,2,0,1:T(8,128)} fusion(f32[2,7,80,64]{3,2,0,1:T(8,128)} %slice.433), kind=kLoop, calls=%fused_computation.279 | loop fusion | bytes 327680 | tf_op jit(solution)/shard_map/slice | solution.py:27
  139.4 1.9 copy.63
  141.3 3.6 %collective-permute-start.8 = (f32[2,8,80,8]{2,3,1,0:T(8,128)}, f32[2,8,80,8]{2,3,1,0:T(8,128)}, u32[]{:S(2)}, u32[]{:S(2)}) collective-permute-start(f32[2,8,80,8]{2,3,1,0:T(8,128)} %copy.63), channel_id=1, source_target_pairs={{0,1},{1,2},{2,3},{4,5},{5,6},{6,7},{8,9},{9,10},{10,11},{12,13},{... | collective-permute-start | bytes 122888 | tf_op jit(solution)/shard_map/ppermute | solution.py:30
  144.9 3.2 %pad_slice_fusion.51 = (f32[8,80,144]{1,2,0:T(8,128)}, f32[8,80,144]{1,2,0:T(8,128)}, f32[8,80,144]{1,2,0:T(8,128)}) fusion(f32[8,80,144]{1,2,0:T(8,128)S(1)} %get-tuple-element.22, f32[8,80,144]{1,2,0:T(8,128)} %get-tuple-element.23, f32[8,80,144]{1,2,0:T(8,128)} %get-tuple-element.24, f32[3,8,80,144]{2,3,1,0:T(8,128)S(1)} %maximum_convert_fusion), kind=kLoop, calls=%fused_computation.201 | loop fusion | flops 552960 | bytes 2949120 | tf_op jit(solution)/shard_map/slice | solution.py:232
  148.1 1.4 copy.57
  150.2 1.4 copy.54
  155.2 2.0 concatenate.26
  157.2 1.9 copy.66
  159.1 1.9 copy.65
  162.3 2.3 %fusion.107 = (f32[2,8,80,144]{3,2,0,1:T(8,128)S(1)}, f32[2,8,80,144]{3,2,0,1:T(8,128)S(1)}) fusion(f32[2,8,80,144]{3,2,0,1:T(8,128)S(1)} %broadcast_in_dim.2, f32[8,80,144]{2,1,0:T(8,128)S(1)} %copy.57, f32[2,8,80,8]{3,2,0,1:T(8,128)} %copy.66, f32[2,8,80,64]{3,2,0,1:T(8,128)S(1)} %copy-done.6, f32[2,8,80,64]{3,2,0,1:T(8,128)S(1)} %bitcast.116, ...), kind=kLoop, calls=%fused_computation.157 | loop fusion | flops 921600 | bytes 3317760 | tf_op jit(solution)/shard_map/mul | solution.py:240
  166.2 1.8 fusion.9
  168.3 1.8 fusion.25
  170.4 1.8 fusion.41
  172.5 1.8 fusion.57
  174.6 1.8 fusion.73
  176.7 1.8 fusion.89
  180.5 19.0 %all_to_all.22 = f32[2,8,64,128]{3,2,0,1:T(8,128)S(1)} all-to-all(f32[2,8,64,128]{3,2,0,1:T(8,128)S(1)} %slice_add_fusion), channel_id=1, replica_groups=mesh['sec'=8,'strip'=4] {'sec'}, dimensions={1} | all-to-all | bytes 1048576 | tf_op jit(solution)/shard_map/all_to_all | solution.py:257
  (89 shorter events, 38.9 us)
Async XLA Ops:
  0.0 6.6 %copy-start.4 = (bf16[1,512,2048]{2,1,0:T(8,128)(2,1)S(1)}, bf16[1,512,2048]{2,1,0:T(8,128)(2,1)}, u32[]{:S(2)}) copy-start(bf16[1,512,2048]{2,1,0:T(8,128)(2,1)} %param.4) | copy-start | bytes 6291460
  0.9 89.9 %collective-permute-start.3 = (bf16[3,2048]{1,0:T(4,128)(2,1)S(1)}, bf16[3,2048]{1,0:T(4,128)(2,1)S(1)}, u32[]{:S(2)}, u32[]{:S(2)}) collective-permute-start(bf16[3,2048]{1,0:T(4,128)(2,1)S(1)} %get-tuple-element.13), channel_id=1, source_target_pairs={{4,1},{5,2},{6,3},{8,5},{9,6},{10,7},{12,9},{13,10},{14,11},{16,13... | collective-permute-start | bytes 36872 | tf_op jit(solution)/shard_map/ppermute | solution.py:196
  1.6 18.8 %collective-permute-start.7 = (bf16[3,2048]{1,0:T(4,128)(2,1)S(1)}, bf16[3,2048]{1,0:T(4,128)(2,1)S(1)}, u32[]{:S(2)}, u32[]{:S(2)}) collective-permute-start(bf16[3,2048]{1,0:T(4,128)(2,1)S(1)} %get-tuple-element.14), channel_id=1, source_target_pairs={{1,0},{2,1},{3,2},{5,4},{6,5},{7,6},{9,8},{10,9},{11,10},{13,12},{... | collective-permute-start | bytes 36872 | tf_op jit(solution)/shard_map/ppermute | solution.py:19
  5.3 85.6 %collective-permute-start.4 = (bf16[131,2048]{1,0:T(8,128)(2,1)}, bf16[131,2048]{1,0:T(8,128)(2,1)}, u32[]{:S(2)}, u32[]{:S(2)}) collective-permute-start(bf16[131,2048]{1,0:T(8,128)(2,1)} %get-tuple-element.20), channel_id=1, source_target_pairs={{4,0},{8,4},{12,8},{16,12},{20,16},{24,20},{28,24},{5,1},{9,5},{13... | collective-permute-start | bytes 1609736 | tf_op jit(solution)/shard_map/ppermute | solution.py:19
  7.9 12.3 %copy-start.7 = (s32[25,2]{0,1:T(2,128)S(1)}, s32[25,2]{0,1:T(2,128)}, u32[]{:S(2)}) copy-start(s32[25,2]{0,1:T(2,128)} %param.5) | copy-start | bytes 604
  7.9 75.6 %collective-permute-start.6 = (bf16[128,2048]{1,0:T(8,128)(2,1)}, bf16[128,2048]{1,0:T(8,128)(2,1)S(1)}, u32[]{:S(2)}, u32[]{:S(2)}) collective-permute-start(bf16[128,2048]{1,0:T(8,128)(2,1)} %get-tuple-element.16), channel_id=1, source_target_pairs={{0,4},{4,8},{8,12},{12,16},{16,20},{20,24},{24,28},{1,5},{5,9},{9,... | collective-permute-start | bytes 1572872 | tf_op jit(solution)/shard_map/ppermute | solution.py:19
  14.2 44.5 %collective-permute-start = (bf16[128,2048]{1,0:T(8,128)(2,1)}, bf16[128,2048]{1,0:T(8,128)(2,1)}, u32[]{:S(2)}, u32[]{:S(2)}) collective-permute-start(bf16[128,2048]{1,0:T(8,128)(2,1)} %get-tuple-element.19), channel_id=1, source_target_pairs={{0,4},{4,8},{8,12},{12,16},{16,20},{20,24},{24,28},{1,5},{5,9},{9,... | collective-permute-start | bytes 1572872 | tf_op jit(solution)/shard_map/ppermute | solution.py:19
  20.4 79.9 %collective-permute-start.5 = (bf16[128,2048]{1,0:T(8,128)(2,1)}, bf16[128,2048]{1,0:T(8,128)(2,1)}, u32[]{:S(2)}, u32[]{:S(2)}) collective-permute-start(bf16[128,2048]{1,0:T(8,128)(2,1)} %get-tuple-element.17), channel_id=1, source_target_pairs={{4,0},{8,4},{12,8},{16,12},{20,16},{24,20},{28,24},{5,1},{9,5},{13... | collective-permute-start | bytes 1572872 | tf_op jit(solution)/shard_map/ppermute | solution.py:19
  68.8 42.2 %all-to-all-start = ((bf16[3,8,80,128]{3,2,0,1:T(8,128)(2,1)}), bf16[3,8,80,128]{3,2,0,1:T(8,128)(2,1)}, u32[]{:S(2)}, u32[]{:S(2)}) async-start(bf16[3,8,80,128]{3,2,0,1:T(8,128)(2,1)} %fusion.165), calls=%async_computation | async-start | bytes 983040 | tf_op jit(solution)/shard_map/all_to_all | solution.py:183
  111.0 23.0 %all-to-all-start.1 = ((f32[2,8,80,128]{3,2,0,1:T(8,128)}), f32[2,8,80,128]{3,2,0,1:T(8,128)S(1)}, u32[]{:S(2)}, u32[]{:S(2)}) async-start(f32[2,8,80,128]{3,2,0,1:T(8,128)} %copy.62), calls=%async_computation.1 | async-start | bytes 1310720 | tf_op jit(solution)/shard_map/all_to_all | solution.py:183
  118.5 2.6 %collective-permute-start.1 = (bf16[3,8,80,8]{2,3,1,0:T(8,128)(2,1)S(1)}, bf16[3,8,80,8]{2,3,1,0:T(8,128)(2,1)S(1)}, u32[]{:S(2)}, u32[]{:S(2)}) collective-permute-start(bf16[3,8,80,8]{2,3,1,0:T(8,128)(2,1)S(1)} %get-tuple-element.28), channel_id=1, source_target_pairs={{0,1},{1,2},{2,3},{4,5},{5,6},{6,7},{8,9},{9,10},{10,11},{12,13},{... | collective-permute-start | bytes 92168 | tf_op jit(solution)/shard_map/ppermute | solution.py:30
  119.8 5.2 %collective-permute-start.2 = (bf16[3,8,80,8]{2,3,1,0:T(8,128)(2,1)S(1)}, bf16[3,8,80,8]{2,3,1,0:T(8,128)(2,1)S(1)}, u32[]{:S(2)}, u32[]{:S(2)}) collective-permute-start(bf16[3,8,80,8]{2,3,1,0:T(8,128)(2,1)S(1)} %get-tuple-element.29), channel_id=1, source_target_pairs={{1,0},{2,1},{3,2},{5,4},{6,5},{7,6},{9,8},{10,9},{11,10},{13,12},{... | collective-permute-start | bytes 92168 | tf_op jit(solution)/shard_map/ppermute | solution.py:32
  134.1 5.3 %copy-start.2 = (f32[2,8,80,128]{3,2,0,1:T(8,128)}, f32[2,8,80,128]{3,2,0,1:T(8,128)S(1)}, u32[]{:S(2)}) copy-start(f32[2,8,80,128]{3,2,0,1:T(8,128)S(1)} %all-to-all-done.1) | copy-start | bytes 1966084
  134.9 22.2 %collective-permute-start.9 = (f32[2,8,80,8]{2,3,1,0:T(8,128)}, f32[2,8,80,8]{2,3,1,0:T(8,128)}, u32[]{:S(2)}, u32[]{:S(2)}) collective-permute-start(f32[2,8,80,8]{2,3,1,0:T(8,128)} %copy.64), channel_id=1, source_target_pairs={{1,0},{2,1},{3,2},{5,4},{6,5},{7,6},{9,8},{10,9},{11,10},{13,12},{... | collective-permute-start | bytes 122888 | tf_op jit(solution)/shard_map/ppermute | solution.py:32
  141.3 17.8 %collective-permute-start.8 = (f32[2,8,80,8]{2,3,1,0:T(8,128)}, f32[2,8,80,8]{2,3,1,0:T(8,128)}, u32[]{:S(2)}, u32[]{:S(2)}) collective-permute-start(f32[2,8,80,8]{2,3,1,0:T(8,128)} %copy.63), channel_id=1, source_target_pairs={{0,1},{1,2},{2,3},{4,5},{5,6},{6,7},{8,9},{9,10},{10,11},{12,13},{... | collective-permute-start | bytes 122888 | tf_op jit(solution)/shard_map/ppermute | solution.py:30
  148.1 1.5 copy-start.5
  153.0 0.8 copy-start
  161.0 1.1 copy-start.3
  161.0 1.3 copy-start.6
  162.3 2.3 %copy-start.1 = (f32[8,80,144]{2,1,0:T(8,128)S(1)}, f32[8,80,144]{2,1,0:T(8,128)}, u32[]{:S(2)}) copy-start(f32[8,80,144]{2,1,0:T(8,128)} %copy-done) | copy-start | bytes 1105924

commit v9 on v7

--- a/solution.py
+++ b/solution.py
@@ -176,10 +176,10 @@
 
 def tiles_with_halo(fields, halo):
     count = lax.axis_size("sec")
-    columns = jnp.transpose(fields, (0, 2, 1))
-    width = columns.shape[1] // count
-    columns = jnp.pad(columns, ((0, 0), (halo, halo), (0, 0)))
-    windows = jnp.stack([columns[:, j * width : (j + 1) * width + 2 * halo] for j in range(count)], axis=1)
+    fields = extended(fields, (("strip", 1),), halo)
+    width = fields.shape[2] // count
+    columns = jnp.pad(fields, ((0, 0), (0, 0), (halo, halo)))
+    windows = jnp.stack([columns[:, :, j * width : (j + 1) * width + 2 * halo] for j in range(count)], axis=1)
     return lax.all_to_all(windows, "sec", split_axis=1, concat_axis=1, tiled=True)
 
 
@@ -207,21 +207,21 @@
     col_weight = 0.25 * springs[1, 0].astype(jnp.float32) * col_keep[None, :]
     halo = ITERS
     weights = jnp.stack([row_weight, col_weight, match_weight]).astype(jnp.bfloat16)
-    weights = extended(tiles_with_halo(weights, halo), (("strip", 3),), halo).astype(jnp.float32)
+    weights = tiles_with_halo(weights, halo).astype(jnp.float32)
     flow_top = section_flow(pixels[:half], jnp.concatenate([corner, successor_top]), offsets) * keep_mask
     flow_bottom = section_flow(prior_bottom, jnp.concatenate([pixels[half - RAD :], below]), offsets)
     flow_field = jnp.concatenate([flow_top, flow_bottom], axis=1)
     tiled = tiles_with_halo(flow_field, halo)
-    node_half = tiled.shape[3] // 2
-    bottoms = tiled[:, 1:, :, node_half:]
-    bottoms = jnp.concatenate([bottoms, jnp.zeros_like(bottoms[:, :1])], axis=1)
-    tiled = jnp.concatenate([tiled[:, :, :, :node_half], bottoms], axis=3)
-    flow_tiles = extended(tiled, (("strip", 3),), halo)
+    node_half = flow_field.shape[1] // 2
+    following = jnp.concatenate([tiled[:, 1:], jnp.zeros_like(tiled[:, :1])], axis=1)
+    row_ids = jnp.arange(tiled.shape[2], dtype=jnp.int32)[:, None]
+    from_prior = (row_ids < halo) | ((row_ids >= halo + node_half) & (row_ids < halo + 2 * node_half))
+    flow_tiles = jnp.where(from_prior, following, tiled)
     tile_row = weights[0]
     tile_col = weights[1]
     tile_match = weights[2]
-    weight_up = jnp.pad(tile_row, ((0, 0), (0, 0), (1, 0)))[:, :, :-1]
-    weight_left = jnp.pad(tile_col, ((0, 0), (1, 0), (0, 0)))[:, :-1, :]
+    weight_up = jnp.pad(tile_row, ((0, 0), (1, 0), (0, 0)))[:, :-1, :]
+    weight_left = jnp.pad(tile_col, ((0, 0), (0, 0), (1, 0)))[:, :, :-1]
     match_prior = jnp.pad(tile_match, ((1, 0), (0, 0), (0, 0)))[:-1]
     diagonal = tile_row + weight_up + tile_col + weight_left + tile_match + match_prior
     positions = jnp.zeros_like(flow_tiles)
@@ -232,10 +232,10 @@
         pull_prior = jnp.pad(pull_term, ((0, 0), (1, 0), (0, 0), (0, 0)))[:, :-1]
         positions = advance(
             positions,
+            padded[:, :, 2:, 1:-1],
+            padded[:, :, :-2, 1:-1],
             padded[:, :, 1:-1, 2:],
             padded[:, :, 1:-1, :-2],
-            padded[:, :, 2:, 1:-1],
-            padded[:, :, :-2, 1:-1],
             tile_row,
             weight_up,
             tile_col,
@@ -245,8 +245,7 @@
             diagonal,
         )
     core = positions[:, :, halo:-halo, halo:-halo]
-    returned = lax.all_to_all(core, "sec", split_axis=1, concat_axis=2, tiled=True)
-    return jnp.transpose(returned, (0, 1, 3, 2))
+    return lax.all_to_all(core, "sec", split_axis=1, concat_axis=3, tiled=True)
 
 
 def solution(mesh):

time: 191 us -> 197 us (1.031)
  waiting for transfers between devices: 46.6 us -> 83.8 us
  local copies, waits for them, and re-layouts: 40.4 us -> 21.5 us
  other arithmetic: 26.8 us -> 17.5 us
    all_to_all x2, waiting for transfers between devices: 6.83 us -> 44.6 us  [tiles_with_halo(): lax.all_to_all(windows, 'sec', split_axis=1, concat_axis=1, tiled=True)]
    unnamed x31 -> x25, local copies, waits for them, and re-layouts: 7.12 us -> 11.6 us
    slice x3 -> x1, local copies, waits for them, and re-layouts: 4.08 us -> 0.01 us  [extended(): lax.slice_in_dim(cells, cells.shape[dim] - width, cells.shape[dim], axis=...]
    ppermute x2 -> x0, local copies, waits for them, and re-layouts: 3.86 us -> none  [the longest x1 1.93 us: extended(): lax.ppermute(tail, axis, [(i, (i + 1) % count) for i in range(ends)])]
    ppermute x2, waiting for transfers between devices: 3.71 us -> 0.01 us  [extended(): lax.ppermute(head, axis, [((i + 1) % count, i) for i in range(ends)])]
    slice x5 -> x3, local copies, waits for them, and re-layouts: 6.1 us -> 2.96 us  [the longest x1 1.66 us: shards(): pixels[half - RAD:]]
    ppermute x3, waiting for transfers between devices: 36.1 us -> 39.1 us  [shifted_2(): return lax.ppermute(shard, axis, pairs)]
    ppermute x2, starting transfers between devices: 3.19 us -> 6.22 us  [extended(): lax.ppermute(tail, axis, [(i, (i + 1) % count) for i in range(ends)])]
  transfers between devices with their start and end apart: 10 -> 10, of which waited for: 4 -> 4; matrix products, arithmetic and copies ran while one was open for 19% -> 10% of each run, Pallas kernels for 15% -> 14%
where the time goes in v9:
time: 197 us
  waiting for transfers between devices  83.8 us (43%)
  Pallas kernels  28 us (14%)
  starting transfers between devices  27.2 us (14%)
  local copies, waits for them, and re-layouts  21.5 us (11%)
  blocking collectives  18.1 us (9%)
  other arithmetic  17.5 us (9%)
    all_to_all x2, waiting for transfers between devices, tiles_with_halo(): lax.all_to_all(windows, 'sec', split_axis=1, concat_axis=1, tiled=True)  44.6 us
    ppermute x3, waiting for transfers between devices, shifted_2(): return lax.ppermute(shard, axis, pairs)  39.1 us
    pallas_call x2, Pallas kernels, section_flow(): pl.pallas_call(flow_kernel, grid_spec=grid_spec, out_shape=jax.ShapeDtype...  28 us
    all_to_all x1, blocking collectives, shards(): return lax.all_to_all(core, 'sec', split_axis=1, concat_axis=3, tiled=True)  18.1 us
    unnamed x25, local copies, waits for them, and re-layouts  11.6 us
    all_to_all x2, starting transfers between devices, tiles_with_halo(): lax.all_to_all(windows, 'sec', split_axis=1, concat_axis=1, tiled=True)  10.1 us
    add x7, other arithmetic, advance(): return positions + relax_rate * force / (1.0 + diagonal)  8.54 us
    ppermute x3, starting transfers between devices, shifted_2(): return lax.ppermute(shard, axis, pairs)  7.63 us
  transfers between devices with their start and end apart: 10, of which 4 were waited for; matrix products, arithmetic and copies ran while one was open for 10% of the time, Pallas kernels for 14%

profile of v9, /device:TPU:0, one launch (start us, length us, event | category | flops | bytes accessed | tf_op | source)
XLA Modules:
  0.0 196.6 jit_solution(1697281206400571782)
XLA Ops:
  0.0 2.8 %slice_bitcast_fusion.2 = (bf16[256,2048]{1,0:T(8,128)(2,1)S(1)}, bf16[256,2048]{1,0:T(8,128)(2,1)}) fusion(bf16[1,512,2048]{2,1,0:T(8,128)(2,1)} %param.4), kind=kLoop, calls=%fused_computation.141 | loop fusion | bytes 4194304 | tf_op jit(solution)/shard_map/slice | solution.py:211
  2.8 5.1 %collective-permute-start = (bf16[256,2048]{1,0:T(8,128)(2,1)}, bf16[256,2048]{1,0:T(8,128)(2,1)S(1)}, u32[]{:S(2)}, u32[]{:S(2)}) collective-permute-start(bf16[256,2048]{1,0:T(8,128)(2,1)} %get-tuple-element.18), channel_id=1, source_target_pairs={{0,4},{4,8},{8,12},{12,16},{16,20},{20,24},{24,28},{1,5},{5,9},{9,... | collective-permute-start | bytes 3145736 | tf_op jit(solution)/shard_map/ppermute | solution.py:19
  7.9 1.7 slice_bitcast_fusion.1
  9.6 1.3 collective-permute-start.6
  11.6 1.3 collective-permute-start.3
  13.2 1.4 collective-permute-done.3
  14.6 1.6 fusion.61.following_ref
  16.2 37.7 %collective-permute-done.current_ref = bf16[256,2048]{1,0:T(8,128)(2,1)S(1)} collective-permute-done((bf16[256,2048]{1,0:T(8,128)(2,1)}, bf16[256,2048]{1,0:T(8,128)(2,1)S(1)}, u32[]{:S(2)}, u32[]{:S(2)}) %collective-permute-start) | collective-permute-done | bytes 1048608 | tf_op jit(solution)/shard_map/ppermute | solution.py:19
  54.1 1.3 collective-permute-start.1
  55.4 1.3 collective-permute-start.2
  56.7 14.0 %shard_map.46 = f32[2,64,512]{2,1,0:T(8,128)S(1)} custom-call(s32[25,2]{1,0:T(8,128)S(1)} %copy.17.offsets_ref, bf16[256,2048]{1,0:T(8,128)(2,1)S(1)} %collective-permute-done.current_ref, bf16[288,2048]{1,0:T(8,128)(2,1)S(1)} %fusion.61.following_ref, bf16[512,512]{1,0:T(8,128)(2,1)S(1)} %fusion.96.permute_ref), custom_call_target="tpu_custom_call" | custom-call | tf_op jit(solution)/shard_map/pallas_call | solution.py:147
  70.7 4.9 %collective-permute-start.4 = (f32[2,8,512]{2,1,0:T(8,128)S(1)}, f32[2,8,512]{2,1,0:T(8,128)S(1)}, u32[]{:S(2)}, u32[]{:S(2)}) collective-permute-start(f32[2,8,512]{2,1,0:T(8,128)S(1)} %slice.381), channel_id=1, source_target_pairs={{0,1},{1,2},{2,3},{4,5},{5,6},{6,7},{8,9},{9,10},{10,11},{12,13},{... | collective-permute-start | bytes 98312 | tf_op jit(solution)/shard_map/ppermute | solution.py:30
  75.6 1.5 select_maximum_fusion.following_ref
  77.2 14.0 %shard_map.47 = f32[2,64,512]{2,1,0:T(8,128)S(1)} custom-call(s32[25,2]{1,0:T(8,128)S(1)} %copy.17.offsets_ref, bf16[256,2048]{1,0:T(8,128)(2,1)S(1)} %get-tuple-element.17.current_ref, bf16[288,2048]{1,0:T(8,128)(2,1)S(1)} %select_maximum_fusion.following_ref, bf16[512,512]{1,0:T(8,128)(2,1)S(1)} %fusion.96.permute_ref), custom_call_target="tpu_custom_call" | custom-call | tf_op jit(solution)/shard_map/pallas_call | solution.py:147
  91.2 1.3 collective-permute-start.7
  98.5 5.7 %all-to-all-start = ((bf16[3,8,144,80]{3,2,0,1:T(8,128)(2,1)}), bf16[3,8,144,80]{3,2,0,1:T(8,128)(2,1)S(1)}, u32[]{:S(2)}, u32[]{:S(2)}) async-start(bf16[3,8,144,80]{3,2,0,1:T(8,128)(2,1)} %fusion.114), calls=%async_computation | async-start | bytes 1769472 | tf_op jit(solution)/shard_map/all_to_all | solution.py:183
  110.4 16.6 %all-to-all-done = bf16[3,8,144,80]{3,2,0,1:T(8,128)(2,1)S(1)} async-done(((bf16[3,8,144,80]{3,2,0,1:T(8,128)(2,1)}), bf16[3,8,144,80]{3,2,0,1:T(8,128)(2,1)S(1)}, u32[]{:S(2)}, u32[]{:S(2)}) %all-to-all-start) | async-done | bytes 552992 | tf_op jit(solution)/shard_map/all_to_all | solution.py:183
  127.0 4.4 %all-to-all-start.1 = ((f32[2,8,144,80]{3,2,0,1:T(8,128)}), f32[2,8,144,80]{3,2,0,1:T(8,128)}, u32[]{:S(2)}, u32[]{:S(2)}) async-start(f32[2,8,144,80]{3,2,0,1:T(8,128)} %fusion.104), calls=%async_computation.1 | async-start | bytes 2359296 | tf_op jit(solution)/shard_map/all_to_all | solution.py:183
  132.2 1.0 slice.394
  133.2 28.0 %all-to-all-done.1 = f32[2,8,144,80]{3,2,0,1:T(8,128)} async-done(((f32[2,8,144,80]{3,2,0,1:T(8,128)}), f32[2,8,144,80]{3,2,0,1:T(8,128)}, u32[]{:S(2)}, u32[]{:S(2)}) %all-to-all-start.1) | async-done | bytes 737312 | tf_op jit(solution)/shard_map/all_to_all | solution.py:183
  161.2 1.3 slice.389
  162.6 1.6 fusion.2
  165.3 1.2 fusion.12
  166.8 1.2 fusion.19
  168.2 1.2 fusion.26
  169.6 1.2 fusion.33
  171.0 1.2 fusion.40
  172.4 1.2 fusion.47
  173.6 1.0 multiply_add_fusion
  175.7 1.4 slice_add_fusion
  177.4 18.1 %all_to_all.28 = f32[2,8,128,64]{2,3,0,1:T(8,128)S(1)} all-to-all(f32[2,8,128,64]{2,3,0,1:T(8,128)S(1)} %copy.19), channel_id=1, replica_groups=mesh['sec'=8,'strip'=4] {'sec'}, dimensions={1} | all-to-all | bytes 1048576 | tf_op jit(solution)/shard_map/all_to_all | solution.py:248
  195.6 1.0 copy.21
  (62 shorter events, 17.7 us)
Async XLA Ops:
  0.0 7.9 %copy-start = (bf16[1,512,2048]{2,1,0:T(8,128)(2,1)S(1)}, bf16[1,512,2048]{2,1,0:T(8,128)(2,1)}, u32[]{:S(2)}) copy-start(bf16[1,512,2048]{2,1,0:T(8,128)(2,1)} %param.4) | copy-start | bytes 6291460
  2.8 10.2 %copy-start.4 = (s32[25,2]{0,1:T(2,128)S(1)}, s32[25,2]{0,1:T(2,128)}, u32[]{:S(2)}) copy-start(s32[25,2]{0,1:T(2,128)} %param.5) | copy-start | bytes 604
  2.8 51.1 %collective-permute-start = (bf16[256,2048]{1,0:T(8,128)(2,1)}, bf16[256,2048]{1,0:T(8,128)(2,1)S(1)}, u32[]{:S(2)}, u32[]{:S(2)}) collective-permute-start(bf16[256,2048]{1,0:T(8,128)(2,1)} %get-tuple-element.18), channel_id=1, source_target_pairs={{0,4},{4,8},{8,12},{12,16},{16,20},{20,24},{24,28},{1,5},{5,9},{9,... | collective-permute-start | bytes 3145736 | tf_op jit(solution)/shard_map/ppermute | solution.py:19
  9.6 66.1 %collective-permute-start.6 = (bf16[259,2048]{1,0:T(8,128)(2,1)}, bf16[259,2048]{1,0:T(8,128)(2,1)}, u32[]{:S(2)}, u32[]{:S(2)}) collective-permute-start(bf16[259,2048]{1,0:T(8,128)(2,1)} %get-tuple-element.14), channel_id=1, source_target_pairs={{4,0},{8,4},{12,8},{16,12},{20,16},{24,20},{28,24},{5,1},{9,5},{13... | collective-permute-start | bytes 3182600 | tf_op jit(solution)/shard_map/ppermute | solution.py:19
  10.9 64.7 %collective-permute-start.5 = (bf16[3,2048]{1,0:T(4,128)(2,1)S(1)}, bf16[3,2048]{1,0:T(4,128)(2,1)S(1)}, u32[]{:S(2)}, u32[]{:S(2)}) collective-permute-start(bf16[3,2048]{1,0:T(4,128)(2,1)S(1)} %get-tuple-element.16), channel_id=1, source_target_pairs={{4,1},{5,2},{6,3},{8,5},{9,6},{10,7},{12,9},{13,10},{14,11},{16,13... | collective-permute-start | bytes 36872 | tf_op jit(solution)/shard_map/ppermute | solution.py:193
  11.6 3.1 %collective-permute-start.3 = (bf16[3,2048]{1,0:T(4,128)(2,1)S(1)}, bf16[3,2048]{1,0:T(4,128)(2,1)S(1)}, u32[]{:S(2)}, u32[]{:S(2)}) collective-permute-start(bf16[3,2048]{1,0:T(4,128)(2,1)S(1)} %get-tuple-element.15), channel_id=1, source_target_pairs={{1,0},{2,1},{3,2},{5,4},{6,5},{7,6},{9,8},{10,9},{11,10},{13,12},{... | collective-permute-start | bytes 36872 | tf_op jit(solution)/shard_map/ppermute | solution.py:19
  13.0 40.9 %copy-start.3 = (s32[1,128,512]{2,1,0:T(8,128)S(1)}, s32[1,128,512]{2,1,0:T(8,128)}, u32[]{:S(2)}) copy-start(s32[1,128,512]{2,1,0:T(8,128)} %param.7) | copy-start | bytes 786436
  14.6 39.3 %copy-start.2 = (s32[2,1,128,512]{3,2,1,0:T(8,128)S(1)}, s32[2,1,128,512]{3,2,1,0:T(8,128)}, u32[]{:S(2)}) copy-start(s32[2,1,128,512]{3,2,1,0:T(8,128)} %param.6) | copy-start | bytes 1572868
  54.1 38.5 %collective-permute-start.1 = (bf16[3,8,512]{2,1,0:T(8,128)(2,1)S(1)}, bf16[3,8,512]{2,1,0:T(8,128)(2,1)S(1)}, u32[]{:S(2)}, u32[]{:S(2)}) collective-permute-start(bf16[3,8,512]{2,1,0:T(8,128)(2,1)S(1)} %get-tuple-element.30), channel_id=1, source_target_pairs={{0,1},{1,2},{2,3},{4,5},{5,6},{6,7},{8,9},{9,10},{10,11},{12,13},{... | collective-permute-start | bytes 73736 | tf_op jit(solution)/shard_map/ppermute | solution.py:30
  55.4 37.2 %collective-permute-start.2 = (bf16[3,8,512]{2,1,0:T(8,128)(2,1)S(1)}, bf16[3,8,512]{2,1,0:T(8,128)(2,1)S(1)}, u32[]{:S(2)}, u32[]{:S(2)}) collective-permute-start(bf16[3,8,512]{2,1,0:T(8,128)(2,1)S(1)} %get-tuple-element.31), channel_id=1, source_target_pairs={{1,0},{2,1},{3,2},{5,4},{6,5},{7,6},{9,8},{10,9},{11,10},{13,12},{... | collective-permute-start | bytes 73736 | tf_op jit(solution)/shard_map/ppermute | solution.py:32
  70.7 33.5 %collective-permute-start.4 = (f32[2,8,512]{2,1,0:T(8,128)S(1)}, f32[2,8,512]{2,1,0:T(8,128)S(1)}, u32[]{:S(2)}, u32[]{:S(2)}) collective-permute-start(f32[2,8,512]{2,1,0:T(8,128)S(1)} %slice.381), channel_id=1, source_target_pairs={{0,1},{1,2},{2,3},{4,5},{5,6},{6,7},{8,9},{9,10},{10,11},{12,13},{... | collective-permute-start | bytes 98312 | tf_op jit(solution)/shard_map/ppermute | solution.py:30
  91.2 13.0 %collective-permute-start.7 = (f32[2,8,512]{2,1,0:T(8,128)S(1)}, f32[2,8,512]{2,1,0:T(8,128)S(1)}, u32[]{:S(2)}, u32[]{:S(2)}) collective-permute-start(f32[2,8,512]{2,1,0:T(8,128)S(1)} %slice.382), channel_id=1, source_target_pairs={{1,0},{2,1},{3,2},{5,4},{6,5},{7,6},{9,8},{10,9},{11,10},{13,12},{... | collective-permute-start | bytes 98312 | tf_op jit(solution)/shard_map/ppermute | solution.py:32
  98.5 28.5 %all-to-all-start = ((bf16[3,8,144,80]{3,2,0,1:T(8,128)(2,1)}), bf16[3,8,144,80]{3,2,0,1:T(8,128)(2,1)S(1)}, u32[]{:S(2)}, u32[]{:S(2)}) async-start(bf16[3,8,144,80]{3,2,0,1:T(8,128)(2,1)} %fusion.114), calls=%async_computation | async-start | bytes 1769472 | tf_op jit(solution)/shard_map/all_to_all | solution.py:183
  127.0 34.1 %all-to-all-start.1 = ((f32[2,8,144,80]{3,2,0,1:T(8,128)}), f32[2,8,144,80]{3,2,0,1:T(8,128)}, u32[]{:S(2)}, u32[]{:S(2)}) async-start(f32[2,8,144,80]{3,2,0,1:T(8,128)} %fusion.104), calls=%async_computation.1 | async-start | bytes 2359296 | tf_op jit(solution)/shard_map/all_to_all | solution.py:183
  174.6 1.0 copy-start.1

commit v10 on v9

--- a/solution.py
+++ b/solution.py
@@ -180,7 +180,9 @@
     width = fields.shape[2] // count
     columns = jnp.pad(fields, ((0, 0), (0, 0), (halo, halo)))
     windows = jnp.stack([columns[:, :, j * width : (j + 1) * width + 2 * halo] for j in range(count)], axis=1)
-    return lax.all_to_all(windows, "sec", split_axis=1, concat_axis=1, tiled=True)
+    shape = windows.shape
+    flat = windows.reshape(shape[0], shape[1], shape[2] * shape[3])
+    return lax.all_to_all(flat, "sec", split_axis=1, concat_axis=1, tiled=True).reshape(shape)
 
 
 def shards(images, offsets, springs, validity):
@@ -245,7 +247,10 @@
             diagonal,
         )
     core = positions[:, :, halo:-halo, halo:-halo]
-    return lax.all_to_all(core, "sec", split_axis=1, concat_axis=3, tiled=True)
+    shape = core.shape
+    flat = core.reshape(shape[0], shape[1], shape[2] * shape[3])
+    returned = lax.all_to_all(flat, "sec", split_axis=1, concat_axis=1, tiled=True).reshape(shape)
+    return jnp.transpose(returned, (0, 2, 1, 3)).reshape(shape[0], 1, shape[2], shape[1] * shape[3])
 
 
 def solution(mesh):

time: 197 us -> 191 us (0.970)
  waiting for transfers between devices: 83.8 us -> 66 us
  local copies, waits for them, and re-layouts: 21.5 us -> 34.4 us
    all_to_all x2, waiting for transfers between devices: 44.6 us -> 26.8 us  [tiles_with_halo(): lax.all_to_all(flat, 'sec', split_axis=1, concat_axis=1, tiled=True)]
    reshape x0 -> x5, local copies, waits for them, and re-layouts: none -> 5.2 us  [the longest x1 3.03 us: tiles_with_halo(): lax.all_to_all(flat, 'sec', split_axis=1, concat_axis=1, tiled=True)]
    slice x0 -> x3, local copies, waits for them, and re-layouts: none -> 3.54 us  [the longest x1 2.86 us: shards(): tile_row = weights[0]]
    another operation x2 -> x18, local copies, waits for them, and re-layouts: 1.49 us -> 4.22 us  [tiles_with_halo(): jnp.stack([columns[:, :, j * width:(j + 1) * width + 2 * halo] for j in r...]
    unnamed x25 -> x27, local copies, waits for them, and re-layouts: 11.6 us -> 11.4 us
  transfers between devices with their start and end apart: 10 -> 10, of which waited for: 4 -> 4; matrix products, arithmetic and copies ran while one was open for 10% -> 13% of each run, Pallas kernels for 14% -> 15%
where the time goes in v10:
time: 191 us; the launch traced here: 190 us
  waiting for transfers between devices  66 us (35%)
  local copies, waits for them, and re-layouts  34.4 us (18%)
  Pallas kernels  28 us (15%)
  starting transfers between devices  27.3 us (14%)
  blocking collectives  18 us (9%)
  other arithmetic  15.8 us (8%)
    ppermute x3, waiting for transfers between devices, shifted_2(): return lax.ppermute(shard, axis, pairs)  39.1 us
    pallas_call x2, Pallas kernels, section_flow(): pl.pallas_call(flow_kernel, grid_spec=grid_spec, out_shape=jax.ShapeDtype...  28 us
    all_to_all x2, waiting for transfers between devices, tiles_with_halo(): lax.all_to_all(flat, 'sec', split_axis=1, concat_axis=1, tiled=True)  26.8 us
    all_to_all x1, blocking collectives, shards(): lax.all_to_all(flat, 'sec', split_axis=1, concat_axis=1, tiled=True)  18 us
    unnamed x27, local copies, waits for them, and re-layouts  11.4 us
    all_to_all x2, starting transfers between devices, tiles_with_halo(): lax.all_to_all(flat, 'sec', split_axis=1, concat_axis=1, tiled=True)  10.2 us
    add x7, other arithmetic, advance(): return positions + relax_rate * force / (1.0 + diagonal)  8.23 us
    ppermute x3, starting transfers between devices, shifted_2(): return lax.ppermute(shard, axis, pairs)  7.63 us
  transfers between devices with their start and end apart: 10, of which 4 were waited for; matrix products, arithmetic and copies ran while one was open for 13% of the time, Pallas kernels for 15%

profile of v10, /device:TPU:0, one launch (start us, length us, event | category | flops | bytes accessed | tf_op | source)
XLA Modules:
  0.0 190.0 jit_solution(13533758542655695471)
XLA Ops:
  0.0 2.8 %slice_bitcast_fusion.2 = (bf16[256,2048]{1,0:T(8,128)(2,1)S(1)}, bf16[256,2048]{1,0:T(8,128)(2,1)}) fusion(bf16[1,512,2048]{2,1,0:T(8,128)(2,1)} %param.4), kind=kLoop, calls=%fused_computation.141 | loop fusion | bytes 4194304 | tf_op jit(solution)/shard_map/slice | solution.py:213
  2.8 5.1 %collective-permute-start = (bf16[256,2048]{1,0:T(8,128)(2,1)}, bf16[256,2048]{1,0:T(8,128)(2,1)S(1)}, u32[]{:S(2)}, u32[]{:S(2)}) collective-permute-start(bf16[256,2048]{1,0:T(8,128)(2,1)} %get-tuple-element.21), channel_id=1, source_target_pairs={{0,4},{4,8},{8,12},{12,16},{16,20},{20,24},{24,28},{1,5},{5,9},{9,... | collective-permute-start | bytes 3145736 | tf_op jit(solution)/shard_map/ppermute | solution.py:19
  7.9 1.7 slice_bitcast_fusion.1
  9.6 1.3 collective-permute-start.6
  11.6 1.3 collective-permute-start.3
  13.2 1.4 collective-permute-done.3
  14.6 1.6 fusion.61.following_ref
  16.2 37.7 %collective-permute-done.current_ref = bf16[256,2048]{1,0:T(8,128)(2,1)S(1)} collective-permute-done((bf16[256,2048]{1,0:T(8,128)(2,1)}, bf16[256,2048]{1,0:T(8,128)(2,1)S(1)}, u32[]{:S(2)}, u32[]{:S(2)}) %collective-permute-start) | collective-permute-done | bytes 1048608 | tf_op jit(solution)/shard_map/ppermute | solution.py:19
  54.1 1.3 collective-permute-start.1
  55.4 1.3 collective-permute-start.2
  56.7 14.0 %shard_map.46 = f32[2,64,512]{2,1,0:T(8,128)S(1)} custom-call(s32[25,2]{1,0:T(8,128)S(1)} %copy.12.offsets_ref, bf16[256,2048]{1,0:T(8,128)(2,1)S(1)} %collective-permute-done.current_ref, bf16[288,2048]{1,0:T(8,128)(2,1)S(1)} %fusion.61.following_ref, bf16[512,512]{1,0:T(8,128)(2,1)S(1)} %fusion.96.permute_ref), custom_call_target="tpu_custom_call" | custom-call | tf_op jit(solution)/shard_map/pallas_call | solution.py:147
  70.7 4.9 %collective-permute-start.4 = (f32[2,8,512]{2,1,0:T(8,128)S(1)}, f32[2,8,512]{2,1,0:T(8,128)S(1)}, u32[]{:S(2)}, u32[]{:S(2)}) collective-permute-start(f32[2,8,512]{2,1,0:T(8,128)S(1)} %slice.384), channel_id=1, source_target_pairs={{0,1},{1,2},{2,3},{4,5},{5,6},{6,7},{8,9},{9,10},{10,11},{12,13},{... | collective-permute-start | bytes 98312 | tf_op jit(solution)/shard_map/ppermute | solution.py:30
  75.7 1.5 select_maximum_fusion.following_ref
  77.2 14.0 %shard_map.47 = f32[2,64,512]{2,1,0:T(8,128)S(1)} custom-call(s32[25,2]{1,0:T(8,128)S(1)} %copy.12.offsets_ref, bf16[256,2048]{1,0:T(8,128)(2,1)S(1)} %get-tuple-element.20.current_ref, bf16[288,2048]{1,0:T(8,128)(2,1)S(1)} %select_maximum_fusion.following_ref, bf16[512,512]{1,0:T(8,128)(2,1)S(1)} %fusion.96.permute_ref), custom_call_target="tpu_custom_call" | custom-call | tf_op jit(solution)/shard_map/pallas_call | solution.py:147
  91.3 1.3 collective-permute-start.7
  99.8 5.7 %all-to-all-start = ((bf16[3,8,11520]{2,0,1:T(4,128)(2,1)}), bf16[3,8,11520]{2,0,1:T(4,128)(2,1)S(1)}, u32[]{:S(2)}, u32[]{:S(2)}) async-start(bf16[3,8,11520]{2,0,1:T(4,128)(2,1)} %constant_dynamic-update-slice_fusion), calls=%async_computation | async-start | bytes 1474560 | tf_op jit(solution)/shard_map/all_to_all | solution.py:185
  112.4 12.5 %all-to-all-done = bf16[3,8,11520]{2,0,1:T(4,128)(2,1)S(1)} async-done(((bf16[3,8,11520]{2,0,1:T(4,128)(2,1)}), bf16[3,8,11520]{2,0,1:T(4,128)(2,1)S(1)}, u32[]{:S(2)}, u32[]{:S(2)}) %all-to-all-start) | async-done | bytes 552992 | tf_op jit(solution)/shard_map/all_to_all | solution.py:185
  124.9 4.6 %all-to-all-start.1 = ((f32[2,8,11520]{2,0,1:T(2,128)}), f32[2,8,11520]{2,0,1:T(2,128)}, u32[]{:S(2)}, u32[]{:S(2)}) async-start(f32[2,8,11520]{2,0,1:T(2,128)} %constant_dynamic-update-slice_fusion.8), calls=%async_computation.1 | async-start | bytes 1474560 | tf_op jit(solution)/shard_map/all_to_all | solution.py:185
  129.6 2.9 %slice_reduce_fusion.2 = (f32[8,11520]{1,0:T(8,128)S(1)}, f32[8,11520]{1,0:T(8,128)S(1)}, f32[8,11520]{1,0:T(8,128)S(1)}) fusion(f32[3,8,11520]{2,0,1:T(4,128)S(1)} %convert_element_type.100), kind=kLoop, calls=%fused_computation.158 | loop fusion | bytes 2211840 | tf_op jit(solution)/shard_map/slice | solution.py:222
  134.2 1.0 slice.397
  135.2 14.3 %all-to-all-done.1 = f32[2,8,11520]{2,0,1:T(2,128)} async-done(((f32[2,8,11520]{2,0,1:T(2,128)}), f32[2,8,11520]{2,0,1:T(2,128)}, u32[]{:S(2)}, u32[]{:S(2)}) %all-to-all-start.1) | async-done | bytes 737312 | tf_op jit(solution)/shard_map/all_to_all | solution.py:185
  149.6 2.0 %copy.14 = f32[2,8,11520]{2,1,0:T(8,128)} copy(f32[2,8,11520]{2,0,1:T(2,128)} %all-to-all-done.1) | data formatting | bytes 1474560 | tf_op jit(solution)/shard_map/all_to_all | solution.py:185
  151.6 3.0 %reshape.203 = f32[2,8,144,80]{3,2,1,0:T(8,128)} reshape(f32[2,8,11520]{2,1,0:T(8,128)} %copy.14) | data formatting | bytes 1474560 | tf_op jit(solution)/shard_map/reshape | solution.py:185
  154.7 1.2 copy-done
  157.7 1.1 fusion.12
  159.0 1.1 fusion.19
  160.4 1.1 fusion.26
  161.7 1.3 fusion.33
  163.3 1.1 fusion.40
  164.6 1.1 fusion.47
  167.7 1.4 slice_add_fusion
  169.9 18.0 %all_to_all.15 = f32[2,8,8192]{2,0,1:T(2,128)S(1)} all-to-all(f32[2,8,8192]{2,0,1:T(2,128)S(1)} %copy.15), channel_id=1, replica_groups=mesh['sec'=8,'strip'=4] {'sec'}, dimensions={1} | all-to-all | bytes 1048576 | tf_op jit(solution)/shard_map/all_to_all | solution.py:252
  (91 shorter events, 24.9 us)
Async XLA Ops:
  0.0 7.9 %copy-start.1 = (bf16[1,512,2048]{2,1,0:T(8,128)(2,1)S(1)}, bf16[1,512,2048]{2,1,0:T(8,128)(2,1)}, u32[]{:S(2)}) copy-start(bf16[1,512,2048]{2,1,0:T(8,128)(2,1)} %param.4) | copy-start | bytes 6291460
  2.8 10.2 %copy-start.5 = (s32[25,2]{0,1:T(2,128)S(1)}, s32[25,2]{0,1:T(2,128)}, u32[]{:S(2)}) copy-start(s32[25,2]{0,1:T(2,128)} %param.5) | copy-start | bytes 604
  2.8 51.1 %collective-permute-start = (bf16[256,2048]{1,0:T(8,128)(2,1)}, bf16[256,2048]{1,0:T(8,128)(2,1)S(1)}, u32[]{:S(2)}, u32[]{:S(2)}) collective-permute-start(bf16[256,2048]{1,0:T(8,128)(2,1)} %get-tuple-element.21), channel_id=1, source_target_pairs={{0,4},{4,8},{8,12},{12,16},{16,20},{20,24},{24,28},{1,5},{5,9},{9,... | collective-permute-start | bytes 3145736 | tf_op jit(solution)/shard_map/ppermute | solution.py:19
  9.6 66.1 %collective-permute-start.6 = (bf16[259,2048]{1,0:T(8,128)(2,1)}, bf16[259,2048]{1,0:T(8,128)(2,1)}, u32[]{:S(2)}, u32[]{:S(2)}) collective-permute-start(bf16[259,2048]{1,0:T(8,128)(2,1)} %get-tuple-element.17), channel_id=1, source_target_pairs={{4,0},{8,4},{12,8},{16,12},{20,16},{24,20},{28,24},{5,1},{9,5},{13... | collective-permute-start | bytes 3182600 | tf_op jit(solution)/shard_map/ppermute | solution.py:19
  10.9 64.7 %collective-permute-start.5 = (bf16[3,2048]{1,0:T(4,128)(2,1)S(1)}, bf16[3,2048]{1,0:T(4,128)(2,1)S(1)}, u32[]{:S(2)}, u32[]{:S(2)}) collective-permute-start(bf16[3,2048]{1,0:T(4,128)(2,1)S(1)} %get-tuple-element.19), channel_id=1, source_target_pairs={{4,1},{5,2},{6,3},{8,5},{9,6},{10,7},{12,9},{13,10},{14,11},{16,13... | collective-permute-start | bytes 36872 | tf_op jit(solution)/shard_map/ppermute | solution.py:195
  11.6 3.1 %collective-permute-start.3 = (bf16[3,2048]{1,0:T(4,128)(2,1)S(1)}, bf16[3,2048]{1,0:T(4,128)(2,1)S(1)}, u32[]{:S(2)}, u32[]{:S(2)}) collective-permute-start(bf16[3,2048]{1,0:T(4,128)(2,1)S(1)} %get-tuple-element.18), channel_id=1, source_target_pairs={{1,0},{2,1},{3,2},{5,4},{6,5},{7,6},{9,8},{10,9},{11,10},{13,12},{... | collective-permute-start | bytes 36872 | tf_op jit(solution)/shard_map/ppermute | solution.py:19
  13.0 40.9 %copy-start.4 = (s32[1,128,512]{2,1,0:T(8,128)S(1)}, s32[1,128,512]{2,1,0:T(8,128)}, u32[]{:S(2)}) copy-start(s32[1,128,512]{2,1,0:T(8,128)} %param.7) | copy-start | bytes 786436
  14.6 39.3 %copy-start.3 = (s32[2,1,128,512]{3,2,1,0:T(8,128)S(1)}, s32[2,1,128,512]{3,2,1,0:T(8,128)}, u32[]{:S(2)}) copy-start(s32[2,1,128,512]{3,2,1,0:T(8,128)} %param.6) | copy-start | bytes 1572868
  54.1 38.5 %collective-permute-start.1 = (bf16[3,8,512]{2,1,0:T(8,128)(2,1)S(1)}, bf16[3,8,512]{2,1,0:T(8,128)(2,1)S(1)}, u32[]{:S(2)}, u32[]{:S(2)}) collective-permute-start(bf16[3,8,512]{2,1,0:T(8,128)(2,1)S(1)} %get-tuple-element.46), channel_id=1, source_target_pairs={{0,1},{1,2},{2,3},{4,5},{5,6},{6,7},{8,9},{9,10},{10,11},{12,13},{... | collective-permute-start | bytes 73736 | tf_op jit(solution)/shard_map/ppermute | solution.py:30
  55.4 37.2 %collective-permute-start.2 = (bf16[3,8,512]{2,1,0:T(8,128)(2,1)S(1)}, bf16[3,8,512]{2,1,0:T(8,128)(2,1)S(1)}, u32[]{:S(2)}, u32[]{:S(2)}) collective-permute-start(bf16[3,8,512]{2,1,0:T(8,128)(2,1)S(1)} %get-tuple-element.47), channel_id=1, source_target_pairs={{1,0},{2,1},{3,2},{5,4},{6,5},{7,6},{9,8},{10,9},{11,10},{13,12},{... | collective-permute-start | bytes 73736 | tf_op jit(solution)/shard_map/ppermute | solution.py:32
  70.7 34.8 %collective-permute-start.4 = (f32[2,8,512]{2,1,0:T(8,128)S(1)}, f32[2,8,512]{2,1,0:T(8,128)S(1)}, u32[]{:S(2)}, u32[]{:S(2)}) collective-permute-start(f32[2,8,512]{2,1,0:T(8,128)S(1)} %slice.384), channel_id=1, source_target_pairs={{0,1},{1,2},{2,3},{4,5},{5,6},{6,7},{8,9},{9,10},{10,11},{12,13},{... | collective-permute-start | bytes 98312 | tf_op jit(solution)/shard_map/ppermute | solution.py:30
  91.3 14.2 %collective-permute-start.7 = (f32[2,8,512]{2,1,0:T(8,128)S(1)}, f32[2,8,512]{2,1,0:T(8,128)S(1)}, u32[]{:S(2)}, u32[]{:S(2)}) collective-permute-start(f32[2,8,512]{2,1,0:T(8,128)S(1)} %slice.385), channel_id=1, source_target_pairs={{1,0},{2,1},{3,2},{5,4},{6,5},{7,6},{9,8},{10,9},{11,10},{13,12},{... | collective-permute-start | bytes 98312 | tf_op jit(solution)/shard_map/ppermute | solution.py:32
  99.8 25.1 %all-to-all-start = ((bf16[3,8,11520]{2,0,1:T(4,128)(2,1)}), bf16[3,8,11520]{2,0,1:T(4,128)(2,1)S(1)}, u32[]{:S(2)}, u32[]{:S(2)}) async-start(bf16[3,8,11520]{2,0,1:T(4,128)(2,1)} %constant_dynamic-update-slice_fusion), calls=%async_computation | async-start | bytes 1474560 | tf_op jit(solution)/shard_map/all_to_all | solution.py:185
  124.9 24.7 %all-to-all-start.1 = ((f32[2,8,11520]{2,0,1:T(2,128)}), f32[2,8,11520]{2,0,1:T(2,128)}, u32[]{:S(2)}, u32[]{:S(2)}) async-start(f32[2,8,11520]{2,0,1:T(2,128)} %constant_dynamic-update-slice_fusion.8), calls=%async_computation.1 | async-start | bytes 1474560 | tf_op jit(solution)/shard_map/all_to_all | solution.py:185
  154.6 1.3 copy-start
  154.6 1.6 slice-start
  166.7 1.0 copy-start.2

commit v11 on v10

--- a/solution.py
+++ b/solution.py
@@ -208,12 +208,12 @@
     row_weight = 0.25 * springs[0, 0].astype(jnp.float32) * row_keep[:, None]
     col_weight = 0.25 * springs[1, 0].astype(jnp.float32) * col_keep[None, :]
     halo = ITERS
-    weights = jnp.stack([row_weight, col_weight, match_weight]).astype(jnp.bfloat16)
-    weights = tiles_with_halo(weights, halo).astype(jnp.float32)
     flow_top = section_flow(pixels[:half], jnp.concatenate([corner, successor_top]), offsets) * keep_mask
     flow_bottom = section_flow(prior_bottom, jnp.concatenate([pixels[half - RAD :], below]), offsets)
     flow_field = jnp.concatenate([flow_top, flow_bottom], axis=1)
-    tiled = tiles_with_halo(flow_field, halo)
+    tiled = tiles_with_halo(jnp.concatenate([flow_field, jnp.stack([row_weight, col_weight, match_weight])]), halo)
+    weights = tiled[2:]
+    tiled = tiled[:2]
     node_half = flow_field.shape[1] // 2
     following = jnp.concatenate([tiled[:, 1:], jnp.zeros_like(tiled[:, :1])], axis=1)
     row_ids = jnp.arange(tiled.shape[2], dtype=jnp.int32)[:, None]

time: 191 us -> 220 us (1.15)
  waiting for transfers between devices: 66 us -> 110 us
  starting transfers between devices: 27.3 us -> 17.8 us
  local copies, waits for them, and re-layouts: 34.4 us -> 28.1 us
    all_to_all x2 -> x1, waiting for transfers between devices: 26.8 us -> 66.5 us  [tiles_with_halo(): lax.all_to_all(flat, 'sec', split_axis=1, concat_axis=1, tiled=True)]
    slice x6 -> x4, local copies, waits for them, and re-layouts: 1.99 us -> 8.5 us  [the longest x2 5.06 us: shards(): tiled = tiled[:2]]
    unnamed x27 -> x20, local copies, waits for them, and re-layouts: 11.4 us -> 5.5 us
    all_to_all x2 -> x1, starting transfers between devices: 10.2 us -> 5.68 us  [tiles_with_halo(): lax.all_to_all(flat, 'sec', split_axis=1, concat_axis=1, tiled=True)]
    ppermute x2 -> x1, starting transfers between devices: 6.22 us -> 1.92 us  [extended(): lax.ppermute(tail, axis, [(i, (i + 1) % count) for i in range(ends)])]
    ppermute x2 -> x1, waiting for transfers between devices: 0.01 us -> 3.13 us  [extended(): lax.ppermute(head, axis, [((i + 1) % count, i) for i in range(ends)])]
    reshape x1 -> x0, local copies, waits for them, and re-layouts: 3.03 us -> none  [tiles_with_halo(): lax.all_to_all(flat, 'sec', split_axis=1, concat_axis=1, tiled=True)]
  transfers between devices with their start and end apart: 10 -> 7, of which waited for: 4 -> 4; matrix products, arithmetic and copies ran while one was open for 13% -> 1% of each run, Pallas kernels for 15% -> 6%
where the time goes in v11:
time: 220 us; the launch traced here: 219 us
  waiting for transfers between devices  110 us (50%)
  local copies, waits for them, and re-layouts  28.1 us (13%)
  Pallas kernels  28 us (13%)
  blocking collectives  19.6 us (9%)
  starting transfers between devices  17.8 us (8%)
  other arithmetic  16 us (7%)
    all_to_all x1, waiting for transfers between devices, tiles_with_halo(): lax.all_to_all(flat, 'sec', split_axis=1, concat_axis=1, tiled=True)  66.5 us
    ppermute x3, waiting for transfers between devices, shifted_2(): return lax.ppermute(shard, axis, pairs)  40 us
    pallas_call x2, Pallas kernels, section_flow(): pl.pallas_call(flow_kernel, grid_spec=grid_spec, out_shape=jax.ShapeDtype...  28 us
    all_to_all x1, blocking collectives, shards(): lax.all_to_all(flat, 'sec', split_axis=1, concat_axis=1, tiled=True)  19.6 us
    add x7, other arithmetic, advance(): return positions + relax_rate * force / (1.0 + diagonal)  8.5 us
    ppermute x3, starting transfers between devices, shifted_2(): return lax.ppermute(shard, axis, pairs)  8.26 us
    all_to_all x1, starting transfers between devices, tiles_with_halo(): lax.all_to_all(flat, 'sec', split_axis=1, concat_axis=1, tiled=True)  5.68 us
    unnamed x20, local copies, waits for them, and re-layouts  5.5 us
  transfers between devices with their start and end apart: 7, of which 4 were waited for; matrix products, arithmetic and copies ran while one was open for 1% of the time, Pallas kernels for 6%

profile of v11, /device:TPU:0, one launch (start us, length us, event | category | flops | bytes accessed | tf_op | source)
XLA Modules:
  0.0 219.5 jit_solution(4085514635238749533)
XLA Ops:
  0.0 3.4 %slice_bitcast_fusion.1 = (bf16[259,2048]{1,0:T(8,128)(2,1)}, bf16[259,2048]{1,0:T(8,128)(2,1)}) fusion(bf16[1,512,2048]{2,1,0:T(8,128)(2,1)} %param.4), kind=kLoop, calls=%fused_computation.137 | loop fusion | bytes 4243456 | tf_op jit(solution)/shard_map/slice | solution.py:193
  3.4 1.4 collective-permute-start.1
  4.8 1.1 slice_bitcast_fusion.3
  6.0 5.6 %collective-permute-start.2 = (bf16[256,2048]{1,0:T(8,128)(2,1)}, bf16[256,2048]{1,0:T(8,128)(2,1)S(1)}, u32[]{:S(2)}, u32[]{:S(2)}) collective-permute-start(bf16[256,2048]{1,0:T(8,128)(2,1)} %get-tuple-element.21), channel_id=1, source_target_pairs={{0,4},{4,8},{8,12},{12,16},{16,20},{20,24},{24,28},{1,5},{5,9},{9,... | collective-permute-start | bytes 3145736 | tf_op jit(solution)/shard_map/ppermute | solution.py:19
  12.2 1.3 collective-permute-start.3
  13.8 1.5 collective-permute-done.3
  15.3 1.6 select_maximum_fusion.following_ref
  16.9 38.5 %collective-permute-done.2.current_ref = bf16[256,2048]{1,0:T(8,128)(2,1)S(1)} collective-permute-done((bf16[256,2048]{1,0:T(8,128)(2,1)}, bf16[256,2048]{1,0:T(8,128)(2,1)S(1)}, u32[]{:S(2)}, u32[]{:S(2)}) %collective-permute-start.2) | collective-permute-done | bytes 1048608 | tf_op jit(solution)/shard_map/ppermute | solution.py:19
  55.5 14.0 %shard_map.47 = f32[2,64,512]{2,1,0:T(8,128)S(1)} custom-call(s32[25,2]{1,0:T(8,128)S(1)} %copy.13.offsets_ref, bf16[256,2048]{1,0:T(8,128)(2,1)S(1)} %collective-permute-done.2.current_ref, bf16[288,2048]{1,0:T(8,128)(2,1)S(1)} %select_maximum_fusion.following_ref, bf16[512,512]{1,0:T(8,128)(2,1)S(1)} %fusion.96.permute_ref), custom_call_target="tpu_custom_call" | custom-call | tf_op jit(solution)/shard_map/pallas_call | solution.py:147
  69.6 1.5 fusion.61.following_ref
  71.1 14.0 %shard_map.46 = f32[2,64,512]{2,1,0:T(8,128)S(1)} custom-call(s32[25,2]{1,0:T(8,128)S(1)} %copy.13.offsets_ref, bf16[256,2048]{1,0:T(8,128)(2,1)S(1)} %get-tuple-element.20.current_ref, bf16[288,2048]{1,0:T(8,128)(2,1)S(1)} %fusion.61.following_ref, bf16[512,512]{1,0:T(8,128)(2,1)S(1)} %fusion.96.permute_ref), custom_call_target="tpu_custom_call" | custom-call | tf_op jit(solution)/shard_map/pallas_call | solution.py:147
  85.2 1.9 collective-permute-start.4
  87.1 1.3 collective-permute-start.5
  88.4 3.1 %collective-permute-done.5 = f32[5,8,512]{2,1,0:T(8,128)S(1)} collective-permute-done((f32[5,8,512]{2,1,0:T(8,128)S(1)}, f32[5,8,512]{2,1,0:T(8,128)S(1)}, u32[]{:S(2)}, u32[]{:S(2)}) %collective-permute-start.5) | collective-permute-done | bytes 81952 | tf_op jit(solution)/shard_map/ppermute | solution.py:32
  91.7 0.8 pad_slice_fusion.4
  100.7 5.7 %all-to-all-start = ((f32[5,8,11520]{2,0,1:T(8,128)}), f32[5,8,11520]{2,0,1:T(8,128)S(1)}, u32[]{:S(2)}, u32[]{:S(2)}) async-start(f32[5,8,11520]{2,0,1:T(8,128)} %constant_dynamic-update-slice_fusion), calls=%async_computation | async-start | bytes 5898240 | tf_op jit(solution)/shard_map/all_to_all | solution.py:185
  106.4 66.5 %all-to-all-done = f32[5,8,11520]{2,0,1:T(8,128)S(1)} async-done(((f32[5,8,11520]{2,0,1:T(8,128)}), f32[5,8,11520]{2,0,1:T(8,128)S(1)}, u32[]{:S(2)}, u32[]{:S(2)}) %all-to-all-start) | async-done | bytes 1843232 | tf_op jit(solution)/shard_map/all_to_all | solution.py:185
  172.9 3.8 %slice_reduce_fusion.2 = (f32[8,11520]{1,0:T(8,128)}, f32[8,11520]{1,0:T(8,128)S(1)}, f32[8,11520]{1,0:T(8,128)}) fusion(f32[5,8,11520]{2,0,1:T(8,128)S(1)} %all-to-all-done), kind=kLoop, calls=%fused_computation.155 | loop fusion | bytes 2211840 | tf_op jit(solution)/shard_map/slice | solution.py:222
  176.7 1.5 mul.176
  179.1 2.9 %slice.351 = f32[2,8,11520]{2,0,1:T(2,128)} slice(f32[5,8,11520]{2,0,1:T(8,128)} %copy-done.1), slice={[0:2], [0:8], [0:11520]} | slice | bytes 1474560 | tf_op jit(solution)/shard_map/slice | solution.py:216
  182.1 2.1 slice.295
  185.1 0.9 fusion.5
  186.3 1.1 fusion.12
  187.7 1.1 fusion.19
  189.1 1.1 fusion.26
  190.5 1.4 fusion.33
  192.1 1.1 fusion.40
  193.5 1.1 fusion.47
  194.6 1.0 multiply_add_fusion
  195.7 1.4 slice_add_fusion
  197.9 19.6 %all_to_all.10 = f32[2,8,8192]{2,0,1:T(2,128)S(1)} all-to-all(f32[2,8,8192]{2,0,1:T(2,128)S(1)} %copy.17), channel_id=1, replica_groups=mesh['sec'=8,'strip'=4] {'sec'}, dimensions={1} | all-to-all | bytes 1048576 | tf_op jit(solution)/shard_map/all_to_all | solution.py:252
  218.5 1.0 copy.20
  (62 shorter events, 14.6 us)
Async XLA Ops:
  0.0 4.8 %copy-start = (bf16[1,512,2048]{2,1,0:T(8,128)(2,1)S(1)}, bf16[1,512,2048]{2,1,0:T(8,128)(2,1)}, u32[]{:S(2)}) copy-start(bf16[1,512,2048]{2,1,0:T(8,128)(2,1)} %param.4) | copy-start | bytes 6291460
  3.4 10.3 %copy-start.5 = (s32[25,2]{0,1:T(2,128)S(1)}, s32[25,2]{0,1:T(2,128)}, u32[]{:S(2)}) copy-start(s32[25,2]{0,1:T(2,128)} %param.5) | copy-start | bytes 604
  3.4 66.1 %collective-permute-start.1 = (bf16[259,2048]{1,0:T(8,128)(2,1)}, bf16[259,2048]{1,0:T(8,128)(2,1)}, u32[]{:S(2)}, u32[]{:S(2)}) collective-permute-start(bf16[259,2048]{1,0:T(8,128)(2,1)} %get-tuple-element.18), channel_id=1, source_target_pairs={{4,0},{8,4},{12,8},{16,12},{20,16},{24,20},{28,24},{5,1},{9,5},{13... | collective-permute-start | bytes 3182600 | tf_op jit(solution)/shard_map/ppermute | solution.py:19
  6.0 49.4 %collective-permute-start.2 = (bf16[256,2048]{1,0:T(8,128)(2,1)}, bf16[256,2048]{1,0:T(8,128)(2,1)S(1)}, u32[]{:S(2)}, u32[]{:S(2)}) collective-permute-start(bf16[256,2048]{1,0:T(8,128)(2,1)} %get-tuple-element.21), channel_id=1, source_target_pairs={{0,4},{4,8},{8,12},{12,16},{16,20},{20,24},{24,28},{1,5},{5,9},{9,... | collective-permute-start | bytes 3145736 | tf_op jit(solution)/shard_map/ppermute | solution.py:19
  11.6 58.0 %collective-permute-start = (bf16[3,2048]{1,0:T(4,128)(2,1)S(1)}, bf16[3,2048]{1,0:T(4,128)(2,1)S(1)}, u32[]{:S(2)}, u32[]{:S(2)}) collective-permute-start(bf16[3,2048]{1,0:T(4,128)(2,1)S(1)} %get-tuple-element.16), channel_id=1, source_target_pairs={{4,1},{5,2},{6,3},{8,5},{9,6},{10,7},{12,9},{13,10},{14,11},{16,13... | collective-permute-start | bytes 36872 | tf_op jit(solution)/shard_map/ppermute | solution.py:195
  12.2 3.1 %collective-permute-start.3 = (bf16[3,2048]{1,0:T(4,128)(2,1)S(1)}, bf16[3,2048]{1,0:T(4,128)(2,1)S(1)}, u32[]{:S(2)}, u32[]{:S(2)}) collective-permute-start(bf16[3,2048]{1,0:T(4,128)(2,1)S(1)} %get-tuple-element.17), channel_id=1, source_target_pairs={{1,0},{2,1},{3,2},{5,4},{6,5},{7,6},{9,8},{10,9},{11,10},{13,12},{... | collective-permute-start | bytes 36872 | tf_op jit(solution)/shard_map/ppermute | solution.py:19
  13.7 41.7 %copy-start.3 = (s32[2,1,128,512]{3,2,1,0:T(8,128)S(1)}, s32[2,1,128,512]{3,2,1,0:T(8,128)}, u32[]{:S(2)}) copy-start(s32[2,1,128,512]{3,2,1,0:T(8,128)} %param.6) | copy-start | bytes 1572868
  15.3 40.2 %copy-start.4 = (s32[1,128,512]{2,1,0:T(8,128)S(1)}, s32[1,128,512]{2,1,0:T(8,128)}, u32[]{:S(2)}) copy-start(s32[1,128,512]{2,1,0:T(8,128)} %param.7) | copy-start | bytes 786436
  85.2 3.2 %collective-permute-start.4 = (f32[5,8,512]{2,1,0:T(8,128)S(1)}, f32[5,8,512]{2,1,0:T(8,128)S(1)}, u32[]{:S(2)}, u32[]{:S(2)}) collective-permute-start(f32[5,8,512]{2,1,0:T(8,128)S(1)} %get-tuple-element.30), channel_id=1, source_target_pairs={{0,1},{1,2},{2,3},{4,5},{5,6},{6,7},{8,9},{9,10},{10,11},{12,13},{... | collective-permute-start | bytes 245768 | tf_op jit(solution)/shard_map/ppermute | solution.py:30
  87.1 4.4 %collective-permute-start.5 = (f32[5,8,512]{2,1,0:T(8,128)S(1)}, f32[5,8,512]{2,1,0:T(8,128)S(1)}, u32[]{:S(2)}, u32[]{:S(2)}) collective-permute-start(f32[5,8,512]{2,1,0:T(8,128)S(1)} %get-tuple-element.31), channel_id=1, source_target_pairs={{1,0},{2,1},{3,2},{5,4},{6,5},{7,6},{9,8},{10,9},{11,10},{13,12},{... | collective-permute-start | bytes 245768 | tf_op jit(solution)/shard_map/ppermute | solution.py:32
  100.7 72.1 %all-to-all-start = ((f32[5,8,11520]{2,0,1:T(8,128)}), f32[5,8,11520]{2,0,1:T(8,128)S(1)}, u32[]{:S(2)}, u32[]{:S(2)}) async-start(f32[5,8,11520]{2,0,1:T(8,128)} %constant_dynamic-update-slice_fusion), calls=%async_computation | async-start | bytes 5898240 | tf_op jit(solution)/shard_map/all_to_all | solution.py:185
  172.9 3.8 %copy-start.1 = (f32[5,8,11520]{2,0,1:T(8,128)}, f32[5,8,11520]{2,0,1:T(8,128)S(1)}, u32[]{:S(2)}) copy-start(f32[5,8,11520]{2,0,1:T(8,128)S(1)} %all-to-all-done) | copy-start | bytes 5529604
  176.7 1.5 copy-start.2

commit v12 on v10

--- a/solution.py
+++ b/solution.py
@@ -199,7 +199,7 @@
     )
     below = shifted_2(pixels[:RAD], "strip", -1)
     keep_mask = (lax.axis_index("sec") < sec_count - 1).astype(jnp.float32)
-    springs, validity, prior_bottom = lax.optimization_barrier((springs, validity, prior_bottom))
+    springs, validity, below = lax.optimization_barrier((springs, validity, below))
     match_weight = validity[0].astype(jnp.float32) * keep_mask
     node_rows, node_cols = (springs.shape[2], springs.shape[3])
     global_rows = lax.axis_index("strip") * node_rows + jnp.arange(node_rows, dtype=jnp.int32)
@@ -209,7 +209,9 @@
     col_weight = 0.25 * springs[1, 0].astype(jnp.float32) * col_keep[None, :]
     halo = ITERS
     weights = jnp.stack([row_weight, col_weight, match_weight]).astype(jnp.bfloat16)
-    weights = tiles_with_halo(weights, halo).astype(jnp.float32)
+    weights = tiles_with_halo(weights, halo)
+    weights, successor_top, prior_bottom = lax.optimization_barrier((weights, successor_top, prior_bottom))
+    weights = weights.astype(jnp.float32)
     flow_top = section_flow(pixels[:half], jnp.concatenate([corner, successor_top]), offsets) * keep_mask
     flow_bottom = section_flow(prior_bottom, jnp.concatenate([pixels[half - RAD :], below]), offsets)
     flow_field = jnp.concatenate([flow_top, flow_bottom], axis=1)

time: 191 us -> 182 us (0.953)
  waiting for transfers between devices: 66 us -> 49.7 us
  starting transfers between devices: 27.3 us -> 30.3 us
    ppermute x3, waiting for transfers between devices: 39.1 us -> 0.01 us  [shifted_2(): return lax.ppermute(shard, axis, pairs)]
    all_to_all x2, waiting for transfers between devices: 26.8 us -> 46.7 us  [tiles_with_halo(): lax.all_to_all(flat, 'sec', split_axis=1, concat_axis=1, tiled=True)]
    reshape x1 -> x2, local copies, waits for them, and re-layouts: 3.03 us -> 6.46 us  [tiles_with_halo(): lax.all_to_all(flat, 'sec', split_axis=1, concat_axis=1, tiled=True)]
    ppermute x2, waiting for transfers between devices: 0.01 us -> 3.03 us  [extended(): lax.ppermute(head, axis, [((i + 1) % count, i) for i in range(ends)])]
    all_to_all x2, starting transfers between devices: 10.2 us -> 13.3 us  [tiles_with_halo(): lax.all_to_all(flat, 'sec', split_axis=1, concat_axis=1, tiled=True)]
    slice x2 -> x1, local copies, waits for them, and re-layouts: 2.88 us -> 0.79 us  [shards(): pixels[-RAD:]]
  transfers between devices with their start and end apart: 10 -> 10, of which waited for: 4 -> 3; matrix products, arithmetic and copies ran while one was open for 13% -> 12% of each run, Pallas kernels for 15% -> 16%
where the time goes in v12:
time: 182 us; the launch traced here: 181 us
  waiting for transfers between devices  49.7 us (27%)
  local copies, waits for them, and re-layouts  35.4 us (19%)
  starting transfers between devices  30.3 us (17%)
  Pallas kernels  29.1 us (16%)
  blocking collectives  19.4 us (11%)
  other arithmetic  16.8 us (9%)
    all_to_all x2, waiting for transfers between devices, tiles_with_halo(): lax.all_to_all(flat, 'sec', split_axis=1, concat_axis=1, tiled=True)  46.7 us
    pallas_call x2, Pallas kernels, section_flow(): pl.pallas_call(flow_kernel, grid_spec=grid_spec, out_shape=jax.ShapeDtype...  29.1 us
    all_to_all x1, blocking collectives, shards(): lax.all_to_all(flat, 'sec', split_axis=1, concat_axis=1, tiled=True)  19.4 us
    all_to_all x2, starting transfers between devices, tiles_with_halo(): lax.all_to_all(flat, 'sec', split_axis=1, concat_axis=1, tiled=True)  13.3 us
    unnamed x27, local copies, waits for them, and re-layouts  11.4 us
    ppermute x3, starting transfers between devices, shifted_2(): return lax.ppermute(shard, axis, pairs)  8.55 us
    add x7, other arithmetic, advance(): return positions + relax_rate * force / (1.0 + diagonal)  8.23 us
    reshape x2, local copies, waits for them, and re-layouts, tiles_with_halo(): lax.all_to_all(flat, 'sec', split_axis=1, concat_axis=1, tiled=True)  6.46 us
  transfers between devices with their start and end apart: 10, of which 3 were waited for; matrix products, arithmetic and copies ran while one was open for 12% of the time, Pallas kernels for 16%

profile of v12, /device:TPU:0, one launch (start us, length us, event | category | flops | bytes accessed | tf_op | source)
XLA Modules:
  0.0 181.1 jit_solution(2525891068997678087)
XLA Ops:
  0.8 1.4 collective-permute-start
  2.2 2.9 %slice_bitcast_fusion.2 = (bf16[256,2048]{1,0:T(8,128)(2,1)S(1)}, bf16[256,2048]{1,0:T(8,128)(2,1)}) fusion(bf16[1,512,2048]{2,1,0:T(8,128)(2,1)} %param.4), kind=kLoop, calls=%fused_computation.141 | loop fusion | bytes 4194304 | tf_op jit(solution)/shard_map/slice | solution.py:215
  5.2 5.8 %collective-permute-start.4 = (bf16[256,2048]{1,0:T(8,128)(2,1)}, bf16[256,2048]{1,0:T(8,128)(2,1)}, u32[]{:S(2)}, u32[]{:S(2)}) collective-permute-start(bf16[256,2048]{1,0:T(8,128)(2,1)} %get-tuple-element.24), channel_id=1, source_target_pairs={{0,4},{4,8},{8,12},{12,16},{16,20},{20,24},{24,28},{1,5},{5,9},{9,... | collective-permute-start | bytes 3145736 | tf_op jit(solution)/shard_map/ppermute | solution.py:19
  11.0 1.1 fusion.100
  12.2 2.8 %collective-permute-start.1 = (bf16[3,8,512]{2,1,0:T(8,128)(2,1)S(1)}, bf16[3,8,512]{2,1,0:T(8,128)(2,1)S(1)}, u32[]{:S(2)}, u32[]{:S(2)}) collective-permute-start(bf16[3,8,512]{2,1,0:T(8,128)(2,1)S(1)} %get-tuple-element.52), channel_id=1, source_target_pairs={{0,1},{1,2},{2,3},{4,5},{5,6},{6,7},{8,9},{9,10},{10,11},{12,13},{... | collective-permute-start | bytes 73736 | tf_op jit(solution)/shard_map/ppermute | solution.py:30
  14.9 1.3 collective-permute-start.2
  16.2 1.6 slice_bitcast_fusion
  17.8 1.3 collective-permute-start.3
  26.4 7.0 %all-to-all-start = ((bf16[3,8,11520]{2,0,1:T(4,128)(2,1)}), bf16[3,8,11520]{2,0,1:T(4,128)(2,1)S(1)}, u32[]{:S(2)}, u32[]{:S(2)}) async-start(bf16[3,8,11520]{2,0,1:T(4,128)(2,1)} %constant_dynamic-update-slice_fusion), calls=%async_computation | async-start | bytes 1474560 | tf_op jit(solution)/shard_map/all_to_all | solution.py:185
  34.3 1.5 fusion.61.following_ref
  35.9 29.1 %all-to-all-done = bf16[3,8,11520]{2,0,1:T(4,128)(2,1)S(1)} async-done(((bf16[3,8,11520]{2,0,1:T(4,128)(2,1)}), bf16[3,8,11520]{2,0,1:T(4,128)(2,1)S(1)}, u32[]{:S(2)}, u32[]{:S(2)}) %all-to-all-start) | async-done | bytes 552992 | tf_op jit(solution)/shard_map/all_to_all | solution.py:185
  65.8 3.4 %reshape.198 = bf16[3,8,144,80]{3,2,1,0:T(8,128)(2,1)} reshape(bf16[3,8,11520]{2,1,0:T(8,128)(2,1)} %copy.22) | data formatting | bytes 1105920 | tf_op jit(solution)/shard_map/reshape | solution.py:185
  69.3 15.0 %shard_map.46 = f32[2,64,512]{2,1,0:T(8,128)S(1)} custom-call(s32[25,2]{1,0:T(8,128)S(1)} %copy.23.offsets_ref, bf16[256,2048]{1,0:T(8,128)(2,1)} %collective-permute-done.4.current_ref, bf16[288,2048]{1,0:T(8,128)(2,1)S(1)} %fusion.61.following_ref, bf16[512,512]{1,0:T(8,128)(2,1)S(1)} %fusion.96.permute_ref), custom_call_target="tpu_custom_call" | custom-call | tf_op jit(solution)/shard_map/pallas_call | solution.py:147
  84.3 2.5 %collective-permute-start.5 = (f32[2,8,512]{2,1,0:T(8,128)S(1)}, f32[2,8,512]{2,1,0:T(8,128)S(1)}, u32[]{:S(2)}, u32[]{:S(2)}) collective-permute-start(f32[2,8,512]{2,1,0:T(8,128)S(1)} %slice.381), channel_id=1, source_target_pairs={{0,1},{1,2},{2,3},{4,5},{5,6},{6,7},{8,9},{9,10},{10,11},{12,13},{... | collective-permute-start | bytes 98312 | tf_op jit(solution)/shard_map/ppermute | solution.py:30
  86.8 1.5 select_maximum_fusion.following_ref
  88.4 14.0 %shard_map.47 = f32[2,64,512]{2,1,0:T(8,128)S(1)} custom-call(s32[25,2]{1,0:T(8,128)S(1)} %copy.23.offsets_ref, bf16[256,2048]{1,0:T(8,128)(2,1)S(1)} %get-tuple-element.23.current_ref, bf16[288,2048]{1,0:T(8,128)(2,1)S(1)} %select_maximum_fusion.following_ref, bf16[512,512]{1,0:T(8,128)(2,1)S(1)} %fusion.96.permute_ref), custom_call_target="tpu_custom_call" | custom-call | tf_op jit(solution)/shard_map/pallas_call | solution.py:147
  102.4 1.3 collective-permute-start.7
  103.8 3.0 %collective-permute-done.7 = f32[2,8,512]{2,1,0:T(8,128)S(1)} collective-permute-done((f32[2,8,512]{2,1,0:T(8,128)S(1)}, f32[2,8,512]{2,1,0:T(8,128)S(1)}, u32[]{:S(2)}, u32[]{:S(2)}) %collective-permute-start.7) | collective-permute-done | bytes 32800 | tf_op jit(solution)/shard_map/ppermute | solution.py:32
  113.7 6.3 %all-to-all-start.1 = ((f32[2,8,11520]{2,0,1:T(2,128)}), f32[2,8,11520]{2,0,1:T(2,128)}, u32[]{:S(2)}, u32[]{:S(2)}) async-start(f32[2,8,11520]{2,0,1:T(2,128)} %constant_dynamic-update-slice_fusion.8), calls=%async_computation.1 | async-start | bytes 1474560 | tf_op jit(solution)/shard_map/all_to_all | solution.py:185
  120.7 1.0 slice.394
  121.7 17.6 %all-to-all-done.1 = f32[2,8,11520]{2,0,1:T(2,128)} async-done(((f32[2,8,11520]{2,0,1:T(2,128)}), f32[2,8,11520]{2,0,1:T(2,128)}, u32[]{:S(2)}, u32[]{:S(2)}) %all-to-all-start.1) | async-done | bytes 737312 | tf_op jit(solution)/shard_map/all_to_all | solution.py:185
  139.3 2.1 %copy.25 = f32[2,8,11520]{2,1,0:T(8,128)} copy(f32[2,8,11520]{2,0,1:T(2,128)} %all-to-all-done.1) | data formatting | bytes 1474560 | tf_op jit(solution)/shard_map/all_to_all | solution.py:185
  141.3 3.0 %reshape.199 = f32[2,8,144,80]{3,2,1,0:T(8,128)} reshape(f32[2,8,11520]{2,1,0:T(8,128)} %copy.25) | data formatting | bytes 1474560 | tf_op jit(solution)/shard_map/reshape | solution.py:185
  144.4 1.2 copy-done
  147.4 1.1 fusion.12
  148.8 1.1 fusion.19
  150.1 1.1 fusion.26
  151.5 1.1 fusion.33
  152.8 1.1 fusion.40
  154.2 1.1 fusion.47
  157.3 1.6 slice_add_fusion
  159.7 19.4 %all_to_all.15 = f32[2,8,8192]{2,0,1:T(2,128)S(1)} all-to-all(f32[2,8,8192]{2,0,1:T(2,128)S(1)} %copy.26), channel_id=1, replica_groups=mesh['sec'=8,'strip'=4] {'sec'}, dimensions={1} | all-to-all | bytes 1048576 | tf_op jit(solution)/shard_map/all_to_all | solution.py:254
  (89 shorter events, 25.3 us)
Async XLA Ops:
  0.8 10.2 %copy-start.4 = (s32[1,128,512]{2,1,0:T(8,128)S(1)}, s32[1,128,512]{2,1,0:T(8,128)}, u32[]{:S(2)}) copy-start(s32[1,128,512]{2,1,0:T(8,128)} %param.7) | copy-start | bytes 786436
  0.8 10.2 %collective-permute-start = (bf16[3,2048]{1,0:T(4,128)(2,1)S(1)}, bf16[3,2048]{1,0:T(4,128)(2,1)S(1)}, u32[]{:S(2)}, u32[]{:S(2)}) collective-permute-start(bf16[3,2048]{1,0:T(4,128)(2,1)S(1)} %get-tuple-element.22), channel_id=1, source_target_pairs={{1,0},{2,1},{3,2},{5,4},{6,5},{7,6},{9,8},{10,9},{11,10},{13,12},{... | collective-permute-start | bytes 36872 | tf_op jit(solution)/shard_map/ppermute | solution.py:19
  2.2 14.0 %copy-start.1 = (bf16[1,512,2048]{2,1,0:T(8,128)(2,1)S(1)}, bf16[1,512,2048]{2,1,0:T(8,128)(2,1)}, u32[]{:S(2)}) copy-start(bf16[1,512,2048]{2,1,0:T(8,128)(2,1)} %param.4) | copy-start | bytes 6291460
  5.2 64.1 %collective-permute-start.4 = (bf16[256,2048]{1,0:T(8,128)(2,1)}, bf16[256,2048]{1,0:T(8,128)(2,1)}, u32[]{:S(2)}, u32[]{:S(2)}) collective-permute-start(bf16[256,2048]{1,0:T(8,128)(2,1)} %get-tuple-element.24), channel_id=1, source_target_pairs={{0,4},{4,8},{8,12},{12,16},{16,20},{20,24},{24,28},{1,5},{5,9},{9,... | collective-permute-start | bytes 3145736 | tf_op jit(solution)/shard_map/ppermute | solution.py:19
  12.2 7.0 %collective-permute-start.1 = (bf16[3,8,512]{2,1,0:T(8,128)(2,1)S(1)}, bf16[3,8,512]{2,1,0:T(8,128)(2,1)S(1)}, u32[]{:S(2)}, u32[]{:S(2)}) collective-permute-start(bf16[3,8,512]{2,1,0:T(8,128)(2,1)S(1)} %get-tuple-element.52), channel_id=1, source_target_pairs={{0,1},{1,2},{2,3},{4,5},{5,6},{6,7},{8,9},{9,10},{10,11},{12,13},{... | collective-permute-start | bytes 73736 | tf_op jit(solution)/shard_map/ppermute | solution.py:30
  14.9 4.2 %collective-permute-start.2 = (bf16[3,8,512]{2,1,0:T(8,128)(2,1)S(1)}, bf16[3,8,512]{2,1,0:T(8,128)(2,1)S(1)}, u32[]{:S(2)}, u32[]{:S(2)}) collective-permute-start(bf16[3,8,512]{2,1,0:T(8,128)(2,1)S(1)} %get-tuple-element.53), channel_id=1, source_target_pairs={{1,0},{2,1},{3,2},{5,4},{6,5},{7,6},{9,8},{10,9},{11,10},{13,12},{... | collective-permute-start | bytes 73736 | tf_op jit(solution)/shard_map/ppermute | solution.py:32
  17.8 51.4 %collective-permute-start.3 = (bf16[259,2048]{1,0:T(8,128)(2,1)}, bf16[259,2048]{1,0:T(8,128)(2,1)}, u32[]{:S(2)}, u32[]{:S(2)}) collective-permute-start(bf16[259,2048]{1,0:T(8,128)(2,1)} %get-tuple-element.20), channel_id=1, source_target_pairs={{4,0},{8,4},{12,8},{16,12},{20,16},{24,20},{28,24},{5,1},{9,5},{13... | collective-permute-start | bytes 3182600 | tf_op jit(solution)/shard_map/ppermute | solution.py:19
  23.1 11.0 %copy-start.5 = (s32[25,2]{0,1:T(2,128)S(1)}, s32[25,2]{0,1:T(2,128)}, u32[]{:S(2)}) copy-start(s32[25,2]{0,1:T(2,128)} %param.5) | copy-start | bytes 604
  26.4 38.6 %all-to-all-start = ((bf16[3,8,11520]{2,0,1:T(4,128)(2,1)}), bf16[3,8,11520]{2,0,1:T(4,128)(2,1)S(1)}, u32[]{:S(2)}, u32[]{:S(2)}) async-start(bf16[3,8,11520]{2,0,1:T(4,128)(2,1)} %constant_dynamic-update-slice_fusion), calls=%async_computation | async-start | bytes 1474560 | tf_op jit(solution)/shard_map/all_to_all | solution.py:185
  33.4 53.4 %collective-permute-start.6 = (bf16[3,2048]{1,0:T(4,128)(2,1)S(1)}, bf16[3,2048]{1,0:T(4,128)(2,1)S(1)}, u32[]{:S(2)}, u32[]{:S(2)}) collective-permute-start(bf16[3,2048]{1,0:T(4,128)(2,1)S(1)} %get-tuple-element.21), channel_id=1, source_target_pairs={{4,1},{5,2},{6,3},{8,5},{9,6},{10,7},{12,9},{13,10},{14,11},{16,13... | collective-permute-start | bytes 36872 | tf_op jit(solution)/shard_map/ppermute | solution.py:195
  84.3 19.4 %collective-permute-start.5 = (f32[2,8,512]{2,1,0:T(8,128)S(1)}, f32[2,8,512]{2,1,0:T(8,128)S(1)}, u32[]{:S(2)}, u32[]{:S(2)}) collective-permute-start(f32[2,8,512]{2,1,0:T(8,128)S(1)} %slice.381), channel_id=1, source_target_pairs={{0,1},{1,2},{2,3},{4,5},{5,6},{6,7},{8,9},{9,10},{10,11},{12,13},{... | collective-permute-start | bytes 98312 | tf_op jit(solution)/shard_map/ppermute | solution.py:30
  102.4 4.3 %collective-permute-start.7 = (f32[2,8,512]{2,1,0:T(8,128)S(1)}, f32[2,8,512]{2,1,0:T(8,128)S(1)}, u32[]{:S(2)}, u32[]{:S(2)}) collective-permute-start(f32[2,8,512]{2,1,0:T(8,128)S(1)} %slice.382), channel_id=1, source_target_pairs={{1,0},{2,1},{3,2},{5,4},{6,5},{7,6},{9,8},{10,9},{11,10},{13,12},{... | collective-permute-start | bytes 98312 | tf_op jit(solution)/shard_map/ppermute | solution.py:32
  110.5 9.5 %copy-start.2 = (bf16[3,8,144,80]{3,2,1,0:T(8,128)(2,1)S(1)}, bf16[3,8,144,80]{3,2,1,0:T(8,128)(2,1)}, u32[]{:S(2)}) copy-start(bf16[3,8,144,80]{3,2,1,0:T(8,128)(2,1)} %reshape.198) | copy-start | bytes 1658884
  113.7 25.5 %all-to-all-start.1 = ((f32[2,8,11520]{2,0,1:T(2,128)}), f32[2,8,11520]{2,0,1:T(2,128)}, u32[]{:S(2)}, u32[]{:S(2)}) async-start(f32[2,8,11520]{2,0,1:T(2,128)} %constant_dynamic-update-slice_fusion.8), calls=%async_computation.1 | async-start | bytes 1474560 | tf_op jit(solution)/shard_map/all_to_all | solution.py:185
  144.4 1.3 copy-start
  144.4 1.6 slice-start
  156.2 1.0 copy-start.3

commit v13 on v12

--- a/solution.py
+++ b/solution.py
@@ -55,7 +55,7 @@
 
 
 def flow_kernel(
-    offsets_ref, current_ref, following_ref, permute_ref, flow_ref, current_ph, following_ph, lanes_ref, shifted_ref, scores_ref
+    offsets_ref, current_ref, following_ref, permute_ref, flow_ref, current_ph, following_ph, lanes_ref, shifted_ref, scores_ref, sources_ref
 ):
     tile_rows = current_ph.shape[1]
     node_cols = current_ph.shape[2]
@@ -84,26 +84,33 @@
     chunks = tile_rows // 8
     offset_count = scores_ref.shape[0]
 
-    def score(k, carry):
+    def fill(k, carry):
         row_off = offsets_ref[k, 0]
         col_off = offsets_ref[k, 1]
-        sources = []
         for q in range(4):
             u = q + row_off + 4
             u_node, u_phase = lax.shift_right_logical(u, 2), u & 3
             for t in range(4):
                 v = t + col_off + 4
                 v_node, v_phase = lax.shift_right_logical(v, 2), v & 3
-                sources.append((u_node * 3 + v_node) * 16 + u_phase * 4 + v_phase)
-        for c in range(chunks):
+                sources_ref[k * 16 + q * 4 + t] = (u_node * 3 + v_node) * 16 + u_phase * 4 + v_phase
+        return carry
+
+    lax.fori_loop(0, offset_count, fill, 0)
+    for c in range(chunks):
+        for h in range(node_cols // 256):
             rows = pl.ds(c * 8, 8)
-            acc = current_ph[0, rows, :] * shifted_ref[sources[0], rows, :]
-            for p in range(1, 16):
-                acc = acc + current_ph[p, rows, :] * shifted_ref[sources[p], rows, :]
-            scores_ref[k, rows, :] = sharpness * acc
-        return carry
-
-    lax.fori_loop(0, offset_count, score, 0)
+            lanes = pl.ds(h * 256, 256)
+            current = [current_ph[p, rows, lanes] for p in range(16)]
+
+            def score(k, carry):
+                acc = current[0] * shifted_ref[sources_ref[k * 16], rows, lanes]
+                for p in range(1, 16):
+                    acc = acc + current[p] * shifted_ref[sources_ref[k * 16 + p], rows, lanes]
+                scores_ref[k, rows, lanes] = sharpness * acc
+                return carry
+
+            lax.fori_loop(0, offset_count, score, 0)
     for c in range(chunks):
         rows = pl.ds(c * 8, 8)
         highest = scores_ref[0, rows, :]
@@ -142,6 +149,7 @@
             pltpu.VMEM((col_count // 128, window * 4, 128), jnp.float32),
             pltpu.VMEM((144, tile_rows, node_cols), jnp.float32),
             pltpu.VMEM((offset_count, tile_rows, node_cols), jnp.float32),
+            pltpu.SMEM((offset_count * 16,), jnp.int32),
         ],
     )
     return pl.pallas_call(

time: 182 us -> 194 us (1.066)
  Pallas kernels: 29.1 us -> 40.6 us
    pallas_call x2, Pallas kernels: 29.1 us -> 40.6 us  [section_flow(): pl.pallas_call(flow_kernel, grid_spec=grid_spec, out_shape=jax.ShapeDtype...]
  transfers between devices with their start and end apart: 10 -> 10, of which waited for: 3 -> 3; matrix products, arithmetic and copies ran while one was open for 12% -> 12% of each run, Pallas kernels for 16% -> 21%
where the time goes in v13:
time: 194 us; the launch traced here: 193 us
  waiting for transfers between devices  49.8 us (26%)
  Pallas kernels  40.6 us (21%)
  local copies, waits for them, and re-layouts  35.4 us (18%)
  starting transfers between devices  30.2 us (16%)
  blocking collectives  19.4 us (10%)
  other arithmetic  16.8 us (9%)
    all_to_all x2, waiting for transfers between devices, tiles_with_halo(): lax.all_to_all(flat, 'sec', split_axis=1, concat_axis=1, tiled=True)  46.7 us
    pallas_call x2, Pallas kernels, section_flow(): pl.pallas_call(flow_kernel, grid_spec=grid_spec, out_shape=jax.ShapeDtype...  40.6 us
    all_to_all x1, blocking collectives, shards(): lax.all_to_all(flat, 'sec', split_axis=1, concat_axis=1, tiled=True)  19.4 us
    all_to_all x2, starting transfers between devices, tiles_with_halo(): lax.all_to_all(flat, 'sec', split_axis=1, concat_axis=1, tiled=True)  13.2 us
    unnamed x27, local copies, waits for them, and re-layouts  11.4 us
    ppermute x3, starting transfers between devices, shifted_2(): return lax.ppermute(shard, axis, pairs)  8.55 us
    add x7, other arithmetic, advance(): return positions + relax_rate * force / (1.0 + diagonal)  8.23 us
    reshape x2, local copies, waits for them, and re-layouts, tiles_with_halo(): lax.all_to_all(flat, 'sec', split_axis=1, concat_axis=1, tiled=True)  6.46 us
  transfers between devices with their start and end apart: 10, of which 3 were waited for; matrix products, arithmetic and copies ran while one was open for 12% of the time, Pallas kernels for 21%

profile of v13, /device:TPU:0, one launch (start us, length us, event | category | flops | bytes accessed | tf_op | source)
XLA Modules:
  0.0 192.7 jit_solution(17926749538749558740)
XLA Ops:
  0.8 1.4 collective-permute-start
  2.2 2.9 %slice_bitcast_fusion.2 = (bf16[256,2048]{1,0:T(8,128)(2,1)S(1)}, bf16[256,2048]{1,0:T(8,128)(2,1)}) fusion(bf16[1,512,2048]{2,1,0:T(8,128)(2,1)} %param.4), kind=kLoop, calls=%fused_computation.141 | loop fusion | bytes 4194304 | tf_op jit(solution)/shard_map/slice | solution.py:223
  5.2 5.8 %collective-permute-start.4 = (bf16[256,2048]{1,0:T(8,128)(2,1)}, bf16[256,2048]{1,0:T(8,128)(2,1)}, u32[]{:S(2)}, u32[]{:S(2)}) collective-permute-start(bf16[256,2048]{1,0:T(8,128)(2,1)} %get-tuple-element.24), channel_id=1, source_target_pairs={{0,4},{4,8},{8,12},{12,16},{16,20},{20,24},{24,28},{1,5},{5,9},{9,... | collective-permute-start | bytes 3145736 | tf_op jit(solution)/shard_map/ppermute | solution.py:19
  11.0 1.1 fusion.100
  12.2 2.8 %collective-permute-start.1 = (bf16[3,8,512]{2,1,0:T(8,128)(2,1)S(1)}, bf16[3,8,512]{2,1,0:T(8,128)(2,1)S(1)}, u32[]{:S(2)}, u32[]{:S(2)}) collective-permute-start(bf16[3,8,512]{2,1,0:T(8,128)(2,1)S(1)} %get-tuple-element.52), channel_id=1, source_target_pairs={{0,1},{1,2},{2,3},{4,5},{5,6},{6,7},{8,9},{9,10},{10,11},{12,13},{... | collective-permute-start | bytes 73736 | tf_op jit(solution)/shard_map/ppermute | solution.py:30
  14.9 1.3 collective-permute-start.2
  16.2 1.6 slice_bitcast_fusion
  17.8 1.3 collective-permute-start.3
  26.4 7.0 %all-to-all-start = ((bf16[3,8,11520]{2,0,1:T(4,128)(2,1)}), bf16[3,8,11520]{2,0,1:T(4,128)(2,1)S(1)}, u32[]{:S(2)}, u32[]{:S(2)}) async-start(bf16[3,8,11520]{2,0,1:T(4,128)(2,1)} %constant_dynamic-update-slice_fusion), calls=%async_computation | async-start | bytes 1474560 | tf_op jit(solution)/shard_map/all_to_all | solution.py:193
  34.3 1.5 fusion.61.following_ref
  35.9 29.1 %all-to-all-done = bf16[3,8,11520]{2,0,1:T(4,128)(2,1)S(1)} async-done(((bf16[3,8,11520]{2,0,1:T(4,128)(2,1)}), bf16[3,8,11520]{2,0,1:T(4,128)(2,1)S(1)}, u32[]{:S(2)}, u32[]{:S(2)}) %all-to-all-start) | async-done | bytes 552992 | tf_op jit(solution)/shard_map/all_to_all | solution.py:193
  65.8 3.4 %reshape.198 = bf16[3,8,144,80]{3,2,1,0:T(8,128)(2,1)} reshape(bf16[3,8,11520]{2,1,0:T(8,128)(2,1)} %copy.22) | data formatting | bytes 1105920 | tf_op jit(solution)/shard_map/reshape | solution.py:193
  69.3 20.8 %shard_map.46 = f32[2,64,512]{2,1,0:T(8,128)S(1)} custom-call(s32[25,2]{1,0:T(8,128)S(1)} %copy.23.offsets_ref, bf16[256,2048]{1,0:T(8,128)(2,1)} %collective-permute-done.4.current_ref, bf16[288,2048]{1,0:T(8,128)(2,1)S(1)} %fusion.61.following_ref, bf16[512,512]{1,0:T(8,128)(2,1)S(1)} %fusion.96.permute_ref), custom_call_target="tpu_custom_call" | custom-call | tf_op jit(solution)/shard_map/pallas_call | solution.py:155
  90.1 2.5 %collective-permute-start.5 = (f32[2,8,512]{2,1,0:T(8,128)S(1)}, f32[2,8,512]{2,1,0:T(8,128)S(1)}, u32[]{:S(2)}, u32[]{:S(2)}) collective-permute-start(f32[2,8,512]{2,1,0:T(8,128)S(1)} %slice.381), channel_id=1, source_target_pairs={{0,1},{1,2},{2,3},{4,5},{5,6},{6,7},{8,9},{9,10},{10,11},{12,13},{... | collective-permute-start | bytes 98312 | tf_op jit(solution)/shard_map/ppermute | solution.py:30
  92.6 1.5 select_maximum_fusion.following_ref
  94.1 19.8 %shard_map.47 = f32[2,64,512]{2,1,0:T(8,128)S(1)} custom-call(s32[25,2]{1,0:T(8,128)S(1)} %copy.23.offsets_ref, bf16[256,2048]{1,0:T(8,128)(2,1)S(1)} %get-tuple-element.23.current_ref, bf16[288,2048]{1,0:T(8,128)(2,1)S(1)} %select_maximum_fusion.following_ref, bf16[512,512]{1,0:T(8,128)(2,1)S(1)} %fusion.96.permute_ref), custom_call_target="tpu_custom_call" | custom-call | tf_op jit(solution)/shard_map/pallas_call | solution.py:155
  114.0 1.3 collective-permute-start.7
  115.3 3.1 %collective-permute-done.7 = f32[2,8,512]{2,1,0:T(8,128)S(1)} collective-permute-done((f32[2,8,512]{2,1,0:T(8,128)S(1)}, f32[2,8,512]{2,1,0:T(8,128)S(1)}, u32[]{:S(2)}, u32[]{:S(2)}) %collective-permute-start.7) | collective-permute-done | bytes 32800 | tf_op jit(solution)/shard_map/ppermute | solution.py:32
  125.3 6.2 %all-to-all-start.1 = ((f32[2,8,11520]{2,0,1:T(2,128)}), f32[2,8,11520]{2,0,1:T(2,128)}, u32[]{:S(2)}, u32[]{:S(2)}) async-start(f32[2,8,11520]{2,0,1:T(2,128)} %constant_dynamic-update-slice_fusion.8), calls=%async_computation.1 | async-start | bytes 1474560 | tf_op jit(solution)/shard_map/all_to_all | solution.py:193
  132.2 1.0 slice.394
  133.2 17.6 %all-to-all-done.1 = f32[2,8,11520]{2,0,1:T(2,128)} async-done(((f32[2,8,11520]{2,0,1:T(2,128)}), f32[2,8,11520]{2,0,1:T(2,128)}, u32[]{:S(2)}, u32[]{:S(2)}) %all-to-all-start.1) | async-done | bytes 737312 | tf_op jit(solution)/shard_map/all_to_all | solution.py:193
  150.8 2.1 %copy.25 = f32[2,8,11520]{2,1,0:T(8,128)} copy(f32[2,8,11520]{2,0,1:T(2,128)} %all-to-all-done.1) | data formatting | bytes 1474560 | tf_op jit(solution)/shard_map/all_to_all | solution.py:193
  152.9 3.0 %reshape.199 = f32[2,8,144,80]{3,2,1,0:T(8,128)} reshape(f32[2,8,11520]{2,1,0:T(8,128)} %copy.25) | data formatting | bytes 1474560 | tf_op jit(solution)/shard_map/reshape | solution.py:193
  156.0 1.2 copy-done
  158.9 1.1 fusion.12
  160.3 1.1 fusion.19
  161.6 1.1 fusion.26
  163.0 1.1 fusion.33
  164.3 1.1 fusion.40
  165.7 1.1 fusion.47
  168.8 1.6 slice_add_fusion
  171.2 19.4 %all_to_all.15 = f32[2,8,8192]{2,0,1:T(2,128)S(1)} all-to-all(f32[2,8,8192]{2,0,1:T(2,128)S(1)} %copy.26), channel_id=1, replica_groups=mesh['sec'=8,'strip'=4] {'sec'}, dimensions={1} | all-to-all | bytes 1048576 | tf_op jit(solution)/shard_map/all_to_all | solution.py:262
  (89 shorter events, 25.3 us)
Async XLA Ops:
  0.8 10.2 %copy-start.4 = (s32[1,128,512]{2,1,0:T(8,128)S(1)}, s32[1,128,512]{2,1,0:T(8,128)}, u32[]{:S(2)}) copy-start(s32[1,128,512]{2,1,0:T(8,128)} %param.7) | copy-start | bytes 786436
  0.8 10.2 %collective-permute-start = (bf16[3,2048]{1,0:T(4,128)(2,1)S(1)}, bf16[3,2048]{1,0:T(4,128)(2,1)S(1)}, u32[]{:S(2)}, u32[]{:S(2)}) collective-permute-start(bf16[3,2048]{1,0:T(4,128)(2,1)S(1)} %get-tuple-element.22), channel_id=1, source_target_pairs={{1,0},{2,1},{3,2},{5,4},{6,5},{7,6},{9,8},{10,9},{11,10},{13,12},{... | collective-permute-start | bytes 36872 | tf_op jit(solution)/shard_map/ppermute | solution.py:19
  2.2 14.0 %copy-start.1 = (bf16[1,512,2048]{2,1,0:T(8,128)(2,1)S(1)}, bf16[1,512,2048]{2,1,0:T(8,128)(2,1)}, u32[]{:S(2)}) copy-start(bf16[1,512,2048]{2,1,0:T(8,128)(2,1)} %param.4) | copy-start | bytes 6291460
  5.2 64.1 %collective-permute-start.4 = (bf16[256,2048]{1,0:T(8,128)(2,1)}, bf16[256,2048]{1,0:T(8,128)(2,1)}, u32[]{:S(2)}, u32[]{:S(2)}) collective-permute-start(bf16[256,2048]{1,0:T(8,128)(2,1)} %get-tuple-element.24), channel_id=1, source_target_pairs={{0,4},{4,8},{8,12},{12,16},{16,20},{20,24},{24,28},{1,5},{5,9},{9,... | collective-permute-start | bytes 3145736 | tf_op jit(solution)/shard_map/ppermute | solution.py:19
  12.2 7.0 %collective-permute-start.1 = (bf16[3,8,512]{2,1,0:T(8,128)(2,1)S(1)}, bf16[3,8,512]{2,1,0:T(8,128)(2,1)S(1)}, u32[]{:S(2)}, u32[]{:S(2)}) collective-permute-start(bf16[3,8,512]{2,1,0:T(8,128)(2,1)S(1)} %get-tuple-element.52), channel_id=1, source_target_pairs={{0,1},{1,2},{2,3},{4,5},{5,6},{6,7},{8,9},{9,10},{10,11},{12,13},{... | collective-permute-start | bytes 73736 | tf_op jit(solution)/shard_map/ppermute | solution.py:30
  14.9 4.2 %collective-permute-start.2 = (bf16[3,8,512]{2,1,0:T(8,128)(2,1)S(1)}, bf16[3,8,512]{2,1,0:T(8,128)(2,1)S(1)}, u32[]{:S(2)}, u32[]{:S(2)}) collective-permute-start(bf16[3,8,512]{2,1,0:T(8,128)(2,1)S(1)} %get-tuple-element.53), channel_id=1, source_target_pairs={{1,0},{2,1},{3,2},{5,4},{6,5},{7,6},{9,8},{10,9},{11,10},{13,12},{... | collective-permute-start | bytes 73736 | tf_op jit(solution)/shard_map/ppermute | solution.py:32
  17.8 51.4 %collective-permute-start.3 = (bf16[259,2048]{1,0:T(8,128)(2,1)}, bf16[259,2048]{1,0:T(8,128)(2,1)}, u32[]{:S(2)}, u32[]{:S(2)}) collective-permute-start(bf16[259,2048]{1,0:T(8,128)(2,1)} %get-tuple-element.20), channel_id=1, source_target_pairs={{4,0},{8,4},{12,8},{16,12},{20,16},{24,20},{28,24},{5,1},{9,5},{13... | collective-permute-start | bytes 3182600 | tf_op jit(solution)/shard_map/ppermute | solution.py:19
  23.1 11.0 %copy-start.5 = (s32[25,2]{0,1:T(2,128)S(1)}, s32[25,2]{0,1:T(2,128)}, u32[]{:S(2)}) copy-start(s32[25,2]{0,1:T(2,128)} %param.5) | copy-start | bytes 604
  26.4 38.6 %all-to-all-start = ((bf16[3,8,11520]{2,0,1:T(4,128)(2,1)}), bf16[3,8,11520]{2,0,1:T(4,128)(2,1)S(1)}, u32[]{:S(2)}, u32[]{:S(2)}) async-start(bf16[3,8,11520]{2,0,1:T(4,128)(2,1)} %constant_dynamic-update-slice_fusion), calls=%async_computation | async-start | bytes 1474560 | tf_op jit(solution)/shard_map/all_to_all | solution.py:193
  33.4 59.2 %collective-permute-start.6 = (bf16[3,2048]{1,0:T(4,128)(2,1)S(1)}, bf16[3,2048]{1,0:T(4,128)(2,1)S(1)}, u32[]{:S(2)}, u32[]{:S(2)}) collective-permute-start(bf16[3,2048]{1,0:T(4,128)(2,1)S(1)} %get-tuple-element.21), channel_id=1, source_target_pairs={{4,1},{5,2},{6,3},{8,5},{9,6},{10,7},{12,9},{13,10},{14,11},{16,13... | collective-permute-start | bytes 36872 | tf_op jit(solution)/shard_map/ppermute | solution.py:203
  90.1 25.2 %collective-permute-start.5 = (f32[2,8,512]{2,1,0:T(8,128)S(1)}, f32[2,8,512]{2,1,0:T(8,128)S(1)}, u32[]{:S(2)}, u32[]{:S(2)}) collective-permute-start(f32[2,8,512]{2,1,0:T(8,128)S(1)} %slice.381), channel_id=1, source_target_pairs={{0,1},{1,2},{2,3},{4,5},{5,6},{6,7},{8,9},{9,10},{10,11},{12,13},{... | collective-permute-start | bytes 98312 | tf_op jit(solution)/shard_map/ppermute | solution.py:30
  114.0 4.4 %collective-permute-start.7 = (f32[2,8,512]{2,1,0:T(8,128)S(1)}, f32[2,8,512]{2,1,0:T(8,128)S(1)}, u32[]{:S(2)}, u32[]{:S(2)}) collective-permute-start(f32[2,8,512]{2,1,0:T(8,128)S(1)} %slice.382), channel_id=1, source_target_pairs={{1,0},{2,1},{3,2},{5,4},{6,5},{7,6},{9,8},{10,9},{11,10},{13,12},{... | collective-permute-start | bytes 98312 | tf_op jit(solution)/shard_map/ppermute | solution.py:32
  122.1 9.4 %copy-start.2 = (bf16[3,8,144,80]{3,2,1,0:T(8,128)(2,1)S(1)}, bf16[3,8,144,80]{3,2,1,0:T(8,128)(2,1)}, u32[]{:S(2)}) copy-start(bf16[3,8,144,80]{3,2,1,0:T(8,128)(2,1)} %reshape.198) | copy-start | bytes 1658884
  125.3 25.5 %all-to-all-start.1 = ((f32[2,8,11520]{2,0,1:T(2,128)}), f32[2,8,11520]{2,0,1:T(2,128)}, u32[]{:S(2)}, u32[]{:S(2)}) async-start(f32[2,8,11520]{2,0,1:T(2,128)} %constant_dynamic-update-slice_fusion.8), calls=%async_computation.1 | async-start | bytes 1474560 | tf_op jit(solution)/shard_map/all_to_all | solution.py:193
  155.9 1.3 copy-start
  155.9 1.6 slice-start
  167.8 1.0 copy-start.3

commit v14 on v12

--- a/solution.py
+++ b/solution.py
@@ -190,14 +190,15 @@
     half = pixels.shape[0] // 2
     sec_count = lax.axis_size("sec")
     strip_count = lax.axis_size("strip")
-    successor_top = shifted_2(pixels[: half + RAD], "sec", -1)
+    aligned = -(-RAD // 16) * 16
+    successor_top = shifted_2(pixels[: half + aligned], "sec", -1)[: half + RAD]
     prior_bottom = shifted_2(pixels[half:], "sec", 1)
     corner = lax.ppermute(
-        pixels[-RAD:],
+        pixels[-aligned:],
         ("sec", "strip"),
         [((s + 1) * strip_count + p - 1, s * strip_count + p) for s in range(sec_count - 1) for p in range(1, strip_count)],
-    )
-    below = shifted_2(pixels[:RAD], "strip", -1)
+    )[-RAD:]
+    below = shifted_2(pixels[:aligned], "strip", -1)[:RAD]
     keep_mask = (lax.axis_index("sec") < sec_count - 1).astype(jnp.float32)
     springs, validity, below = lax.optimization_barrier((springs, validity, below))
     match_weight = validity[0].astype(jnp.float32) * keep_mask

time: 182 us -> 188 us (1.033)
  local copies, waits for them, and re-layouts: 35.4 us -> 53.2 us
  waiting for transfers between devices: 49.7 us -> 37.2 us
    all_to_all x2, waiting for transfers between devices: 46.7 us -> 32.6 us  [tiles_with_halo(): lax.all_to_all(flat, 'sec', split_axis=1, concat_axis=1, tiled=True)]
    another operation x18, local copies, waits for them, and re-layouts: 4.22 us -> 13.8 us  [tiles_with_halo(): jnp.stack([columns[:, :, j * width:(j + 1) * width + 2 * halo] for j in r...]
    slice x1 -> x5, local copies, waits for them, and re-layouts: 0.79 us -> 6.59 us  [the longest x2 3.7 us: shards(): successor_top = shifted_2(pixels[:half + aligned], 'sec', -1)[:half + RAD]]
    unnamed x27 -> x37, local copies, waits for them, and re-layouts: 11.4 us -> 15.9 us
    all_to_all x2, starting transfers between devices: 13.3 us -> 10.7 us  [tiles_with_halo(): lax.all_to_all(flat, 'sec', split_axis=1, concat_axis=1, tiled=True)]
    ppermute x2, starting transfers between devices: 5.23 us -> 7.23 us  [extended(): lax.ppermute(tail, axis, [(i, (i + 1) % count) for i in range(ends)])]
  transfers between devices with their start and end apart: 10 -> 10, of which waited for: 3 -> 4; matrix products, arithmetic and copies ran while one was open for 12% -> 21% of each run, Pallas kernels for 16% -> 8%
where the time goes in v14:
time: 188 us; the launch traced here: 187 us
  local copies, waits for them, and re-layouts  53.2 us (28%)
  waiting for transfers between devices  37.2 us (20%)
  starting transfers between devices  31.7 us (17%)
  Pallas kernels  29.1 us (15%)
  blocking collectives  19.1 us (10%)
  other arithmetic  16.2 us (9%)
    all_to_all x2, waiting for transfers between devices, tiles_with_halo(): lax.all_to_all(flat, 'sec', split_axis=1, concat_axis=1, tiled=True)  32.6 us
    pallas_call x2, Pallas kernels, section_flow(): pl.pallas_call(flow_kernel, grid_spec=grid_spec, out_shape=jax.ShapeDtype...  29.1 us
    all_to_all x1, blocking collectives, shards(): lax.all_to_all(flat, 'sec', split_axis=1, concat_axis=1, tiled=True)  19.1 us
    unnamed x37, local copies, waits for them, and re-layouts  15.9 us
    another operation x18, local copies, waits for them, and re-layouts, tiles_with_halo(): jnp.stack([columns[:, :, j * width:(j + 1) * width + 2 * halo] for j in r...  13.8 us
    all_to_all x2, starting transfers between devices, tiles_with_halo(): lax.all_to_all(flat, 'sec', split_axis=1, concat_axis=1, tiled=True)  10.7 us
    ppermute x3, starting transfers between devices, shifted_2(): return lax.ppermute(shard, axis, pairs)  9.82 us
    add x7, other arithmetic, advance(): return positions + relax_rate * force / (1.0 + diagonal)  8.23 us
  transfers between devices with their start and end apart: 10, of which 4 were waited for; matrix products, arithmetic and copies ran while one was open for 21% of the time, Pallas kernels for 8%

profile of v14, /device:TPU:0, one launch (start us, length us, event | category | flops | bytes accessed | tf_op | source)
XLA Modules:
  0.0 186.8 jit_solution(477080348124343478)
XLA Ops:
  0.0 1.5 slice_bitcast_fusion.7
  1.5 1.4 collective-permute-start.6
  4.2 2.4 %slice_bitcast_fusion = bf16[272,2048]{1,0:T(8,128)(2,1)} fusion(bf16[1,512,2048]{2,1,0:T(8,128)(2,1)} %param.4), kind=kLoop, calls=%fused_computation.133 | loop fusion | bytes 2228224 | tf_op jit(solution)/shard_map/slice | solution.py:194
  6.6 1.4 collective-permute-start.3
  9.2 7.1 %collective-permute-start.4 = (bf16[256,2048]{1,0:T(8,128)(2,1)}, bf16[256,2048]{1,0:T(8,128)(2,1)}, u32[]{:S(2)}, u32[]{:S(2)}) collective-permute-start(bf16[256,2048]{1,0:T(8,128)(2,1)} %get-tuple-element.22), channel_id=1, source_target_pairs={{0,4},{4,8},{8,12},{12,16},{16,20},{20,24},{24,28},{1,5},{5,9},{9,... | collective-permute-start | bytes 3145736 | tf_op jit(solution)/shard_map/ppermute | solution.py:19
  18.1 3.8 %collective-permute-start.1 = (bf16[3,8,512]{2,1,0:T(8,128)(2,1)S(1)}, bf16[3,8,512]{2,1,0:T(8,128)(2,1)S(1)}, u32[]{:S(2)}, u32[]{:S(2)}) collective-permute-start(bf16[3,8,512]{2,1,0:T(8,128)(2,1)S(1)} %get-tuple-element.50), channel_id=1, source_target_pairs={{0,1},{1,2},{2,3},{4,5},{5,6},{6,7},{8,9},{9,10},{10,11},{12,13},{... | collective-permute-start | bytes 73736 | tf_op jit(solution)/shard_map/ppermute | solution.py:30
  23.8 2.7 %collective-permute-done.2 = bf16[3,8,512]{2,1,0:T(8,128)(2,1)S(1)} collective-permute-done((bf16[3,8,512]{2,1,0:T(8,128)(2,1)S(1)}, bf16[3,8,512]{2,1,0:T(8,128)(2,1)S(1)}, u32[]{:S(2)}, u32[]{:S(2)}) %collective-permute-start.2) | collective-permute-done | bytes 24608 | tf_op jit(solution)/shard_map/ppermute | solution.py:32
  27.6 1.7 stack.69
  29.3 1.7 stack.68
  31.1 1.7 stack.67
  32.8 1.7 stack.66
  34.5 1.7 stack.65
  38.7 1.6 constant_dynamic-update-slice_fusion.7
  40.3 1.6 constant_dynamic-update-slice_fusion.6
  41.8 1.6 constant_dynamic-update-slice_fusion.5
  43.4 1.6 constant_dynamic-update-slice_fusion.4
  45.0 1.6 constant_dynamic-update-slice_fusion.3
  48.5 6.3 %all-to-all-start = ((bf16[3,8,11520]{2,0,1:T(4,128)(2,1)}), bf16[3,8,11520]{2,0,1:T(4,128)(2,1)}, u32[]{:S(2)}, u32[]{:S(2)}) async-start(bf16[3,8,11520]{2,0,1:T(4,128)(2,1)} %constant_dynamic-update-slice_fusion), calls=%async_computation | async-start | bytes 1474560 | tf_op jit(solution)/shard_map/all_to_all | solution.py:185
  57.2 1.5 fusion.61.following_ref
  58.7 15.1 %all-to-all-done = bf16[3,8,11520]{2,0,1:T(4,128)(2,1)} async-done(((bf16[3,8,11520]{2,0,1:T(4,128)(2,1)}), bf16[3,8,11520]{2,0,1:T(4,128)(2,1)}, u32[]{:S(2)}, u32[]{:S(2)}) %all-to-all-start) | async-done | bytes 552992 | tf_op jit(solution)/shard_map/all_to_all | solution.py:185
  75.0 2.4 %reshape.198 = bf16[3,8,144,80]{3,2,1,0:T(8,128)(2,1)} reshape(bf16[3,8,11520]{2,1,0:T(8,128)(2,1)S(1)} %copy.22) | data formatting | bytes 1105920 | tf_op jit(solution)/shard_map/reshape | solution.py:185
  77.3 1.3 slice.391
  78.7 15.1 %shard_map.46 = f32[2,64,512]{2,1,0:T(8,128)S(1)} custom-call(s32[25,2]{1,0:T(8,128)S(1)} %copy.23.offsets_ref, bf16[256,2048]{1,0:T(8,128)(2,1)} %collective-permute-done.4.current_ref, bf16[288,2048]{1,0:T(8,128)(2,1)S(1)} %fusion.61.following_ref, bf16[512,512]{1,0:T(8,128)(2,1)S(1)} %fusion.96.permute_ref), custom_call_target="tpu_custom_call" | custom-call | tf_op jit(solution)/shard_map/pallas_call | solution.py:147
  93.8 3.4 %collective-permute-start.5 = (f32[2,8,512]{2,1,0:T(8,128)S(1)}, f32[2,8,512]{2,1,0:T(8,128)S(1)}, u32[]{:S(2)}, u32[]{:S(2)}) collective-permute-start(f32[2,8,512]{2,1,0:T(8,128)S(1)} %slice.395), channel_id=1, source_target_pairs={{0,1},{1,2},{2,3},{4,5},{5,6},{6,7},{8,9},{9,10},{10,11},{12,13},{... | collective-permute-start | bytes 98312 | tf_op jit(solution)/shard_map/ppermute | solution.py:30
  97.5 14.0 %shard_map.47 = f32[2,64,512]{2,1,0:T(8,128)S(1)} custom-call(s32[25,2]{1,0:T(8,128)S(1)} %copy.23.offsets_ref, bf16[256,2048]{1,0:T(8,128)(2,1)S(1)} %get-tuple-element.21.current_ref, bf16[288,2048]{1,0:T(8,128)(2,1)S(1)} %select_maximum_fusion.following_ref, bf16[512,512]{1,0:T(8,128)(2,1)S(1)} %fusion.96.permute_ref), custom_call_target="tpu_custom_call" | custom-call | tf_op jit(solution)/shard_map/pallas_call | solution.py:147
  112.9 1.8 collective-permute-done.7
  121.6 4.4 %all-to-all-start.1 = ((f32[2,8,11520]{2,0,1:T(2,128)}), f32[2,8,11520]{2,0,1:T(2,128)}, u32[]{:S(2)}, u32[]{:S(2)}) async-start(f32[2,8,11520]{2,0,1:T(2,128)} %constant_dynamic-update-slice_fusion.8), calls=%async_computation.1 | async-start | bytes 1474560 | tf_op jit(solution)/shard_map/all_to_all | solution.py:185
  127.7 17.5 %all-to-all-done.1 = f32[2,8,11520]{2,0,1:T(2,128)} async-done(((f32[2,8,11520]{2,0,1:T(2,128)}), f32[2,8,11520]{2,0,1:T(2,128)}, u32[]{:S(2)}, u32[]{:S(2)}) %all-to-all-start.1) | async-done | bytes 737312 | tf_op jit(solution)/shard_map/all_to_all | solution.py:185
  145.2 2.0 %copy.25 = f32[2,8,11520]{2,1,0:T(8,128)} copy(f32[2,8,11520]{2,0,1:T(2,128)} %all-to-all-done.1) | data formatting | bytes 1474560 | tf_op jit(solution)/shard_map/all_to_all | solution.py:185
  147.3 3.0 %reshape.199 = f32[2,8,144,80]{3,2,1,0:T(8,128)} reshape(f32[2,8,11520]{2,1,0:T(8,128)} %copy.25) | data formatting | bytes 1474560 | tf_op jit(solution)/shard_map/reshape | solution.py:185
  163.2 1.6 slice_add_fusion
  165.6 19.1 %all_to_all.15 = f32[2,8,8192]{2,0,1:T(2,128)S(1)} all-to-all(f32[2,8,8192]{2,0,1:T(2,128)S(1)} %copy.26), channel_id=1, replica_groups=mesh['sec'=8,'strip'=4] {'sec'}, dimensions={1} | all-to-all | bytes 1048576 | tf_op jit(solution)/shard_map/all_to_all | solution.py:255
  (103 shorter events, 41.0 us)
Async XLA Ops:
  1.5 6.5 %copy-start.1 = (bf16[1,512,2048]{2,1,0:T(8,128)(2,1)S(1)}, bf16[1,512,2048]{2,1,0:T(8,128)(2,1)}, u32[]{:S(2)}) copy-start(bf16[1,512,2048]{2,1,0:T(8,128)(2,1)} %param.4) | copy-start | bytes 6291460
  1.5 54.9 %collective-permute-start.6 = (bf16[16,2048]{1,0:T(8,128)(2,1)}, bf16[16,2048]{1,0:T(8,128)(2,1)}, u32[]{:S(2)}, u32[]{:S(2)}) collective-permute-start(bf16[16,2048]{1,0:T(8,128)(2,1)} %get-tuple-element.19), channel_id=1, source_target_pairs={{4,1},{5,2},{6,3},{8,5},{9,6},{10,7},{12,9},{13,10},{14,11},{16,13... | collective-permute-start | bytes 196616 | tf_op jit(solution)/shard_map/ppermute | solution.py:196
  2.9 13.4 %collective-permute-start = (bf16[16,2048]{1,0:T(8,128)(2,1)S(1)}, bf16[16,2048]{1,0:T(8,128)(2,1)S(1)}, u32[]{:S(2)}, u32[]{:S(2)}) collective-permute-start(bf16[16,2048]{1,0:T(8,128)(2,1)S(1)} %get-tuple-element.20), channel_id=1, source_target_pairs={{1,0},{2,1},{3,2},{5,4},{6,5},{7,6},{9,8},{10,9},{11,10},{13,12},{... | collective-permute-start | bytes 196616 | tf_op jit(solution)/shard_map/ppermute | solution.py:19
  6.6 10.4 %copy-start.7 = (s32[1,128,512]{2,1,0:T(8,128)S(1)}, s32[1,128,512]{2,1,0:T(8,128)}, u32[]{:S(2)}) copy-start(s32[1,128,512]{2,1,0:T(8,128)} %param.7) | copy-start | bytes 786436
  6.6 70.8 %collective-permute-start.3 = (bf16[272,2048]{1,0:T(8,128)(2,1)}, bf16[272,2048]{1,0:T(8,128)(2,1)}, u32[]{:S(2)}, u32[]{:S(2)}) collective-permute-start(bf16[272,2048]{1,0:T(8,128)(2,1)} %slice_bitcast_fusion), channel_id=1, source_target_pairs={{4,0},{8,4},{12,8},{16,12},{20,16},{24,20},{28,24},{5,1},{9,5},{13... | collective-permute-start | bytes 3342344 | tf_op jit(solution)/shard_map/ppermute | solution.py:19
  9.2 69.5 %collective-permute-start.4 = (bf16[256,2048]{1,0:T(8,128)(2,1)}, bf16[256,2048]{1,0:T(8,128)(2,1)}, u32[]{:S(2)}, u32[]{:S(2)}) collective-permute-start(bf16[256,2048]{1,0:T(8,128)(2,1)} %get-tuple-element.22), channel_id=1, source_target_pairs={{0,4},{4,8},{8,12},{12,16},{16,20},{20,24},{24,28},{1,5},{5,9},{9,... | collective-permute-start | bytes 3145736 | tf_op jit(solution)/shard_map/ppermute | solution.py:19
  18.1 5.7 %collective-permute-start.1 = (bf16[3,8,512]{2,1,0:T(8,128)(2,1)S(1)}, bf16[3,8,512]{2,1,0:T(8,128)(2,1)S(1)}, u32[]{:S(2)}, u32[]{:S(2)}) collective-permute-start(bf16[3,8,512]{2,1,0:T(8,128)(2,1)S(1)} %get-tuple-element.50), channel_id=1, source_target_pairs={{0,1},{1,2},{2,3},{4,5},{5,6},{6,7},{8,9},{9,10},{10,11},{12,13},{... | collective-permute-start | bytes 73736 | tf_op jit(solution)/shard_map/ppermute | solution.py:30
  21.9 4.6 %collective-permute-start.2 = (bf16[3,8,512]{2,1,0:T(8,128)(2,1)S(1)}, bf16[3,8,512]{2,1,0:T(8,128)(2,1)S(1)}, u32[]{:S(2)}, u32[]{:S(2)}) collective-permute-start(bf16[3,8,512]{2,1,0:T(8,128)(2,1)S(1)} %get-tuple-element.51), channel_id=1, source_target_pairs={{1,0},{2,1},{3,2},{5,4},{6,5},{7,6},{9,8},{10,9},{11,10},{13,12},{... | collective-permute-start | bytes 73736 | tf_op jit(solution)/shard_map/ppermute | solution.py:32
  37.0 10.2 %copy-start.5 = (bf16[3,1,11520]{2,0,1:T(4,128)(2,1)S(1)}, bf16[3,1,11520]{2,0,1:T(4,128)(2,1)}, u32[]{:S(2)}) copy-start(bf16[3,1,11520]{2,0,1:T(4,128)(2,1)} %stack.68) | copy-start | bytes 207364
  37.0 10.8 %copy-start.4 = (bf16[3,1,11520]{2,0,1:T(4,128)(2,1)S(1)}, bf16[3,1,11520]{2,0,1:T(4,128)(2,1)}, u32[]{:S(2)}) copy-start(bf16[3,1,11520]{2,0,1:T(4,128)(2,1)} %stack.69) | copy-start | bytes 207364
  37.9 8.6 %copy-start.6 = (bf16[3,1,11520]{2,0,1:T(4,128)(2,1)S(1)}, bf16[3,1,11520]{2,0,1:T(4,128)(2,1)}, u32[]{:S(2)}) copy-start(bf16[3,1,11520]{2,0,1:T(4,128)(2,1)} %stack.67) | copy-start | bytes 207364
  48.5 25.2 %all-to-all-start = ((bf16[3,8,11520]{2,0,1:T(4,128)(2,1)}), bf16[3,8,11520]{2,0,1:T(4,128)(2,1)}, u32[]{:S(2)}, u32[]{:S(2)}) async-start(bf16[3,8,11520]{2,0,1:T(4,128)(2,1)} %constant_dynamic-update-slice_fusion), calls=%async_computation | async-start | bytes 1474560 | tf_op jit(solution)/shard_map/all_to_all | solution.py:185
  54.8 1.3 copy-start.9
  54.8 1.4 copy-start.10
  54.8 2.3 %copy-start.8 = (bf16[3,2048]{1,0:T(4,128)(2,1)S(1)}, bf16[3,2048]{1,0:T(4,128)(2,1)}, u32[]{:S(2)}) copy-start(bf16[3,2048]{1,0:T(4,128)(2,1)} %slice.384) | copy-start | bytes 36868
  93.8 19.1 %collective-permute-start.5 = (f32[2,8,512]{2,1,0:T(8,128)S(1)}, f32[2,8,512]{2,1,0:T(8,128)S(1)}, u32[]{:S(2)}, u32[]{:S(2)}) collective-permute-start(f32[2,8,512]{2,1,0:T(8,128)S(1)} %slice.395), channel_id=1, source_target_pairs={{0,1},{1,2},{2,3},{4,5},{5,6},{6,7},{8,9},{9,10},{10,11},{12,13},{... | collective-permute-start | bytes 98312 | tf_op jit(solution)/shard_map/ppermute | solution.py:30
  111.6 3.1 %collective-permute-start.7 = (f32[2,8,512]{2,1,0:T(8,128)S(1)}, f32[2,8,512]{2,1,0:T(8,128)S(1)}, u32[]{:S(2)}, u32[]{:S(2)}) collective-permute-start(f32[2,8,512]{2,1,0:T(8,128)S(1)} %slice.397), channel_id=1, source_target_pairs={{1,0},{2,1},{3,2},{5,4},{6,5},{7,6},{9,8},{10,9},{11,10},{13,12},{... | collective-permute-start | bytes 98312 | tf_op jit(solution)/shard_map/ppermute | solution.py:32
  118.4 7.6 %copy-start.2 = (bf16[3,8,144,80]{3,2,1,0:T(8,128)(2,1)S(1)}, bf16[3,8,144,80]{3,2,1,0:T(8,128)(2,1)}, u32[]{:S(2)}) copy-start(bf16[3,8,144,80]{3,2,1,0:T(8,128)(2,1)} %reshape.198) | copy-start | bytes 1658884
  121.6 23.6 %all-to-all-start.1 = ((f32[2,8,11520]{2,0,1:T(2,128)}), f32[2,8,11520]{2,0,1:T(2,128)}, u32[]{:S(2)}, u32[]{:S(2)}) async-start(f32[2,8,11520]{2,0,1:T(2,128)} %constant_dynamic-update-slice_fusion.8), calls=%async_computation.1 | async-start | bytes 1474560 | tf_op jit(solution)/shard_map/all_to_all | solution.py:185
  150.3 1.3 copy-start
  150.3 1.6 slice-start
  162.2 1.0 copy-start.3

commit v15 on v12

--- a/solution.py
+++ b/solution.py
@@ -121,7 +121,7 @@
         flow_ref[1, rows, :] = col_sum / weight_sum
 
 
-def section_flow(current, following, offsets, tile_rows=32):
+def section_flow(current, following, offsets, tile_rows=64):
     row_count, col_count = current.shape
     node_rows, node_cols = row_count // 4, col_count // 4
     window = tile_rows + 8

time: 182 us -> 178 us (0.978)
  Pallas kernels: 29.1 us -> 24.7 us
    pallas_call x2, Pallas kernels: 29.1 us -> 24.7 us  [section_flow(): pl.pallas_call(flow_kernel, grid_spec=grid_spec, out_shape=jax.ShapeDtype...]
  transfers between devices with their start and end apart: 10 -> 10, of which waited for: 3 -> 3; matrix products, arithmetic and copies ran while one was open for 12% -> 13% of each run, Pallas kernels for 16% -> 14%
where the time goes in v15:
time: 178 us; the launch traced here: 177 us
  waiting for transfers between devices  49.8 us (28%)
  local copies, waits for them, and re-layouts  35.4 us (20%)
  starting transfers between devices  30.2 us (17%)
  Pallas kernels  24.7 us (14%)
  blocking collectives  19.4 us (11%)
  other arithmetic  16.8 us (9%)
    all_to_all x2, waiting for transfers between devices, tiles_with_halo(): lax.all_to_all(flat, 'sec', split_axis=1, concat_axis=1, tiled=True)  46.7 us
    pallas_call x2, Pallas kernels, section_flow(): pl.pallas_call(flow_kernel, grid_spec=grid_spec, out_shape=jax.ShapeDtype...  24.7 us
    all_to_all x1, blocking collectives, shards(): lax.all_to_all(flat, 'sec', split_axis=1, concat_axis=1, tiled=True)  19.4 us
    all_to_all x2, starting transfers between devices, tiles_with_halo(): lax.all_to_all(flat, 'sec', split_axis=1, concat_axis=1, tiled=True)  13.2 us
    unnamed x27, local copies, waits for them, and re-layouts  11.4 us
    ppermute x3, starting transfers between devices, shifted_2(): return lax.ppermute(shard, axis, pairs)  8.55 us
    add x7, other arithmetic, advance(): return positions + relax_rate * force / (1.0 + diagonal)  8.23 us
    reshape x2, local copies, waits for them, and re-layouts, tiles_with_halo(): lax.all_to_all(flat, 'sec', split_axis=1, concat_axis=1, tiled=True)  6.46 us
  transfers between devices with their start and end apart: 10, of which 3 were waited for; matrix products, arithmetic and copies ran while one was open for 13% of the time, Pallas kernels for 14%

profile of v15, /device:TPU:0, one launch (start us, length us, event | category | flops | bytes accessed | tf_op | source)
XLA Modules:
  0.0 176.7 jit_solution(8099317274447649169)
XLA Ops:
  0.8 1.4 collective-permute-start
  2.2 2.9 %slice_bitcast_fusion.2 = (bf16[256,2048]{1,0:T(8,128)(2,1)S(1)}, bf16[256,2048]{1,0:T(8,128)(2,1)}) fusion(bf16[1,512,2048]{2,1,0:T(8,128)(2,1)} %param.4), kind=kLoop, calls=%fused_computation.141 | loop fusion | bytes 4194304 | tf_op jit(solution)/shard_map/slice | solution.py:215
  5.2 5.8 %collective-permute-start.4 = (bf16[256,2048]{1,0:T(8,128)(2,1)}, bf16[256,2048]{1,0:T(8,128)(2,1)}, u32[]{:S(2)}, u32[]{:S(2)}) collective-permute-start(bf16[256,2048]{1,0:T(8,128)(2,1)} %get-tuple-element.24), channel_id=1, source_target_pairs={{0,4},{4,8},{8,12},{12,16},{16,20},{20,24},{24,28},{1,5},{5,9},{9,... | collective-permute-start | bytes 3145736 | tf_op jit(solution)/shard_map/ppermute | solution.py:19
  11.0 1.1 fusion.100
  12.2 2.8 %collective-permute-start.1 = (bf16[3,8,512]{2,1,0:T(8,128)(2,1)S(1)}, bf16[3,8,512]{2,1,0:T(8,128)(2,1)S(1)}, u32[]{:S(2)}, u32[]{:S(2)}) collective-permute-start(bf16[3,8,512]{2,1,0:T(8,128)(2,1)S(1)} %get-tuple-element.52), channel_id=1, source_target_pairs={{0,1},{1,2},{2,3},{4,5},{5,6},{6,7},{8,9},{9,10},{10,11},{12,13},{... | collective-permute-start | bytes 73736 | tf_op jit(solution)/shard_map/ppermute | solution.py:30
  14.9 1.3 collective-permute-start.2
  16.2 1.6 slice_bitcast_fusion
  17.8 1.3 collective-permute-start.3
  26.4 7.0 %all-to-all-start = ((bf16[3,8,11520]{2,0,1:T(4,128)(2,1)}), bf16[3,8,11520]{2,0,1:T(4,128)(2,1)S(1)}, u32[]{:S(2)}, u32[]{:S(2)}) async-start(bf16[3,8,11520]{2,0,1:T(4,128)(2,1)} %constant_dynamic-update-slice_fusion), calls=%async_computation | async-start | bytes 1474560 | tf_op jit(solution)/shard_map/all_to_all | solution.py:185
  34.3 1.5 fusion.61.following_ref
  35.9 29.1 %all-to-all-done = bf16[3,8,11520]{2,0,1:T(4,128)(2,1)S(1)} async-done(((bf16[3,8,11520]{2,0,1:T(4,128)(2,1)}), bf16[3,8,11520]{2,0,1:T(4,128)(2,1)S(1)}, u32[]{:S(2)}, u32[]{:S(2)}) %all-to-all-start) | async-done | bytes 552992 | tf_op jit(solution)/shard_map/all_to_all | solution.py:185
  65.8 3.4 %reshape.198 = bf16[3,8,144,80]{3,2,1,0:T(8,128)(2,1)} reshape(bf16[3,8,11520]{2,1,0:T(8,128)(2,1)} %copy.22) | data formatting | bytes 1105920 | tf_op jit(solution)/shard_map/reshape | solution.py:185
  69.3 13.0 %shard_map.46 = f32[2,64,512]{2,1,0:T(8,128)S(1)} custom-call(s32[25,2]{1,0:T(8,128)S(1)} %copy.23.offsets_ref, bf16[256,2048]{1,0:T(8,128)(2,1)} %collective-permute-done.4.current_ref, bf16[288,2048]{1,0:T(8,128)(2,1)S(1)} %fusion.61.following_ref, bf16[512,512]{1,0:T(8,128)(2,1)S(1)} %fusion.96.permute_ref), custom_call_target="tpu_custom_call" | custom-call | tf_op jit(solution)/shard_map/pallas_call | solution.py:147
  82.2 2.5 %collective-permute-start.5 = (f32[2,8,512]{2,1,0:T(8,128)S(1)}, f32[2,8,512]{2,1,0:T(8,128)S(1)}, u32[]{:S(2)}, u32[]{:S(2)}) collective-permute-start(f32[2,8,512]{2,1,0:T(8,128)S(1)} %slice.381), channel_id=1, source_target_pairs={{0,1},{1,2},{2,3},{4,5},{5,6},{6,7},{8,9},{9,10},{10,11},{12,13},{... | collective-permute-start | bytes 98312 | tf_op jit(solution)/shard_map/ppermute | solution.py:30
  84.7 1.5 select_maximum_fusion.following_ref
  86.3 11.7 %shard_map.47 = f32[2,64,512]{2,1,0:T(8,128)S(1)} custom-call(s32[25,2]{1,0:T(8,128)S(1)} %copy.23.offsets_ref, bf16[256,2048]{1,0:T(8,128)(2,1)S(1)} %get-tuple-element.23.current_ref, bf16[288,2048]{1,0:T(8,128)(2,1)S(1)} %select_maximum_fusion.following_ref, bf16[512,512]{1,0:T(8,128)(2,1)S(1)} %fusion.96.permute_ref), custom_call_target="tpu_custom_call" | custom-call | tf_op jit(solution)/shard_map/pallas_call | solution.py:147
  98.0 1.3 collective-permute-start.7
  99.3 3.1 %collective-permute-done.7 = f32[2,8,512]{2,1,0:T(8,128)S(1)} collective-permute-done((f32[2,8,512]{2,1,0:T(8,128)S(1)}, f32[2,8,512]{2,1,0:T(8,128)S(1)}, u32[]{:S(2)}, u32[]{:S(2)}) %collective-permute-start.7) | collective-permute-done | bytes 32800 | tf_op jit(solution)/shard_map/ppermute | solution.py:32
  109.3 6.2 %all-to-all-start.1 = ((f32[2,8,11520]{2,0,1:T(2,128)}), f32[2,8,11520]{2,0,1:T(2,128)}, u32[]{:S(2)}, u32[]{:S(2)}) async-start(f32[2,8,11520]{2,0,1:T(2,128)} %constant_dynamic-update-slice_fusion.8), calls=%async_computation.1 | async-start | bytes 1474560 | tf_op jit(solution)/shard_map/all_to_all | solution.py:185
  116.3 1.0 slice.394
  117.3 17.6 %all-to-all-done.1 = f32[2,8,11520]{2,0,1:T(2,128)} async-done(((f32[2,8,11520]{2,0,1:T(2,128)}), f32[2,8,11520]{2,0,1:T(2,128)}, u32[]{:S(2)}, u32[]{:S(2)}) %all-to-all-start.1) | async-done | bytes 737312 | tf_op jit(solution)/shard_map/all_to_all | solution.py:185
  134.9 2.1 %copy.25 = f32[2,8,11520]{2,1,0:T(8,128)} copy(f32[2,8,11520]{2,0,1:T(2,128)} %all-to-all-done.1) | data formatting | bytes 1474560 | tf_op jit(solution)/shard_map/all_to_all | solution.py:185
  136.9 3.0 %reshape.199 = f32[2,8,144,80]{3,2,1,0:T(8,128)} reshape(f32[2,8,11520]{2,1,0:T(8,128)} %copy.25) | data formatting | bytes 1474560 | tf_op jit(solution)/shard_map/reshape | solution.py:185
  140.0 1.2 copy-done
  143.0 1.1 fusion.12
  144.4 1.1 fusion.19
  145.7 1.1 fusion.26
  147.0 1.1 fusion.33
  148.4 1.1 fusion.40
  149.7 1.1 fusion.47
  152.9 1.6 slice_add_fusion
  155.3 19.4 %all_to_all.15 = f32[2,8,8192]{2,0,1:T(2,128)S(1)} all-to-all(f32[2,8,8192]{2,0,1:T(2,128)S(1)} %copy.26), channel_id=1, replica_groups=mesh['sec'=8,'strip'=4] {'sec'}, dimensions={1} | all-to-all | bytes 1048576 | tf_op jit(solution)/shard_map/all_to_all | solution.py:254
  (89 shorter events, 25.3 us)
Async XLA Ops:
  0.8 10.2 %copy-start.4 = (s32[1,128,512]{2,1,0:T(8,128)S(1)}, s32[1,128,512]{2,1,0:T(8,128)}, u32[]{:S(2)}) copy-start(s32[1,128,512]{2,1,0:T(8,128)} %param.7) | copy-start | bytes 786436
  0.8 10.2 %collective-permute-start = (bf16[3,2048]{1,0:T(4,128)(2,1)S(1)}, bf16[3,2048]{1,0:T(4,128)(2,1)S(1)}, u32[]{:S(2)}, u32[]{:S(2)}) collective-permute-start(bf16[3,2048]{1,0:T(4,128)(2,1)S(1)} %get-tuple-element.22), channel_id=1, source_target_pairs={{1,0},{2,1},{3,2},{5,4},{6,5},{7,6},{9,8},{10,9},{11,10},{13,12},{... | collective-permute-start | bytes 36872 | tf_op jit(solution)/shard_map/ppermute | solution.py:19
  2.2 14.0 %copy-start.1 = (bf16[1,512,2048]{2,1,0:T(8,128)(2,1)S(1)}, bf16[1,512,2048]{2,1,0:T(8,128)(2,1)}, u32[]{:S(2)}) copy-start(bf16[1,512,2048]{2,1,0:T(8,128)(2,1)} %param.4) | copy-start | bytes 6291460
  5.2 64.1 %collective-permute-start.4 = (bf16[256,2048]{1,0:T(8,128)(2,1)}, bf16[256,2048]{1,0:T(8,128)(2,1)}, u32[]{:S(2)}, u32[]{:S(2)}) collective-permute-start(bf16[256,2048]{1,0:T(8,128)(2,1)} %get-tuple-element.24), channel_id=1, source_target_pairs={{0,4},{4,8},{8,12},{12,16},{16,20},{20,24},{24,28},{1,5},{5,9},{9,... | collective-permute-start | bytes 3145736 | tf_op jit(solution)/shard_map/ppermute | solution.py:19
  12.2 7.0 %collective-permute-start.1 = (bf16[3,8,512]{2,1,0:T(8,128)(2,1)S(1)}, bf16[3,8,512]{2,1,0:T(8,128)(2,1)S(1)}, u32[]{:S(2)}, u32[]{:S(2)}) collective-permute-start(bf16[3,8,512]{2,1,0:T(8,128)(2,1)S(1)} %get-tuple-element.52), channel_id=1, source_target_pairs={{0,1},{1,2},{2,3},{4,5},{5,6},{6,7},{8,9},{9,10},{10,11},{12,13},{... | collective-permute-start | bytes 73736 | tf_op jit(solution)/shard_map/ppermute | solution.py:30
  14.9 4.2 %collective-permute-start.2 = (bf16[3,8,512]{2,1,0:T(8,128)(2,1)S(1)}, bf16[3,8,512]{2,1,0:T(8,128)(2,1)S(1)}, u32[]{:S(2)}, u32[]{:S(2)}) collective-permute-start(bf16[3,8,512]{2,1,0:T(8,128)(2,1)S(1)} %get-tuple-element.53), channel_id=1, source_target_pairs={{1,0},{2,1},{3,2},{5,4},{6,5},{7,6},{9,8},{10,9},{11,10},{13,12},{... | collective-permute-start | bytes 73736 | tf_op jit(solution)/shard_map/ppermute | solution.py:32
  17.8 51.4 %collective-permute-start.3 = (bf16[259,2048]{1,0:T(8,128)(2,1)}, bf16[259,2048]{1,0:T(8,128)(2,1)}, u32[]{:S(2)}, u32[]{:S(2)}) collective-permute-start(bf16[259,2048]{1,0:T(8,128)(2,1)} %get-tuple-element.20), channel_id=1, source_target_pairs={{4,0},{8,4},{12,8},{16,12},{20,16},{24,20},{28,24},{5,1},{9,5},{13... | collective-permute-start | bytes 3182600 | tf_op jit(solution)/shard_map/ppermute | solution.py:19
  23.1 11.0 %copy-start.5 = (s32[25,2]{0,1:T(2,128)S(1)}, s32[25,2]{0,1:T(2,128)}, u32[]{:S(2)}) copy-start(s32[25,2]{0,1:T(2,128)} %param.5) | copy-start | bytes 604
  26.4 38.6 %all-to-all-start = ((bf16[3,8,11520]{2,0,1:T(4,128)(2,1)}), bf16[3,8,11520]{2,0,1:T(4,128)(2,1)S(1)}, u32[]{:S(2)}, u32[]{:S(2)}) async-start(bf16[3,8,11520]{2,0,1:T(4,128)(2,1)} %constant_dynamic-update-slice_fusion), calls=%async_computation | async-start | bytes 1474560 | tf_op jit(solution)/shard_map/all_to_all | solution.py:185
  33.4 51.3 %collective-permute-start.6 = (bf16[3,2048]{1,0:T(4,128)(2,1)S(1)}, bf16[3,2048]{1,0:T(4,128)(2,1)S(1)}, u32[]{:S(2)}, u32[]{:S(2)}) collective-permute-start(bf16[3,2048]{1,0:T(4,128)(2,1)S(1)} %get-tuple-element.21), channel_id=1, source_target_pairs={{4,1},{5,2},{6,3},{8,5},{9,6},{10,7},{12,9},{13,10},{14,11},{16,13... | collective-permute-start | bytes 36872 | tf_op jit(solution)/shard_map/ppermute | solution.py:195
  82.2 17.1 %collective-permute-start.5 = (f32[2,8,512]{2,1,0:T(8,128)S(1)}, f32[2,8,512]{2,1,0:T(8,128)S(1)}, u32[]{:S(2)}, u32[]{:S(2)}) collective-permute-start(f32[2,8,512]{2,1,0:T(8,128)S(1)} %slice.381), channel_id=1, source_target_pairs={{0,1},{1,2},{2,3},{4,5},{5,6},{6,7},{8,9},{9,10},{10,11},{12,13},{... | collective-permute-start | bytes 98312 | tf_op jit(solution)/shard_map/ppermute | solution.py:30
  98.0 4.4 %collective-permute-start.7 = (f32[2,8,512]{2,1,0:T(8,128)S(1)}, f32[2,8,512]{2,1,0:T(8,128)S(1)}, u32[]{:S(2)}, u32[]{:S(2)}) collective-permute-start(f32[2,8,512]{2,1,0:T(8,128)S(1)} %slice.382), channel_id=1, source_target_pairs={{1,0},{2,1},{3,2},{5,4},{6,5},{7,6},{9,8},{10,9},{11,10},{13,12},{... | collective-permute-start | bytes 98312 | tf_op jit(solution)/shard_map/ppermute | solution.py:32
  106.1 9.4 %copy-start.2 = (bf16[3,8,144,80]{3,2,1,0:T(8,128)(2,1)S(1)}, bf16[3,8,144,80]{3,2,1,0:T(8,128)(2,1)}, u32[]{:S(2)}) copy-start(bf16[3,8,144,80]{3,2,1,0:T(8,128)(2,1)} %reshape.198) | copy-start | bytes 1658884
  109.3 25.5 %all-to-all-start.1 = ((f32[2,8,11520]{2,0,1:T(2,128)}), f32[2,8,11520]{2,0,1:T(2,128)}, u32[]{:S(2)}, u32[]{:S(2)}) async-start(f32[2,8,11520]{2,0,1:T(2,128)} %constant_dynamic-update-slice_fusion.8), calls=%async_computation.1 | async-start | bytes 1474560 | tf_op jit(solution)/shard_map/all_to_all | solution.py:185
  139.9 1.3 copy-start
  139.9 1.6 slice-start
  151.8 1.0 copy-start.3

commit v16 on v15

--- a/solution.py
+++ b/solution.py
@@ -66,18 +66,34 @@
     split_phases(following_ref[pl.ds(base, window * 4), :], permute, lanes_ref, following_ph, window)
     column = lax.broadcasted_iota(jnp.int32, (window, node_cols), 1)
 
+    def reachable(shift, phase_of):
+        if shift == 0:
+            return phase_of != 0
+        if shift == 2:
+            return phase_of != 3
+        return phase_of >= 0
+
     def build(phase, carry):
-        block = following_ph[phase]
+        row_phase = lax.shift_right_logical(phase, 2)
+        col_phase = phase & 3
         for col_shift in range(3):
-            if col_shift == 1:
-                moved = block
-            else:
-                moved = pltpu.roll(block, (1 - col_shift) % node_cols, 1)
-                inside = (column + col_shift - 1 >= 0) & (column + col_shift - 1 < node_cols)
-                moved = jnp.where(inside, moved, 0.0)
-            for row_shift in range(3):
-                rows = moved if row_shift == 0 else pltpu.roll(moved, window - row_shift, 0)
-                shifted_ref[(row_shift * 3 + col_shift) * 16 + phase] = rows[:tile_rows]
+
+            @pl.when(reachable(col_shift, col_phase))
+            def _():
+                block = following_ph[phase]
+                if col_shift == 1:
+                    moved = block
+                else:
+                    moved = pltpu.roll(block, (1 - col_shift) % node_cols, 1)
+                    inside = (column + col_shift - 1 >= 0) & (column + col_shift - 1 < node_cols)
+                    moved = jnp.where(inside, moved, 0.0)
+                for row_shift in range(3):
+
+                    @pl.when(reachable(row_shift, row_phase))
+                    def _():
+                        rows = moved if row_shift == 0 else pltpu.roll(moved, window - row_shift, 0)
+                        shifted_ref[(row_shift * 3 + col_shift) * 16 + phase] = rows[:tile_rows]
+
         return carry
 
     lax.fori_loop(0, 16, build, 0)

time: 178 us -> 179 us (level)
  transfers between devices with their start and end apart: 10 -> 10, of which waited for: 3 -> 3; matrix products, arithmetic and copies ran while one was open for 13% -> 12% of each run, Pallas kernels for 14% -> 15%
where the time goes in v16:
time: 179 us; the launch traced here: 178 us
  waiting for transfers between devices  49.8 us (28%)
  local copies, waits for them, and re-layouts  35.4 us (20%)
  starting transfers between devices  30.2 us (17%)
  Pallas kernels  26.1 us (15%)
  blocking collectives  19.4 us (11%)
  other arithmetic  16.8 us (9%)
    all_to_all x2, waiting for transfers between devices, tiles_with_halo(): lax.all_to_all(flat, 'sec', split_axis=1, concat_axis=1, tiled=True)  46.7 us
    pallas_call x2, Pallas kernels, section_flow(): pl.pallas_call(flow_kernel, grid_spec=grid_spec, out_shape=jax.ShapeDtype...  26.1 us
    all_to_all x1, blocking collectives, shards(): lax.all_to_all(flat, 'sec', split_axis=1, concat_axis=1, tiled=True)  19.4 us
    all_to_all x2, starting transfers between devices, tiles_with_halo(): lax.all_to_all(flat, 'sec', split_axis=1, concat_axis=1, tiled=True)  13.2 us
    unnamed x27, local copies, waits for them, and re-layouts  11.4 us
    ppermute x3, starting transfers between devices, shifted_2(): return lax.ppermute(shard, axis, pairs)  8.55 us
    add x7, other arithmetic, advance(): return positions + relax_rate * force / (1.0 + diagonal)  8.23 us
    reshape x2, local copies, waits for them, and re-layouts, tiles_with_halo(): lax.all_to_all(flat, 'sec', split_axis=1, concat_axis=1, tiled=True)  6.46 us
  transfers between devices with their start and end apart: 10, of which 3 were waited for; matrix products, arithmetic and copies ran while one was open for 12% of the time, Pallas kernels for 15%

profile of v16, /device:TPU:0, one launch (start us, length us, event | category | flops | bytes accessed | tf_op | source)
XLA Modules:
  0.0 178.1 jit_solution(12534062820950537654)
XLA Ops:
  0.8 1.4 collective-permute-start
  2.2 2.9 %slice_bitcast_fusion.2 = (bf16[256,2048]{1,0:T(8,128)(2,1)S(1)}, bf16[256,2048]{1,0:T(8,128)(2,1)}) fusion(bf16[1,512,2048]{2,1,0:T(8,128)(2,1)} %param.4), kind=kLoop, calls=%fused_computation.141 | loop fusion | bytes 4194304 | tf_op jit(solution)/shard_map/slice | solution.py:231
  5.2 5.8 %collective-permute-start.4 = (bf16[256,2048]{1,0:T(8,128)(2,1)}, bf16[256,2048]{1,0:T(8,128)(2,1)}, u32[]{:S(2)}, u32[]{:S(2)}) collective-permute-start(bf16[256,2048]{1,0:T(8,128)(2,1)} %get-tuple-element.24), channel_id=1, source_target_pairs={{0,4},{4,8},{8,12},{12,16},{16,20},{20,24},{24,28},{1,5},{5,9},{9,... | collective-permute-start | bytes 3145736 | tf_op jit(solution)/shard_map/ppermute | solution.py:19
  11.0 1.1 fusion.100
  12.2 2.8 %collective-permute-start.1 = (bf16[3,8,512]{2,1,0:T(8,128)(2,1)S(1)}, bf16[3,8,512]{2,1,0:T(8,128)(2,1)S(1)}, u32[]{:S(2)}, u32[]{:S(2)}) collective-permute-start(bf16[3,8,512]{2,1,0:T(8,128)(2,1)S(1)} %get-tuple-element.52), channel_id=1, source_target_pairs={{0,1},{1,2},{2,3},{4,5},{5,6},{6,7},{8,9},{9,10},{10,11},{12,13},{... | collective-permute-start | bytes 73736 | tf_op jit(solution)/shard_map/ppermute | solution.py:30
  14.9 1.3 collective-permute-start.2
  16.2 1.6 slice_bitcast_fusion
  17.8 1.3 collective-permute-start.3
  26.4 7.0 %all-to-all-start = ((bf16[3,8,11520]{2,0,1:T(4,128)(2,1)}), bf16[3,8,11520]{2,0,1:T(4,128)(2,1)S(1)}, u32[]{:S(2)}, u32[]{:S(2)}) async-start(bf16[3,8,11520]{2,0,1:T(4,128)(2,1)} %constant_dynamic-update-slice_fusion), calls=%async_computation | async-start | bytes 1474560 | tf_op jit(solution)/shard_map/all_to_all | solution.py:201
  34.3 1.5 fusion.61.following_ref
  35.9 29.1 %all-to-all-done = bf16[3,8,11520]{2,0,1:T(4,128)(2,1)S(1)} async-done(((bf16[3,8,11520]{2,0,1:T(4,128)(2,1)}), bf16[3,8,11520]{2,0,1:T(4,128)(2,1)S(1)}, u32[]{:S(2)}, u32[]{:S(2)}) %all-to-all-start) | async-done | bytes 552992 | tf_op jit(solution)/shard_map/all_to_all | solution.py:201
  65.8 3.4 %reshape.198 = bf16[3,8,144,80]{3,2,1,0:T(8,128)(2,1)} reshape(bf16[3,8,11520]{2,1,0:T(8,128)(2,1)} %copy.22) | data formatting | bytes 1105920 | tf_op jit(solution)/shard_map/reshape | solution.py:201
  69.3 13.7 %shard_map.46 = f32[2,64,512]{2,1,0:T(8,128)S(1)} custom-call(s32[25,2]{1,0:T(8,128)S(1)} %copy.23.offsets_ref, bf16[256,2048]{1,0:T(8,128)(2,1)} %collective-permute-done.4.current_ref, bf16[288,2048]{1,0:T(8,128)(2,1)S(1)} %fusion.61.following_ref, bf16[512,512]{1,0:T(8,128)(2,1)S(1)} %fusion.96.permute_ref), custom_call_target="tpu_custom_call" | custom-call | tf_op jit(solution)/shard_map/pallas_call | solution.py:163
  82.9 2.5 %collective-permute-start.5 = (f32[2,8,512]{2,1,0:T(8,128)S(1)}, f32[2,8,512]{2,1,0:T(8,128)S(1)}, u32[]{:S(2)}, u32[]{:S(2)}) collective-permute-start(f32[2,8,512]{2,1,0:T(8,128)S(1)} %slice.381), channel_id=1, source_target_pairs={{0,1},{1,2},{2,3},{4,5},{5,6},{6,7},{8,9},{9,10},{10,11},{12,13},{... | collective-permute-start | bytes 98312 | tf_op jit(solution)/shard_map/ppermute | solution.py:30
  85.4 1.5 select_maximum_fusion.following_ref
  87.0 12.4 %shard_map.47 = f32[2,64,512]{2,1,0:T(8,128)S(1)} custom-call(s32[25,2]{1,0:T(8,128)S(1)} %copy.23.offsets_ref, bf16[256,2048]{1,0:T(8,128)(2,1)S(1)} %get-tuple-element.23.current_ref, bf16[288,2048]{1,0:T(8,128)(2,1)S(1)} %select_maximum_fusion.following_ref, bf16[512,512]{1,0:T(8,128)(2,1)S(1)} %fusion.96.permute_ref), custom_call_target="tpu_custom_call" | custom-call | tf_op jit(solution)/shard_map/pallas_call | solution.py:163
  99.4 1.3 collective-permute-start.7
  100.7 3.1 %collective-permute-done.7 = f32[2,8,512]{2,1,0:T(8,128)S(1)} collective-permute-done((f32[2,8,512]{2,1,0:T(8,128)S(1)}, f32[2,8,512]{2,1,0:T(8,128)S(1)}, u32[]{:S(2)}, u32[]{:S(2)}) %collective-permute-start.7) | collective-permute-done | bytes 32800 | tf_op jit(solution)/shard_map/ppermute | solution.py:32
  110.7 6.2 %all-to-all-start.1 = ((f32[2,8,11520]{2,0,1:T(2,128)}), f32[2,8,11520]{2,0,1:T(2,128)}, u32[]{:S(2)}, u32[]{:S(2)}) async-start(f32[2,8,11520]{2,0,1:T(2,128)} %constant_dynamic-update-slice_fusion.8), calls=%async_computation.1 | async-start | bytes 1474560 | tf_op jit(solution)/shard_map/all_to_all | solution.py:201
  117.7 1.0 slice.394
  118.7 17.6 %all-to-all-done.1 = f32[2,8,11520]{2,0,1:T(2,128)} async-done(((f32[2,8,11520]{2,0,1:T(2,128)}), f32[2,8,11520]{2,0,1:T(2,128)}, u32[]{:S(2)}, u32[]{:S(2)}) %all-to-all-start.1) | async-done | bytes 737312 | tf_op jit(solution)/shard_map/all_to_all | solution.py:201
  136.3 2.1 %copy.25 = f32[2,8,11520]{2,1,0:T(8,128)} copy(f32[2,8,11520]{2,0,1:T(2,128)} %all-to-all-done.1) | data formatting | bytes 1474560 | tf_op jit(solution)/shard_map/all_to_all | solution.py:201
  138.3 3.0 %reshape.199 = f32[2,8,144,80]{3,2,1,0:T(8,128)} reshape(f32[2,8,11520]{2,1,0:T(8,128)} %copy.25) | data formatting | bytes 1474560 | tf_op jit(solution)/shard_map/reshape | solution.py:201
  141.4 1.2 copy-done
  144.4 1.1 fusion.12
  145.8 1.1 fusion.19
  147.1 1.1 fusion.26
  148.4 1.1 fusion.33
  149.8 1.1 fusion.40
  151.1 1.1 fusion.47
  154.3 1.6 slice_add_fusion
  156.7 19.4 %all_to_all.15 = f32[2,8,8192]{2,0,1:T(2,128)S(1)} all-to-all(f32[2,8,8192]{2,0,1:T(2,128)S(1)} %copy.26), channel_id=1, replica_groups=mesh['sec'=8,'strip'=4] {'sec'}, dimensions={1} | all-to-all | bytes 1048576 | tf_op jit(solution)/shard_map/all_to_all | solution.py:270
  (89 shorter events, 25.3 us)
Async XLA Ops:
  0.8 10.2 %copy-start.4 = (s32[1,128,512]{2,1,0:T(8,128)S(1)}, s32[1,128,512]{2,1,0:T(8,128)}, u32[]{:S(2)}) copy-start(s32[1,128,512]{2,1,0:T(8,128)} %param.7) | copy-start | bytes 786436
  0.8 10.2 %collective-permute-start = (bf16[3,2048]{1,0:T(4,128)(2,1)S(1)}, bf16[3,2048]{1,0:T(4,128)(2,1)S(1)}, u32[]{:S(2)}, u32[]{:S(2)}) collective-permute-start(bf16[3,2048]{1,0:T(4,128)(2,1)S(1)} %get-tuple-element.22), channel_id=1, source_target_pairs={{1,0},{2,1},{3,2},{5,4},{6,5},{7,6},{9,8},{10,9},{11,10},{13,12},{... | collective-permute-start | bytes 36872 | tf_op jit(solution)/shard_map/ppermute | solution.py:19
  2.2 14.0 %copy-start.1 = (bf16[1,512,2048]{2,1,0:T(8,128)(2,1)S(1)}, bf16[1,512,2048]{2,1,0:T(8,128)(2,1)}, u32[]{:S(2)}) copy-start(bf16[1,512,2048]{2,1,0:T(8,128)(2,1)} %param.4) | copy-start | bytes 6291460
  5.2 64.1 %collective-permute-start.4 = (bf16[256,2048]{1,0:T(8,128)(2,1)}, bf16[256,2048]{1,0:T(8,128)(2,1)}, u32[]{:S(2)}, u32[]{:S(2)}) collective-permute-start(bf16[256,2048]{1,0:T(8,128)(2,1)} %get-tuple-element.24), channel_id=1, source_target_pairs={{0,4},{4,8},{8,12},{12,16},{16,20},{20,24},{24,28},{1,5},{5,9},{9,... | collective-permute-start | bytes 3145736 | tf_op jit(solution)/shard_map/ppermute | solution.py:19
  12.2 7.0 %collective-permute-start.1 = (bf16[3,8,512]{2,1,0:T(8,128)(2,1)S(1)}, bf16[3,8,512]{2,1,0:T(8,128)(2,1)S(1)}, u32[]{:S(2)}, u32[]{:S(2)}) collective-permute-start(bf16[3,8,512]{2,1,0:T(8,128)(2,1)S(1)} %get-tuple-element.52), channel_id=1, source_target_pairs={{0,1},{1,2},{2,3},{4,5},{5,6},{6,7},{8,9},{9,10},{10,11},{12,13},{... | collective-permute-start | bytes 73736 | tf_op jit(solution)/shard_map/ppermute | solution.py:30
  14.9 4.2 %collective-permute-start.2 = (bf16[3,8,512]{2,1,0:T(8,128)(2,1)S(1)}, bf16[3,8,512]{2,1,0:T(8,128)(2,1)S(1)}, u32[]{:S(2)}, u32[]{:S(2)}) collective-permute-start(bf16[3,8,512]{2,1,0:T(8,128)(2,1)S(1)} %get-tuple-element.53), channel_id=1, source_target_pairs={{1,0},{2,1},{3,2},{5,4},{6,5},{7,6},{9,8},{10,9},{11,10},{13,12},{... | collective-permute-start | bytes 73736 | tf_op jit(solution)/shard_map/ppermute | solution.py:32
  17.8 51.4 %collective-permute-start.3 = (bf16[259,2048]{1,0:T(8,128)(2,1)}, bf16[259,2048]{1,0:T(8,128)(2,1)}, u32[]{:S(2)}, u32[]{:S(2)}) collective-permute-start(bf16[259,2048]{1,0:T(8,128)(2,1)} %get-tuple-element.20), channel_id=1, source_target_pairs={{4,0},{8,4},{12,8},{16,12},{20,16},{24,20},{28,24},{5,1},{9,5},{13... | collective-permute-start | bytes 3182600 | tf_op jit(solution)/shard_map/ppermute | solution.py:19
  23.1 11.0 %copy-start.5 = (s32[25,2]{0,1:T(2,128)S(1)}, s32[25,2]{0,1:T(2,128)}, u32[]{:S(2)}) copy-start(s32[25,2]{0,1:T(2,128)} %param.5) | copy-start | bytes 604
  26.4 38.6 %all-to-all-start = ((bf16[3,8,11520]{2,0,1:T(4,128)(2,1)}), bf16[3,8,11520]{2,0,1:T(4,128)(2,1)S(1)}, u32[]{:S(2)}, u32[]{:S(2)}) async-start(bf16[3,8,11520]{2,0,1:T(4,128)(2,1)} %constant_dynamic-update-slice_fusion), calls=%async_computation | async-start | bytes 1474560 | tf_op jit(solution)/shard_map/all_to_all | solution.py:201
  33.4 52.0 %collective-permute-start.6 = (bf16[3,2048]{1,0:T(4,128)(2,1)S(1)}, bf16[3,2048]{1,0:T(4,128)(2,1)S(1)}, u32[]{:S(2)}, u32[]{:S(2)}) collective-permute-start(bf16[3,2048]{1,0:T(4,128)(2,1)S(1)} %get-tuple-element.21), channel_id=1, source_target_pairs={{4,1},{5,2},{6,3},{8,5},{9,6},{10,7},{12,9},{13,10},{14,11},{16,13... | collective-permute-start | bytes 36872 | tf_op jit(solution)/shard_map/ppermute | solution.py:211
  82.9 17.8 %collective-permute-start.5 = (f32[2,8,512]{2,1,0:T(8,128)S(1)}, f32[2,8,512]{2,1,0:T(8,128)S(1)}, u32[]{:S(2)}, u32[]{:S(2)}) collective-permute-start(f32[2,8,512]{2,1,0:T(8,128)S(1)} %slice.381), channel_id=1, source_target_pairs={{0,1},{1,2},{2,3},{4,5},{5,6},{6,7},{8,9},{9,10},{10,11},{12,13},{... | collective-permute-start | bytes 98312 | tf_op jit(solution)/shard_map/ppermute | solution.py:30
  99.4 4.4 %collective-permute-start.7 = (f32[2,8,512]{2,1,0:T(8,128)S(1)}, f32[2,8,512]{2,1,0:T(8,128)S(1)}, u32[]{:S(2)}, u32[]{:S(2)}) collective-permute-start(f32[2,8,512]{2,1,0:T(8,128)S(1)} %slice.382), channel_id=1, source_target_pairs={{1,0},{2,1},{3,2},{5,4},{6,5},{7,6},{9,8},{10,9},{11,10},{13,12},{... | collective-permute-start | bytes 98312 | tf_op jit(solution)/shard_map/ppermute | solution.py:32
  107.6 9.4 %copy-start.2 = (bf16[3,8,144,80]{3,2,1,0:T(8,128)(2,1)S(1)}, bf16[3,8,144,80]{3,2,1,0:T(8,128)(2,1)}, u32[]{:S(2)}) copy-start(bf16[3,8,144,80]{3,2,1,0:T(8,128)(2,1)} %reshape.198) | copy-start | bytes 1658884
  110.7 25.5 %all-to-all-start.1 = ((f32[2,8,11520]{2,0,1:T(2,128)}), f32[2,8,11520]{2,0,1:T(2,128)}, u32[]{:S(2)}, u32[]{:S(2)}) async-start(f32[2,8,11520]{2,0,1:T(2,128)} %constant_dynamic-update-slice_fusion.8), calls=%async_computation.1 | async-start | bytes 1474560 | tf_op jit(solution)/shard_map/all_to_all | solution.py:201
  141.3 1.3 copy-start
  141.3 1.6 slice-start
  153.2 1.0 copy-start.3

commit v17 on v15

--- a/solution.py
+++ b/solution.py
@@ -215,12 +215,7 @@
     flow_top = section_flow(pixels[:half], jnp.concatenate([corner, successor_top]), offsets) * keep_mask
     flow_bottom = section_flow(prior_bottom, jnp.concatenate([pixels[half - RAD :], below]), offsets)
     flow_field = jnp.concatenate([flow_top, flow_bottom], axis=1)
-    tiled = tiles_with_halo(flow_field, halo)
     node_half = flow_field.shape[1] // 2
-    following = jnp.concatenate([tiled[:, 1:], jnp.zeros_like(tiled[:, :1])], axis=1)
-    row_ids = jnp.arange(tiled.shape[2], dtype=jnp.int32)[:, None]
-    from_prior = (row_ids < halo) | ((row_ids >= halo + node_half) & (row_ids < halo + 2 * node_half))
-    flow_tiles = jnp.where(from_prior, following, tiled)
     tile_row = weights[0]
     tile_col = weights[1]
     tile_match = weights[2]
@@ -228,31 +223,39 @@
     weight_left = jnp.pad(tile_col, ((0, 0), (0, 0), (1, 0)))[:, :, :-1]
     match_prior = jnp.pad(tile_match, ((1, 0), (0, 0), (0, 0)))[:-1]
     diagonal = tile_row + weight_up + tile_col + weight_left + tile_match + match_prior
-    positions = jnp.zeros_like(flow_tiles)
-    for iteration in range(ITERS):
-        padded = jnp.pad(positions, ((0, 0), (0, 0), (1, 1), (1, 1)))
-        following = jnp.pad(positions, ((0, 0), (0, 1), (0, 0), (0, 0)))[:, 1:]
-        pull_term = tile_match * (following - positions - flow_tiles)
-        pull_prior = jnp.pad(pull_term, ((0, 0), (1, 0), (0, 0), (0, 0)))[:, :-1]
-        positions = advance(
-            positions,
-            padded[:, :, 2:, 1:-1],
-            padded[:, :, :-2, 1:-1],
-            padded[:, :, 1:-1, 2:],
-            padded[:, :, 1:-1, :-2],
-            tile_row,
-            weight_up,
-            tile_col,
-            weight_left,
-            pull_term,
-            pull_prior,
-            diagonal,
-        )
-    core = positions[:, :, halo:-halo, halo:-halo]
-    shape = core.shape
-    flat = core.reshape(shape[0], shape[1], shape[2] * shape[3])
-    returned = lax.all_to_all(flat, "sec", split_axis=1, concat_axis=1, tiled=True).reshape(shape)
-    return jnp.transpose(returned, (0, 2, 1, 3)).reshape(shape[0], 1, shape[2], shape[1] * shape[3])
+    results = []
+    for component in range(flow_field.shape[0]):
+        tiled = tiles_with_halo(flow_field[component : component + 1], halo)
+        following = jnp.concatenate([tiled[:, 1:], jnp.zeros_like(tiled[:, :1])], axis=1)
+        row_ids = jnp.arange(tiled.shape[2], dtype=jnp.int32)[:, None]
+        from_prior = (row_ids < halo) | ((row_ids >= halo + node_half) & (row_ids < halo + 2 * node_half))
+        flow_tiles = jnp.where(from_prior, following, tiled)
+        positions = jnp.zeros_like(flow_tiles)
+        for iteration in range(ITERS):
+            padded = jnp.pad(positions, ((0, 0), (0, 0), (1, 1), (1, 1)))
+            following = jnp.pad(positions, ((0, 0), (0, 1), (0, 0), (0, 0)))[:, 1:]
+            pull_term = tile_match * (following - positions - flow_tiles)
+            pull_prior = jnp.pad(pull_term, ((0, 0), (1, 0), (0, 0), (0, 0)))[:, :-1]
+            positions = advance(
+                positions,
+                padded[:, :, 2:, 1:-1],
+                padded[:, :, :-2, 1:-1],
+                padded[:, :, 1:-1, 2:],
+                padded[:, :, 1:-1, :-2],
+                tile_row,
+                weight_up,
+                tile_col,
+                weight_left,
+                pull_term,
+                pull_prior,
+                diagonal,
+            )
+        core = positions[:, :, halo:-halo, halo:-halo]
+        shape = core.shape
+        flat = core.reshape(shape[0], shape[1], shape[2] * shape[3])
+        returned = lax.all_to_all(flat, "sec", split_axis=1, concat_axis=1, tiled=True).reshape(shape)
+        results.append(jnp.transpose(returned, (0, 2, 1, 3)).reshape(shape[0], 1, shape[2], shape[1] * shape[3]))
+    return jnp.concatenate(results)
 
 
 def solution(mesh):

time: 178 us -> 194 us (1.090)
  blocking collectives: 19.4 us -> 0 us
  starting transfers between devices: 30.2 us -> 48.8 us
  waiting for transfers between devices: 49.8 us -> 59.8 us
  other arithmetic: 16.8 us -> 21.8 us
  local copies, waits for them, and re-layouts: 35.4 us -> 37.4 us
    all_to_all x1 -> x0, blocking collectives: 19.4 us -> none  [shards(): lax.all_to_all(flat, 'sec', split_axis=1, concat_axis=1, tiled=True)]
    all_to_all x0 -> x2, waiting for transfers between devices: none -> 15.6 us  [shards(): lax.all_to_all(flat, 'sec', split_axis=1, concat_axis=1, tiled=True)]
    all_to_all x0 -> x2, starting transfers between devices: none -> 7.22 us  [shards(): lax.all_to_all(flat, 'sec', split_axis=1, concat_axis=1, tiled=True)]
    all_to_all x2 -> x3, starting transfers between devices: 13.2 us -> 18.9 us  [tiles_with_halo(): lax.all_to_all(flat, 'sec', split_axis=1, concat_axis=1, tiled=True)]
    all_to_all x0 -> x4, other arithmetic: none -> 4.6 us  [the longest x2 3.37 us: tiles_with_halo(): lax.all_to_all(flat, 'sec', split_axis=1, concat_axis=1, tiled=True)]
    ppermute x2 -> x3, starting transfers between devices: 5.21 us -> 9.63 us  [extended(): lax.ppermute(tail, axis, [(i, (i + 1) % count) for i in range(ends)])]
    all_to_all x2 -> x3, waiting for transfers between devices: 46.7 us -> 42.6 us  [tiles_with_halo(): lax.all_to_all(flat, 'sec', split_axis=1, concat_axis=1, tiled=True)]
    unnamed x27 -> x30, local copies, waits for them, and re-layouts: 11.4 us -> 13.5 us
  transfers between devices with their start and end apart: 10 -> 15, of which waited for: 3 -> 6; matrix products, arithmetic and copies ran while one was open for 13% -> 17% of each run, Pallas kernels for 14% -> 13%
where the time goes in v17:
time: 194 us; the launch traced here: 193 us
  waiting for transfers between devices  59.8 us (31%)
  starting transfers between devices  48.8 us (25%)
  local copies, waits for them, and re-layouts  37.4 us (19%)
  Pallas kernels  24.7 us (13%)
  other arithmetic  21.8 us (11%)
    all_to_all x3, waiting for transfers between devices, tiles_with_halo(): lax.all_to_all(flat, 'sec', split_axis=1, concat_axis=1, tiled=True)  42.6 us
    pallas_call x2, Pallas kernels, section_flow(): pl.pallas_call(flow_kernel, grid_spec=grid_spec, out_shape=jax.ShapeDtype...  24.7 us
    all_to_all x3, starting transfers between devices, tiles_with_halo(): lax.all_to_all(flat, 'sec', split_axis=1, concat_axis=1, tiled=True)  18.9 us
    all_to_all x2, waiting for transfers between devices, shards(): lax.all_to_all(flat, 'sec', split_axis=1, concat_axis=1, tiled=True)  15.6 us
    unnamed x30, local copies, waits for them, and re-layouts  13.5 us
    ppermute x3, starting transfers between devices, extended(): lax.ppermute(tail, axis, [(i, (i + 1) % count) for i in range(ends)])  9.63 us
    add x7, other arithmetic, advance(): return positions + relax_rate * force / (1.0 + diagonal)  8.81 us
    ppermute x3, starting transfers between devices, shifted_2(): return lax.ppermute(shard, axis, pairs)  8.55 us
  transfers between devices with their start and end apart: 15, of which 6 were waited for; matrix products, arithmetic and copies ran while one was open for 17% of the time, Pallas kernels for 13%

profile of v17, /device:TPU:0, one launch (start us, length us, event | category | flops | bytes accessed | tf_op | source)
XLA Modules:
  0.0 193.1 jit_solution(16899127477725106676)
XLA Ops:
  0.8 1.4 collective-permute-start
  2.2 2.9 %slice_bitcast_fusion.2 = (bf16[256,2048]{1,0:T(8,128)(2,1)S(1)}, bf16[256,2048]{1,0:T(8,128)(2,1)}) fusion(bf16[1,512,2048]{2,1,0:T(8,128)(2,1)} %param.4), kind=kLoop, calls=%fused_computation.13 | loop fusion | bytes 4194304 | tf_op jit(solution)/shard_map/slice | solution.py:215
  5.1 5.8 %collective-permute-start.4 = (bf16[256,2048]{1,0:T(8,128)(2,1)}, bf16[256,2048]{1,0:T(8,128)(2,1)}, u32[]{:S(2)}, u32[]{:S(2)}) collective-permute-start(bf16[256,2048]{1,0:T(8,128)(2,1)} %get-tuple-element.47), channel_id=1, source_target_pairs={{0,4},{4,8},{8,12},{12,16},{16,20},{20,24},{24,28},{1,5},{5,9},{9,... | collective-permute-start | bytes 3145736 | tf_op jit(solution)/shard_map/ppermute | solution.py:19
  12.1 2.8 %collective-permute-start.1 = (bf16[3,8,512]{2,1,0:T(8,128)(2,1)S(1)}, bf16[3,8,512]{2,1,0:T(8,128)(2,1)S(1)}, u32[]{:S(2)}, u32[]{:S(2)}) collective-permute-start(bf16[3,8,512]{2,1,0:T(8,128)(2,1)S(1)} %get-tuple-element.76), channel_id=1, source_target_pairs={{0,1},{1,2},{2,3},{4,5},{5,6},{6,7},{8,9},{9,10},{10,11},{12,13},{... | collective-permute-start | bytes 73736 | tf_op jit(solution)/shard_map/ppermute | solution.py:30
  14.9 1.3 collective-permute-start.2
  16.2 1.6 slice_bitcast_fusion
  26.4 7.0 %all-to-all-start = ((bf16[3,8,11520]{2,0,1:T(4,128)(2,1)}), bf16[3,8,11520]{2,0,1:T(4,128)(2,1)}, u32[]{:S(2)}, u32[]{:S(2)}) async-start(bf16[3,8,11520]{2,0,1:T(4,128)(2,1)} %constant_dynamic-update-slice_fusion), calls=%async_computation | async-start | bytes 1474560 | tf_op jit(solution)/shard_map/all_to_all | solution.py:185
  34.3 1.5 fusion.3.following_ref
  35.8 29.1 %all-to-all-done = bf16[3,8,11520]{2,0,1:T(4,128)(2,1)} async-done(((bf16[3,8,11520]{2,0,1:T(4,128)(2,1)}), bf16[3,8,11520]{2,0,1:T(4,128)(2,1)}, u32[]{:S(2)}, u32[]{:S(2)}) %all-to-all-start) | async-done | bytes 552992 | tf_op jit(solution)/shard_map/all_to_all | solution.py:185
  64.9 2.0 %copy.21 = bf16[3,8,11520]{2,1,0:T(8,128)(2,1)} copy(bf16[3,8,11520]{2,0,1:T(4,128)(2,1)} %all-to-all-done) | data formatting | bytes 1105920 | tf_op jit(solution)/shard_map/all_to_all | solution.py:185
  66.9 3.4 %reshape.224 = bf16[3,8,144,80]{3,2,1,0:T(8,128)(2,1)} reshape(bf16[3,8,11520]{2,1,0:T(8,128)(2,1)} %copy.21) | data formatting | bytes 1105920 | tf_op jit(solution)/shard_map/reshape | solution.py:185
  70.4 12.9 %shard_map.46 = f32[2,64,512]{2,1,0:T(8,128)S(1)} custom-call(s32[25,2]{1,0:T(8,128)S(1)} %copy.22.offsets_ref, bf16[256,2048]{1,0:T(8,128)(2,1)} %collective-permute-done.4.current_ref, bf16[288,2048]{1,0:T(8,128)(2,1)S(1)} %fusion.3.following_ref, bf16[512,512]{1,0:T(8,128)(2,1)S(1)} %fusion.4.permute_ref), custom_call_target="tpu_custom_call" | custom-call | tf_op jit(solution)/shard_map/pallas_call | solution.py:147
  83.3 2.6 %collective-permute-start.5 = (f32[1,8,512]{2,1,0:T(8,128)S(1)}, f32[1,8,512]{2,1,0:T(8,128)S(1)}, u32[]{:S(2)}, u32[]{:S(2)}) collective-permute-start(f32[1,8,512]{2,1,0:T(8,128)S(1)} %get-tuple-element.95), channel_id=1, source_target_pairs={{0,1},{1,2},{2,3},{4,5},{5,6},{6,7},{8,9},{9,10},{10,11},{12,13},{... | collective-permute-start | bytes 49160 | tf_op jit(solution)/shard_map/ppermute | solution.py:30
  85.9 1.5 select_maximum_fusion.following_ref
  87.5 11.7 %shard_map.47 = f32[2,64,512]{2,1,0:T(8,128)S(1)} custom-call(s32[25,2]{1,0:T(8,128)S(1)} %copy.22.offsets_ref, bf16[256,2048]{1,0:T(8,128)(2,1)S(1)} %get-tuple-element.46.current_ref, bf16[288,2048]{1,0:T(8,128)(2,1)S(1)} %select_maximum_fusion.following_ref, bf16[512,512]{1,0:T(8,128)(2,1)S(1)} %fusion.4.permute_ref), custom_call_target="tpu_custom_call" | custom-call | tf_op jit(solution)/shard_map/pallas_call | solution.py:147
  99.2 1.3 collective-permute-start.7
  100.6 4.3 %collective-permute-start.8 = (f32[1,8,512]{2,1,0:T(8,128)S(1)}, f32[1,8,512]{2,1,0:T(8,128)S(1)}, u32[]{:S(2)}, u32[]{:S(2)}) collective-permute-start(f32[1,8,512]{2,1,0:T(8,128)S(1)} %get-tuple-element.94), channel_id=1, source_target_pairs={{0,1},{1,2},{2,3},{4,5},{5,6},{6,7},{8,9},{9,10},{10,11},{12,13},{... | collective-permute-start | bytes 49160 | tf_op jit(solution)/shard_map/ppermute | solution.py:30
  107.6 1.6 collective-permute-done.9
  115.5 6.2 %all-to-all-start.3 = ((f32[1,8,11520]{2,0,1:T(1,128)}), f32[1,8,11520]{2,0,1:T(1,128)S(1)}, u32[]{:S(2)}, u32[]{:S(2)}) async-start(f32[1,8,11520]{2,0,1:T(1,128)} %constant_dynamic-update-slice_fusion.16), calls=%async_computation.3 | async-start | bytes 737280 | tf_op jit(solution)/shard_map/all_to_all | solution.py:185
  126.7 5.3 %all-to-all-done.3 = f32[1,8,11520]{2,0,1:T(1,128)S(1)} async-done(((f32[1,8,11520]{2,0,1:T(1,128)}), f32[1,8,11520]{2,0,1:T(1,128)S(1)}, u32[]{:S(2)}, u32[]{:S(2)}) %all-to-all-start.3) | async-done | bytes 368672 | tf_op jit(solution)/shard_map/all_to_all | solution.py:185
  132.0 5.7 %all-to-all-start.1 = ((f32[1,8,11520]{2,0,1:T(1,128)}), f32[1,8,11520]{2,0,1:T(1,128)S(1)}, u32[]{:S(2)}, u32[]{:S(2)}) async-start(f32[1,8,11520]{2,0,1:T(1,128)} %constant_dynamic-update-slice_fusion.8), calls=%async_computation.1 | async-start | bytes 737280 | tf_op jit(solution)/shard_map/all_to_all | solution.py:185
  137.9 1.7 reduce.2
  139.6 1.4 reshape.229
  141.0 8.2 %all-to-all-done.1 = f32[1,8,11520]{2,0,1:T(1,128)S(1)} async-done(((f32[1,8,11520]{2,0,1:T(1,128)}), f32[1,8,11520]{2,0,1:T(1,128)S(1)}, u32[]{:S(2)}, u32[]{:S(2)}) %all-to-all-start.1) | async-done | bytes 368672 | tf_op jit(solution)/shard_map/all_to_all | solution.py:185
  149.1 1.7 reduce
  150.8 1.4 reshape.225
  160.8 1.4 fusion.56
  163.6 1.5 slice_add_fusion.3
  166.2 3.6 %all-to-all-start.2 = ((f32[1,8,8192]{2,0,1:T(1,128)}), f32[1,8,8192]{2,0,1:T(1,128)S(1)}, u32[]{:S(2)}, u32[]{:S(2)}) async-start(f32[1,8,8192]{2,0,1:T(1,128)} %reshape.233), calls=%async_computation.2 | async-start | bytes 524288 | tf_op jit(solution)/shard_map/all_to_all | solution.py:256
  170.8 8.0 %all-to-all-done.2 = f32[1,8,8192]{2,0,1:T(1,128)S(1)} async-done(((f32[1,8,8192]{2,0,1:T(1,128)}), f32[1,8,8192]{2,0,1:T(1,128)S(1)}, u32[]{:S(2)}, u32[]{:S(2)}) %all-to-all-start.2) | async-done | bytes 262176 | tf_op jit(solution)/shard_map/all_to_all | solution.py:256
  178.9 3.6 %all-to-all-start.4 = ((f32[1,8,8192]{2,0,1:T(1,128)}), f32[1,8,8192]{2,0,1:T(1,128)S(1)}, u32[]{:S(2)}, u32[]{:S(2)}) async-start(f32[1,8,8192]{2,0,1:T(1,128)} %reshape.234), calls=%async_computation.4 | async-start | bytes 524288 | tf_op jit(solution)/shard_map/all_to_all | solution.py:256
  183.5 7.5 %all-to-all-done.4 = f32[1,8,8192]{2,0,1:T(1,128)S(1)} async-done(((f32[1,8,8192]{2,0,1:T(1,128)}), f32[1,8,8192]{2,0,1:T(1,128)S(1)}, u32[]{:S(2)}, u32[]{:S(2)}) %all-to-all-start.4) | async-done | bytes 262176 | tf_op jit(solution)/shard_map/all_to_all | solution.py:256
  (119 shorter events, 40.2 us)
Async XLA Ops:
  0.8 10.2 %copy-start.2 = (s32[1,128,512]{2,1,0:T(8,128)S(1)}, s32[1,128,512]{2,1,0:T(8,128)}, u32[]{:S(2)}) copy-start(s32[1,128,512]{2,1,0:T(8,128)} %param.7) | copy-start | bytes 786436
  0.8 10.2 %collective-permute-start = (bf16[3,2048]{1,0:T(4,128)(2,1)S(1)}, bf16[3,2048]{1,0:T(4,128)(2,1)S(1)}, u32[]{:S(2)}, u32[]{:S(2)}) collective-permute-start(bf16[3,2048]{1,0:T(4,128)(2,1)S(1)} %get-tuple-element.45), channel_id=1, source_target_pairs={{1,0},{2,1},{3,2},{5,4},{6,5},{7,6},{9,8},{10,9},{11,10},{13,12},{... | collective-permute-start | bytes 36872 | tf_op jit(solution)/shard_map/ppermute | solution.py:19
  2.2 14.0 %copy-start = (bf16[1,512,2048]{2,1,0:T(8,128)(2,1)S(1)}, bf16[1,512,2048]{2,1,0:T(8,128)(2,1)}, u32[]{:S(2)}) copy-start(bf16[1,512,2048]{2,1,0:T(8,128)(2,1)} %param.4) | copy-start | bytes 6291460
  5.1 65.2 %collective-permute-start.4 = (bf16[256,2048]{1,0:T(8,128)(2,1)}, bf16[256,2048]{1,0:T(8,128)(2,1)}, u32[]{:S(2)}, u32[]{:S(2)}) collective-permute-start(bf16[256,2048]{1,0:T(8,128)(2,1)} %get-tuple-element.47), channel_id=1, source_target_pairs={{0,4},{4,8},{8,12},{12,16},{16,20},{20,24},{24,28},{1,5},{5,9},{9,... | collective-permute-start | bytes 3145736 | tf_op jit(solution)/shard_map/ppermute | solution.py:19
  12.1 7.0 %collective-permute-start.1 = (bf16[3,8,512]{2,1,0:T(8,128)(2,1)S(1)}, bf16[3,8,512]{2,1,0:T(8,128)(2,1)S(1)}, u32[]{:S(2)}, u32[]{:S(2)}) collective-permute-start(bf16[3,8,512]{2,1,0:T(8,128)(2,1)S(1)} %get-tuple-element.76), channel_id=1, source_target_pairs={{0,1},{1,2},{2,3},{4,5},{5,6},{6,7},{8,9},{9,10},{10,11},{12,13},{... | collective-permute-start | bytes 73736 | tf_op jit(solution)/shard_map/ppermute | solution.py:30
  14.9 4.2 %collective-permute-start.2 = (bf16[3,8,512]{2,1,0:T(8,128)(2,1)S(1)}, bf16[3,8,512]{2,1,0:T(8,128)(2,1)S(1)}, u32[]{:S(2)}, u32[]{:S(2)}) collective-permute-start(bf16[3,8,512]{2,1,0:T(8,128)(2,1)S(1)} %get-tuple-element.77), channel_id=1, source_target_pairs={{1,0},{2,1},{3,2},{5,4},{6,5},{7,6},{9,8},{10,9},{11,10},{13,12},{... | collective-permute-start | bytes 73736 | tf_op jit(solution)/shard_map/ppermute | solution.py:32
  17.8 52.5 %collective-permute-start.3 = (bf16[259,2048]{1,0:T(8,128)(2,1)}, bf16[259,2048]{1,0:T(8,128)(2,1)}, u32[]{:S(2)}, u32[]{:S(2)}) collective-permute-start(bf16[259,2048]{1,0:T(8,128)(2,1)} %get-tuple-element.43), channel_id=1, source_target_pairs={{4,0},{8,4},{12,8},{16,12},{20,16},{24,20},{28,24},{5,1},{9,5},{13... | collective-permute-start | bytes 3182600 | tf_op jit(solution)/shard_map/ppermute | solution.py:19
  20.5 13.6 %copy-start.3 = (s32[25,2]{0,1:T(2,128)S(1)}, s32[25,2]{0,1:T(2,128)}, u32[]{:S(2)}) copy-start(s32[25,2]{0,1:T(2,128)} %param.5) | copy-start | bytes 604
  26.4 38.5 %all-to-all-start = ((bf16[3,8,11520]{2,0,1:T(4,128)(2,1)}), bf16[3,8,11520]{2,0,1:T(4,128)(2,1)}, u32[]{:S(2)}, u32[]{:S(2)}) async-start(bf16[3,8,11520]{2,0,1:T(4,128)(2,1)} %constant_dynamic-update-slice_fusion), calls=%async_computation | async-start | bytes 1474560 | tf_op jit(solution)/shard_map/all_to_all | solution.py:185
  33.4 52.5 %collective-permute-start.6 = (bf16[3,2048]{1,0:T(4,128)(2,1)S(1)}, bf16[3,2048]{1,0:T(4,128)(2,1)S(1)}, u32[]{:S(2)}, u32[]{:S(2)}) collective-permute-start(bf16[3,2048]{1,0:T(4,128)(2,1)S(1)} %get-tuple-element.44), channel_id=1, source_target_pairs={{4,1},{5,2},{6,3},{8,5},{9,6},{10,7},{12,9},{13,10},{14,11},{16,13... | collective-permute-start | bytes 36872 | tf_op jit(solution)/shard_map/ppermute | solution.py:195
  83.3 22.8 %collective-permute-start.5 = (f32[1,8,512]{2,1,0:T(8,128)S(1)}, f32[1,8,512]{2,1,0:T(8,128)S(1)}, u32[]{:S(2)}, u32[]{:S(2)}) collective-permute-start(f32[1,8,512]{2,1,0:T(8,128)S(1)} %get-tuple-element.95), channel_id=1, source_target_pairs={{0,1},{1,2},{2,3},{4,5},{5,6},{6,7},{8,9},{9,10},{10,11},{12,13},{... | collective-permute-start | bytes 49160 | tf_op jit(solution)/shard_map/ppermute | solution.py:30
  99.2 6.9 %collective-permute-start.7 = (f32[1,8,512]{2,1,0:T(8,128)S(1)}, f32[1,8,512]{2,1,0:T(8,128)S(1)}, u32[]{:S(2)}, u32[]{:S(2)}) collective-permute-start(f32[1,8,512]{2,1,0:T(8,128)S(1)} %get-tuple-element.97), channel_id=1, source_target_pairs={{1,0},{2,1},{3,2},{5,4},{6,5},{7,6},{9,8},{10,9},{11,10},{13,12},{... | collective-permute-start | bytes 49160 | tf_op jit(solution)/shard_map/ppermute | solution.py:32
  100.6 7.0 %collective-permute-start.8 = (f32[1,8,512]{2,1,0:T(8,128)S(1)}, f32[1,8,512]{2,1,0:T(8,128)S(1)}, u32[]{:S(2)}, u32[]{:S(2)}) collective-permute-start(f32[1,8,512]{2,1,0:T(8,128)S(1)} %get-tuple-element.94), channel_id=1, source_target_pairs={{0,1},{1,2},{2,3},{4,5},{5,6},{6,7},{8,9},{9,10},{10,11},{12,13},{... | collective-permute-start | bytes 49160 | tf_op jit(solution)/shard_map/ppermute | solution.py:30
  104.9 4.3 %collective-permute-start.9 = (f32[1,8,512]{2,1,0:T(8,128)S(1)}, f32[1,8,512]{2,1,0:T(8,128)S(1)}, u32[]{:S(2)}, u32[]{:S(2)}) collective-permute-start(f32[1,8,512]{2,1,0:T(8,128)S(1)} %get-tuple-element.96), channel_id=1, source_target_pairs={{1,0},{2,1},{3,2},{5,4},{6,5},{7,6},{9,8},{10,9},{11,10},{13,12},{... | collective-permute-start | bytes 49160 | tf_op jit(solution)/shard_map/ppermute | solution.py:32
  109.8 27.9 %copy-start.1 = (bf16[3,8,144,80]{3,2,1,0:T(8,128)(2,1)S(1)}, bf16[3,8,144,80]{3,2,1,0:T(8,128)(2,1)}, u32[]{:S(2)}) copy-start(bf16[3,8,144,80]{3,2,1,0:T(8,128)(2,1)} %reshape.224) | copy-start | bytes 1658884
  115.5 16.5 %all-to-all-start.3 = ((f32[1,8,11520]{2,0,1:T(1,128)}), f32[1,8,11520]{2,0,1:T(1,128)S(1)}, u32[]{:S(2)}, u32[]{:S(2)}) async-start(f32[1,8,11520]{2,0,1:T(1,128)} %constant_dynamic-update-slice_fusion.16), calls=%async_computation.3 | async-start | bytes 737280 | tf_op jit(solution)/shard_map/all_to_all | solution.py:185
  132.0 17.1 %all-to-all-start.1 = ((f32[1,8,11520]{2,0,1:T(1,128)}), f32[1,8,11520]{2,0,1:T(1,128)S(1)}, u32[]{:S(2)}, u32[]{:S(2)}) async-start(f32[1,8,11520]{2,0,1:T(1,128)} %constant_dynamic-update-slice_fusion.8), calls=%async_computation.1 | async-start | bytes 737280 | tf_op jit(solution)/shard_map/all_to_all | solution.py:185
  166.2 12.7 %all-to-all-start.2 = ((f32[1,8,8192]{2,0,1:T(1,128)}), f32[1,8,8192]{2,0,1:T(1,128)S(1)}, u32[]{:S(2)}, u32[]{:S(2)}) async-start(f32[1,8,8192]{2,0,1:T(1,128)} %reshape.233), calls=%async_computation.2 | async-start | bytes 524288 | tf_op jit(solution)/shard_map/all_to_all | solution.py:256
  178.9 12.2 %all-to-all-start.4 = ((f32[1,8,8192]{2,0,1:T(1,128)}), f32[1,8,8192]{2,0,1:T(1,128)S(1)}, u32[]{:S(2)}, u32[]{:S(2)}) async-start(f32[1,8,8192]{2,0,1:T(1,128)} %reshape.234), calls=%async_computation.4 | async-start | bytes 524288 | tf_op jit(solution)/shard_map/all_to_all | solution.py:256

commit v18 on v15

--- a/solution.py
+++ b/solution.py
@@ -209,9 +209,16 @@
     col_weight = 0.25 * springs[1, 0].astype(jnp.float32) * col_keep[None, :]
     halo = ITERS
     weights = jnp.stack([row_weight, col_weight, match_weight]).astype(jnp.bfloat16)
-    weights = tiles_with_halo(weights, halo)
-    weights, successor_top, prior_bottom = lax.optimization_barrier((weights, successor_top, prior_bottom))
-    weights = weights.astype(jnp.float32)
+    count = lax.axis_size("sec")
+    weights = extended(weights, (("strip", 1),), halo)
+    width = weights.shape[2] // count
+    columns = jnp.pad(weights, ((0, 0), (0, 0), (halo, halo)))
+    windows = jnp.stack([columns[:, :, j * width : (j + 1) * width + 2 * halo] for j in range(count)], axis=1)
+    shape = windows.shape
+    flat = windows.reshape(shape[0], shape[1], shape[2] * shape[3])
+    flat = lax.all_to_all(flat, "sec", split_axis=1, concat_axis=1, tiled=True)
+    flat, successor_top, prior_bottom = lax.optimization_barrier((flat, successor_top, prior_bottom))
+    weights = flat.reshape(shape).astype(jnp.float32)
     flow_top = section_flow(pixels[:half], jnp.concatenate([corner, successor_top]), offsets) * keep_mask
     flow_bottom = section_flow(prior_bottom, jnp.concatenate([pixels[half - RAD :], below]), offsets)
     flow_field = jnp.concatenate([flow_top, flow_bottom], axis=1)

time: 178 us -> 173 us (0.972)
  waiting for transfers between devices: 49.8 us -> 45.7 us
    all_to_all x2 -> x1, waiting for transfers between devices: 46.7 us -> 13.5 us  [tiles_with_halo(): lax.all_to_all(flat, 'sec', split_axis=1, concat_axis=1, tiled=True)]
    all_to_all x0 -> x1, waiting for transfers between devices: none -> 29.1 us  [shards(): flat = lax.all_to_all(flat, 'sec', split_axis=1, concat_axis=1, tiled=True)]
    all_to_all x0 -> x1, starting transfers between devices: none -> 7.03 us  [shards(): flat = lax.all_to_all(flat, 'sec', split_axis=1, concat_axis=1, tiled=True)]
    all_to_all x2 -> x1, starting transfers between devices: 13.2 us -> 6.23 us  [tiles_with_halo(): lax.all_to_all(flat, 'sec', split_axis=1, concat_axis=1, tiled=True)]
    reshape x2 -> x1, local copies, waits for them, and re-layouts: 6.46 us -> 3.04 us  [tiles_with_halo(): lax.all_to_all(flat, 'sec', split_axis=1, concat_axis=1, tiled=True)]
    slice x0 -> x2, local copies, waits for them, and re-layouts: none -> 3.17 us  [the longest x1 2.86 us: shards(): tile_row = weights[0]]
    another operation x0 -> x9, local copies, waits for them, and re-layouts: none -> 2.19 us  [shards(): jnp.stack([columns[:, :, j * width:(j + 1) * width + 2 * halo] for j in r...]
    another operation x18 -> x9, local copies, waits for them, and re-layouts: 4.22 us -> 2.03 us  [tiles_with_halo(): jnp.stack([columns[:, :, j * width:(j + 1) * width + 2 * halo] for j in r...]
where the time goes in v18:
time: 173 us; the launch traced here: 172 us
  waiting for transfers between devices  45.7 us (26%)
  local copies, waits for them, and re-layouts  35.2 us (20%)
  starting transfers between devices  30.2 us (17%)
  Pallas kernels  24.7 us (14%)
  blocking collectives  19.4 us (11%)
  other arithmetic  16.8 us (10%)
    all_to_all x1, waiting for transfers between devices, shards(): flat = lax.all_to_all(flat, 'sec', split_axis=1, concat_axis=1, tiled=True)  29.1 us
    pallas_call x2, Pallas kernels, section_flow(): pl.pallas_call(flow_kernel, grid_spec=grid_spec, out_shape=jax.ShapeDtype...  24.7 us
    all_to_all x1, blocking collectives, shards(): lax.all_to_all(flat, 'sec', split_axis=1, concat_axis=1, tiled=True)  19.4 us
    all_to_all x1, waiting for transfers between devices, tiles_with_halo(): lax.all_to_all(flat, 'sec', split_axis=1, concat_axis=1, tiled=True)  13.5 us
    unnamed x25, local copies, waits for them, and re-layouts  11.5 us
    ppermute x3, starting transfers between devices, shifted_2(): return lax.ppermute(shard, axis, pairs)  8.53 us
    add x7, other arithmetic, advance(): return positions + relax_rate * force / (1.0 + diagonal)  8.23 us
    all_to_all x1, starting transfers between devices, shards(): flat = lax.all_to_all(flat, 'sec', split_axis=1, concat_axis=1, tiled=True)  7.03 us
  transfers between devices with their start and end apart: 10, of which 3 were waited for; matrix products, arithmetic and copies ran while one was open for 13% of the time, Pallas kernels for 14%

profile of v18, /device:TPU:0, one launch (start us, length us, event | category | flops | bytes accessed | tf_op | source)
XLA Modules:
  0.0 172.3 jit_solution(13468253384509484624)
XLA Ops:
  0.8 1.4 collective-permute-start
  2.2 2.9 %slice_bitcast_fusion.2 = (bf16[256,2048]{1,0:T(8,128)(2,1)S(1)}, bf16[256,2048]{1,0:T(8,128)(2,1)}) fusion(bf16[1,512,2048]{2,1,0:T(8,128)(2,1)} %param.4), kind=kLoop, calls=%fused_computation.141 | loop fusion | bytes 4194304 | tf_op jit(solution)/shard_map/slice | solution.py:222
  5.1 5.8 %collective-permute-start.4 = (bf16[256,2048]{1,0:T(8,128)(2,1)}, bf16[256,2048]{1,0:T(8,128)(2,1)}, u32[]{:S(2)}, u32[]{:S(2)}) collective-permute-start(bf16[256,2048]{1,0:T(8,128)(2,1)} %get-tuple-element.27), channel_id=1, source_target_pairs={{0,4},{4,8},{8,12},{12,16},{16,20},{20,24},{24,28},{1,5},{5,9},{9,... | collective-permute-start | bytes 3145736 | tf_op jit(solution)/shard_map/ppermute | solution.py:19
  11.0 1.1 fusion.100
  12.1 2.8 %collective-permute-start.1 = (bf16[3,8,512]{2,1,0:T(8,128)(2,1)S(1)}, bf16[3,8,512]{2,1,0:T(8,128)(2,1)S(1)}, u32[]{:S(2)}, u32[]{:S(2)}) collective-permute-start(bf16[3,8,512]{2,1,0:T(8,128)(2,1)S(1)} %get-tuple-element.52), channel_id=1, source_target_pairs={{0,1},{1,2},{2,3},{4,5},{5,6},{6,7},{8,9},{9,10},{10,11},{12,13},{... | collective-permute-start | bytes 73736 | tf_op jit(solution)/shard_map/ppermute | solution.py:30
  14.9 1.3 collective-permute-start.2
  16.2 1.6 slice_bitcast_fusion
  17.8 1.3 collective-permute-start.3
  26.4 7.0 %all-to-all-start = ((bf16[3,8,11520]{2,0,1:T(4,128)(2,1)}), bf16[3,8,11520]{2,0,1:T(4,128)(2,1)S(1)}, u32[]{:S(2)}, u32[]{:S(2)}) async-start(bf16[3,8,11520]{2,0,1:T(4,128)(2,1)} %constant_dynamic-update-slice_fusion), calls=%async_computation | async-start | bytes 1474560 | tf_op jit(solution)/shard_map/all_to_all | solution.py:219
  34.4 1.5 fusion.61.following_ref
  35.9 29.1 %all-to-all-done = bf16[3,8,11520]{2,0,1:T(4,128)(2,1)S(1)} async-done(((bf16[3,8,11520]{2,0,1:T(4,128)(2,1)}), bf16[3,8,11520]{2,0,1:T(4,128)(2,1)S(1)}, u32[]{:S(2)}, u32[]{:S(2)}) %all-to-all-start) | async-done | bytes 552992 | tf_op jit(solution)/shard_map/all_to_all | solution.py:219
  64.9 12.9 %shard_map.46 = f32[2,64,512]{2,1,0:T(8,128)S(1)} custom-call(s32[25,2]{1,0:T(8,128)S(1)} %copy.12.offsets_ref, bf16[256,2048]{1,0:T(8,128)(2,1)} %collective-permute-done.4.current_ref, bf16[288,2048]{1,0:T(8,128)(2,1)S(1)} %fusion.61.following_ref, bf16[512,512]{1,0:T(8,128)(2,1)S(1)} %fusion.96.permute_ref), custom_call_target="tpu_custom_call" | custom-call | tf_op jit(solution)/shard_map/pallas_call | solution.py:147
  77.9 2.5 %collective-permute-start.5 = (f32[2,8,512]{2,1,0:T(8,128)S(1)}, f32[2,8,512]{2,1,0:T(8,128)S(1)}, u32[]{:S(2)}, u32[]{:S(2)}) collective-permute-start(f32[2,8,512]{2,1,0:T(8,128)S(1)} %slice.384), channel_id=1, source_target_pairs={{0,1},{1,2},{2,3},{4,5},{5,6},{6,7},{8,9},{9,10},{10,11},{12,13},{... | collective-permute-start | bytes 98312 | tf_op jit(solution)/shard_map/ppermute | solution.py:30
  80.4 1.5 select_maximum_fusion.following_ref
  81.9 11.7 %shard_map.47 = f32[2,64,512]{2,1,0:T(8,128)S(1)} custom-call(s32[25,2]{1,0:T(8,128)S(1)} %copy.12.offsets_ref, bf16[256,2048]{1,0:T(8,128)(2,1)S(1)} %get-tuple-element.26.current_ref, bf16[288,2048]{1,0:T(8,128)(2,1)S(1)} %select_maximum_fusion.following_ref, bf16[512,512]{1,0:T(8,128)(2,1)S(1)} %fusion.96.permute_ref), custom_call_target="tpu_custom_call" | custom-call | tf_op jit(solution)/shard_map/pallas_call | solution.py:147
  93.7 1.3 collective-permute-start.7
  95.0 3.1 %collective-permute-done.7 = f32[2,8,512]{2,1,0:T(8,128)S(1)} collective-permute-done((f32[2,8,512]{2,1,0:T(8,128)S(1)}, f32[2,8,512]{2,1,0:T(8,128)S(1)}, u32[]{:S(2)}, u32[]{:S(2)}) %collective-permute-start.7) | collective-permute-done | bytes 32800 | tf_op jit(solution)/shard_map/ppermute | solution.py:32
  105.0 6.2 %all-to-all-start.1 = ((f32[2,8,11520]{2,0,1:T(2,128)}), f32[2,8,11520]{2,0,1:T(2,128)}, u32[]{:S(2)}, u32[]{:S(2)}) async-start(f32[2,8,11520]{2,0,1:T(2,128)} %constant_dynamic-update-slice_fusion.8), calls=%async_computation.1 | async-start | bytes 1474560 | tf_op jit(solution)/shard_map/all_to_all | solution.py:185
  111.4 2.9 %slice_reduce_fusion.2 = (f32[8,11520]{1,0:T(8,128)S(1)}, f32[8,11520]{1,0:T(8,128)S(1)}, f32[8,11520]{1,0:T(8,128)S(1)}) fusion(f32[3,8,11520]{2,0,1:T(4,128)S(1)} %convert_element_type.100), kind=kLoop, calls=%fused_computation.158 | loop fusion | bytes 2211840 | tf_op jit(solution)/shard_map/slice | solution.py:231
  116.0 1.0 slice.397
  117.0 13.5 %all-to-all-done.1 = f32[2,8,11520]{2,0,1:T(2,128)} async-done(((f32[2,8,11520]{2,0,1:T(2,128)}), f32[2,8,11520]{2,0,1:T(2,128)}, u32[]{:S(2)}, u32[]{:S(2)}) %all-to-all-start.1) | async-done | bytes 737312 | tf_op jit(solution)/shard_map/all_to_all | solution.py:185
  130.5 2.0 %copy.14 = f32[2,8,11520]{2,1,0:T(8,128)} copy(f32[2,8,11520]{2,0,1:T(2,128)} %all-to-all-done.1) | data formatting | bytes 1474560 | tf_op jit(solution)/shard_map/all_to_all | solution.py:185
  132.6 3.0 %reshape.203 = f32[2,8,144,80]{3,2,1,0:T(8,128)} reshape(f32[2,8,11520]{2,1,0:T(8,128)} %copy.14) | data formatting | bytes 1474560 | tf_op jit(solution)/shard_map/reshape | solution.py:185
  135.7 1.2 copy-done
  138.6 1.1 fusion.12
  140.0 1.1 fusion.19
  141.3 1.1 fusion.26
  142.7 1.3 fusion.33
  144.2 1.1 fusion.40
  145.6 1.1 fusion.47
  148.7 1.4 slice_add_fusion
  150.9 19.4 %all_to_all.15 = f32[2,8,8192]{2,0,1:T(2,128)S(1)} all-to-all(f32[2,8,8192]{2,0,1:T(2,128)S(1)} %copy.15), channel_id=1, replica_groups=mesh['sec'=8,'strip'=4] {'sec'}, dimensions={1} | all-to-all | bytes 1048576 | tf_op jit(solution)/shard_map/all_to_all | solution.py:261
  (88 shorter events, 25.6 us)
Async XLA Ops:
  0.8 10.2 %copy-start.3 = (s32[1,128,512]{2,1,0:T(8,128)S(1)}, s32[1,128,512]{2,1,0:T(8,128)}, u32[]{:S(2)}) copy-start(s32[1,128,512]{2,1,0:T(8,128)} %param.7) | copy-start | bytes 786436
  0.8 10.2 %collective-permute-start = (bf16[3,2048]{1,0:T(4,128)(2,1)S(1)}, bf16[3,2048]{1,0:T(4,128)(2,1)S(1)}, u32[]{:S(2)}, u32[]{:S(2)}) collective-permute-start(bf16[3,2048]{1,0:T(4,128)(2,1)S(1)} %get-tuple-element.25), channel_id=1, source_target_pairs={{1,0},{2,1},{3,2},{5,4},{6,5},{7,6},{9,8},{10,9},{11,10},{13,12},{... | collective-permute-start | bytes 36872 | tf_op jit(solution)/shard_map/ppermute | solution.py:19
  2.2 13.9 %copy-start.1 = (bf16[1,512,2048]{2,1,0:T(8,128)(2,1)S(1)}, bf16[1,512,2048]{2,1,0:T(8,128)(2,1)}, u32[]{:S(2)}) copy-start(bf16[1,512,2048]{2,1,0:T(8,128)(2,1)} %param.4) | copy-start | bytes 6291460
  5.1 59.8 %collective-permute-start.4 = (bf16[256,2048]{1,0:T(8,128)(2,1)}, bf16[256,2048]{1,0:T(8,128)(2,1)}, u32[]{:S(2)}, u32[]{:S(2)}) collective-permute-start(bf16[256,2048]{1,0:T(8,128)(2,1)} %get-tuple-element.27), channel_id=1, source_target_pairs={{0,4},{4,8},{8,12},{12,16},{16,20},{20,24},{24,28},{1,5},{5,9},{9,... | collective-permute-start | bytes 3145736 | tf_op jit(solution)/shard_map/ppermute | solution.py:19
  12.1 7.0 %collective-permute-start.1 = (bf16[3,8,512]{2,1,0:T(8,128)(2,1)S(1)}, bf16[3,8,512]{2,1,0:T(8,128)(2,1)S(1)}, u32[]{:S(2)}, u32[]{:S(2)}) collective-permute-start(bf16[3,8,512]{2,1,0:T(8,128)(2,1)S(1)} %get-tuple-element.52), channel_id=1, source_target_pairs={{0,1},{1,2},{2,3},{4,5},{5,6},{6,7},{8,9},{9,10},{10,11},{12,13},{... | collective-permute-start | bytes 73736 | tf_op jit(solution)/shard_map/ppermute | solution.py:30
  14.9 4.2 %collective-permute-start.2 = (bf16[3,8,512]{2,1,0:T(8,128)(2,1)S(1)}, bf16[3,8,512]{2,1,0:T(8,128)(2,1)S(1)}, u32[]{:S(2)}, u32[]{:S(2)}) collective-permute-start(bf16[3,8,512]{2,1,0:T(8,128)(2,1)S(1)} %get-tuple-element.53), channel_id=1, source_target_pairs={{1,0},{2,1},{3,2},{5,4},{6,5},{7,6},{9,8},{10,9},{11,10},{13,12},{... | collective-permute-start | bytes 73736 | tf_op jit(solution)/shard_map/ppermute | solution.py:32
  17.8 47.1 %collective-permute-start.3 = (bf16[259,2048]{1,0:T(8,128)(2,1)}, bf16[259,2048]{1,0:T(8,128)(2,1)}, u32[]{:S(2)}, u32[]{:S(2)}) collective-permute-start(bf16[259,2048]{1,0:T(8,128)(2,1)} %get-tuple-element.23), channel_id=1, source_target_pairs={{4,0},{8,4},{12,8},{16,12},{20,16},{24,20},{28,24},{5,1},{9,5},{13... | collective-permute-start | bytes 3182600 | tf_op jit(solution)/shard_map/ppermute | solution.py:19
  23.0 11.1 %copy-start.4 = (s32[25,2]{0,1:T(2,128)S(1)}, s32[25,2]{0,1:T(2,128)}, u32[]{:S(2)}) copy-start(s32[25,2]{0,1:T(2,128)} %param.5) | copy-start | bytes 604
  26.4 38.5 %all-to-all-start = ((bf16[3,8,11520]{2,0,1:T(4,128)(2,1)}), bf16[3,8,11520]{2,0,1:T(4,128)(2,1)S(1)}, u32[]{:S(2)}, u32[]{:S(2)}) async-start(bf16[3,8,11520]{2,0,1:T(4,128)(2,1)} %constant_dynamic-update-slice_fusion), calls=%async_computation | async-start | bytes 1474560 | tf_op jit(solution)/shard_map/all_to_all | solution.py:219
  33.4 47.0 %collective-permute-start.6 = (bf16[3,2048]{1,0:T(4,128)(2,1)S(1)}, bf16[3,2048]{1,0:T(4,128)(2,1)S(1)}, u32[]{:S(2)}, u32[]{:S(2)}) collective-permute-start(bf16[3,2048]{1,0:T(4,128)(2,1)S(1)} %get-tuple-element.24), channel_id=1, source_target_pairs={{4,1},{5,2},{6,3},{8,5},{9,6},{10,7},{12,9},{13,10},{14,11},{16,13... | collective-permute-start | bytes 36872 | tf_op jit(solution)/shard_map/ppermute | solution.py:195
  77.9 17.1 %collective-permute-start.5 = (f32[2,8,512]{2,1,0:T(8,128)S(1)}, f32[2,8,512]{2,1,0:T(8,128)S(1)}, u32[]{:S(2)}, u32[]{:S(2)}) collective-permute-start(f32[2,8,512]{2,1,0:T(8,128)S(1)} %slice.384), channel_id=1, source_target_pairs={{0,1},{1,2},{2,3},{4,5},{5,6},{6,7},{8,9},{9,10},{10,11},{12,13},{... | collective-permute-start | bytes 98312 | tf_op jit(solution)/shard_map/ppermute | solution.py:30
  93.7 4.4 %collective-permute-start.7 = (f32[2,8,512]{2,1,0:T(8,128)S(1)}, f32[2,8,512]{2,1,0:T(8,128)S(1)}, u32[]{:S(2)}, u32[]{:S(2)}) collective-permute-start(f32[2,8,512]{2,1,0:T(8,128)S(1)} %slice.385), channel_id=1, source_target_pairs={{1,0},{2,1},{3,2},{5,4},{6,5},{7,6},{9,8},{10,9},{11,10},{13,12},{... | collective-permute-start | bytes 98312 | tf_op jit(solution)/shard_map/ppermute | solution.py:32
  105.0 25.5 %all-to-all-start.1 = ((f32[2,8,11520]{2,0,1:T(2,128)}), f32[2,8,11520]{2,0,1:T(2,128)}, u32[]{:S(2)}, u32[]{:S(2)}) async-start(f32[2,8,11520]{2,0,1:T(2,128)} %constant_dynamic-update-slice_fusion.8), calls=%async_computation.1 | async-start | bytes 1474560 | tf_op jit(solution)/shard_map/all_to_all | solution.py:185
  135.6 1.3 copy-start
  135.6 1.6 slice-start
  147.7 1.0 copy-start.2

commit v19 on v18

--- a/solution.py
+++ b/solution.py
@@ -1,5 +1,6 @@
 import jax
 import jax.numpy as jnp
+import numpy as np
 from jax import lax
 from jax.experimental import pallas as pl
 from jax.experimental.pallas import tpu as pltpu
@@ -179,7 +180,8 @@
     fields = extended(fields, (("strip", 1),), halo)
     width = fields.shape[2] // count
     columns = jnp.pad(fields, ((0, 0), (0, 0), (halo, halo)))
-    windows = jnp.stack([columns[:, :, j * width : (j + 1) * width + 2 * halo] for j in range(count)], axis=1)
+    index = np.arange(count)[:, None] * width + np.arange(width + 2 * halo)[None, :]
+    windows = jnp.moveaxis(columns[:, :, index], 2, 1)
     shape = windows.shape
     flat = windows.reshape(shape[0], shape[1], shape[2] * shape[3])
     return lax.all_to_all(flat, "sec", split_axis=1, concat_axis=1, tiled=True).reshape(shape)

time: 173 us -> 172 us (level)
    gather x0 -> x2, local copies, waits for them, and re-layouts: none -> 5.51 us  [tiles_with_halo(): windows = jnp.moveaxis(columns[:, :, index], 2, 1)]
    unnamed x25 -> x21, local copies, waits for them, and re-layouts: 11.5 us -> 7.54 us
    all_to_all x1 -> x0, local copies, waits for them, and re-layouts: 2.03 us -> none  [tiles_with_halo(): lax.all_to_all(flat, 'sec', split_axis=1, concat_axis=1, tiled=True)]
    another operation x9 -> x0, local copies, waits for them, and re-layouts: 2.03 us -> none  [tiles_with_halo(): jnp.stack([columns[:, :, j * width:(j + 1) * width + 2 * halo] for j in r...]
    reshape x0 -> x2, local copies, waits for them, and re-layouts: none -> 1.79 us  [tiles_with_halo(): flat = windows.reshape(shape[0], shape[1], shape[2] * shape[3])]
where the time goes in v19:
time: 172 us
  waiting for transfers between devices  45.5 us (26%)
  local copies, waits for them, and re-layouts  34.3 us (20%)
  starting transfers between devices  30.4 us (18%)
  Pallas kernels  24.7 us (14%)
  blocking collectives  19.4 us (11%)
  other arithmetic  16.8 us (10%)
    all_to_all x1, waiting for transfers between devices, shards(): flat = lax.all_to_all(flat, 'sec', split_axis=1, concat_axis=1, tiled=True)  29.1 us
    pallas_call x2, Pallas kernels, section_flow(): pl.pallas_call(flow_kernel, grid_spec=grid_spec, out_shape=jax.ShapeDtype...  24.7 us
    all_to_all x1, blocking collectives, shards(): lax.all_to_all(flat, 'sec', split_axis=1, concat_axis=1, tiled=True)  19.4 us
    all_to_all x1, waiting for transfers between devices, tiles_with_halo(): lax.all_to_all(flat, 'sec', split_axis=1, concat_axis=1, tiled=True)  13.5 us
    ppermute x3, starting transfers between devices, shifted_2(): return lax.ppermute(shard, axis, pairs)  8.54 us
    add x7, other arithmetic, advance(): return positions + relax_rate * force / (1.0 + diagonal)  8.23 us
    unnamed x21, local copies, waits for them, and re-layouts  7.54 us
    all_to_all x1, starting transfers between devices, shards(): flat = lax.all_to_all(flat, 'sec', split_axis=1, concat_axis=1, tiled=True)  7.01 us
  transfers between devices with their start and end apart: 10, of which 3 were waited for; matrix products, arithmetic and copies ran while one was open for 13% of the time, Pallas kernels for 14%

profile of v19, /device:TPU:0, one launch (start us, length us, event | category | flops | bytes accessed | tf_op | source)
XLA Modules:
  0.0 171.5 jit_solution(9176602896398570479)
XLA Ops:
  0.8 1.4 collective-permute-start
  2.2 2.9 %slice_bitcast_fusion.2 = (bf16[256,2048]{1,0:T(8,128)(2,1)S(1)}, bf16[256,2048]{1,0:T(8,128)(2,1)}) fusion(bf16[1,512,2048]{2,1,0:T(8,128)(2,1)} %param.6), kind=kLoop, calls=%fused_computation.142 | loop fusion | bytes 4194304 | tf_op jit(solution)/shard_map/slice | solution.py:224
  5.1 5.8 %collective-permute-start.4 = (bf16[256,2048]{1,0:T(8,128)(2,1)}, bf16[256,2048]{1,0:T(8,128)(2,1)}, u32[]{:S(2)}, u32[]{:S(2)}) collective-permute-start(bf16[256,2048]{1,0:T(8,128)(2,1)} %get-tuple-element.27), channel_id=1, source_target_pairs={{0,4},{4,8},{8,12},{12,16},{16,20},{20,24},{24,28},{1,5},{5,9},{9,... | collective-permute-start | bytes 3145736 | tf_op jit(solution)/shard_map/ppermute | solution.py:20
  11.0 1.1 fusion.100
  12.1 2.8 %collective-permute-start.1 = (bf16[3,8,512]{2,1,0:T(8,128)(2,1)S(1)}, bf16[3,8,512]{2,1,0:T(8,128)(2,1)S(1)}, u32[]{:S(2)}, u32[]{:S(2)}) collective-permute-start(bf16[3,8,512]{2,1,0:T(8,128)(2,1)S(1)} %get-tuple-element.44), channel_id=1, source_target_pairs={{0,1},{1,2},{2,3},{4,5},{5,6},{6,7},{8,9},{9,10},{10,11},{12,13},{... | collective-permute-start | bytes 73736 | tf_op jit(solution)/shard_map/ppermute | solution.py:31
  14.9 1.3 collective-permute-start.2
  16.2 1.6 slice_bitcast_fusion
  17.8 1.3 collective-permute-start.3
  26.4 7.0 %all-to-all-start = ((bf16[3,8,11520]{2,0,1:T(4,128)(2,1)}), bf16[3,8,11520]{2,0,1:T(4,128)(2,1)S(1)}, u32[]{:S(2)}, u32[]{:S(2)}) async-start(bf16[3,8,11520]{2,0,1:T(4,128)(2,1)} %constant_dynamic-update-slice_fusion), calls=%async_computation | async-start | bytes 1474560 | tf_op jit(solution)/shard_map/all_to_all | solution.py:221
  34.4 1.5 fusion.61.following_ref
  35.9 29.1 %all-to-all-done = bf16[3,8,11520]{2,0,1:T(4,128)(2,1)S(1)} async-done(((bf16[3,8,11520]{2,0,1:T(4,128)(2,1)}), bf16[3,8,11520]{2,0,1:T(4,128)(2,1)S(1)}, u32[]{:S(2)}, u32[]{:S(2)}) %all-to-all-start) | async-done | bytes 552992 | tf_op jit(solution)/shard_map/all_to_all | solution.py:221
  65.0 12.9 %shard_map.64 = f32[2,64,512]{2,1,0:T(8,128)S(1)} custom-call(s32[25,2]{1,0:T(8,128)S(1)} %copy.15.offsets_ref, bf16[256,2048]{1,0:T(8,128)(2,1)} %collective-permute-done.4.current_ref, bf16[288,2048]{1,0:T(8,128)(2,1)S(1)} %fusion.61.following_ref, bf16[512,512]{1,0:T(8,128)(2,1)S(1)} %fusion.96.permute_ref), custom_call_target="tpu_custom_call" | custom-call | tf_op jit(solution)/shard_map/pallas_call | solution.py:148
  77.9 2.5 %collective-permute-start.5 = (f32[2,8,512]{2,1,0:T(8,128)S(1)}, f32[2,8,512]{2,1,0:T(8,128)S(1)}, u32[]{:S(2)}, u32[]{:S(2)}) collective-permute-start(f32[2,8,512]{2,1,0:T(8,128)S(1)} %slice.348), channel_id=1, source_target_pairs={{0,1},{1,2},{2,3},{4,5},{5,6},{6,7},{8,9},{9,10},{10,11},{12,13},{... | collective-permute-start | bytes 98312 | tf_op jit(solution)/shard_map/ppermute | solution.py:31
  80.4 1.5 select_maximum_fusion.following_ref
  82.0 11.7 %shard_map.65 = f32[2,64,512]{2,1,0:T(8,128)S(1)} custom-call(s32[25,2]{1,0:T(8,128)S(1)} %copy.15.offsets_ref, bf16[256,2048]{1,0:T(8,128)(2,1)S(1)} %get-tuple-element.26.current_ref, bf16[288,2048]{1,0:T(8,128)(2,1)S(1)} %select_maximum_fusion.following_ref, bf16[512,512]{1,0:T(8,128)(2,1)S(1)} %fusion.96.permute_ref), custom_call_target="tpu_custom_call" | custom-call | tf_op jit(solution)/shard_map/pallas_call | solution.py:148
  93.7 1.5 collective-permute-start.7
  95.2 2.9 %collective-permute-done.7 = f32[2,8,512]{2,1,0:T(8,128)S(1)} collective-permute-done((f32[2,8,512]{2,1,0:T(8,128)S(1)}, f32[2,8,512]{2,1,0:T(8,128)S(1)}, u32[]{:S(2)}, u32[]{:S(2)}) %collective-permute-start.7) | collective-permute-done | bytes 32800 | tf_op jit(solution)/shard_map/ppermute | solution.py:33
  99.1 3.5 %gather_fusion = f32[640,2,144]{2,1,0:T(2,128)S(1)} fusion(f32[2,144,528]{1,0,2:T(2,128)S(1)} %pad.110.clone, s32[1024]{0:T(1024)S(1)} %pad_clamp_fusion), kind=kCustom, calls=%fused_computation | custom fusion | bytes 1477120 | tf_op jit(solution)/shard_map/gather | solution.py:184
  102.6 2.0 %copy.18 = f32[8,80,2,144]{1,3,0,2:T(8,128)S(1)} copy(f32[8,80,2,144]{3,2,1,0:T(2,128)S(1)} %bitcast.30) | data formatting | bytes 1474560 | tf_op jit(solution)/shard_map/gather | solution.py:184
  105.1 1.3 copy.19
  106.4 6.2 %all-to-all-start.1 = ((f32[2,8,11520]{2,0,1:T(2,128)}), f32[2,8,11520]{2,0,1:T(2,128)}, u32[]{:S(2)}, u32[]{:S(2)}) async-start(f32[2,8,11520]{2,0,1:T(2,128)} %copy.19), calls=%async_computation.1 | async-start | bytes 1474560 | tf_op jit(solution)/shard_map/all_to_all | solution.py:187
  112.7 2.9 %slice_reduce_fusion.2 = (f32[8,11520]{1,0:T(8,128)S(1)}, f32[8,11520]{1,0:T(8,128)S(1)}, f32[8,11520]{1,0:T(8,128)S(1)}) fusion(f32[3,8,11520]{2,0,1:T(4,128)S(1)} %convert_element_type.100), kind=kLoop, calls=%fused_computation.157 | loop fusion | bytes 2211840 | tf_op jit(solution)/shard_map/slice | solution.py:233
  118.4 13.5 %all-to-all-done.1 = f32[2,8,11520]{2,0,1:T(2,128)} async-done(((f32[2,8,11520]{2,0,1:T(2,128)}), f32[2,8,11520]{2,0,1:T(2,128)}, u32[]{:S(2)}, u32[]{:S(2)}) %all-to-all-start.1) | async-done | bytes 737312 | tf_op jit(solution)/shard_map/all_to_all | solution.py:187
  131.9 3.2 %reshape.190 = f32[2,8,144,80]{3,2,0,1:T(8,128)} reshape(f32[2,8,11520]{2,0,1:T(2,128)} %all-to-all-done.1) | data formatting | bytes 1474560 | tf_op jit(solution)/shard_map/reshape | solution.py:187
  135.2 1.2 copy-done
  137.8 1.1 fusion.12
  139.1 1.1 fusion.19
  140.5 1.1 fusion.26
  141.8 1.3 fusion.33
  143.4 1.1 fusion.40
  147.9 1.4 slice_add_fusion
  150.1 19.4 %all_to_all.15 = f32[2,8,8192]{2,0,1:T(2,128)S(1)} all-to-all(f32[2,8,8192]{2,0,1:T(2,128)S(1)} %copy.22), channel_id=1, replica_groups=mesh['sec'=8,'strip'=4] {'sec'}, dimensions={1} | all-to-all | bytes 1048576 | tf_op jit(solution)/shard_map/all_to_all | solution.py:263
  (77 shorter events, 22.0 us)
Async XLA Ops:
  0.8 10.2 %copy-start.3 = (s32[1,128,512]{2,1,0:T(8,128)S(1)}, s32[1,128,512]{2,1,0:T(8,128)}, u32[]{:S(2)}) copy-start(s32[1,128,512]{2,1,0:T(8,128)} %param.9) | copy-start | bytes 786436
  0.8 10.2 %collective-permute-start = (bf16[3,2048]{1,0:T(4,128)(2,1)S(1)}, bf16[3,2048]{1,0:T(4,128)(2,1)S(1)}, u32[]{:S(2)}, u32[]{:S(2)}) collective-permute-start(bf16[3,2048]{1,0:T(4,128)(2,1)S(1)} %get-tuple-element.25), channel_id=1, source_target_pairs={{1,0},{2,1},{3,2},{5,4},{6,5},{7,6},{9,8},{10,9},{11,10},{13,12},{... | collective-permute-start | bytes 36872 | tf_op jit(solution)/shard_map/ppermute | solution.py:20
  2.2 14.0 %copy-start.1 = (bf16[1,512,2048]{2,1,0:T(8,128)(2,1)S(1)}, bf16[1,512,2048]{2,1,0:T(8,128)(2,1)}, u32[]{:S(2)}) copy-start(bf16[1,512,2048]{2,1,0:T(8,128)(2,1)} %param.6) | copy-start | bytes 6291460
  5.1 59.8 %collective-permute-start.4 = (bf16[256,2048]{1,0:T(8,128)(2,1)}, bf16[256,2048]{1,0:T(8,128)(2,1)}, u32[]{:S(2)}, u32[]{:S(2)}) collective-permute-start(bf16[256,2048]{1,0:T(8,128)(2,1)} %get-tuple-element.27), channel_id=1, source_target_pairs={{0,4},{4,8},{8,12},{12,16},{16,20},{20,24},{24,28},{1,5},{5,9},{9,... | collective-permute-start | bytes 3145736 | tf_op jit(solution)/shard_map/ppermute | solution.py:20
  12.1 7.0 %collective-permute-start.1 = (bf16[3,8,512]{2,1,0:T(8,128)(2,1)S(1)}, bf16[3,8,512]{2,1,0:T(8,128)(2,1)S(1)}, u32[]{:S(2)}, u32[]{:S(2)}) collective-permute-start(bf16[3,8,512]{2,1,0:T(8,128)(2,1)S(1)} %get-tuple-element.44), channel_id=1, source_target_pairs={{0,1},{1,2},{2,3},{4,5},{5,6},{6,7},{8,9},{9,10},{10,11},{12,13},{... | collective-permute-start | bytes 73736 | tf_op jit(solution)/shard_map/ppermute | solution.py:31
  14.9 4.2 %collective-permute-start.2 = (bf16[3,8,512]{2,1,0:T(8,128)(2,1)S(1)}, bf16[3,8,512]{2,1,0:T(8,128)(2,1)S(1)}, u32[]{:S(2)}, u32[]{:S(2)}) collective-permute-start(bf16[3,8,512]{2,1,0:T(8,128)(2,1)S(1)} %get-tuple-element.45), channel_id=1, source_target_pairs={{1,0},{2,1},{3,2},{5,4},{6,5},{7,6},{9,8},{10,9},{11,10},{13,12},{... | collective-permute-start | bytes 73736 | tf_op jit(solution)/shard_map/ppermute | solution.py:33
  17.8 47.1 %collective-permute-start.3 = (bf16[259,2048]{1,0:T(8,128)(2,1)}, bf16[259,2048]{1,0:T(8,128)(2,1)}, u32[]{:S(2)}, u32[]{:S(2)}) collective-permute-start(bf16[259,2048]{1,0:T(8,128)(2,1)} %get-tuple-element.23), channel_id=1, source_target_pairs={{4,0},{8,4},{12,8},{16,12},{20,16},{24,20},{28,24},{5,1},{9,5},{13... | collective-permute-start | bytes 3182600 | tf_op jit(solution)/shard_map/ppermute | solution.py:20
  23.0 11.0 %copy-start.5 = (s32[25,2]{0,1:T(2,128)S(1)}, s32[25,2]{0,1:T(2,128)}, u32[]{:S(2)}) copy-start(s32[25,2]{0,1:T(2,128)} %param.7) | copy-start | bytes 604
  26.4 38.5 %all-to-all-start = ((bf16[3,8,11520]{2,0,1:T(4,128)(2,1)}), bf16[3,8,11520]{2,0,1:T(4,128)(2,1)S(1)}, u32[]{:S(2)}, u32[]{:S(2)}) async-start(bf16[3,8,11520]{2,0,1:T(4,128)(2,1)} %constant_dynamic-update-slice_fusion), calls=%async_computation | async-start | bytes 1474560 | tf_op jit(solution)/shard_map/all_to_all | solution.py:221
  33.4 47.0 %collective-permute-start.6 = (bf16[3,2048]{1,0:T(4,128)(2,1)S(1)}, bf16[3,2048]{1,0:T(4,128)(2,1)S(1)}, u32[]{:S(2)}, u32[]{:S(2)}) collective-permute-start(bf16[3,2048]{1,0:T(4,128)(2,1)S(1)} %get-tuple-element.24), channel_id=1, source_target_pairs={{4,1},{5,2},{6,3},{8,5},{9,6},{10,7},{12,9},{13,10},{14,11},{16,13... | collective-permute-start | bytes 36872 | tf_op jit(solution)/shard_map/ppermute | solution.py:197
  77.9 17.3 %collective-permute-start.5 = (f32[2,8,512]{2,1,0:T(8,128)S(1)}, f32[2,8,512]{2,1,0:T(8,128)S(1)}, u32[]{:S(2)}, u32[]{:S(2)}) collective-permute-start(f32[2,8,512]{2,1,0:T(8,128)S(1)} %slice.348), channel_id=1, source_target_pairs={{0,1},{1,2},{2,3},{4,5},{5,6},{6,7},{8,9},{9,10},{10,11},{12,13},{... | collective-permute-start | bytes 98312 | tf_op jit(solution)/shard_map/ppermute | solution.py:31
  81.9 13.3 %copy-start.4 = (s32[640]{0:T(1024)S(1)}, s32[640]{0:T(1024)}, u32[]{:S(2)}) copy-start(s32[640]{0:T(1024)} %constant.150) | copy-start | bytes 7684
  93.7 4.4 %collective-permute-start.7 = (f32[2,8,512]{2,1,0:T(8,128)S(1)}, f32[2,8,512]{2,1,0:T(8,128)S(1)}, u32[]{:S(2)}, u32[]{:S(2)}) collective-permute-start(f32[2,8,512]{2,1,0:T(8,128)S(1)} %slice.349), channel_id=1, source_target_pairs={{1,0},{2,1},{3,2},{5,4},{6,5},{7,6},{9,8},{10,9},{11,10},{13,12},{... | collective-permute-start | bytes 98312 | tf_op jit(solution)/shard_map/ppermute | solution.py:33
  106.4 25.5 %all-to-all-start.1 = ((f32[2,8,11520]{2,0,1:T(2,128)}), f32[2,8,11520]{2,0,1:T(2,128)}, u32[]{:S(2)}, u32[]{:S(2)}) async-start(f32[2,8,11520]{2,0,1:T(2,128)} %copy.19), calls=%async_computation.1 | async-start | bytes 1474560 | tf_op jit(solution)/shard_map/all_to_all | solution.py:187
  135.1 1.3 copy-start
  146.8 1.0 copy-start.2
